TPU v7x, 32 devices: a whole 2x2x4 slice. The times are simulated.
32 devices in a mesh: section: 2 (over core), row: 4 (over y, x), col: 4 (over z).
Axes of the slice: x: 2, y: 2, z: 4, core: 2. Of those that a mesh axis runs over, the one named last changes fastest.
Arguments:
- checkpoints: bfloat16 [2, 4, 64, 128, 128], P('section', None, 'row', 'col'), may hold values from -1 to 1
- kernels: bfloat16 [4, 3, 3, 128, 128], P('section'), may hold values from -0.25 to 0.25
- cotangent: bfloat16 [4, 64, 128, 128], P(None, 'row', 'col'), may hold values from -1.5 to 1.5
- plan: int32 [4], replicated, may hold values from 0 to 3, each once
Outputs:
- boundary_grad: bfloat16 [2, 4, 64, 128, 128], P('section', None, 'row', 'col')
- kernel_grad: float32 [4, 3, 3, 128, 128], P('section')
Inputs may be any that keep to these rules, and one draw needn't show every extreme that they name: plan names each of the 4 microbatches exactly once; slot k of cotangent belongs to microbatch plan[k].
All inputs are finite; a program needn't handle non-finite values.
Results may differ from a plain program's by a relative error of at most 0.015.
Values may be sent and summed in bfloat16 or wider, within the bound.
No kernel may reach another device: no remote copies, remote signals or barrier semaphores. Data moves between devices by JAX's collectives and lax.ppermute only.
A program may use at most 64 MiB of HBM per device.

v0:
```python
import jax
import jax.numpy as jnp
from jax import lax
from jax.sharding import PartitionSpec as P

AXES = ("section", "row", "col")


def sizes():
    return tuple(lax.axis_size(axis) for axis in AXES)


def flat_index(position, shape):
    section, row, col = position
    return (section * shape[1] + row) * shape[2] + col


def rim_piece(block, width, dr, dc):
    rows, cols = block.shape[1], block.shape[2]
    row_span = {-1: (rows - width, rows), 0: (0, rows), 1: (0, width)}[dr]
    col_span = {-1: (cols - width, cols), 0: (0, cols), 1: (0, width)}[dc]
    return block[:, row_span[0] : row_span[1], col_span[0] : col_span[1]]


def from_neighbours(block, width, dim, from_section, sections_used):
    shape = sizes()
    parts = []
    for step in (-1, 0, 1):
        size = block.shape[dim]
        span = {-1: (size - width, size), 0: (0, size), 1: (0, width)}[step]
        piece = lax.slice_in_dim(block, span[0], span[1], axis=dim)
        if from_section == 0 and step == 0:
            parts.append(piece)
            continue
        pairs = []
        for s in sections_used:
            for r in range(shape[1]):
                for c in range(shape[2]):
                    source = [s + from_section, r, c]
                    source[dim] += step
                    if all(0 <= source[k] < shape[k] for k in range(3)):
                        pairs.append((flat_index(source, shape), flat_index((s, r, c), shape)))
        parts.append(lax.ppermute(piece, AXES, pairs))
    return jnp.concatenate(parts, axis=dim)


def with_rim(block, width, from_section, sections_used):
    rows_done = from_neighbours(block, width, 1, from_section, sections_used)
    return from_neighbours(rows_done, width, 2, 0, sections_used)


def inside_mask(tile_rows, tile_cols, width):
    image_rows = tile_rows * lax.axis_size("row")
    image_cols = tile_cols * lax.axis_size("col")
    rows = lax.axis_index("row") * tile_rows - width + jnp.arange(tile_rows + 2 * width)
    cols = lax.axis_index("col") * tile_cols - width + jnp.arange(tile_cols + 2 * width)
    row_ok = (rows >= 0) & (rows < image_rows)
    col_ok = (cols >= 0) & (cols < image_cols)
    return (row_ok[:, None] & col_ok[None, :])[None, :, :, None]


def convolve(padded, kernel):
    return lax.conv_general_dilated(
        padded,
        kernel,
        (1, 1),
        "VALID",
        dimension_numbers=("NHWC", "HWIO", "NHWC"),
        preferred_element_type=jnp.float32,
    )


def kernel_terms(padded, signal):
    terms = lax.conv_general_dilated(
        padded,
        signal,
        (1, 1),
        "VALID",
        dimension_numbers=("CHWN", "IHWO", "NHWC"),
        preferred_element_type=jnp.float32,
    )
    return jnp.transpose(terms, (1, 2, 0, 3))


def crop(block, width):
    return block[:, width : block.shape[1] - width, width : block.shape[2] - width]


def summed_over_tiles(grads):
    shape = sizes()

    def distances(count):
        found, distance = [], 1
        while distance < count:
            found.append(distance)
            distance *= 2
        return found

    def exchange(values, axis, distance):
        count = lax.axis_size(axis)
        return lax.ppermute(values, axis, [(i, i ^ distance) for i in range(count)])

    current = grads.reshape(-1)
    kept = []
    for distance in distances(shape[1]):
        half = current.shape[0] // 2
        upper = (lax.axis_index("row") // distance) % 2 == 1
        low, high = current[:half], current[half:]
        send = jnp.where(upper, low, high).astype(jnp.bfloat16)
        mine = jnp.where(upper, high, low).astype(jnp.bfloat16)
        other = exchange(send, "row", distance)
        current = mine.astype(jnp.float32) + other.astype(jnp.float32)
        kept.append((distance, upper))
    for distance in distances(shape[2]):
        rounded = current.astype(jnp.bfloat16)
        other = exchange(rounded, "col", distance)
        upper = (lax.axis_index("col") // distance) % 2 == 1
        first = jnp.where(upper, other, rounded).astype(jnp.float32)
        second = jnp.where(upper, rounded, other).astype(jnp.float32)
        current = first + second
    current = current.astype(jnp.bfloat16)
    for distance, upper in reversed(kept):
        other = exchange(current, "row", distance)
        current = jnp.where(
            upper, jnp.concatenate([other, current]), jnp.concatenate([current, other])
        )
    return current.astype(jnp.float32).reshape(grads.shape)


def local(checkpoints, kernels, cotangent, plan):
    sections_count, row_count, col_count = sizes()
    section_index = lax.axis_index("section")
    batches, tile_rows, tile_cols, channels = checkpoints.shape[1:]
    layer_count = kernels.shape[0]
    flipped = jnp.transpose(kernels[:, ::-1, ::-1], (0, 1, 2, 4, 3))
    inverse = jnp.sum(
        jnp.arange(batches)[:, None] * (plan[:, None] == jnp.arange(batches)[None, :]), axis=0
    )
    top_cotangent = jnp.take(cotangent, inverse, axis=0)

    deep = layer_count * (sections_count + 1) <= min(tile_rows, tile_cols)
    if deep and sections_count == 2 and batches % 2 == 0:
        return local_split(checkpoints, kernels, cotangent, plan)
    if deep:
        top_rim = [layer_count * (s + 1) for s in range(sections_count)]
    else:
        top_rim = [layer_count] * sections_count
    rim = top_rim[-1] + layer_count
    first = with_rim(checkpoints[0], rim, 0, range(sections_count))
    top_ext = with_rim(top_cotangent, top_rim[-1], 0, (sections_count - 1,))
    inputs_list = [first]
    current = first
    for layer_idx in range(layer_count):
        width = rim - layer_idx - 1
        current = jnp.tanh(convolve(current, kernels[layer_idx]))
        current = jnp.where(inside_mask(tile_rows, tile_cols, width), current, 0.0)
        current = current.astype(jnp.bfloat16)
        inputs_list.append(current)

    def backward(top_ext, top_width):
        gradient = top_ext.astype(jnp.float32)
        terms = [None] * layer_count
        for layer_idx in reversed(range(layer_count)):
            width = top_width - (layer_count - 1 - layer_idx)
            output = crop(inputs_list[layer_idx + 1], rim - layer_idx - 1 - width)
            output = output.astype(jnp.float32)
            signal = gradient * (1.0 - output * output)
            signal = jnp.where(inside_mask(tile_rows, tile_cols, width), signal, 0.0)
            signal = signal.astype(jnp.bfloat16)
            terms[layer_idx] = crop(signal, width)
            gradient = convolve(signal, flipped[layer_idx])
        return gradient.astype(jnp.bfloat16), terms

    def products(signals):
        return jnp.stack(
            [
                kernel_terms(crop(inputs_list[layer_idx], rim - layer_idx - 1), signals[layer_idx])
                for layer_idx in range(layer_count)
            ]
        )

    boundary = jnp.zeros((batches, tile_rows, tile_cols, channels), jnp.bfloat16)
    gathered = jnp.zeros((layer_count, 3, 3, channels, channels), jnp.float32)
    for tick in range(sections_count):
        active = sections_count - 1 - tick
        is_active = section_index == active
        if tick + 1 < sections_count or sections_count > 4:
            result, signals = backward(top_ext, top_rim[active])
        else:
            shapes = jax.eval_shape(lambda top: backward(top, top_rim[active]), top_ext)
            result, signals = lax.cond(
                is_active,
                lambda top: backward(top, top_rim[active]),
                lambda top: jax.tree.map(lambda v: jnp.zeros(v.shape, v.dtype), shapes),
                top_ext,
            )
        result_width = top_rim[active] - layer_count
        boundary = jnp.where(is_active, crop(result, result_width), boundary)
        if tick + 1 < sections_count:
            if deep:
                pairs = [
                    (flat_index((active, r, c), sizes()), flat_index((active - 1, r, c), sizes()))
                    for r in range(row_count)
                    for c in range(col_count)
                ]
                top_ext = lax.ppermute(result, AXES, pairs)
            else:
                top_ext = with_rim(result, layer_count, 1, (active - 1,))
        if sections_count > 4:
            terms = products(signals)
        else:
            terms = lax.cond(
                is_active, products, lambda unused: jnp.zeros_like(gathered), signals
            )
        gathered = jnp.where(is_active, terms, gathered)
    gathered = summed_over_tiles(gathered)
    kernel_grad = gathered / batches
    return (boundary[None], kernel_grad)


def section_chain(top_ext, top_width, inputs_list, rim, flipped_kernels):
    layer_count = len(flipped_kernels)
    tile_rows = inputs_list[0].shape[1] - 2 * rim
    tile_cols = inputs_list[0].shape[2] - 2 * rim
    gradient = top_ext.astype(jnp.float32)
    signals = [None] * layer_count
    for layer_idx in reversed(range(layer_count)):
        width = top_width - (layer_count - 1 - layer_idx)
        output = crop(inputs_list[layer_idx + 1], rim - layer_idx - 1 - width)
        output = output.astype(jnp.float32)
        signal = gradient * (1.0 - output * output)
        signal = jnp.where(inside_mask(tile_rows, tile_cols, width), signal, 0.0)
        signal = signal.astype(jnp.bfloat16)
        signals[layer_idx] = crop(signal, width)
        gradient = convolve(signal, flipped_kernels[layer_idx])
    return gradient.astype(jnp.bfloat16), signals


def local_split(checkpoints, kernels, cotangent, plan):
    section_index = lax.axis_index("section")
    batches, tile_rows, tile_cols, channels = checkpoints.shape[1:]
    layer_count = kernels.shape[0]
    half = batches // 2
    inverse = jnp.sum(
        jnp.arange(batches)[:, None] * (plan[:, None] == jnp.arange(batches)[None, :]), axis=0
    )
    top_cotangent = jnp.take(cotangent, inverse, axis=0)

    def swap(values):
        return lax.ppermute(values, "section", [(0, 1), (1, 0)])

    def by_section(mine, theirs, section):
        return jnp.where(section_index == section, mine, theirs)

    own = checkpoints[0]
    mine = lax.dynamic_slice_in_dim(own, section_index * half, half, 0)
    theirs = swap(lax.dynamic_slice_in_dim(own, (1 - section_index) * half, half, 0))
    other_kernels = swap(kernels)
    section_kernels = [by_section(kernels, other_kernels, s) for s in range(2)]

    top_rim = [layer_count * (s + 1) for s in range(2)]
    rims = [r + layer_count for r in top_rim]
    stacked = jnp.concatenate([by_section(mine, theirs, s) for s in range(2)], axis=0)
    stacked = with_rim(stacked, rims[1], 0, range(2))
    firsts = [crop(stacked[:half], rims[1] - rims[0]), stacked[half:]]
    group_cotangent = lax.dynamic_slice_in_dim(top_cotangent, section_index * half, half, 0)
    top_ext = with_rim(group_cotangent, top_rim[1], 0, range(2))

    results, partials = [None, None], [None, None]
    for s in (1, 0):
        rim = rims[s]
        inputs_list = [firsts[s]]
        current = firsts[s]
        for layer_idx in range(layer_count):
            current = jnp.tanh(convolve(current, section_kernels[s][layer_idx]))
            current = jnp.where(
                inside_mask(tile_rows, tile_cols, rim - layer_idx - 1), current, 0.0
            )
            current = current.astype(jnp.bfloat16)
            inputs_list.append(current)
        flipped = jnp.transpose(section_kernels[s][:, ::-1, ::-1], (0, 1, 2, 4, 3))
        top_ext, signals = section_chain(top_ext, top_rim[s], inputs_list, rim, flipped)
        results[s] = crop(top_ext, top_rim[s] - layer_count)
        partials[s] = jnp.stack(
            [
                kernel_terms(crop(inputs_list[layer_idx], rim - layer_idx - 1), signals[layer_idx])
                for layer_idx in range(layer_count)
            ]
        )

    mine_terms = by_section(partials[0], partials[1], 0)
    other_terms = by_section(partials[1], partials[0], 0)
    gathered = summed_over_tiles(mine_terms + swap(other_terms))
    mine_back = by_section(results[0], results[1], 0)
    other_back = swap(by_section(results[1], results[0], 0))
    boundary = jnp.where(
        section_index == 0,
        jnp.concatenate([mine_back, other_back], axis=0),
        jnp.concatenate([other_back, mine_back], axis=0),
    )
    return (boundary[None], gathered / batches)


def solution(mesh):
    return jax.shard_map(
        local,
        mesh=mesh,
        in_specs=(
            P("section", None, "row", "col", None),
            P("section", None, None, None, None),
            P(None, "row", "col", None),
            P(),
        ),
        out_specs=(P("section", None, "row", "col", None), P("section", None, None, None, None)),
        check_vma=False,
    )
```

profile of v0, /device:TPU:0, one launch (start us, length us, event | category | flops | bytes accessed | tf_op | source)
XLA Modules:
  0.0 133.7 jit_solution(7388934969608170302)
XLA Ops:
  5.1 5.4 %collective-permute-start = (bf16[2,4,32,128]{3,2,0,1:T(8,128)(2,1)S(1)}, bf16[2,4,32,128]{3,2,0,1:T(8,128)(2,1)S(1)}, u32[]{:S(2)}, u32[]{:S(2)}) collective-permute-start(bf16[2,4,32,128]{3,2,0,1:T(8,128)(2,1)S(1)} %get-tuple-element.30), channel_id=1, source_target_pairs={{0,4},{1,5},{2,6},{3,7},{4,8},{5,9},{6,10},{7,11},{8,12},{9,13},{1... | collective-permute-start | bytes 196616 | tf_op jit(solution)/shard_map/ppermute | solution.py:43
  13.8 5.5 %collective-permute-start.5 = (bf16[4,6,32,128]{3,0,2,1:T(4,128)(2,1)S(1)}, bf16[4,6,32,128]{3,0,2,1:T(4,128)(2,1)S(1)}, u32[]{:S(2)}, u32[]{:S(2)}) collective-permute-start(bf16[4,6,32,128]{3,0,2,1:T(4,128)(2,1)S(1)} %get-tuple-element.22), channel_id=1, source_target_pairs={{0,4},{1,5},{2,6},{3,7},{4,8},{5,9},{6,10},{7,11},{8,12},{9,13},{1... | collective-permute-start | bytes 589832 | tf_op jit(solution)/shard_map/ppermute | solution.py:43
  21.4 5.2 %collective-permute-start.2 = (bf16[2,24,4,128]{3,2,0,1:T(4,128)(2,1)}, bf16[2,24,4,128]{3,2,0,1:T(4,128)(2,1)}, u32[]{:S(2)}, u32[]{:S(2)}) collective-permute-start(bf16[2,24,4,128]{3,2,0,1:T(4,128)(2,1)} %get-tuple-element.28), channel_id=1, source_target_pairs={{0,1},{1,2},{2,3},{4,5},{5,6},{6,7},{8,9},{9,10},{10,11},{12,13},{... | collective-permute-start | bytes 147464 | tf_op jit(solution)/shard_map/ppermute | solution.py:43
  28.1 4.7 %collective-permute-start.7 = (bf16[4,28,6,128]{3,0,2,1:T(4,128)(2,1)S(1)}, bf16[4,28,6,128]{3,0,2,1:T(4,128)(2,1)S(1)}, u32[]{:S(2)}, u32[]{:S(2)}) collective-permute-start(bf16[4,28,6,128]{3,0,2,1:T(4,128)(2,1)S(1)} %get-tuple-element.16), channel_id=1, source_target_pairs={{0,1},{1,2},{2,3},{4,5},{5,6},{6,7},{8,9},{9,10},{10,11},{12,13},{... | collective-permute-start | bytes 516104 | tf_op jit(solution)/shard_map/ppermute | solution.py:43
  35.6 2.9 %pad_maximum_fusion = bf16[4,28,44,128]{3,0,2,1:T(4,128)(2,1)S(1)} fusion(bf16[4,28,6,128]{3,0,2,1:T(4,128)(2,1)S(1)} %collective-permute-done.8, bf16[4,6,32,128]{3,0,2,1:T(4,128)(2,1)S(1)} %collective-permute-done.6, bf16[2,16,32,128]{3,0,2,1:T(2,128)(2,1)S(1)} %get-tuple-element.25, bf16[2,16,32,128]{3,0,2,1:T(2,128)(2,1)S(1)} %get-tuple-element.24, ...), kind=kLoop, calls=%fused_computation.24 | loop fusion | flops 7569408 | bytes 2523136 | tf_op jit(solution)/shard_map/concatenate | solution.py:44
  38.5 1.7 %slice_bitcast_fusion = (bf16[28,2,44,128]{3,1,2,0:T(2,128)(2,1)}, bf16[28,2,44,128]{3,1,2,0:T(2,128)(2,1)S(1)}) fusion(bf16[4,28,44,128]{3,0,2,1:T(4,128)(2,1)S(1)} %pad_maximum_fusion), kind=kLoop, calls=%fused_computation.118 | loop fusion | bytes 2523136 | tf_op jit(solution)/shard_map/slice | solution.py:265
  40.9 1.7 %fusion.3 = bf16[26,16,6,128]{3,1,2,0:T(8,128)(2,1)S(1)} fusion(bf16[28,2,7,2,128]{4,2,1,3,0:T(8,128)(2,1)S(1)} %slice.146, bf16[28,2,8,6,128]{4,2,1,3,0:T(8,128)(2,1)S(1)} %copy.143, pred[16,6]{0,1:T(8,128)(4,1)S(1)} %copy-done.25, bf16[2,3,3,128,128]{4,3,2,1,0:T(8,128)(2,1)S(1)} %get-tuple-element.15), kind=kOutput, calls=%fused_computation.8 | convolution fusion | flops 739491840 | bytes 1852416 | tf_op jit(solution)/shard_map/conv_general_dilated | solution.py:63
  43.1 1.7 %fusion.13 = bf16[26,2,42,128]{3,1,2,0:T(2,128)(2,1)S(1)} fusion(bf16[26,2,42,128]{3,2,1,0:T(8,128)(2,1)S(1)} %bitcast.140, pred[26,42]{1,0:T(8,128)(4,1)S(1)} %broadcast_and_fusion), kind=kLoop, calls=%fused_computation.38 | loop fusion | flops 279552 | bytes 1119300 | tf_op jit(solution)/shard_map/convert_element_type | solution.py:279
  44.8 1.7 %fusion.114 = bf16[2,26,42,128]{3,0,2,1:T(2,128)(2,1)S(1)} fusion(bf16[26,2,42,128]{3,2,1,0:T(8,128)(2,1)S(1)} %bitcast.141, pred[26,42]{1,0:T(8,128)(4,1)S(1)} %broadcast_and_fusion), kind=kLoop, calls=%fused_computation.204 | loop fusion | flops 279552 | bytes 1119300 | tf_op jit(solution)/shard_map/convert_element_type | solution.py:279
  51.0 1.6 %fusion.4 = bf16[24,16,6,128]{3,1,2,0:T(8,128)(2,1)S(1)} fusion(bf16[26,2,7,2,128]{4,2,1,3,0:T(8,128)(2,1)S(1)} %slice.149, bf16[26,2,8,6,128]{4,2,1,3,0:T(8,128)(2,1)S(1)} %copy.147, pred[16,6]{0,1:T(8,128)(4,1)S(1)} %copy-done.24, bf16[2,3,3,128,128]{4,3,2,1,0:T(8,128)(2,1)S(1)} %copy-done.6), kind=kOutput, calls=%fused_computation.10 | convolution fusion | flops 682622976 | bytes 1737728 | tf_op jit(solution)/shard_map/conv_general_dilated | solution.py:63
  52.6 2.8 %fusion.25 = bf16[22,2,38,128]{3,1,2,0:T(2,128)(2,1)S(1)} fusion(bf16[22,2,38,128]{3,0,2,1:T(8,128)(2,1)S(1)} %slice.163, pred[22,38]{1,0:T(8,128)(4,1)S(1)} %broadcast_and_fusion.2), kind=kLoop, calls=%fused_computation.53 | loop fusion | flops 214016 | bytes 856900 | tf_op jit(solution)/shard_map/convert_element_type | solution.py:279
  55.4 2.8 %fusion.113 = bf16[2,22,38,128]{3,0,2,1:T(2,128)(2,1)S(1)} fusion(bf16[22,2,38,128]{3,0,2,1:T(8,128)(2,1)S(1)} %slice.163, pred[22,38]{1,0:T(8,128)(4,1)S(1)} %broadcast_and_fusion.2), kind=kLoop, calls=%fused_computation.203 | loop fusion | flops 214016 | bytes 856900 | tf_op jit(solution)/shard_map/convert_element_type | solution.py:279
  59.1 1.9 %fusion.17 = bf16[2,24,40,128]{3,2,0,1:T(8,128)(2,1)S(1)} fusion(bf16[24,2,40,128]{3,0,2,1:T(8,128)(2,1)S(1)} %slice.151, bf16[2,24,4,128]{3,2,0,1:T(4,128)(2,1)} %collective-permute-done.3, bf16[2,4,32,128]{3,2,0,1:T(8,128)(2,1)S(1)} %copy-done.15, bf16[2,16,32,128]{3,2,0,1:T(8,128)(2,1)S(1)} %copy_select_fusion.4, ...), kind=kLoop, calls=%fused_computation.45 | loop fusion | flops 4177920 | bytes 1475520 | tf_op jit(solution)/shard_map/convert_element_type | solution.py:233
  63.8 2.9 %fusion.28 = bf16[2,22,38,128]{3,0,2,1:T(2,128)(2,1)S(1)} fusion(f32[22,2,38,128]{3,0,2,1:T(8,128)S(1)} %slice.154, pred[22,38]{1,0:T(8,128)(4,1)S(1)} %broadcast_and_fusion.2, bf16[2,26,42,128]{3,0,2,1:T(2,128)(2,1)S(1)} %fusion.114), kind=kLoop, calls=%fused_computation.57 | loop fusion | flops 1284096 | bytes 1712964 | tf_op jit(solution)/shard_map/convert_element_type | solution.py:233
  66.6 2.0 %convolution_bitcast_fusion.2 = f32[1,3,3,128,128]{4,3,2,1,0:T(8,128)S(1)} fusion(bf16[4,28,44,128]{3,0,2,1:T(4,128)(2,1)S(1)} %pad_maximum_fusion, bf16[2,22,38,128]{3,0,2,1:T(2,128)(2,1)S(1)} %fusion.28), kind=kOutput, calls=%fused_computation.28 | convolution fusion | flops 301989888 | bytes 1482752 | tf_op jit(solution)/shard_map/transpose | solution.py:82
  73.5 1.9 %fusion.43 = bf16[20,2,36,128]{3,1,2,0:T(2,128)(2,1)S(1)} fusion(f32[20,2,36,128]{3,0,2,1:T(8,128)S(1)} %slice.158, pred[20,36]{1,0:T(8,128)(4,1)S(1)} %copy-done.18, bf16[20,2,36,128]{3,0,2,1:T(8,128)(2,1)S(1)} %slice.166), kind=kLoop, calls=%fused_computation.72 | loop fusion | flops 1290240 | bytes 1475280 | tf_op jit(solution)/shard_map/convert_element_type | solution.py:233
  77.9 1.8 %convolution_bitcast_fusion = f32[1,3,3,128,128]{4,3,2,1,0:T(8,128)S(1)} fusion(bf16[26,2,42,128]{3,1,2,0:T(2,128)(2,1)S(1)} %fusion.13, bf16[2,16,32,128]{3,2,0,1:T(8,128)(2,1)S(1)} %slice.179), kind=kOutput, calls=%fused_computation.26 | convolution fusion | flops 301989888 | bytes 1411072 | tf_op jit(solution)/shard_map/transpose | solution.py:82
  79.7 1.8 %convolution_bitcast_fusion.1 = f32[1,3,3,128,128]{4,3,2,1,0:T(8,128)S(1)} fusion(bf16[22,2,38,128]{3,1,2,0:T(2,128)(2,1)S(1)} %fusion.25, bf16[2,20,36,128]{3,0,2,1:T(2,128)(2,1)S(1)} %bitcast.159), kind=kOutput, calls=%fused_computation.27 | convolution fusion | flops 301989888 | bytes 1280000 | tf_op jit(solution)/shard_map/transpose | solution.py:82
  81.5 2.0 %fusion.61 = bf16[2,18,34,128]{3,0,2,1:T(2,128)(2,1)S(1)} fusion(f32[18,2,34,128]{3,0,2,1:T(8,128)S(1)} %slice.169, pred[18,34]{1,0:T(8,128)(4,1)S(1)} %broadcast_and_fusion.4, bf16[2,22,38,128]{3,0,2,1:T(2,128)(2,1)S(1)} %fusion.113), kind=kLoop, calls=%fused_computation.89 | loop fusion | flops 940032 | bytes 1253988 | tf_op jit(solution)/shard_map/convert_element_type | solution.py:233
  83.5 1.7 %convolution_bitcast_fusion.3 = f32[1,3,3,128,128]{4,3,2,1,0:T(8,128)S(1)} fusion(bf16[4,28,44,128]{3,0,2,1:T(4,128)(2,1)S(1)} %pad_maximum_fusion, bf16[2,18,34,128]{3,0,2,1:T(2,128)(2,1)S(1)} %fusion.61), kind=kOutput, calls=%fused_computation.29 | convolution fusion | flops 301989888 | bytes 1482752 | tf_op jit(solution)/shard_map/transpose | solution.py:82
  86.5 3.1 %collective-permute-done.11 = f32[2,3,3,128,128]{4,3,2,1,0:T(8,128)S(1)} collective-permute-done((f32[2,3,3,128,128]{4,3,2,1,0:T(8,128)}, f32[2,3,3,128,128]{4,3,2,1,0:T(8,128)S(1)}, u32[]{:S(2)}, u32[]{:S(2)}) %collective-permute-start.11) | collective-permute-done | bytes 1179680 | tf_op jit(solution)/shard_map/ppermute | solution.py:250
  89.6 1.5 %select_add_fusion = bf16[2,3,3,128,128]{4,3,2,1,0:T(8,128)(2,1)S(1)} fusion(f32[2,3,3,128,128]{4,3,2,1,0:T(8,128)S(1)} %collective-permute-done.11, f32[1,3,3,128,128]{4,3,2,1,0:T(8,128)S(1)} %convolution_bitcast_fusion, f32[1,3,3,128,128]{4,3,2,1,0:T(8,128)S(1)} %convolution_bitcast_fusion.2, f32[1,3,3,128,128]{4,3,2,1,0:T(8,128)} %copy-done.1, ...), kind=kLoop, calls=%fused_computation.34 | loop fusion | flops 1474560 | bytes 4128769 | tf_op jit(solution)/shard_map/add | solution.py:293
  91.1 3.0 %collective-permute-start.12 = (bf16[147456]{0:T(1024)(128)(2,1)S(1)}, bf16[147456]{0:T(1024)(128)(2,1)S(1)}, u32[]{:S(2)}, u32[]{:S(2)}) collective-permute-start(bf16[147456]{0:T(1024)(128)(2,1)S(1)} %bitcast.166), channel_id=1, source_target_pairs={{0,4},{4,0},{8,12},{12,8},{1,5},{5,1},{9,13},{13,9},{2,6},{6,2},{1... | collective-permute-start | bytes 884744 | tf_op jit(solution)/shard_map/ppermute | solution.py:101
  94.1 7.3 %collective-permute-done.12 = bf16[147456]{0:T(1024)(128)(2,1)S(1)} collective-permute-done((bf16[147456]{0:T(1024)(128)(2,1)S(1)}, bf16[147456]{0:T(1024)(128)(2,1)S(1)}, u32[]{:S(2)}, u32[]{:S(2)}) %collective-permute-start.12) | collective-permute-done | bytes 294944 | tf_op jit(solution)/shard_map/ppermute | solution.py:101
  101.8 5.0 %collective-permute-done.13 = bf16[73728]{0:T(1024)(128)(2,1)S(1)} collective-permute-done((bf16[73728]{0:T(1024)(128)(2,1)S(1)}, bf16[73728]{0:T(1024)(128)(2,1)S(1)}, u32[]{:S(2)}, u32[]{:S(2)}) %collective-permute-start.13) | collective-permute-done | bytes 147488 | tf_op jit(solution)/shard_map/ppermute | solution.py:101
  106.9 2.5 %collective-permute-start.14 = (bf16[73728]{0:T(1024)(128)(2,1)S(1)}, bf16[73728]{0:T(1024)(128)(2,1)S(1)}, u32[]{:S(2)}, u32[]{:S(2)}) collective-permute-start(bf16[73728]{0:T(1024)(128)(2,1)S(1)} %add_convert_fusion.2), channel_id=1, source_target_pairs={{0,1},{1,0},{2,3},{3,2},{4,5},{5,4},{6,7},{7,6},{8,9},{9,8},{10,11... | collective-permute-start | bytes 442376 | tf_op jit(solution)/shard_map/ppermute | solution.py:101
  110.0 2.6 %collective-permute-done.14 = bf16[73728]{0:T(1024)(128)(2,1)S(1)} collective-permute-done((bf16[73728]{0:T(1024)(128)(2,1)S(1)}, bf16[73728]{0:T(1024)(128)(2,1)S(1)}, u32[]{:S(2)}, u32[]{:S(2)}) %collective-permute-start.14) | collective-permute-done | bytes 147488 | tf_op jit(solution)/shard_map/ppermute | solution.py:101
  112.7 2.7 %collective-permute-start.15 = (bf16[73728]{0:T(1024)(128)(2,1)S(1)}, bf16[73728]{0:T(1024)(128)(2,1)S(1)}, u32[]{:S(2)}, u32[]{:S(2)}) collective-permute-start(bf16[73728]{0:T(1024)(128)(2,1)S(1)} %add_convert_fusion.1), channel_id=1, source_target_pairs={{0,2},{1,3},{2,0},{3,1},{4,6},{5,7},{6,4},{7,5},{8,10},{9,11},{10,... | collective-permute-start | bytes 442376 | tf_op jit(solution)/shard_map/ppermute | solution.py:101
  116.8 3.6 %collective-permute-done.15 = bf16[73728]{0:T(1024)(128)(2,1)S(1)} collective-permute-done((bf16[73728]{0:T(1024)(128)(2,1)S(1)}, bf16[73728]{0:T(1024)(128)(2,1)S(1)}, u32[]{:S(2)}, u32[]{:S(2)}) %collective-permute-start.15) | collective-permute-done | bytes 147488 | tf_op jit(solution)/shard_map/ppermute | solution.py:101
  121.4 4.3 %collective-permute-done.16 = bf16[73728]{0:T(1024)(128)(2,1)S(1)} collective-permute-done((bf16[73728]{0:T(1024)(128)(2,1)S(1)}, bf16[73728]{0:T(1024)(128)(2,1)S(1)}, u32[]{:S(2)}, u32[]{:S(2)}) %collective-permute-start.16) | collective-permute-done | bytes 147488 | tf_op jit(solution)/shard_map/ppermute | solution.py:101
  125.7 1.6 %collective-permute-start.17 = (bf16[147456]{0:T(1024)(128)(2,1)S(1)}, bf16[147456]{0:T(1024)(128)(2,1)S(1)}, u32[]{:S(2)}, u32[]{:S(2)}) collective-permute-start(bf16[147456]{0:T(1024)(128)(2,1)S(1)} %maximum_select_fusion.2), channel_id=1, source_target_pairs={{0,4},{4,0},{8,12},{12,8},{1,5},{5,1},{9,13},{13,9},{2,6},{6,2},{1... | collective-permute-start | bytes 884744 | tf_op jit(solution)/shard_map/ppermute | solution.py:101
  129.2 3.3 %collective-permute-done.17 = bf16[147456]{0:T(1024)(128)(2,1)S(1)} collective-permute-done((bf16[147456]{0:T(1024)(128)(2,1)S(1)}, bf16[147456]{0:T(1024)(128)(2,1)S(1)}, u32[]{:S(2)}, u32[]{:S(2)}) %collective-permute-start.17) | collective-permute-done | bytes 294944 | tf_op jit(solution)/shard_map/ppermute | solution.py:101
  (166 shorter events, 37.8 us)
Async XLA Ops:
  0.6 2.3 %copy-start = (bf16[4,16,32,128]{3,2,1,0:T(8,128)(2,1)S(1)}, bf16[4,16,32,128]{3,2,1,0:T(8,128)(2,1)}, u32[]{:S(2)}) copy-start(bf16[4,16,32,128]{3,2,1,0:T(8,128)(2,1)} %param.6) | copy-start | bytes 1572868
  0.6 2.0 %copy-start.10 = (bf16[2,3,3,128,128]{4,3,2,1,0:T(8,128)(2,1)S(1)}, bf16[2,3,3,128,128]{4,3,2,1,0:T(8,128)(2,1)}, u32[]{:S(2)}) copy-start(bf16[2,3,3,128,128]{4,3,2,1,0:T(8,128)(2,1)} %param.5) | copy-start | bytes 1769476
  0.7 2.1 %copy-start.19 = (s32[4]{0:T(128)S(1)}, s32[4]{0:T(128)}, u32[]{:S(2)}) copy-start(s32[4]{0:T(128)} %param.7) | copy-start | bytes 52
  2.1 9.5 %collective-permute-start.4 = (bf16[2,16,32,128]{3,0,2,1:T(2,128)(2,1)S(1)}, bf16[2,16,32,128]{3,0,2,1:T(2,128)(2,1)S(1)}, u32[]{:S(2)}, u32[]{:S(2)}) collective-permute-start(bf16[2,16,32,128]{3,0,2,1:T(2,128)(2,1)S(1)} %bitcast.168), channel_id=1, source_target_pairs={{0,16},{16,0},{1,17},{17,1},{2,18},{18,2},{3,19},{19,3},{4,20},{20... | collective-permute-start | bytes 786440 | tf_op jit(solution)/shard_map/ppermute | solution.py:250
  2.7 30.2 %collective-permute-start.9 = (bf16[2,3,3,128,128]{4,3,2,1,0:T(8,128)(2,1)S(1)}, bf16[2,3,3,128,128]{4,3,2,1,0:T(8,128)(2,1)S(1)}, u32[]{:S(2)}, u32[]{:S(2)}) collective-permute-start(bf16[2,3,3,128,128]{4,3,2,1,0:T(8,128)(2,1)S(1)} %copy-done.10), channel_id=1, source_target_pairs={{0,16},{16,0},{1,17},{17,1},{2,18},{18,2},{3,19},{19,3},{4,20},{20... | collective-permute-start | bytes 1769480 | tf_op jit(solution)/shard_map/ppermute | solution.py:250
  3.8 15.6 %collective-permute-start.1 = (bf16[2,4,32,128]{3,2,0,1:T(8,128)(2,1)S(1)}, bf16[2,4,32,128]{3,2,0,1:T(8,128)(2,1)S(1)}, u32[]{:S(2)}, u32[]{:S(2)}) collective-permute-start(bf16[2,4,32,128]{3,2,0,1:T(8,128)(2,1)S(1)} %get-tuple-element.31), channel_id=1, source_target_pairs={{4,0},{5,1},{6,2},{7,3},{8,4},{9,5},{10,6},{11,7},{12,8},{13,9},{1... | collective-permute-start | bytes 196616 | tf_op jit(solution)/shard_map/ppermute | solution.py:43
  5.1 14.3 %collective-permute-start = (bf16[2,4,32,128]{3,2,0,1:T(8,128)(2,1)S(1)}, bf16[2,4,32,128]{3,2,0,1:T(8,128)(2,1)S(1)}, u32[]{:S(2)}, u32[]{:S(2)}) collective-permute-start(bf16[2,4,32,128]{3,2,0,1:T(8,128)(2,1)S(1)} %get-tuple-element.30), channel_id=1, source_target_pairs={{0,4},{1,5},{2,6},{3,7},{4,8},{5,9},{6,10},{7,11},{8,12},{9,13},{1... | collective-permute-start | bytes 196616 | tf_op jit(solution)/shard_map/ppermute | solution.py:43
  12.5 14.0 %collective-permute-start.6 = (bf16[4,6,32,128]{3,0,2,1:T(4,128)(2,1)S(1)}, bf16[4,6,32,128]{3,0,2,1:T(4,128)(2,1)S(1)}, u32[]{:S(2)}, u32[]{:S(2)}) collective-permute-start(bf16[4,6,32,128]{3,0,2,1:T(4,128)(2,1)S(1)} %get-tuple-element.23), channel_id=1, source_target_pairs={{4,0},{5,1},{6,2},{7,3},{8,4},{9,5},{10,6},{11,7},{12,8},{13,9},{1... | collective-permute-start | bytes 589832 | tf_op jit(solution)/shard_map/ppermute | solution.py:43
  13.8 12.7 %collective-permute-start.5 = (bf16[4,6,32,128]{3,0,2,1:T(4,128)(2,1)S(1)}, bf16[4,6,32,128]{3,0,2,1:T(4,128)(2,1)S(1)}, u32[]{:S(2)}, u32[]{:S(2)}) collective-permute-start(bf16[4,6,32,128]{3,0,2,1:T(4,128)(2,1)S(1)} %get-tuple-element.22), channel_id=1, source_target_pairs={{0,4},{1,5},{2,6},{3,7},{4,8},{5,9},{6,10},{7,11},{8,12},{9,13},{1... | collective-permute-start | bytes 589832 | tf_op jit(solution)/shard_map/ppermute | solution.py:43
  19.4 13.6 %copy-start.14 = (bf16[2,4,32,128]{3,2,0,1:T(8,128)(2,1)}, bf16[2,4,32,128]{3,2,0,1:T(8,128)(2,1)S(1)}, u32[]{:S(2)}) copy-start(bf16[2,4,32,128]{3,2,0,1:T(8,128)(2,1)S(1)} %collective-permute-done.1) | copy-start | bytes 196612
  19.4 13.6 %copy-start.16 = (bf16[2,4,32,128]{3,2,0,1:T(8,128)(2,1)}, bf16[2,4,32,128]{3,2,0,1:T(8,128)(2,1)S(1)}, u32[]{:S(2)}) copy-start(bf16[2,4,32,128]{3,2,0,1:T(8,128)(2,1)S(1)} %collective-permute-done) | copy-start | bytes 196612
  20.1 38.5 %collective-permute-start.3 = (bf16[2,24,4,128]{3,2,0,1:T(4,128)(2,1)}, bf16[2,24,4,128]{3,2,0,1:T(4,128)(2,1)}, u32[]{:S(2)}, u32[]{:S(2)}) collective-permute-start(bf16[2,24,4,128]{3,2,0,1:T(4,128)(2,1)} %get-tuple-element.29), channel_id=1, source_target_pairs={{1,0},{2,1},{3,2},{5,4},{6,5},{7,6},{9,8},{10,9},{11,10},{13,12},{... | collective-permute-start | bytes 147464 | tf_op jit(solution)/shard_map/ppermute | solution.py:43
  21.4 37.2 %collective-permute-start.2 = (bf16[2,24,4,128]{3,2,0,1:T(4,128)(2,1)}, bf16[2,24,4,128]{3,2,0,1:T(4,128)(2,1)}, u32[]{:S(2)}, u32[]{:S(2)}) collective-permute-start(bf16[2,24,4,128]{3,2,0,1:T(4,128)(2,1)} %get-tuple-element.28), channel_id=1, source_target_pairs={{0,1},{1,2},{2,3},{4,5},{5,6},{6,7},{8,9},{9,10},{10,11},{12,13},{... | collective-permute-start | bytes 147464 | tf_op jit(solution)/shard_map/ppermute | solution.py:43
  26.8 7.4 %collective-permute-start.8 = (bf16[4,28,6,128]{3,0,2,1:T(4,128)(2,1)S(1)}, bf16[4,28,6,128]{3,0,2,1:T(4,128)(2,1)S(1)}, u32[]{:S(2)}, u32[]{:S(2)}) collective-permute-start(bf16[4,28,6,128]{3,0,2,1:T(4,128)(2,1)S(1)} %get-tuple-element.17), channel_id=1, source_target_pairs={{1,0},{2,1},{3,2},{5,4},{6,5},{7,6},{9,8},{10,9},{11,10},{13,12},{... | collective-permute-start | bytes 516104 | tf_op jit(solution)/shard_map/ppermute | solution.py:43
  28.1 7.5 %collective-permute-start.7 = (bf16[4,28,6,128]{3,0,2,1:T(4,128)(2,1)S(1)}, bf16[4,28,6,128]{3,0,2,1:T(4,128)(2,1)S(1)}, u32[]{:S(2)}, u32[]{:S(2)}) collective-permute-start(bf16[4,28,6,128]{3,0,2,1:T(4,128)(2,1)S(1)} %get-tuple-element.16), channel_id=1, source_target_pairs={{0,1},{1,2},{2,3},{4,5},{5,6},{6,7},{8,9},{9,10},{10,11},{12,13},{... | collective-permute-start | bytes 516104 | tf_op jit(solution)/shard_map/ppermute | solution.py:43
  33.0 1.2 copy-start.3
  33.0 7.9 %copy-start.5 = (bf16[2,3,3,128,128]{4,3,2,1,0:T(8,128)(2,1)}, bf16[2,3,3,128,128]{4,3,2,1,0:T(8,128)(2,1)S(1)}, u32[]{:S(2)}) copy-start(bf16[2,3,3,128,128]{4,3,2,1,0:T(8,128)(2,1)S(1)} %get-tuple-element.15) | copy-start | bytes 1769476
  46.6 1.1 copy-start.7
  75.4 1.1 copy-start.11
  81.5 3.8 %copy-start.1 = (f32[1,3,3,128,128]{4,3,2,1,0:T(8,128)}, f32[1,3,3,128,128]{4,3,2,1,0:T(8,128)S(1)}, u32[]{:S(2)}) copy-start(f32[1,3,3,128,128]{4,3,2,1,0:T(8,128)S(1)} %convolution_bitcast_fusion.1) | copy-start | bytes 1769476
  85.3 1.2 copy-start.2
  86.5 3.1 %collective-permute-start.11 = (f32[2,3,3,128,128]{4,3,2,1,0:T(8,128)}, f32[2,3,3,128,128]{4,3,2,1,0:T(8,128)S(1)}, u32[]{:S(2)}, u32[]{:S(2)}) collective-permute-start(f32[2,3,3,128,128]{4,3,2,1,0:T(8,128)} %fusion.18), channel_id=1, source_target_pairs={{0,16},{16,0},{1,17},{17,1},{2,18},{18,2},{3,19},{19,3},{4,20},{20... | collective-permute-start | bytes 3538952 | tf_op jit(solution)/shard_map/ppermute | solution.py:250
  91.1 18.4 %copy-start.9 = (bf16[20,16,5,128]{3,1,2,0:T(8,128)(2,1)S(1)}, bf16[20,16,5,128]{3,1,2,0:T(8,128)(2,1)}, u32[]{:S(2)}) copy-start(bf16[20,16,5,128]{3,1,2,0:T(8,128)(2,1)} %copy-done.8) | copy-start | bytes 1228804
  91.1 10.3 %collective-permute-start.12 = (bf16[147456]{0:T(1024)(128)(2,1)S(1)}, bf16[147456]{0:T(1024)(128)(2,1)S(1)}, u32[]{:S(2)}, u32[]{:S(2)}) collective-permute-start(bf16[147456]{0:T(1024)(128)(2,1)S(1)} %bitcast.166), channel_id=1, source_target_pairs={{0,4},{4,0},{8,12},{12,8},{1,5},{5,1},{9,13},{13,9},{2,6},{6,2},{1... | collective-permute-start | bytes 884744 | tf_op jit(solution)/shard_map/ppermute | solution.py:101
  101.5 5.4 %collective-permute-start.13 = (bf16[73728]{0:T(1024)(128)(2,1)S(1)}, bf16[73728]{0:T(1024)(128)(2,1)S(1)}, u32[]{:S(2)}, u32[]{:S(2)}) collective-permute-start(bf16[73728]{0:T(1024)(128)(2,1)S(1)} %select_convert_fusion.2), channel_id=1, source_target_pairs={{0,8},{4,12},{8,0},{12,4},{1,9},{5,13},{9,1},{13,5},{2,10},{6,14},... | collective-permute-start | bytes 442376 | tf_op jit(solution)/shard_map/ppermute | solution.py:101
  106.9 5.7 %collective-permute-start.14 = (bf16[73728]{0:T(1024)(128)(2,1)S(1)}, bf16[73728]{0:T(1024)(128)(2,1)S(1)}, u32[]{:S(2)}, u32[]{:S(2)}) collective-permute-start(bf16[73728]{0:T(1024)(128)(2,1)S(1)} %add_convert_fusion.2), channel_id=1, source_target_pairs={{0,1},{1,0},{2,3},{3,2},{4,5},{5,4},{6,7},{7,6},{8,9},{9,8},{10,11... | collective-permute-start | bytes 442376 | tf_op jit(solution)/shard_map/ppermute | solution.py:101
  109.6 5.7 %copy-start.12 = (bf16[2,3,3,128,128]{3,4,2,1,0:T(8,128)(2,1)S(1)}, bf16[2,3,3,128,128]{3,4,2,1,0:T(8,128)(2,1)}, u32[]{:S(2)}) copy-start(bf16[2,3,3,128,128]{3,4,2,1,0:T(8,128)(2,1)} %get-tuple-element.32) | copy-start | bytes 1769476
  109.6 5.7 %copy-start.20 = (pred[16,5]{0,1:T(8,128)(4,1)S(1)}, pred[16,5]{0,1:T(8,128)(4,1)}, u32[]{:S(2)}) copy-start(pred[16,5]{0,1:T(8,128)(4,1)} %constant.176) | copy-start | bytes 244
  112.7 7.7 %collective-permute-start.15 = (bf16[73728]{0:T(1024)(128)(2,1)S(1)}, bf16[73728]{0:T(1024)(128)(2,1)S(1)}, u32[]{:S(2)}, u32[]{:S(2)}) collective-permute-start(bf16[73728]{0:T(1024)(128)(2,1)S(1)} %add_convert_fusion.1), channel_id=1, source_target_pairs={{0,2},{1,3},{2,0},{3,1},{4,6},{5,7},{6,4},{7,5},{8,10},{9,11},{10,... | collective-permute-start | bytes 442376 | tf_op jit(solution)/shard_map/ppermute | solution.py:101
  120.4 5.2 %collective-permute-start.16 = (bf16[73728]{0:T(1024)(128)(2,1)S(1)}, bf16[73728]{0:T(1024)(128)(2,1)S(1)}, u32[]{:S(2)}, u32[]{:S(2)}) collective-permute-start(bf16[73728]{0:T(1024)(128)(2,1)S(1)} %add_convert_fusion), channel_id=1, source_target_pairs={{0,8},{4,12},{8,0},{12,4},{1,9},{5,13},{9,1},{13,5},{2,10},{6,14},... | collective-permute-start | bytes 442376 | tf_op jit(solution)/shard_map/ppermute | solution.py:101
  121.3 6.0 %collective-permute-start.10 = (bf16[2,16,32,128]{3,0,2,1:T(2,128)(2,1)S(1)}, bf16[2,16,32,128]{3,0,2,1:T(2,128)(2,1)S(1)}, u32[]{:S(2)}, u32[]{:S(2)}) collective-permute-start(bf16[2,16,32,128]{3,0,2,1:T(2,128)(2,1)S(1)} %get-tuple-element.19), channel_id=1, source_target_pairs={{0,16},{16,0},{1,17},{17,1},{2,18},{18,2},{3,19},{19,3},{4,20},{20... | collective-permute-start | bytes 786440 | tf_op jit(solution)/shard_map/ppermute | solution.py:250
  125.7 6.8 %collective-permute-start.17 = (bf16[147456]{0:T(1024)(128)(2,1)S(1)}, bf16[147456]{0:T(1024)(128)(2,1)S(1)}, u32[]{:S(2)}, u32[]{:S(2)}) collective-permute-start(bf16[147456]{0:T(1024)(128)(2,1)S(1)} %maximum_select_fusion.2), channel_id=1, source_target_pairs={{0,4},{4,0},{8,12},{12,8},{1,5},{5,1},{9,13},{13,9},{2,6},{6,2},{1... | collective-permute-start | bytes 884744 | tf_op jit(solution)/shard_map/ppermute | solution.py:101
  (12 other events, 10.9 us)
where the time goes:
time: 134 us
  starting transfers between devices  37.2 us (28%)
  waiting for transfers between devices  30.6 us (23%)
  other arithmetic  29.7 us (22%)
  local copies, waits for them, and re-layouts  17.3 us (13%)
  matrix products  17.3 us (13%)
  between operations  1.61 us (1%)
    ppermute x6, waiting for transfers between devices, exchange(): return lax.ppermute(values, axis, [(i, i ^ distance) for i in range(count)])  26.2 us
    ppermute x8, starting transfers between devices, from_neighbours(): parts.append(lax.ppermute(piece, AXES, pairs))  25.9 us
    ppermute x6, starting transfers between devices, exchange(): return lax.ppermute(values, axis, [(i, i ^ distance) for i in range(count)])  10.5 us
    conv_general_dilated x8, matrix products, convolve(): lax.conv_general_dilated(padded, kernel, (1, 1), 'VALID', dimension_numbe...  10 us
    convert_element_type x4, other arithmetic, local_split(): current = current.astype(jnp.bfloat16)  9.08 us
    convert_element_type x4, other arithmetic, section_chain(): signal = signal.astype(jnp.bfloat16)  8.69 us
    transpose x4, matrix products, kernel_terms(): return jnp.transpose(terms, (1, 2, 0, 3))  7.3 us
    unnamed x54, local copies, waits for them, and re-layouts  6.29 us
  transfers between devices with their start and end apart: 18, of which 8 were waited for; matrix products, arithmetic and copies ran while one was open for 23% of the time, Pallas kernels for 0%

commit v1 on v0

--- a/solution.py
+++ b/solution.py
@@ -262,9 +262,10 @@
     rims = [r + layer_count for r in top_rim]
     stacked = jnp.concatenate([by_section(mine, theirs, s) for s in range(2)], axis=0)
     stacked = with_rim(stacked, rims[1], 0, range(2))
+    group_cotangent = lax.dynamic_slice_in_dim(top_cotangent, section_index * half, half, 0)
+    stacked, group_cotangent = lax.optimization_barrier((stacked, group_cotangent))
+    top_ext = with_rim(group_cotangent, top_rim[1], 0, range(2))
     firsts = [crop(stacked[:half], rims[1] - rims[0]), stacked[half:]]
-    group_cotangent = lax.dynamic_slice_in_dim(top_cotangent, section_index * half, half, 0)
-    top_ext = with_rim(group_cotangent, top_rim[1], 0, range(2))
 
     results, partials = [None, None], [None, None]
     for s in (1, 0):

time: 134 us -> 140 us (1.045)
  waiting for transfers between devices: 30.6 us -> 36.9 us
  starting transfers between devices: 37.2 us -> 38.7 us
    ppermute x8, waiting for transfers between devices: 1.38 us -> 9.97 us  [from_neighbours(): parts.append(lax.ppermute(piece, AXES, pairs))]
    ppermute x6, starting transfers between devices: 10.5 us -> 13.1 us  [exchange(): return lax.ppermute(values, axis, [(i, i ^ distance) for i in range(count)])]
    ppermute x6, waiting for transfers between devices: 26.2 us -> 23.8 us  [exchange(): return lax.ppermute(values, axis, [(i, i ^ distance) for i in range(count)])]
    unnamed x54 -> x50, local copies, waits for them, and re-layouts: 6.29 us -> 5.39 us
  transfers between devices with their start and end apart: 18 -> 18, of which waited for: 8 -> 12; matrix products, arithmetic and copies ran while one was open for 23% -> 15% of each run, Pallas kernels for 0% -> 0%
where the time goes in v1:
time: 140 us
  starting transfers between devices  38.7 us (28%)
  waiting for transfers between devices  36.9 us (26%)
  other arithmetic  28.9 us (21%)
  matrix products  17.2 us (12%)
  local copies, waits for them, and re-layouts  16.4 us (12%)
  between operations  1.66 us (1%)
    ppermute x8, starting transfers between devices, from_neighbours(): parts.append(lax.ppermute(piece, AXES, pairs))  24.9 us
    ppermute x6, waiting for transfers between devices, exchange(): return lax.ppermute(values, axis, [(i, i ^ distance) for i in range(count)])  23.8 us
    ppermute x6, starting transfers between devices, exchange(): return lax.ppermute(values, axis, [(i, i ^ distance) for i in range(count)])  13.1 us
    ppermute x8, waiting for transfers between devices, from_neighbours(): parts.append(lax.ppermute(piece, AXES, pairs))  9.97 us
    conv_general_dilated x8, matrix products, convolve(): lax.conv_general_dilated(padded, kernel, (1, 1), 'VALID', dimension_numbe...  9.94 us
    convert_element_type x4, other arithmetic, local_split(): current = current.astype(jnp.bfloat16)  9.08 us
    convert_element_type x4, other arithmetic, section_chain(): signal = signal.astype(jnp.bfloat16)  7.69 us
    transpose x4, matrix products, kernel_terms(): return jnp.transpose(terms, (1, 2, 0, 3))  7.24 us
  transfers between devices with their start and end apart: 18, of which 12 were waited for; matrix products, arithmetic and copies ran while one was open for 15% of the time, Pallas kernels for 0%

profile of v1, /device:TPU:0, one launch (start us, length us, event | category | flops | bytes accessed | tf_op | source)
XLA Modules:
  0.0 139.8 jit_solution(17720055602583815690)
XLA Ops:
  6.5 5.4 %collective-permute-start.1 = (bf16[4,6,32,128]{3,0,2,1:T(4,128)(2,1)S(1)}, bf16[4,6,32,128]{3,0,2,1:T(4,128)(2,1)S(1)}, u32[]{:S(2)}, u32[]{:S(2)}) collective-permute-start(bf16[4,6,32,128]{3,0,2,1:T(4,128)(2,1)S(1)} %get-tuple-element.26), channel_id=1, source_target_pairs={{0,4},{1,5},{2,6},{3,7},{4,8},{5,9},{6,10},{7,11},{8,12},{9,13},{1... | collective-permute-start | bytes 589832 | tf_op jit(solution)/shard_map/ppermute | solution.py:43
  12.6 2.5 %collective-permute-done.2 = bf16[4,6,32,128]{3,0,2,1:T(4,128)(2,1)S(1)} collective-permute-done((bf16[4,6,32,128]{3,0,2,1:T(4,128)(2,1)S(1)}, bf16[4,6,32,128]{3,0,2,1:T(4,128)(2,1)S(1)}, u32[]{:S(2)}, u32[]{:S(2)}) %collective-permute-start.2) | collective-permute-done | bytes 196640 | tf_op jit(solution)/shard_map/ppermute | solution.py:43
  17.9 4.6 %collective-permute-start.3 = (bf16[4,28,6,128]{3,0,2,1:T(4,128)(2,1)S(1)}, bf16[4,28,6,128]{3,0,2,1:T(4,128)(2,1)S(1)}, u32[]{:S(2)}, u32[]{:S(2)}) collective-permute-start(bf16[4,28,6,128]{3,0,2,1:T(4,128)(2,1)S(1)} %get-tuple-element.20), channel_id=1, source_target_pairs={{0,1},{1,2},{2,3},{4,5},{5,6},{6,7},{8,9},{9,10},{10,11},{12,13},{... | collective-permute-start | bytes 516104 | tf_op jit(solution)/shard_map/ppermute | solution.py:43
  25.4 2.9 %pad_maximum_fusion = bf16[4,28,44,128]{3,0,2,1:T(4,128)(2,1)S(1)} fusion(bf16[4,28,6,128]{3,0,2,1:T(4,128)(2,1)S(1)} %collective-permute-done.4, bf16[4,6,32,128]{3,0,2,1:T(4,128)(2,1)S(1)} %collective-permute-done.2, bf16[2,16,32,128]{3,0,2,1:T(2,128)(2,1)S(1)} %get-tuple-element.29, bf16[2,16,32,128]{3,0,2,1:T(2,128)(2,1)S(1)} %get-tuple-element.28, ...), kind=kLoop, calls=%fused_computation.24 | loop fusion | flops 7569408 | bytes 2523136 | tf_op jit(solution)/shard_map/concatenate | solution.py:44
  28.3 1.7 %slice_bitcast_fusion = (bf16[28,2,44,128]{3,1,2,0:T(2,128)(2,1)}, bf16[28,2,44,128]{3,1,2,0:T(2,128)(2,1)S(1)}) fusion(bf16[4,28,44,128]{3,0,2,1:T(4,128)(2,1)S(1)} %pad_maximum_fusion), kind=kLoop, calls=%fused_computation.118 | loop fusion | bytes 2523136 | tf_op jit(solution)/shard_map/slice | solution.py:268
  30.7 1.7 %fusion.3 = bf16[26,16,6,128]{3,1,2,0:T(8,128)(2,1)S(1)} fusion(bf16[28,2,7,2,128]{4,2,1,3,0:T(8,128)(2,1)S(1)} %slice.145, bf16[28,2,8,6,128]{4,2,1,3,0:T(8,128)(2,1)S(1)} %copy.143, pred[16,6]{0,1:T(8,128)(4,1)S(1)} %copy-done.22, bf16[2,3,3,128,128]{4,3,2,1,0:T(8,128)(2,1)S(1)} %get-tuple-element.19), kind=kOutput, calls=%fused_computation.8 | convolution fusion | flops 739491840 | bytes 1852416 | tf_op jit(solution)/shard_map/conv_general_dilated | solution.py:63
  32.9 1.7 %fusion.13 = bf16[26,2,42,128]{3,1,2,0:T(2,128)(2,1)S(1)} fusion(bf16[26,2,42,128]{3,2,1,0:T(8,128)(2,1)S(1)} %bitcast.140, pred[26,42]{1,0:T(8,128)(4,1)S(1)} %broadcast_and_fusion), kind=kLoop, calls=%fused_computation.38 | loop fusion | flops 279552 | bytes 1119300 | tf_op jit(solution)/shard_map/convert_element_type | solution.py:280
  34.6 1.7 %fusion.115 = bf16[2,26,42,128]{3,0,2,1:T(2,128)(2,1)S(1)} fusion(bf16[26,2,42,128]{3,2,1,0:T(8,128)(2,1)S(1)} %bitcast.141, pred[26,42]{1,0:T(8,128)(4,1)S(1)} %broadcast_and_fusion), kind=kLoop, calls=%fused_computation.205 | loop fusion | flops 279552 | bytes 1119300 | tf_op jit(solution)/shard_map/convert_element_type | solution.py:280
  37.0 4.7 %collective-permute-start.5 = (bf16[2,4,32,128]{3,2,0,1:T(8,128)(2,1)S(1)}, bf16[2,4,32,128]{3,2,0,1:T(8,128)(2,1)S(1)}, u32[]{:S(2)}, u32[]{:S(2)}) collective-permute-start(bf16[2,4,32,128]{3,2,0,1:T(8,128)(2,1)S(1)} %get-tuple-element.35), channel_id=1, source_target_pairs={{0,4},{1,5},{2,6},{3,7},{4,8},{5,9},{6,10},{7,11},{8,12},{9,13},{1... | collective-permute-start | bytes 196616 | tf_op jit(solution)/shard_map/ppermute | solution.py:43
  45.1 1.6 %fusion.4 = bf16[24,16,6,128]{3,1,2,0:T(8,128)(2,1)S(1)} fusion(bf16[26,2,7,2,128]{4,2,1,3,0:T(8,128)(2,1)S(1)} %slice.148, bf16[26,2,8,6,128]{4,2,1,3,0:T(8,128)(2,1)S(1)} %copy.147, pred[16,6]{0,1:T(8,128)(4,1)S(1)} %copy-done.21, bf16[2,3,3,128,128]{4,3,2,1,0:T(8,128)(2,1)S(1)} %copy-done.5), kind=kOutput, calls=%fused_computation.10 | convolution fusion | flops 682622976 | bytes 1737728 | tf_op jit(solution)/shard_map/conv_general_dilated | solution.py:63
  46.7 2.8 %fusion.25 = bf16[22,2,38,128]{3,1,2,0:T(2,128)(2,1)S(1)} fusion(bf16[22,2,38,128]{3,0,2,1:T(8,128)(2,1)S(1)} %slice.161, pred[22,38]{1,0:T(8,128)(4,1)S(1)} %broadcast_and_fusion.2), kind=kLoop, calls=%fused_computation.53 | loop fusion | flops 214016 | bytes 856900 | tf_op jit(solution)/shard_map/convert_element_type | solution.py:280
  49.5 2.8 %fusion.114 = bf16[2,22,38,128]{3,0,2,1:T(2,128)(2,1)S(1)} fusion(bf16[22,2,38,128]{3,0,2,1:T(8,128)(2,1)S(1)} %slice.161, pred[22,38]{1,0:T(8,128)(4,1)S(1)} %broadcast_and_fusion.2), kind=kLoop, calls=%fused_computation.204 | loop fusion | flops 214016 | bytes 856900 | tf_op jit(solution)/shard_map/convert_element_type | solution.py:280
  54.2 5.7 %collective-permute-done.6 = bf16[2,4,32,128]{3,2,0,1:T(8,128)(2,1)S(1)} collective-permute-done((bf16[2,4,32,128]{3,2,0,1:T(8,128)(2,1)S(1)}, bf16[2,4,32,128]{3,2,0,1:T(8,128)(2,1)S(1)}, u32[]{:S(2)}, u32[]{:S(2)}) %collective-permute-start.6) | collective-permute-done | bytes 65568 | tf_op jit(solution)/shard_map/ppermute | solution.py:43
  61.2 5.0 %collective-permute-start.7 = (bf16[2,24,4,128]{3,2,0,1:T(4,128)(2,1)S(1)}, bf16[2,24,4,128]{3,2,0,1:T(4,128)(2,1)S(1)}, u32[]{:S(2)}, u32[]{:S(2)}) collective-permute-start(bf16[2,24,4,128]{3,2,0,1:T(4,128)(2,1)S(1)} %get-tuple-element.32), channel_id=1, source_target_pairs={{0,1},{1,2},{2,3},{4,5},{5,6},{6,7},{8,9},{9,10},{10,11},{12,13},{... | collective-permute-start | bytes 147464 | tf_op jit(solution)/shard_map/ppermute | solution.py:43
  71.6 2.9 %fusion.28 = bf16[2,22,38,128]{3,0,2,1:T(2,128)(2,1)S(1)} fusion(f32[22,2,38,128]{3,0,2,1:T(8,128)S(1)} %slice.153, pred[22,38]{1,0:T(8,128)(4,1)S(1)} %broadcast_and_fusion.2, bf16[2,26,42,128]{3,0,2,1:T(2,128)(2,1)S(1)} %fusion.115), kind=kLoop, calls=%fused_computation.57 | loop fusion | flops 1284096 | bytes 1712964 | tf_op jit(solution)/shard_map/convert_element_type | solution.py:233
  74.5 1.9 %convolution_bitcast_fusion.2 = f32[1,3,3,128,128]{4,3,2,1,0:T(8,128)S(1)} fusion(bf16[4,28,44,128]{3,0,2,1:T(4,128)(2,1)S(1)} %pad_maximum_fusion, bf16[2,22,38,128]{3,0,2,1:T(2,128)(2,1)S(1)} %fusion.28), kind=kOutput, calls=%fused_computation.28 | convolution fusion | flops 301989888 | bytes 1482752 | tf_op jit(solution)/shard_map/transpose | solution.py:82
  78.8 1.7 %fusion.43 = bf16[20,2,36,128]{3,1,2,0:T(2,128)(2,1)S(1)} fusion(f32[20,2,36,128]{3,0,2,1:T(8,128)S(1)} %slice.157, pred[20,36]{1,0:T(8,128)(4,1)S(1)} %broadcast_and_fusion.3, bf16[20,2,36,128]{3,0,2,1:T(8,128)(2,1)S(1)} %slice.164), kind=kLoop, calls=%fused_computation.72 | loop fusion | flops 1290240 | bytes 1475280 | tf_op jit(solution)/shard_map/convert_element_type | solution.py:233
  82.9 1.8 %convolution_bitcast_fusion = f32[1,3,3,128,128]{4,3,2,1,0:T(8,128)S(1)} fusion(bf16[26,2,42,128]{3,1,2,0:T(2,128)(2,1)S(1)} %fusion.13, bf16[2,16,32,128]{3,2,0,1:T(8,128)(2,1)S(1)} %slice.177), kind=kOutput, calls=%fused_computation.26 | convolution fusion | flops 301989888 | bytes 1411072 | tf_op jit(solution)/shard_map/transpose | solution.py:82
  84.7 1.8 %convolution_bitcast_fusion.1 = f32[1,3,3,128,128]{4,3,2,1,0:T(8,128)S(1)} fusion(bf16[22,2,38,128]{3,1,2,0:T(2,128)(2,1)S(1)} %fusion.25, bf16[2,20,36,128]{3,0,2,1:T(2,128)(2,1)S(1)} %bitcast.159), kind=kOutput, calls=%fused_computation.27 | convolution fusion | flops 301989888 | bytes 1280000 | tf_op jit(solution)/shard_map/transpose | solution.py:82
  86.5 2.3 %fusion.61 = bf16[2,18,34,128]{3,0,2,1:T(2,128)(2,1)S(1)} fusion(f32[18,2,34,128]{3,0,2,1:T(8,128)S(1)} %slice.167, pred[18,34]{1,0:T(8,128)(4,1)S(1)} %copy-done.15, bf16[2,22,38,128]{3,0,2,1:T(2,128)(2,1)S(1)} %fusion.114), kind=kLoop, calls=%fused_computation.89 | loop fusion | flops 940032 | bytes 1253988 | tf_op jit(solution)/shard_map/convert_element_type | solution.py:233
  89.6 1.7 %convolution_bitcast_fusion.3 = f32[1,3,3,128,128]{4,3,2,1,0:T(8,128)S(1)} fusion(bf16[4,28,44,128]{3,0,2,1:T(4,128)(2,1)S(1)} %pad_maximum_fusion, bf16[2,18,34,128]{3,0,2,1:T(2,128)(2,1)S(1)} %fusion.61), kind=kOutput, calls=%fused_computation.29 | convolution fusion | flops 301989888 | bytes 1482752 | tf_op jit(solution)/shard_map/transpose | solution.py:82
  92.5 3.1 %collective-permute-done.11 = f32[2,3,3,128,128]{4,3,2,1,0:T(8,128)S(1)} collective-permute-done((f32[2,3,3,128,128]{4,3,2,1,0:T(8,128)}, f32[2,3,3,128,128]{4,3,2,1,0:T(8,128)S(1)}, u32[]{:S(2)}, u32[]{:S(2)}) %collective-permute-start.11) | collective-permute-done | bytes 1179680 | tf_op jit(solution)/shard_map/ppermute | solution.py:250
  96.9 3.0 %collective-permute-start.12 = (bf16[147456]{0:T(1024)(128)(2,1)S(1)}, bf16[147456]{0:T(1024)(128)(2,1)S(1)}, u32[]{:S(2)}, u32[]{:S(2)}) collective-permute-start(bf16[147456]{0:T(1024)(128)(2,1)S(1)} %bitcast.166), channel_id=1, source_target_pairs={{0,4},{4,0},{8,12},{12,8},{1,5},{5,1},{9,13},{13,9},{2,6},{6,2},{1... | collective-permute-start | bytes 884744 | tf_op jit(solution)/shard_map/ppermute | solution.py:101
  99.9 7.3 %collective-permute-done.12 = bf16[147456]{0:T(1024)(128)(2,1)S(1)} collective-permute-done((bf16[147456]{0:T(1024)(128)(2,1)S(1)}, bf16[147456]{0:T(1024)(128)(2,1)S(1)}, u32[]{:S(2)}, u32[]{:S(2)}) %collective-permute-start.12) | collective-permute-done | bytes 294944 | tf_op jit(solution)/shard_map/ppermute | solution.py:101
  108.4 4.3 %collective-permute-done.13 = bf16[73728]{0:T(1024)(128)(2,1)S(1)} collective-permute-done((bf16[73728]{0:T(1024)(128)(2,1)S(1)}, bf16[73728]{0:T(1024)(128)(2,1)S(1)}, u32[]{:S(2)}, u32[]{:S(2)}) %collective-permute-start.13) | collective-permute-done | bytes 147488 | tf_op jit(solution)/shard_map/ppermute | solution.py:101
  112.8 2.2 %collective-permute-start.14 = (bf16[73728]{0:T(1024)(128)(2,1)S(1)}, bf16[73728]{0:T(1024)(128)(2,1)S(1)}, u32[]{:S(2)}, u32[]{:S(2)}) collective-permute-start(bf16[73728]{0:T(1024)(128)(2,1)S(1)} %add_convert_fusion.2), channel_id=1, source_target_pairs={{0,1},{1,0},{2,3},{3,2},{4,5},{5,4},{6,7},{7,6},{8,9},{9,8},{10,11... | collective-permute-start | bytes 442376 | tf_op jit(solution)/shard_map/ppermute | solution.py:101
  115.5 2.6 %collective-permute-done.14 = bf16[73728]{0:T(1024)(128)(2,1)S(1)} collective-permute-done((bf16[73728]{0:T(1024)(128)(2,1)S(1)}, bf16[73728]{0:T(1024)(128)(2,1)S(1)}, u32[]{:S(2)}, u32[]{:S(2)}) %collective-permute-start.14) | collective-permute-done | bytes 147488 | tf_op jit(solution)/shard_map/ppermute | solution.py:101
  118.2 3.5 %collective-permute-start.15 = (bf16[73728]{0:T(1024)(128)(2,1)S(1)}, bf16[73728]{0:T(1024)(128)(2,1)S(1)}, u32[]{:S(2)}, u32[]{:S(2)}) collective-permute-start(bf16[73728]{0:T(1024)(128)(2,1)S(1)} %add_convert_fusion.1), channel_id=1, source_target_pairs={{0,2},{1,3},{2,0},{3,1},{4,6},{5,7},{6,4},{7,5},{8,10},{9,11},{10,... | collective-permute-start | bytes 442376 | tf_op jit(solution)/shard_map/ppermute | solution.py:101
  123.1 3.3 %collective-permute-done.15 = bf16[73728]{0:T(1024)(128)(2,1)S(1)} collective-permute-done((bf16[73728]{0:T(1024)(128)(2,1)S(1)}, bf16[73728]{0:T(1024)(128)(2,1)S(1)}, u32[]{:S(2)}, u32[]{:S(2)}) %collective-permute-start.15) | collective-permute-done | bytes 147488 | tf_op jit(solution)/shard_map/ppermute | solution.py:101
  128.5 3.3 %collective-permute-done.16 = bf16[73728]{0:T(1024)(128)(2,1)S(1)} collective-permute-done((bf16[73728]{0:T(1024)(128)(2,1)S(1)}, bf16[73728]{0:T(1024)(128)(2,1)S(1)}, u32[]{:S(2)}, u32[]{:S(2)}) %collective-permute-start.16) | collective-permute-done | bytes 147488 | tf_op jit(solution)/shard_map/ppermute | solution.py:101
  131.8 1.9 %collective-permute-start.17 = (bf16[147456]{0:T(1024)(128)(2,1)S(1)}, bf16[147456]{0:T(1024)(128)(2,1)S(1)}, u32[]{:S(2)}, u32[]{:S(2)}) collective-permute-start(bf16[147456]{0:T(1024)(128)(2,1)S(1)} %maximum_select_fusion.2), channel_id=1, source_target_pairs={{0,4},{4,0},{8,12},{12,8},{1,5},{5,1},{9,13},{13,9},{2,6},{6,2},{1... | collective-permute-start | bytes 884744 | tf_op jit(solution)/shard_map/ppermute | solution.py:101
  135.5 3.1 %collective-permute-done.17 = bf16[147456]{0:T(1024)(128)(2,1)S(1)} collective-permute-done((bf16[147456]{0:T(1024)(128)(2,1)S(1)}, bf16[147456]{0:T(1024)(128)(2,1)S(1)}, u32[]{:S(2)}, u32[]{:S(2)}) %collective-permute-start.17) | collective-permute-done | bytes 294944 | tf_op jit(solution)/shard_map/ppermute | solution.py:101
  (163 shorter events, 41.7 us)
Async XLA Ops:
  0.6 2.8 %copy-start = (bf16[4,16,32,128]{3,2,1,0:T(8,128)(2,1)S(1)}, bf16[4,16,32,128]{3,2,1,0:T(8,128)(2,1)}, u32[]{:S(2)}) copy-start(bf16[4,16,32,128]{3,2,1,0:T(8,128)(2,1)} %param.6) | copy-start | bytes 1572868
  0.6 2.0 %copy-start.11 = (bf16[2,3,3,128,128]{4,3,2,1,0:T(8,128)(2,1)S(1)}, bf16[2,3,3,128,128]{4,3,2,1,0:T(8,128)(2,1)}, u32[]{:S(2)}) copy-start(bf16[2,3,3,128,128]{4,3,2,1,0:T(8,128)(2,1)} %param.5) | copy-start | bytes 1769476
  0.7 2.1 %copy-start.16 = (s32[4]{0:T(128)S(1)}, s32[4]{0:T(128)}, u32[]{:S(2)}) copy-start(s32[4]{0:T(128)} %param.7) | copy-start | bytes 52
  2.1 2.1 %collective-permute-start = (bf16[2,16,32,128]{3,0,2,1:T(2,128)(2,1)S(1)}, bf16[2,16,32,128]{3,0,2,1:T(2,128)(2,1)S(1)}, u32[]{:S(2)}, u32[]{:S(2)}) collective-permute-start(bf16[2,16,32,128]{3,0,2,1:T(2,128)(2,1)S(1)} %bitcast.168), channel_id=1, source_target_pairs={{0,16},{16,0},{1,17},{17,1},{2,18},{18,2},{3,19},{19,3},{4,20},{20... | collective-permute-start | bytes 786440 | tf_op jit(solution)/shard_map/ppermute | solution.py:250
  2.7 19.8 %collective-permute-start.9 = (bf16[2,3,3,128,128]{4,3,2,1,0:T(8,128)(2,1)S(1)}, bf16[2,3,3,128,128]{4,3,2,1,0:T(8,128)(2,1)}, u32[]{:S(2)}, u32[]{:S(2)}) collective-permute-start(bf16[2,3,3,128,128]{4,3,2,1,0:T(8,128)(2,1)S(1)} %copy-done.11), channel_id=1, source_target_pairs={{0,16},{16,0},{1,17},{17,1},{2,18},{18,2},{3,19},{19,3},{4,20},{20... | collective-permute-start | bytes 1769480 | tf_op jit(solution)/shard_map/ppermute | solution.py:250
  5.2 10.0 %collective-permute-start.2 = (bf16[4,6,32,128]{3,0,2,1:T(4,128)(2,1)S(1)}, bf16[4,6,32,128]{3,0,2,1:T(4,128)(2,1)S(1)}, u32[]{:S(2)}, u32[]{:S(2)}) collective-permute-start(bf16[4,6,32,128]{3,0,2,1:T(4,128)(2,1)S(1)} %get-tuple-element.27), channel_id=1, source_target_pairs={{4,0},{5,1},{6,2},{7,3},{8,4},{9,5},{10,6},{11,7},{12,8},{13,9},{1... | collective-permute-start | bytes 589832 | tf_op jit(solution)/shard_map/ppermute | solution.py:43
  6.5 9.8 %collective-permute-start.1 = (bf16[4,6,32,128]{3,0,2,1:T(4,128)(2,1)S(1)}, bf16[4,6,32,128]{3,0,2,1:T(4,128)(2,1)S(1)}, u32[]{:S(2)}, u32[]{:S(2)}) collective-permute-start(bf16[4,6,32,128]{3,0,2,1:T(4,128)(2,1)S(1)} %get-tuple-element.26), channel_id=1, source_target_pairs={{0,4},{1,5},{2,6},{3,7},{4,8},{5,9},{6,10},{7,11},{8,12},{9,13},{1... | collective-permute-start | bytes 589832 | tf_op jit(solution)/shard_map/ppermute | solution.py:43
  16.6 8.2 %collective-permute-start.4 = (bf16[4,28,6,128]{3,0,2,1:T(4,128)(2,1)S(1)}, bf16[4,28,6,128]{3,0,2,1:T(4,128)(2,1)S(1)}, u32[]{:S(2)}, u32[]{:S(2)}) collective-permute-start(bf16[4,28,6,128]{3,0,2,1:T(4,128)(2,1)S(1)} %get-tuple-element.21), channel_id=1, source_target_pairs={{1,0},{2,1},{3,2},{5,4},{6,5},{7,6},{9,8},{10,9},{11,10},{13,12},{... | collective-permute-start | bytes 516104 | tf_op jit(solution)/shard_map/ppermute | solution.py:43
  17.9 7.5 %collective-permute-start.3 = (bf16[4,28,6,128]{3,0,2,1:T(4,128)(2,1)S(1)}, bf16[4,28,6,128]{3,0,2,1:T(4,128)(2,1)S(1)}, u32[]{:S(2)}, u32[]{:S(2)}) collective-permute-start(bf16[4,28,6,128]{3,0,2,1:T(4,128)(2,1)S(1)} %get-tuple-element.20), channel_id=1, source_target_pairs={{0,1},{1,2},{2,3},{4,5},{5,6},{6,7},{8,9},{9,10},{10,11},{12,13},{... | collective-permute-start | bytes 516104 | tf_op jit(solution)/shard_map/ppermute | solution.py:43
  23.6 1.2 copy-start.2
  23.6 7.1 %copy-start.4 = (bf16[2,3,3,128,128]{4,3,2,1,0:T(8,128)(2,1)}, bf16[2,3,3,128,128]{4,3,2,1,0:T(8,128)(2,1)S(1)}, u32[]{:S(2)}) copy-start(bf16[2,3,3,128,128]{4,3,2,1,0:T(8,128)(2,1)S(1)} %get-tuple-element.19) | copy-start | bytes 1769476
  36.8 4.9 %copy-start.6 = (bf16[28,2,44,128]{3,1,2,0:T(2,128)(2,1)S(1)}, bf16[28,2,44,128]{3,1,2,0:T(2,128)(2,1)}, u32[]{:S(2)}) copy-start(bf16[28,2,44,128]{3,1,2,0:T(2,128)(2,1)} %get-tuple-element.16) | copy-start | bytes 1892356
  37.0 17.1 %collective-permute-start.5 = (bf16[2,4,32,128]{3,2,0,1:T(8,128)(2,1)S(1)}, bf16[2,4,32,128]{3,2,0,1:T(8,128)(2,1)S(1)}, u32[]{:S(2)}, u32[]{:S(2)}) collective-permute-start(bf16[2,4,32,128]{3,2,0,1:T(8,128)(2,1)S(1)} %get-tuple-element.35), channel_id=1, source_target_pairs={{0,4},{1,5},{2,6},{3,7},{4,8},{5,9},{6,10},{7,11},{8,12},{9,13},{1... | collective-permute-start | bytes 196616 | tf_op jit(solution)/shard_map/ppermute | solution.py:43
  41.7 1.1 copy-start.3
  52.3 7.5 %collective-permute-start.6 = (bf16[2,4,32,128]{3,2,0,1:T(8,128)(2,1)S(1)}, bf16[2,4,32,128]{3,2,0,1:T(8,128)(2,1)S(1)}, u32[]{:S(2)}, u32[]{:S(2)}) collective-permute-start(bf16[2,4,32,128]{3,2,0,1:T(8,128)(2,1)S(1)} %get-tuple-element.34), channel_id=1, source_target_pairs={{4,0},{5,1},{6,2},{7,3},{8,4},{9,5},{10,6},{11,7},{12,8},{13,9},{1... | collective-permute-start | bytes 196616 | tf_op jit(solution)/shard_map/ppermute | solution.py:43
  54.0 12.3 %copy-start.19 = (pred[16,5]{0,1:T(8,128)(4,1)S(1)}, pred[16,5]{0,1:T(8,128)(4,1)}, u32[]{:S(2)}) copy-start(pred[16,5]{0,1:T(8,128)(4,1)} %constant.178) | copy-start | bytes 244
  59.9 8.0 %collective-permute-start.8 = (bf16[2,24,4,128]{3,2,0,1:T(4,128)(2,1)S(1)}, bf16[2,24,4,128]{3,2,0,1:T(4,128)(2,1)S(1)}, u32[]{:S(2)}, u32[]{:S(2)}) collective-permute-start(bf16[2,24,4,128]{3,2,0,1:T(4,128)(2,1)S(1)} %get-tuple-element.33), channel_id=1, source_target_pairs={{1,0},{2,1},{3,2},{5,4},{6,5},{7,6},{9,8},{10,9},{11,10},{13,12},{... | collective-permute-start | bytes 147464 | tf_op jit(solution)/shard_map/ppermute | solution.py:43
  61.2 6.8 %collective-permute-start.7 = (bf16[2,24,4,128]{3,2,0,1:T(4,128)(2,1)S(1)}, bf16[2,24,4,128]{3,2,0,1:T(4,128)(2,1)S(1)}, u32[]{:S(2)}, u32[]{:S(2)}) collective-permute-start(bf16[2,24,4,128]{3,2,0,1:T(4,128)(2,1)S(1)} %get-tuple-element.32), channel_id=1, source_target_pairs={{0,1},{1,2},{2,3},{4,5},{5,6},{6,7},{8,9},{9,10},{10,11},{12,13},{... | collective-permute-start | bytes 147464 | tf_op jit(solution)/shard_map/ppermute | solution.py:43
  84.7 1.8 %copy-start.15 = (pred[18,34]{1,0:T(8,128)(4,1)S(1)}, pred[18,34]{1,0:T(8,128)(4,1)}, u32[]{:S(2)}) copy-start(pred[18,34]{1,0:T(8,128)(4,1)} %broadcast_and_fusion.4) | copy-start | bytes 1840
  91.3 1.2 copy-start.1
  92.5 3.1 %collective-permute-start.11 = (f32[2,3,3,128,128]{4,3,2,1,0:T(8,128)}, f32[2,3,3,128,128]{4,3,2,1,0:T(8,128)S(1)}, u32[]{:S(2)}, u32[]{:S(2)}) collective-permute-start(f32[2,3,3,128,128]{4,3,2,1,0:T(8,128)} %fusion.18), channel_id=1, source_target_pairs={{0,16},{16,0},{1,17},{17,1},{2,18},{18,2},{3,19},{19,3},{4,20},{20... | collective-permute-start | bytes 3538952 | tf_op jit(solution)/shard_map/ppermute | solution.py:250
  96.9 18.1 %copy-start.8 = (bf16[20,16,5,128]{3,1,2,0:T(8,128)(2,1)S(1)}, bf16[20,16,5,128]{3,1,2,0:T(8,128)(2,1)}, u32[]{:S(2)}) copy-start(bf16[20,16,5,128]{3,1,2,0:T(8,128)(2,1)} %copy-done.7) | copy-start | bytes 1228804
  96.9 10.3 %collective-permute-start.12 = (bf16[147456]{0:T(1024)(128)(2,1)S(1)}, bf16[147456]{0:T(1024)(128)(2,1)S(1)}, u32[]{:S(2)}, u32[]{:S(2)}) collective-permute-start(bf16[147456]{0:T(1024)(128)(2,1)S(1)} %bitcast.166), channel_id=1, source_target_pairs={{0,4},{4,0},{8,12},{12,8},{1,5},{5,1},{9,13},{13,9},{2,6},{6,2},{1... | collective-permute-start | bytes 884744 | tf_op jit(solution)/shard_map/ppermute | solution.py:101
  107.2 7.9 %copy-start.10 = (bf16[2,18,34,128]{3,0,2,1:T(2,128)(2,1)S(1)}, bf16[2,18,34,128]{3,0,2,1:T(2,128)(2,1)}, u32[]{:S(2)}) copy-start(bf16[2,18,34,128]{3,0,2,1:T(2,128)(2,1)} %copy-done.9) | copy-start | bytes 940036
  107.3 5.4 %collective-permute-start.13 = (bf16[73728]{0:T(1024)(128)(2,1)S(1)}, bf16[73728]{0:T(1024)(128)(2,1)S(1)}, u32[]{:S(2)}, u32[]{:S(2)}) collective-permute-start(bf16[73728]{0:T(1024)(128)(2,1)S(1)} %select_convert_fusion.2), channel_id=1, source_target_pairs={{0,8},{4,12},{8,0},{12,4},{1,9},{5,13},{9,1},{13,5},{2,10},{6,14},... | collective-permute-start | bytes 442376 | tf_op jit(solution)/shard_map/ppermute | solution.py:101
  112.8 5.4 %collective-permute-start.14 = (bf16[73728]{0:T(1024)(128)(2,1)S(1)}, bf16[73728]{0:T(1024)(128)(2,1)S(1)}, u32[]{:S(2)}, u32[]{:S(2)}) collective-permute-start(bf16[73728]{0:T(1024)(128)(2,1)S(1)} %add_convert_fusion.2), channel_id=1, source_target_pairs={{0,1},{1,0},{2,3},{3,2},{4,5},{5,4},{6,7},{7,6},{8,9},{9,8},{10,11... | collective-permute-start | bytes 442376 | tf_op jit(solution)/shard_map/ppermute | solution.py:101
  115.1 6.6 %copy-start.13 = (bf16[2,3,3,128,128]{3,4,2,1,0:T(8,128)(2,1)S(1)}, bf16[2,3,3,128,128]{3,4,2,1,0:T(8,128)(2,1)}, u32[]{:S(2)}) copy-start(bf16[2,3,3,128,128]{3,4,2,1,0:T(8,128)(2,1)} %get-tuple-element.36) | copy-start | bytes 1769476
  115.1 6.6 %copy-start.17 = (pred[16,5]{0,1:T(8,128)(4,1)S(1)}, pred[16,5]{0,1:T(8,128)(4,1)}, u32[]{:S(2)}) copy-start(pred[16,5]{0,1:T(8,128)(4,1)} %constant.176) | copy-start | bytes 244
  118.2 8.3 %collective-permute-start.15 = (bf16[73728]{0:T(1024)(128)(2,1)S(1)}, bf16[73728]{0:T(1024)(128)(2,1)S(1)}, u32[]{:S(2)}, u32[]{:S(2)}) collective-permute-start(bf16[73728]{0:T(1024)(128)(2,1)S(1)} %add_convert_fusion.1), channel_id=1, source_target_pairs={{0,2},{1,3},{2,0},{3,1},{4,6},{5,7},{6,4},{7,5},{8,10},{9,11},{10,... | collective-permute-start | bytes 442376 | tf_op jit(solution)/shard_map/ppermute | solution.py:101
  126.5 5.2 %collective-permute-start.16 = (bf16[73728]{0:T(1024)(128)(2,1)S(1)}, bf16[73728]{0:T(1024)(128)(2,1)S(1)}, u32[]{:S(2)}, u32[]{:S(2)}) collective-permute-start(bf16[73728]{0:T(1024)(128)(2,1)S(1)} %add_convert_fusion), channel_id=1, source_target_pairs={{0,8},{4,12},{8,0},{12,4},{1,9},{5,13},{9,1},{13,5},{2,10},{6,14},... | collective-permute-start | bytes 442376 | tf_op jit(solution)/shard_map/ppermute | solution.py:101
  128.4 5.3 %collective-permute-start.10 = (bf16[2,16,32,128]{3,0,2,1:T(2,128)(2,1)S(1)}, bf16[2,16,32,128]{3,0,2,1:T(2,128)(2,1)S(1)}, u32[]{:S(2)}, u32[]{:S(2)}) collective-permute-start(bf16[2,16,32,128]{3,0,2,1:T(2,128)(2,1)S(1)} %get-tuple-element.23), channel_id=1, source_target_pairs={{0,16},{16,0},{1,17},{17,1},{2,18},{18,2},{3,19},{19,3},{4,20},{20... | collective-permute-start | bytes 786440 | tf_op jit(solution)/shard_map/ppermute | solution.py:250
  131.8 6.8 %collective-permute-start.17 = (bf16[147456]{0:T(1024)(128)(2,1)S(1)}, bf16[147456]{0:T(1024)(128)(2,1)S(1)}, u32[]{:S(2)}, u32[]{:S(2)}) collective-permute-start(bf16[147456]{0:T(1024)(128)(2,1)S(1)} %maximum_select_fusion.2), channel_id=1, source_target_pairs={{0,4},{4,0},{8,12},{12,8},{1,5},{5,1},{9,13},{13,9},{2,6},{6,2},{1... | collective-permute-start | bytes 884744 | tf_op jit(solution)/shard_map/ppermute | solution.py:101
  (9 other events, 8.6 us)

commit v2 on v0

--- a/solution.py
+++ b/solution.py
@@ -260,11 +260,11 @@
 
     top_rim = [layer_count * (s + 1) for s in range(2)]
     rims = [r + layer_count for r in top_rim]
-    stacked = jnp.concatenate([by_section(mine, theirs, s) for s in range(2)], axis=0)
-    stacked = with_rim(stacked, rims[1], 0, range(2))
-    firsts = [crop(stacked[:half], rims[1] - rims[0]), stacked[half:]]
     group_cotangent = lax.dynamic_slice_in_dim(top_cotangent, section_index * half, half, 0)
-    top_ext = with_rim(group_cotangent, top_rim[1], 0, range(2))
+    stacked = [by_section(mine, theirs, s) for s in range(2)] + [group_cotangent]
+    stacked = with_rim(jnp.concatenate(stacked, axis=0), rims[1], 0, range(2))
+    firsts = [crop(stacked[:half], rims[1] - rims[0]), stacked[half : 2 * half]]
+    top_ext = crop(stacked[2 * half :], rims[1] - top_rim[1])
 
     results, partials = [None, None], [None, None]
     for s in (1, 0):

time: 134 us -> 131 us (0.978)
  waiting for transfers between devices: 30.6 us -> 37.5 us
  starting transfers between devices: 37.2 us -> 31.5 us
  local copies, waits for them, and re-layouts: 17.3 us -> 14.6 us
  other arithmetic: 29.7 us -> 28.1 us
    ppermute x8 -> x4, starting transfers between devices: 25.9 us -> 12.6 us  [from_neighbours(): parts.append(lax.ppermute(piece, AXES, pairs))]
    ppermute x8 -> x4, waiting for transfers between devices: 1.38 us -> 10.4 us  [from_neighbours(): parts.append(lax.ppermute(piece, AXES, pairs))]
    ppermute x6, starting transfers between devices: 10.5 us -> 18.2 us  [exchange(): return lax.ppermute(values, axis, [(i, i ^ distance) for i in range(count)])]
    ppermute x6, waiting for transfers between devices: 26.2 us -> 24 us  [exchange(): return lax.ppermute(values, axis, [(i, i ^ distance) for i in range(count)])]
    conv_general_dilated x1 -> x3, other arithmetic: 0.07 us -> 1.93 us  [convolve(): lax.conv_general_dilated(padded, kernel, (1, 1), 'VALID', dimension_numbe...]
    slice x4 -> x3, local copies, waits for them, and re-layouts: 2.6 us -> 1.14 us  [local_split(): firsts = [crop(stacked[:half], rims[1] - rims[0]), stacked[half:2 * half]]]
    unnamed x54 -> x57, local copies, waits for them, and re-layouts: 6.29 us -> 5.38 us
  transfers between devices with their start and end apart: 18 -> 14, of which waited for: 8 -> 11; matrix products, arithmetic and copies ran while one was open for 23% -> 5% of each run, Pallas kernels for 0% -> 0%
where the time goes in v2:
time: 131 us; the launch traced here: 130 us
  waiting for transfers between devices  37.5 us (29%)
  starting transfers between devices  31.5 us (24%)
  other arithmetic  28.1 us (21%)
  matrix products  17 us (13%)
  local copies, waits for them, and re-layouts  14.6 us (11%)
  between operations  1.6 us (1%)
    ppermute x6, waiting for transfers between devices, exchange(): return lax.ppermute(values, axis, [(i, i ^ distance) for i in range(count)])  24 us
    ppermute x6, starting transfers between devices, exchange(): return lax.ppermute(values, axis, [(i, i ^ distance) for i in range(count)])  18.2 us
    ppermute x4, starting transfers between devices, from_neighbours(): parts.append(lax.ppermute(piece, AXES, pairs))  12.6 us
    ppermute x4, waiting for transfers between devices, from_neighbours(): parts.append(lax.ppermute(piece, AXES, pairs))  10.4 us
    conv_general_dilated x8, matrix products, convolve(): lax.conv_general_dilated(padded, kernel, (1, 1), 'VALID', dimension_numbe...  9.95 us
    convert_element_type x4, other arithmetic, local_split(): current = current.astype(jnp.bfloat16)  9.08 us
    convert_element_type x4, other arithmetic, section_chain(): signal = signal.astype(jnp.bfloat16)  8.96 us
    transpose x4, matrix products, kernel_terms(): return jnp.transpose(terms, (1, 2, 0, 3))  7.09 us
  transfers between devices with their start and end apart: 14, of which 11 were waited for; matrix products, arithmetic and copies ran while one was open for 5% of the time, Pallas kernels for 0%

profile of v2, /device:TPU:0, one launch (start us, length us, event | category | flops | bytes accessed | tf_op | source)
XLA Modules:
  0.0 130.4 jit_solution(16467170611617583104)
XLA Ops:
  5.4 5.4 %collective-permute-start.1 = (bf16[6,6,32,128]{3,2,0,1:T(8,128)(2,1)S(1)}, bf16[6,6,32,128]{3,2,0,1:T(8,128)(2,1)S(1)}, u32[]{:S(2)}, u32[]{:S(2)}) collective-permute-start(bf16[6,6,32,128]{3,2,0,1:T(8,128)(2,1)S(1)} %get-tuple-element.18), channel_id=1, source_target_pairs={{0,4},{1,5},{2,6},{3,7},{4,8},{5,9},{6,10},{7,11},{8,12},{9,13},{1... | collective-permute-start | bytes 884744 | tf_op jit(solution)/shard_map/ppermute | solution.py:43
  10.9 5.8 %collective-permute-done.2 = bf16[6,6,32,128]{3,2,0,1:T(8,128)(2,1)S(1)} collective-permute-done((bf16[6,6,32,128]{3,2,0,1:T(8,128)(2,1)S(1)}, bf16[6,6,32,128]{3,2,0,1:T(8,128)(2,1)S(1)}, u32[]{:S(2)}, u32[]{:S(2)}) %collective-permute-start.2) | collective-permute-done | bytes 294944 | tf_op jit(solution)/shard_map/ppermute | solution.py:43
  18.8 4.6 %collective-permute-start.3 = (bf16[6,28,6,128]{3,2,0,1:T(8,128)(2,1)S(1)}, bf16[6,28,6,128]{3,2,0,1:T(8,128)(2,1)S(1)}, u32[]{:S(2)}, u32[]{:S(2)}) collective-permute-start(bf16[6,28,6,128]{3,2,0,1:T(8,128)(2,1)S(1)} %get-tuple-element.14), channel_id=1, source_target_pairs={{0,1},{1,2},{2,3},{4,5},{5,6},{6,7},{8,9},{9,10},{10,11},{12,13},{... | collective-permute-start | bytes 774152 | tf_op jit(solution)/shard_map/ppermute | solution.py:43
  25.8 2.8 %collective-permute-done.4 = bf16[6,28,6,128]{3,2,0,1:T(8,128)(2,1)S(1)} collective-permute-done((bf16[6,28,6,128]{3,2,0,1:T(8,128)(2,1)S(1)}, bf16[6,28,6,128]{3,2,0,1:T(8,128)(2,1)S(1)}, u32[]{:S(2)}, u32[]{:S(2)}) %collective-permute-start.4) | collective-permute-done | bytes 258080 | tf_op jit(solution)/shard_map/ppermute | solution.py:43
  29.7 1.6 %pad_maximum_fusion.2 = (bf16[2,28,44,128]{3,2,0,1:T(8,128)(2,1)}, bf16[2,28,44,128]{3,2,0,1:T(8,128)(2,1)S(1)}) fusion(bf16[6,28,6,128]{3,2,0,1:T(8,128)(2,1)S(1)} %collective-permute-done.4, bf16[6,28,6,128]{3,2,0,1:T(8,128)(2,1)S(1)} %collective-permute-done.3, bf16[6,6,32,128]{3,2,0,1:T(8,128)(2,1)S(1)} %collective-permute-done.2, ...), kind=kLoop, calls=%fused_computation.67 | loop fusion | flops 8830976 | bytes 3153920 | tf_op jit(solution)/shard_map/concatenate | solution.py:44
  33.8 1.7 %fusion.1 = bf16[26,16,6,128]{3,1,2,0:T(8,128)(2,1)S(1)} fusion(bf16[28,2,8,8,128]{4,1,3,2,0:T(2,128)(2,1)S(1)} %fusion.17, pred[16,6]{0,1:T(8,128)(4,1)S(1)} %copy-done.26, bf16[2,3,3,128,128]{4,3,2,1,0:T(8,128)(2,1)S(1)} %get-tuple-element.17), kind=kOutput, calls=%fused_computation.6 | convolution fusion | flops 736739328 | bytes 1852416 | tf_op jit(solution)/shard_map/conv_general_dilated | solution.py:63
  35.9 1.7 %fusion.11 = bf16[26,2,42,128]{3,1,2,0:T(2,128)(2,1)S(1)} fusion(bf16[26,2,42,128]{3,2,1,0:T(8,128)(2,1)S(1)} %bitcast.138, pred[26,42]{1,0:T(8,128)(4,1)S(1)} %broadcast_and_fusion), kind=kLoop, calls=%fused_computation.35 | loop fusion | flops 279552 | bytes 1119300 | tf_op jit(solution)/shard_map/convert_element_type | solution.py:279
  37.6 1.7 %fusion.96 = bf16[2,26,42,128]{3,0,2,1:T(2,128)(2,1)S(1)} fusion(bf16[26,2,42,128]{3,2,1,0:T(8,128)(2,1)S(1)} %bitcast.139, pred[26,42]{1,0:T(8,128)(4,1)S(1)} %broadcast_and_fusion), kind=kLoop, calls=%fused_computation.191 | loop fusion | flops 279552 | bytes 1119300 | tf_op jit(solution)/shard_map/convert_element_type | solution.py:279
  42.6 2.8 %fusion.20 = bf16[22,2,38,128]{3,1,2,0:T(2,128)(2,1)S(1)} fusion(bf16[22,2,38,128]{3,0,2,1:T(8,128)(2,1)S(1)} %slice.149, pred[22,38]{1,0:T(8,128)(4,1)S(1)} %broadcast_and_fusion.2), kind=kLoop, calls=%fused_computation.48 | loop fusion | flops 214016 | bytes 856900 | tf_op jit(solution)/shard_map/convert_element_type | solution.py:279
  45.4 2.8 %fusion.95 = bf16[2,22,38,128]{3,0,2,1:T(2,128)(2,1)S(1)} fusion(bf16[22,2,38,128]{3,0,2,1:T(8,128)(2,1)S(1)} %slice.149, pred[22,38]{1,0:T(8,128)(4,1)S(1)} %broadcast_and_fusion.2), kind=kLoop, calls=%fused_computation.190 | loop fusion | flops 214016 | bytes 856900 | tf_op jit(solution)/shard_map/convert_element_type | solution.py:279
  49.3 1.6 %fusion.2 = bf16[24,16,6,128]{3,1,2,0:T(8,128)(2,1)S(1)} fusion(bf16[26,2,7,2,128]{4,2,1,3,0:T(8,128)(2,1)S(1)} %slice.136, bf16[26,2,8,6,128]{4,2,1,3,0:T(8,128)(2,1)S(1)} %copy.147, pred[16,6]{0,1:T(8,128)(4,1)S(1)} %copy-done.25, bf16[2,3,3,128,128]{4,3,2,1,0:T(8,128)(2,1)S(1)} %copy-done.8), kind=kOutput, calls=%fused_computation.8 | convolution fusion | flops 682622976 | bytes 1737728 | tf_op jit(solution)/shard_map/conv_general_dilated | solution.py:63
  52.1 2.1 %fusion.15 = bf16[2,24,40,128]{3,2,0,1:T(8,128)(2,1)S(1)} fusion(bf16[24,2,40,128]{3,0,2,1:T(8,128)(2,1)S(1)} %slice.138, bf16[6,28,6,128]{3,2,0,1:T(8,128)(2,1)S(1)} %copy-done.11, bf16[6,28,6,128]{3,2,0,1:T(8,128)(2,1)S(1)} %copy-done.13, bf16[6,6,32,128]{3,2,0,1:T(8,128)(2,1)S(1)} %copy-done.2, bf16[6,6,32,128]{3,2,0,1:T(8,128)(2,1)S(1)} %copy-done.4, ...), kind=kLoop, calls=%fused_computation.42 | loop fusion | flops 5160960 | bytes 2876352 | tf_op jit(solution)/shard_map/convert_element_type | solution.py:233
  57.0 2.9 %fusion.23 = bf16[2,22,38,128]{3,0,2,1:T(2,128)(2,1)S(1)} fusion(f32[22,2,38,128]{3,0,2,1:T(8,128)S(1)} %slice.141, pred[22,38]{1,0:T(8,128)(4,1)S(1)} %broadcast_and_fusion.2, bf16[2,26,42,128]{3,0,2,1:T(2,128)(2,1)S(1)} %fusion.96), kind=kLoop, calls=%fused_computation.52 | loop fusion | flops 1284096 | bytes 1712964 | tf_op jit(solution)/shard_map/convert_element_type | solution.py:233
  59.9 1.7 %convolution_bitcast_fusion.2 = f32[1,3,3,128,128]{4,3,2,1,0:T(8,128)S(1)} fusion(bf16[2,28,44,128]{3,2,0,1:T(8,128)(2,1)S(1)} %get-tuple-element.13, bf16[2,22,38,128]{3,0,2,1:T(2,128)(2,1)S(1)} %fusion.23), kind=kOutput, calls=%fused_computation.25 | convolution fusion | flops 301989888 | bytes 1540096 | tf_op jit(solution)/shard_map/transpose | solution.py:82
  65.4 2.0 %fusion.35 = bf16[20,2,36,128]{3,1,2,0:T(2,128)(2,1)S(1)} fusion(f32[20,2,36,128]{3,0,2,1:T(8,128)S(1)} %slice.145, pred[20,36]{1,0:T(8,128)(4,1)S(1)} %broadcast_and_fusion.3, bf16[20,2,36,128]{3,0,2,1:T(8,128)(2,1)S(1)} %slice.152), kind=kLoop, calls=%fused_computation.65 | loop fusion | flops 1290240 | bytes 1475280 | tf_op jit(solution)/shard_map/convert_element_type | solution.py:233
  69.8 1.8 %convolution_bitcast_fusion = f32[1,3,3,128,128]{4,3,2,1,0:T(8,128)S(1)} fusion(bf16[26,2,42,128]{3,1,2,0:T(2,128)(2,1)S(1)} %fusion.11, bf16[2,16,32,128]{3,2,0,1:T(8,128)(2,1)S(1)} %slice.165), kind=kOutput, calls=%fused_computation.23 | convolution fusion | flops 301989888 | bytes 1411072 | tf_op jit(solution)/shard_map/transpose | solution.py:82
  71.6 1.8 %convolution_bitcast_fusion.1 = f32[1,3,3,128,128]{4,3,2,1,0:T(8,128)S(1)} fusion(bf16[22,2,38,128]{3,1,2,0:T(2,128)(2,1)S(1)} %fusion.20, bf16[2,20,36,128]{3,0,2,1:T(2,128)(2,1)S(1)} %bitcast.161), kind=kOutput, calls=%fused_computation.24 | convolution fusion | flops 301989888 | bytes 1280000 | tf_op jit(solution)/shard_map/transpose | solution.py:82
  73.4 2.0 %fusion.55 = bf16[2,18,34,128]{3,0,2,1:T(2,128)(2,1)S(1)} fusion(f32[18,2,34,128]{3,0,2,1:T(8,128)S(1)} %slice.155, pred[18,34]{1,0:T(8,128)(4,1)S(1)} %broadcast_and_fusion.4, bf16[2,22,38,128]{3,0,2,1:T(2,128)(2,1)S(1)} %fusion.95), kind=kLoop, calls=%fused_computation.91 | loop fusion | flops 940032 | bytes 1253988 | tf_op jit(solution)/shard_map/convert_element_type | solution.py:233
  76.2 1.8 %convolution_bitcast_fusion.3 = f32[1,3,3,128,128]{4,3,2,1,0:T(8,128)S(1)} fusion(bf16[2,28,44,128]{3,2,0,1:T(8,128)(2,1)S(1)} %copy-done.9, bf16[2,18,34,128]{3,0,2,1:T(2,128)(2,1)S(1)} %fusion.55), kind=kOutput, calls=%fused_computation.26 | convolution fusion | flops 301989888 | bytes 1540096 | tf_op jit(solution)/shard_map/transpose | solution.py:82
  79.1 3.2 %collective-permute-done.7 = f32[2,3,3,128,128]{4,3,2,1,0:T(8,128)} collective-permute-done((f32[2,3,3,128,128]{4,3,2,1,0:T(8,128)}, f32[2,3,3,128,128]{4,3,2,1,0:T(8,128)}, u32[]{:S(2)}, u32[]{:S(2)}) %collective-permute-start.7) | collective-permute-done | bytes 1179680 | tf_op jit(solution)/shard_map/ppermute | solution.py:250
  83.8 5.0 %collective-permute-start.8 = (bf16[147456]{0:T(1024)(128)(2,1)S(1)}, bf16[147456]{0:T(1024)(128)(2,1)S(1)}, u32[]{:S(2)}, u32[]{:S(2)}) collective-permute-start(bf16[147456]{0:T(1024)(128)(2,1)S(1)} %bitcast.168), channel_id=1, source_target_pairs={{0,4},{4,0},{8,12},{12,8},{1,5},{5,1},{9,13},{13,9},{2,6},{6,2},{1... | collective-permute-start | bytes 884744 | tf_op jit(solution)/shard_map/ppermute | solution.py:101
  88.9 7.3 %collective-permute-done.8 = bf16[147456]{0:T(1024)(128)(2,1)S(1)} collective-permute-done((bf16[147456]{0:T(1024)(128)(2,1)S(1)}, bf16[147456]{0:T(1024)(128)(2,1)S(1)}, u32[]{:S(2)}, u32[]{:S(2)}) %collective-permute-start.8) | collective-permute-done | bytes 294944 | tf_op jit(solution)/shard_map/ppermute | solution.py:101
  96.3 3.7 %collective-permute-start.9 = (bf16[73728]{0:T(1024)(128)(2,1)S(1)}, bf16[73728]{0:T(1024)(128)(2,1)S(1)}, u32[]{:S(2)}, u32[]{:S(2)}) collective-permute-start(bf16[73728]{0:T(1024)(128)(2,1)S(1)} %select_convert_fusion.2), channel_id=1, source_target_pairs={{0,8},{4,12},{8,0},{12,4},{1,9},{5,13},{9,1},{13,5},{2,10},{6,14},... | collective-permute-start | bytes 442376 | tf_op jit(solution)/shard_map/ppermute | solution.py:101
  100.0 3.3 %collective-permute-done.9 = bf16[73728]{0:T(1024)(128)(2,1)S(1)} collective-permute-done((bf16[73728]{0:T(1024)(128)(2,1)S(1)}, bf16[73728]{0:T(1024)(128)(2,1)S(1)}, u32[]{:S(2)}, u32[]{:S(2)}) %collective-permute-start.9) | collective-permute-done | bytes 147488 | tf_op jit(solution)/shard_map/ppermute | solution.py:101
  103.4 2.5 %collective-permute-start.10 = (bf16[73728]{0:T(1024)(128)(2,1)S(1)}, bf16[73728]{0:T(1024)(128)(2,1)S(1)}, u32[]{:S(2)}, u32[]{:S(2)}) collective-permute-start(bf16[73728]{0:T(1024)(128)(2,1)S(1)} %add_convert_fusion.2), channel_id=1, source_target_pairs={{0,1},{1,0},{2,3},{3,2},{4,5},{5,4},{6,7},{7,6},{8,9},{9,8},{10,11... | collective-permute-start | bytes 442376 | tf_op jit(solution)/shard_map/ppermute | solution.py:101
  106.4 2.6 %collective-permute-done.10 = bf16[73728]{0:T(1024)(128)(2,1)S(1)} collective-permute-done((bf16[73728]{0:T(1024)(128)(2,1)S(1)}, bf16[73728]{0:T(1024)(128)(2,1)S(1)}, u32[]{:S(2)}, u32[]{:S(2)}) %collective-permute-start.10) | collective-permute-done | bytes 147488 | tf_op jit(solution)/shard_map/ppermute | solution.py:101
  109.1 3.1 %collective-permute-start.11 = (bf16[73728]{0:T(1024)(128)(2,1)S(1)}, bf16[73728]{0:T(1024)(128)(2,1)S(1)}, u32[]{:S(2)}, u32[]{:S(2)}) collective-permute-start(bf16[73728]{0:T(1024)(128)(2,1)S(1)} %add_convert_fusion.1), channel_id=1, source_target_pairs={{0,2},{1,3},{2,0},{3,1},{4,6},{5,7},{6,4},{7,5},{8,10},{9,11},{10,... | collective-permute-start | bytes 442376 | tf_op jit(solution)/shard_map/ppermute | solution.py:101
  113.3 3.5 %collective-permute-done.11 = bf16[73728]{0:T(1024)(128)(2,1)S(1)} collective-permute-done((bf16[73728]{0:T(1024)(128)(2,1)S(1)}, bf16[73728]{0:T(1024)(128)(2,1)S(1)}, u32[]{:S(2)}, u32[]{:S(2)}) %collective-permute-start.11) | collective-permute-done | bytes 147488 | tf_op jit(solution)/shard_map/ppermute | solution.py:101
  116.9 2.3 %collective-permute-start.12 = (bf16[73728]{0:T(1024)(128)(2,1)S(1)}, bf16[73728]{0:T(1024)(128)(2,1)S(1)}, u32[]{:S(2)}, u32[]{:S(2)}) collective-permute-start(bf16[73728]{0:T(1024)(128)(2,1)S(1)} %add_convert_fusion), channel_id=1, source_target_pairs={{0,8},{4,12},{8,0},{12,4},{1,9},{5,13},{9,1},{13,5},{2,10},{6,14},... | collective-permute-start | bytes 442376 | tf_op jit(solution)/shard_map/ppermute | solution.py:101
  119.4 2.9 %collective-permute-done.12 = bf16[73728]{0:T(1024)(128)(2,1)S(1)} collective-permute-done((bf16[73728]{0:T(1024)(128)(2,1)S(1)}, bf16[73728]{0:T(1024)(128)(2,1)S(1)}, u32[]{:S(2)}, u32[]{:S(2)}) %collective-permute-start.12) | collective-permute-done | bytes 147488 | tf_op jit(solution)/shard_map/ppermute | solution.py:101
  122.4 1.6 %collective-permute-start.13 = (bf16[147456]{0:T(1024)(128)(2,1)S(1)}, bf16[147456]{0:T(1024)(128)(2,1)S(1)}, u32[]{:S(2)}, u32[]{:S(2)}) collective-permute-start(bf16[147456]{0:T(1024)(128)(2,1)S(1)} %maximum_select_fusion.2), channel_id=1, source_target_pairs={{0,4},{4,0},{8,12},{12,8},{1,5},{5,1},{9,13},{13,9},{2,6},{6,2},{1... | collective-permute-start | bytes 884744 | tf_op jit(solution)/shard_map/ppermute | solution.py:101
  124.9 4.3 %collective-permute-done.13 = bf16[147456]{0:T(1024)(128)(2,1)S(1)} collective-permute-done((bf16[147456]{0:T(1024)(128)(2,1)S(1)}, bf16[147456]{0:T(1024)(128)(2,1)S(1)}, u32[]{:S(2)}, u32[]{:S(2)}) %collective-permute-start.13) | collective-permute-done | bytes 294944 | tf_op jit(solution)/shard_map/ppermute | solution.py:101
  (159 shorter events, 34.8 us)
Async XLA Ops:
  0.6 2.5 %copy-start = (bf16[4,16,32,128]{3,2,1,0:T(8,128)(2,1)S(1)}, bf16[4,16,32,128]{3,2,1,0:T(8,128)(2,1)}, u32[]{:S(2)}) copy-start(bf16[4,16,32,128]{3,2,1,0:T(8,128)(2,1)} %param.6) | copy-start | bytes 1572868
  0.6 1.8 %copy-start.16 = (bf16[2,3,3,128,128]{4,3,2,1,0:T(8,128)(2,1)S(1)}, bf16[2,3,3,128,128]{4,3,2,1,0:T(8,128)(2,1)}, u32[]{:S(2)}) copy-start(bf16[2,3,3,128,128]{4,3,2,1,0:T(8,128)(2,1)} %param.5) | copy-start | bytes 1769476
  0.7 1.9 %copy-start.20 = (s32[4]{0:T(128)S(1)}, s32[4]{0:T(128)}, u32[]{:S(2)}) copy-start(s32[4]{0:T(128)} %param.7) | copy-start | bytes 52
  1.9 2.1 %collective-permute-start = (bf16[2,16,32,128]{3,2,0,1:T(8,128)(2,1)S(1)}, bf16[2,16,32,128]{3,2,0,1:T(8,128)(2,1)S(1)}, u32[]{:S(2)}, u32[]{:S(2)}) collective-permute-start(bf16[2,16,32,128]{3,2,0,1:T(8,128)(2,1)S(1)} %bitcast.170), channel_id=1, source_target_pairs={{0,16},{16,0},{1,17},{17,1},{2,18},{18,2},{3,19},{19,3},{4,20},{20... | collective-permute-start | bytes 786440 | tf_op jit(solution)/shard_map/ppermute | solution.py:250
  2.4 20.9 %collective-permute-start.5 = (bf16[2,3,3,128,128]{4,3,2,1,0:T(8,128)(2,1)S(1)}, bf16[2,3,3,128,128]{4,3,2,1,0:T(8,128)(2,1)}, u32[]{:S(2)}, u32[]{:S(2)}) collective-permute-start(bf16[2,3,3,128,128]{4,3,2,1,0:T(8,128)(2,1)S(1)} %copy-done.16), channel_id=1, source_target_pairs={{0,16},{16,0},{1,17},{17,1},{2,18},{18,2},{3,19},{19,3},{4,20},{20... | collective-permute-start | bytes 1769480 | tf_op jit(solution)/shard_map/ppermute | solution.py:250
  4.1 12.7 %collective-permute-start.2 = (bf16[6,6,32,128]{3,2,0,1:T(8,128)(2,1)S(1)}, bf16[6,6,32,128]{3,2,0,1:T(8,128)(2,1)S(1)}, u32[]{:S(2)}, u32[]{:S(2)}) collective-permute-start(bf16[6,6,32,128]{3,2,0,1:T(8,128)(2,1)S(1)} %get-tuple-element.19), channel_id=1, source_target_pairs={{4,0},{5,1},{6,2},{7,3},{8,4},{9,5},{10,6},{11,7},{12,8},{13,9},{1... | collective-permute-start | bytes 884744 | tf_op jit(solution)/shard_map/ppermute | solution.py:43
  5.4 11.9 %collective-permute-start.1 = (bf16[6,6,32,128]{3,2,0,1:T(8,128)(2,1)S(1)}, bf16[6,6,32,128]{3,2,0,1:T(8,128)(2,1)S(1)}, u32[]{:S(2)}, u32[]{:S(2)}) collective-permute-start(bf16[6,6,32,128]{3,2,0,1:T(8,128)(2,1)S(1)} %get-tuple-element.18), channel_id=1, source_target_pairs={{0,4},{1,5},{2,6},{3,7},{4,8},{5,9},{6,10},{7,11},{8,12},{9,13},{1... | collective-permute-start | bytes 884744 | tf_op jit(solution)/shard_map/ppermute | solution.py:43
  16.7 13.0 %copy-start.1 = (bf16[6,6,32,128]{3,2,0,1:T(8,128)(2,1)}, bf16[6,6,32,128]{3,2,0,1:T(8,128)(2,1)S(1)}, u32[]{:S(2)}) copy-start(bf16[6,6,32,128]{3,2,0,1:T(8,128)(2,1)S(1)} %collective-permute-done.2) | copy-start | bytes 884740
  17.3 12.4 %copy-start.3 = (bf16[6,6,32,128]{3,2,0,1:T(8,128)(2,1)}, bf16[6,6,32,128]{3,2,0,1:T(8,128)(2,1)S(1)}, u32[]{:S(2)}) copy-start(bf16[6,6,32,128]{3,2,0,1:T(8,128)(2,1)S(1)} %collective-permute-done.1) | copy-start | bytes 884740
  17.5 11.1 %collective-permute-start.4 = (bf16[6,28,6,128]{3,2,0,1:T(8,128)(2,1)S(1)}, bf16[6,28,6,128]{3,2,0,1:T(8,128)(2,1)S(1)}, u32[]{:S(2)}, u32[]{:S(2)}) collective-permute-start(bf16[6,28,6,128]{3,2,0,1:T(8,128)(2,1)S(1)} %get-tuple-element.15), channel_id=1, source_target_pairs={{1,0},{2,1},{3,2},{5,4},{6,5},{7,6},{9,8},{10,9},{11,10},{13,12},{... | collective-permute-start | bytes 774152 | tf_op jit(solution)/shard_map/ppermute | solution.py:43
  18.8 11.0 %collective-permute-start.3 = (bf16[6,28,6,128]{3,2,0,1:T(8,128)(2,1)S(1)}, bf16[6,28,6,128]{3,2,0,1:T(8,128)(2,1)S(1)}, u32[]{:S(2)}, u32[]{:S(2)}) collective-permute-start(bf16[6,28,6,128]{3,2,0,1:T(8,128)(2,1)S(1)} %get-tuple-element.14), channel_id=1, source_target_pairs={{0,1},{1,2},{2,3},{4,5},{5,6},{6,7},{8,9},{9,10},{10,11},{12,13},{... | collective-permute-start | bytes 774152 | tf_op jit(solution)/shard_map/ppermute | solution.py:43
  24.5 1.3 copy-start.5
  24.5 9.2 %copy-start.7 = (bf16[2,3,3,128,128]{4,3,2,1,0:T(8,128)(2,1)}, bf16[2,3,3,128,128]{4,3,2,1,0:T(8,128)(2,1)S(1)}, u32[]{:S(2)}) copy-start(bf16[2,3,3,128,128]{4,3,2,1,0:T(8,128)(2,1)S(1)} %get-tuple-element.17) | copy-start | bytes 1769476
  28.6 2.8 %copy-start.10 = (bf16[6,28,6,128]{3,2,0,1:T(8,128)(2,1)}, bf16[6,28,6,128]{3,2,0,1:T(8,128)(2,1)S(1)}, u32[]{:S(2)}) copy-start(bf16[6,28,6,128]{3,2,0,1:T(8,128)(2,1)S(1)} %collective-permute-done.4) | copy-start | bytes 774148
  29.7 1.7 %copy-start.12 = (bf16[6,28,6,128]{3,2,0,1:T(8,128)(2,1)}, bf16[6,28,6,128]{3,2,0,1:T(8,128)(2,1)S(1)}, u32[]{:S(2)}) copy-start(bf16[6,28,6,128]{3,2,0,1:T(8,128)(2,1)S(1)} %collective-permute-done.3) | copy-start | bytes 774148
  32.4 1.4 %copy-start.26 = (pred[16,6]{0,1:T(8,128)(4,1)S(1)}, pred[16,6]{0,1:T(8,128)(4,1)}, u32[]{:S(2)}) copy-start(pred[16,6]{0,1:T(8,128)(4,1)} %constant.181) | copy-start | bytes 292
  35.9 3.5 %copy-start.9 = (bf16[2,28,44,128]{3,2,0,1:T(8,128)(2,1)S(1)}, bf16[2,28,44,128]{3,2,0,1:T(8,128)(2,1)}, u32[]{:S(2)}) copy-start(bf16[2,28,44,128]{3,2,0,1:T(8,128)(2,1)} %get-tuple-element.12) | copy-start | bytes 1892356
  40.0 1.1 copy-start.6
  48.2 1.1 copy-start.8
  50.9 1.1 copy-start.11
  50.9 1.2 copy-start.13
  79.1 3.2 %collective-permute-start.7 = (f32[2,3,3,128,128]{4,3,2,1,0:T(8,128)}, f32[2,3,3,128,128]{4,3,2,1,0:T(8,128)}, u32[]{:S(2)}, u32[]{:S(2)}) collective-permute-start(f32[2,3,3,128,128]{4,3,2,1,0:T(8,128)} %fusion.16), channel_id=1, source_target_pairs={{0,16},{16,0},{1,17},{17,1},{2,18},{18,2},{3,19},{19,3},{4,20},{20... | collective-permute-start | bytes 3538952 | tf_op jit(solution)/shard_map/ppermute | solution.py:250
  83.8 12.3 %collective-permute-start.8 = (bf16[147456]{0:T(1024)(128)(2,1)S(1)}, bf16[147456]{0:T(1024)(128)(2,1)S(1)}, u32[]{:S(2)}, u32[]{:S(2)}) collective-permute-start(bf16[147456]{0:T(1024)(128)(2,1)S(1)} %bitcast.168), channel_id=1, source_target_pairs={{0,4},{4,0},{8,12},{12,8},{1,5},{5,1},{9,13},{13,9},{2,6},{6,2},{1... | collective-permute-start | bytes 884744 | tf_op jit(solution)/shard_map/ppermute | solution.py:101
  96.2 9.8 %copy-start.15 = (bf16[2,18,34,128]{3,0,2,1:T(2,128)(2,1)S(1)}, bf16[2,18,34,128]{3,0,2,1:T(2,128)(2,1)}, u32[]{:S(2)}) copy-start(bf16[2,18,34,128]{3,0,2,1:T(2,128)(2,1)} %copy-done.14) | copy-start | bytes 940036
  96.3 7.0 %collective-permute-start.9 = (bf16[73728]{0:T(1024)(128)(2,1)S(1)}, bf16[73728]{0:T(1024)(128)(2,1)S(1)}, u32[]{:S(2)}, u32[]{:S(2)}) collective-permute-start(bf16[73728]{0:T(1024)(128)(2,1)S(1)} %select_convert_fusion.2), channel_id=1, source_target_pairs={{0,8},{4,12},{8,0},{12,4},{1,9},{5,13},{9,1},{13,5},{2,10},{6,14},... | collective-permute-start | bytes 442376 | tf_op jit(solution)/shard_map/ppermute | solution.py:101
  103.4 5.7 %collective-permute-start.10 = (bf16[73728]{0:T(1024)(128)(2,1)S(1)}, bf16[73728]{0:T(1024)(128)(2,1)S(1)}, u32[]{:S(2)}, u32[]{:S(2)}) collective-permute-start(bf16[73728]{0:T(1024)(128)(2,1)S(1)} %add_convert_fusion.2), channel_id=1, source_target_pairs={{0,1},{1,0},{2,3},{3,2},{4,5},{5,4},{6,7},{7,6},{8,9},{9,8},{10,11... | collective-permute-start | bytes 442376 | tf_op jit(solution)/shard_map/ppermute | solution.py:101
  106.0 6.1 %copy-start.18 = (bf16[2,3,3,128,128]{3,4,2,1,0:T(8,128)(2,1)S(1)}, bf16[2,3,3,128,128]{3,4,2,1,0:T(8,128)(2,1)}, u32[]{:S(2)}) copy-start(bf16[2,3,3,128,128]{3,4,2,1,0:T(8,128)(2,1)} %get-tuple-element.28) | copy-start | bytes 1769476
  106.0 6.1 %copy-start.21 = (pred[16,5]{0,1:T(8,128)(4,1)S(1)}, pred[16,5]{0,1:T(8,128)(4,1)}, u32[]{:S(2)}) copy-start(pred[16,5]{0,1:T(8,128)(4,1)} %constant.176) | copy-start | bytes 244
  109.1 7.8 %collective-permute-start.11 = (bf16[73728]{0:T(1024)(128)(2,1)S(1)}, bf16[73728]{0:T(1024)(128)(2,1)S(1)}, u32[]{:S(2)}, u32[]{:S(2)}) collective-permute-start(bf16[73728]{0:T(1024)(128)(2,1)S(1)} %add_convert_fusion.1), channel_id=1, source_target_pairs={{0,2},{1,3},{2,0},{3,1},{4,6},{5,7},{6,4},{7,5},{8,10},{9,11},{10,... | collective-permute-start | bytes 442376 | tf_op jit(solution)/shard_map/ppermute | solution.py:101
  116.9 5.4 %collective-permute-start.12 = (bf16[73728]{0:T(1024)(128)(2,1)S(1)}, bf16[73728]{0:T(1024)(128)(2,1)S(1)}, u32[]{:S(2)}, u32[]{:S(2)}) collective-permute-start(bf16[73728]{0:T(1024)(128)(2,1)S(1)} %add_convert_fusion), channel_id=1, source_target_pairs={{0,8},{4,12},{8,0},{12,4},{1,9},{5,13},{9,1},{13,5},{2,10},{6,14},... | collective-permute-start | bytes 442376 | tf_op jit(solution)/shard_map/ppermute | solution.py:101
  119.3 4.7 %collective-permute-start.6 = (bf16[2,16,32,128]{3,2,0,1:T(8,128)(2,1)S(1)}, bf16[2,16,32,128]{3,2,0,1:T(8,128)(2,1)S(1)}, u32[]{:S(2)}, u32[]{:S(2)}) collective-permute-start(bf16[2,16,32,128]{3,2,0,1:T(8,128)(2,1)S(1)} %get-tuple-element.21), channel_id=1, source_target_pairs={{0,16},{16,0},{1,17},{17,1},{2,18},{18,2},{3,19},{19,3},{4,20},{20... | collective-permute-start | bytes 786440 | tf_op jit(solution)/shard_map/ppermute | solution.py:250
  122.4 6.8 %collective-permute-start.13 = (bf16[147456]{0:T(1024)(128)(2,1)S(1)}, bf16[147456]{0:T(1024)(128)(2,1)S(1)}, u32[]{:S(2)}, u32[]{:S(2)}) collective-permute-start(bf16[147456]{0:T(1024)(128)(2,1)S(1)} %maximum_select_fusion.2), channel_id=1, source_target_pairs={{0,4},{4,0},{8,12},{12,8},{1,5},{5,1},{9,13},{13,9},{2,6},{6,2},{1... | collective-permute-start | bytes 884744 | tf_op jit(solution)/shard_map/ppermute | solution.py:101
  (9 other events, 8.7 us)

commit v3 on v2

--- a/solution.py
+++ b/solution.py
@@ -218,21 +218,57 @@
     return (boundary[None], kernel_grad)
 
 
+def hw_crop(block, width):
+    return block[width : block.shape[0] - width, width : block.shape[1] - width]
+
+
+def hw_mask(tile_rows, tile_cols, width):
+    return inside_mask(tile_rows, tile_cols, width)[0, :, :, :, None]
+
+
+def hw_convolve(padded, kernel):
+    return lax.conv_general_dilated(
+        padded,
+        kernel,
+        (1, 1),
+        "VALID",
+        dimension_numbers=("HWNC", "HWIO", "HWNC"),
+        preferred_element_type=jnp.float32,
+    )
+
+
+def hw_kernel_terms(padded, signal):
+    terms = lax.conv_general_dilated(
+        padded,
+        signal,
+        (1, 1),
+        "VALID",
+        dimension_numbers=("HWCN", "HWIO", "NHWC"),
+        preferred_element_type=jnp.float32,
+    )
+    return jnp.transpose(terms, (1, 2, 0, 3))
+
+
+def hw_with_rim(block, width):
+    moved = jnp.transpose(block, (2, 0, 1, 3))
+    return jnp.transpose(with_rim(moved, width, 0, range(lax.axis_size("section"))), (1, 2, 0, 3))
+
+
 def section_chain(top_ext, top_width, inputs_list, rim, flipped_kernels):
     layer_count = len(flipped_kernels)
-    tile_rows = inputs_list[0].shape[1] - 2 * rim
-    tile_cols = inputs_list[0].shape[2] - 2 * rim
+    tile_rows = inputs_list[0].shape[0] - 2 * rim
+    tile_cols = inputs_list[0].shape[1] - 2 * rim
     gradient = top_ext.astype(jnp.float32)
     signals = [None] * layer_count
     for layer_idx in reversed(range(layer_count)):
         width = top_width - (layer_count - 1 - layer_idx)
-        output = crop(inputs_list[layer_idx + 1], rim - layer_idx - 1 - width)
+        output = hw_crop(inputs_list[layer_idx + 1], rim - layer_idx - 1 - width)
         output = output.astype(jnp.float32)
         signal = gradient * (1.0 - output * output)
-        signal = jnp.where(inside_mask(tile_rows, tile_cols, width), signal, 0.0)
+        signal = jnp.where(hw_mask(tile_rows, tile_cols, width), signal, 0.0)
         signal = signal.astype(jnp.bfloat16)
-        signals[layer_idx] = crop(signal, width)
-        gradient = convolve(signal, flipped_kernels[layer_idx])
+        signals[layer_idx] = hw_crop(signal, width)
+        gradient = hw_convolve(signal, flipped_kernels[layer_idx])
     return gradient.astype(jnp.bfloat16), signals
 
 
@@ -262,9 +298,10 @@
     rims = [r + layer_count for r in top_rim]
     group_cotangent = lax.dynamic_slice_in_dim(top_cotangent, section_index * half, half, 0)
     stacked = [by_section(mine, theirs, s) for s in range(2)] + [group_cotangent]
-    stacked = with_rim(jnp.concatenate(stacked, axis=0), rims[1], 0, range(2))
-    firsts = [crop(stacked[:half], rims[1] - rims[0]), stacked[half : 2 * half]]
-    top_ext = crop(stacked[2 * half :], rims[1] - top_rim[1])
+    stacked = jnp.transpose(jnp.concatenate(stacked, axis=0), (1, 2, 0, 3))
+    stacked = hw_with_rim(stacked, rims[1])
+    firsts = [hw_crop(stacked[:, :, :half], rims[1] - rims[0]), stacked[:, :, half : 2 * half]]
+    top_ext = hw_crop(stacked[:, :, 2 * half :], rims[1] - top_rim[1])
 
     results, partials = [None, None], [None, None]
     for s in (1, 0):
@@ -272,18 +309,18 @@
         inputs_list = [firsts[s]]
         current = firsts[s]
         for layer_idx in range(layer_count):
-            current = jnp.tanh(convolve(current, section_kernels[s][layer_idx]))
-            current = jnp.where(
-                inside_mask(tile_rows, tile_cols, rim - layer_idx - 1), current, 0.0
-            )
+            current = jnp.tanh(hw_convolve(current, section_kernels[s][layer_idx]))
+            current = jnp.where(hw_mask(tile_rows, tile_cols, rim - layer_idx - 1), current, 0.0)
             current = current.astype(jnp.bfloat16)
             inputs_list.append(current)
         flipped = jnp.transpose(section_kernels[s][:, ::-1, ::-1], (0, 1, 2, 4, 3))
         top_ext, signals = section_chain(top_ext, top_rim[s], inputs_list, rim, flipped)
-        results[s] = crop(top_ext, top_rim[s] - layer_count)
+        results[s] = hw_crop(top_ext, top_rim[s] - layer_count)
         partials[s] = jnp.stack(
             [
-                kernel_terms(crop(inputs_list[layer_idx], rim - layer_idx - 1), signals[layer_idx])
+                hw_kernel_terms(
+                    hw_crop(inputs_list[layer_idx], rim - layer_idx - 1), signals[layer_idx]
+                )
                 for layer_idx in range(layer_count)
             ]
         )
@@ -295,10 +332,10 @@
     other_back = swap(by_section(results[1], results[0], 0))
     boundary = jnp.where(
         section_index == 0,
-        jnp.concatenate([mine_back, other_back], axis=0),
-        jnp.concatenate([other_back, mine_back], axis=0),
-    )
-    return (boundary[None], gathered / batches)
+        jnp.concatenate([mine_back, other_back], axis=2),
+        jnp.concatenate([other_back, mine_back], axis=2),
+    )
+    return (jnp.transpose(boundary, (2, 0, 1, 3))[None], gathered / batches)
 
 
 def solution(mesh):

time: 131 us -> 132 us (level)
  other arithmetic: 28.1 us -> 25.8 us
  local copies, waits for them, and re-layouts: 14.6 us -> 16.9 us
    tanh x8, local copies, waits for them, and re-layouts: 1.07 us -> 3.09 us  [local_split(): current = jnp.tanh(hw_convolve(current, section_kernels[s][layer_idx]))]
    transpose x0 -> x1, other arithmetic: none -> 1.85 us  [hw_with_rim(): jnp.transpose(with_rim(moved, width, 0, range(lax.axis_size('section'))),...]
    concatenate x2 -> x0, other arithmetic: 1.76 us -> none  [the longest x1 1.65 us: from_neighbours(): return jnp.concatenate(parts, axis=dim)]
    slice x4 -> x5, local copies, waits for them, and re-layouts: 1.22 us -> 2.78 us  [the longest x3 2.21 us: local_split(): stacked[:, :, :half]]
    convert_element_type x4, other arithmetic: 8.96 us -> 7.54 us  [section_chain(): signal = signal.astype(jnp.bfloat16)]
    unnamed x57 -> x44, local copies, waits for them, and re-layouts: 5.38 us -> 4.13 us
  transfers between devices with their start and end apart: 14 -> 14, of which waited for: 11 -> 11; matrix products, arithmetic and copies ran while one was open for 5% -> 4% of each run, Pallas kernels for 0% -> 0%
where the time goes in v3:
time: 132 us; the launch traced here: 131 us
  waiting for transfers between devices  38.6 us (29%)
  starting transfers between devices  31.5 us (24%)
  other arithmetic  25.8 us (20%)
  matrix products  17.1 us (13%)
  local copies, waits for them, and re-layouts  16.9 us (13%)
  between operations  1.58 us (1%)
    ppermute x6, waiting for transfers between devices, exchange(): return lax.ppermute(values, axis, [(i, i ^ distance) for i in range(count)])  24 us
    ppermute x6, starting transfers between devices, exchange(): return lax.ppermute(values, axis, [(i, i ^ distance) for i in range(count)])  18.2 us
    ppermute x4, starting transfers between devices, from_neighbours(): parts.append(lax.ppermute(piece, AXES, pairs))  12.6 us
    ppermute x4, waiting for transfers between devices, from_neighbours(): parts.append(lax.ppermute(piece, AXES, pairs))  11.5 us
    conv_general_dilated x8, matrix products, hw_convolve(): lax.conv_general_dilated(padded, kernel, (1, 1), 'VALID', dimension_numbe...  9.98 us
    convert_element_type x4, other arithmetic, local_split(): current = current.astype(jnp.bfloat16)  9.26 us
    convert_element_type x4, other arithmetic, section_chain(): signal = signal.astype(jnp.bfloat16)  7.54 us
    transpose x4, matrix products, hw_kernel_terms(): return jnp.transpose(terms, (1, 2, 0, 3))  7.08 us
  transfers between devices with their start and end apart: 14, of which 11 were waited for; matrix products, arithmetic and copies ran while one was open for 4% of the time, Pallas kernels for 0%

profile of v3, /device:TPU:0, one launch (start us, length us, event | category | flops | bytes accessed | tf_op | source)
XLA Modules:
  0.0 131.5 jit_solution(16278964274302236332)
XLA Ops:
  5.4 5.4 %collective-permute-start.1 = (bf16[6,6,32,128]{3,2,0,1:T(8,128)(2,1)S(1)}, bf16[6,6,32,128]{3,2,0,1:T(8,128)(2,1)S(1)}, u32[]{:S(2)}, u32[]{:S(2)}) collective-permute-start(bf16[6,6,32,128]{3,2,0,1:T(8,128)(2,1)S(1)} %get-tuple-element.18), channel_id=1, source_target_pairs={{0,4},{1,5},{2,6},{3,7},{4,8},{5,9},{6,10},{7,11},{8,12},{9,13},{1... | collective-permute-start | bytes 884744 | tf_op jit(solution)/shard_map/ppermute | solution.py:43
  10.9 5.8 %collective-permute-done.2 = bf16[6,6,32,128]{3,2,0,1:T(8,128)(2,1)S(1)} collective-permute-done((bf16[6,6,32,128]{3,2,0,1:T(8,128)(2,1)S(1)}, bf16[6,6,32,128]{3,2,0,1:T(8,128)(2,1)S(1)}, u32[]{:S(2)}, u32[]{:S(2)}) %collective-permute-start.2) | collective-permute-done | bytes 294944 | tf_op jit(solution)/shard_map/ppermute | solution.py:43
  18.8 4.6 %collective-permute-start.3 = (bf16[6,28,6,128]{3,2,0,1:T(8,128)(2,1)S(1)}, bf16[6,28,6,128]{3,2,0,1:T(8,128)(2,1)S(1)}, u32[]{:S(2)}, u32[]{:S(2)}) collective-permute-start(bf16[6,28,6,128]{3,2,0,1:T(8,128)(2,1)S(1)} %get-tuple-element.14), channel_id=1, source_target_pairs={{0,1},{1,2},{2,3},{4,5},{5,6},{6,7},{8,9},{9,10},{10,11},{12,13},{... | collective-permute-start | bytes 774152 | tf_op jit(solution)/shard_map/ppermute | solution.py:43
  24.6 3.9 %collective-permute-done.4 = bf16[6,28,6,128]{3,2,0,1:T(8,128)(2,1)S(1)} collective-permute-done((bf16[6,28,6,128]{3,2,0,1:T(8,128)(2,1)S(1)}, bf16[6,28,6,128]{3,2,0,1:T(8,128)(2,1)S(1)}, u32[]{:S(2)}, u32[]{:S(2)}) %collective-permute-start.4) | collective-permute-done | bytes 258080 | tf_op jit(solution)/shard_map/ppermute | solution.py:43
  29.7 1.9 %maximum_bitcast_fusion = bf16[28,44,6,128]{3,1,2,0:T(8,128)(2,1)S(1)} fusion(bf16[6,28,6,128]{3,2,0,1:T(8,128)(2,1)S(1)} %collective-permute-done.4, bf16[6,6,32,128]{3,2,0,1:T(8,128)(2,1)S(1)} %collective-permute-done.2, bf16[2,16,32,128]{3,2,0,1:T(8,128)(2,1)S(1)} %copy_select_fusion.4, bf16[2,16,32,128]{3,2,0,1:T(8,128)(2,1)S(1)} %get-tuple-element.25, ...), kind=kLoop, calls=%fused_computation.3 | loop fusion | flops 13246464 | bytes 3784704 | tf_op jit(solution)/shard_map/transpose | solution.py:254
  31.6 1.6 %fusion.94 = (bf16[28,44,2,128]{3,1,2,0:T(8,128)(2,1)}, bf16[28,2,44,128]{3,2,1,0:T(8,128)(2,1)S(1)}, bf16[28,2,44,128]{3,2,1,0:T(8,128)(2,1)}, bf16[28,44,2,128]{3,1,2,0:T(8,128)(2,1)}) fusion(bf16[28,44,6,128]{3,1,2,0:T(8,128)(2,1)S(1)} %maximum_bitcast_fusion), kind=kLoop, calls=%fused_computation.187 | loop fusion | bytes 3784704 | tf_op jit(solution)/shard_map/slice | solution.py:303
  35.3 1.7 %fusion.1 = bf16[26,16,6,128]{3,1,2,0:T(8,128)(2,1)S(1)} fusion(bf16[28,2,8,8,128]{4,1,3,2,0:T(2,128)(2,1)S(1)} %fusion.17, pred[16,6]{0,1:T(8,128)(4,1)S(1)} %copy-done.20, bf16[2,3,3,128,128]{4,3,2,1,0:T(8,128)(2,1)S(1)} %get-tuple-element.17), kind=kOutput, calls=%fused_computation.7 | convolution fusion | flops 736739328 | bytes 1852416 | tf_op jit(solution)/shard_map/conv_general_dilated | solution.py:230
  39.5 1.7 %fusion.11 = bf16[26,2,42,128]{3,1,2,0:T(2,128)(2,1)S(1)} fusion(bf16[26,2,42,128]{3,2,1,0:T(8,128)(2,1)S(1)} %bitcast.142, pred[26,42]{1,0:T(8,128)(4,1)S(1)} %broadcast_and_fusion), kind=kLoop, calls=%fused_computation.36 | loop fusion | flops 279552 | bytes 1119300 | tf_op jit(solution)/shard_map/convert_element_type | solution.py:314
  41.2 1.7 %fusion.98 = bf16[26,42,2,128]{3,2,1,0:T(2,128)(2,1)S(1)} fusion(bf16[26,2,42,128]{3,2,1,0:T(8,128)(2,1)S(1)} %bitcast.143, pred[26,42]{1,0:T(8,128)(4,1)S(1)} %broadcast_and_fusion), kind=kLoop, calls=%fused_computation.189 | loop fusion | flops 279552 | bytes 1119300 | tf_op jit(solution)/shard_map/convert_element_type | solution.py:314
  46.0 2.8 %fusion.20 = bf16[22,2,38,128]{3,1,2,0:T(2,128)(2,1)S(1)} fusion(bf16[22,2,38,128]{3,0,2,1:T(8,128)(2,1)S(1)} %slice.152, pred[22,38]{1,0:T(8,128)(4,1)S(1)} %broadcast_and_fusion.2), kind=kLoop, calls=%fused_computation.49 | loop fusion | flops 214016 | bytes 856900 | tf_op jit(solution)/shard_map/convert_element_type | solution.py:314
  48.8 3.0 %fusion.97 = bf16[22,38,2,128]{3,2,1,0:T(2,128)(2,1)S(1)} fusion(bf16[22,2,38,128]{3,0,2,1:T(8,128)(2,1)S(1)} %slice.152, pred[22,38]{1,0:T(8,128)(4,1)S(1)} %broadcast_and_fusion.2), kind=kLoop, calls=%fused_computation.188 | loop fusion | flops 214016 | bytes 856900 | tf_op jit(solution)/shard_map/convert_element_type | solution.py:314
  52.9 1.6 %fusion.2 = bf16[24,16,6,128]{3,1,2,0:T(8,128)(2,1)S(1)} fusion(bf16[26,2,7,2,128]{4,2,1,3,0:T(8,128)(2,1)S(1)} %slice.138, bf16[26,2,8,6,128]{4,2,1,3,0:T(8,128)(2,1)S(1)} %copy.140, pred[16,6]{0,1:T(8,128)(4,1)S(1)} %copy-done.19, bf16[2,3,3,128,128]{4,3,2,1,0:T(8,128)(2,1)S(1)} %copy-done.4), kind=kOutput, calls=%fused_computation.9 | convolution fusion | flops 682622976 | bytes 1737728 | tf_op jit(solution)/shard_map/conv_general_dilated | solution.py:230
  58.2 2.9 %fusion.23 = bf16[22,38,2,128]{3,2,1,0:T(2,128)(2,1)S(1)} fusion(f32[22,2,38,128]{3,0,2,1:T(8,128)S(1)} %slice.143, pred[22,38]{1,0:T(8,128)(4,1)S(1)} %broadcast_and_fusion.2, bf16[26,42,2,128]{3,2,1,0:T(2,128)(2,1)S(1)} %fusion.98), kind=kLoop, calls=%fused_computation.53 | loop fusion | flops 1284096 | bytes 1712964 | tf_op jit(solution)/shard_map/convert_element_type | solution.py:269
  65.5 1.9 %fusion.35 = bf16[20,2,36,128]{3,1,2,0:T(2,128)(2,1)S(1)} fusion(f32[20,2,36,128]{3,0,2,1:T(8,128)S(1)} %slice.147, pred[20,36]{1,0:T(8,128)(4,1)S(1)} %broadcast_and_fusion.3, bf16[20,2,36,128]{3,0,2,1:T(8,128)(2,1)S(1)} %slice.155), kind=kLoop, calls=%fused_computation.66 | loop fusion | flops 1290240 | bytes 1475280 | tf_op jit(solution)/shard_map/convert_element_type | solution.py:269
  69.9 1.8 %convolution_bitcast_fusion = f32[1,3,3,128,128]{4,3,2,1,0:T(8,128)S(1)} fusion(bf16[26,2,42,128]{3,1,2,0:T(2,128)(2,1)S(1)} %fusion.11, bf16[16,32,2,128]{3,1,2,0:T(8,128)(2,1)S(1)} %slice.168), kind=kOutput, calls=%fused_computation.24 | convolution fusion | flops 301989888 | bytes 1411072 | tf_op jit(solution)/shard_map/transpose | solution.py:249
  71.7 1.8 %convolution_bitcast_fusion.2 = f32[1,3,3,128,128]{4,3,2,1,0:T(8,128)S(1)} fusion(bf16[28,44,2,128]{3,1,2,0:T(8,128)(2,1)S(1)} %copy-done.9, bf16[22,38,2,128]{3,2,1,0:T(2,128)(2,1)S(1)} %fusion.23), kind=kOutput, calls=%fused_computation.26 | convolution fusion | flops 301989888 | bytes 1540096 | tf_op jit(solution)/shard_map/transpose | solution.py:249
  73.5 1.8 %convolution_bitcast_fusion.1 = f32[1,3,3,128,128]{4,3,2,1,0:T(8,128)S(1)} fusion(bf16[22,2,38,128]{3,1,2,0:T(2,128)(2,1)S(1)} %fusion.20, bf16[20,36,2,128]{3,2,1,0:T(2,128)(2,1)S(1)} %bitcast.163), kind=kOutput, calls=%fused_computation.25 | convolution fusion | flops 301989888 | bytes 1280000 | tf_op jit(solution)/shard_map/transpose | solution.py:249
  75.3 2.0 %fusion.55 = bf16[18,34,2,128]{3,2,1,0:T(2,128)(2,1)S(1)} fusion(f32[18,2,34,128]{3,0,2,1:T(8,128)S(1)} %slice.158, pred[18,34]{1,0:T(8,128)(4,1)S(1)} %broadcast_and_fusion.4, bf16[22,38,2,128]{3,2,1,0:T(2,128)(2,1)S(1)} %fusion.97), kind=kLoop, calls=%fused_computation.85 | loop fusion | flops 940032 | bytes 1253988 | tf_op jit(solution)/shard_map/convert_element_type | solution.py:269
  77.3 1.7 %convolution_bitcast_fusion.3 = f32[1,3,3,128,128]{4,3,2,1,0:T(8,128)S(1)} fusion(bf16[28,44,2,128]{3,1,2,0:T(8,128)(2,1)S(1)} %copy-done.8, bf16[18,34,2,128]{3,2,1,0:T(2,128)(2,1)S(1)} %fusion.55), kind=kOutput, calls=%fused_computation.27 | convolution fusion | flops 301989888 | bytes 1540096 | tf_op jit(solution)/shard_map/transpose | solution.py:249
  80.2 3.2 %collective-permute-done.7 = f32[2,3,3,128,128]{4,3,2,1,0:T(8,128)} collective-permute-done((f32[2,3,3,128,128]{4,3,2,1,0:T(8,128)}, f32[2,3,3,128,128]{4,3,2,1,0:T(8,128)}, u32[]{:S(2)}, u32[]{:S(2)}) %collective-permute-start.7) | collective-permute-done | bytes 1179680 | tf_op jit(solution)/shard_map/ppermute | solution.py:286
  85.0 5.0 %collective-permute-start.8 = (bf16[147456]{0:T(1024)(128)(2,1)S(1)}, bf16[147456]{0:T(1024)(128)(2,1)S(1)}, u32[]{:S(2)}, u32[]{:S(2)}) collective-permute-start(bf16[147456]{0:T(1024)(128)(2,1)S(1)} %bitcast.169), channel_id=1, source_target_pairs={{0,4},{4,0},{8,12},{12,8},{1,5},{5,1},{9,13},{13,9},{2,6},{6,2},{1... | collective-permute-start | bytes 884744 | tf_op jit(solution)/shard_map/ppermute | solution.py:101
  90.0 7.3 %collective-permute-done.8 = bf16[147456]{0:T(1024)(128)(2,1)S(1)} collective-permute-done((bf16[147456]{0:T(1024)(128)(2,1)S(1)}, bf16[147456]{0:T(1024)(128)(2,1)S(1)}, u32[]{:S(2)}, u32[]{:S(2)}) %collective-permute-start.8) | collective-permute-done | bytes 294944 | tf_op jit(solution)/shard_map/ppermute | solution.py:101
  97.4 3.7 %collective-permute-start.9 = (bf16[73728]{0:T(1024)(128)(2,1)S(1)}, bf16[73728]{0:T(1024)(128)(2,1)S(1)}, u32[]{:S(2)}, u32[]{:S(2)}) collective-permute-start(bf16[73728]{0:T(1024)(128)(2,1)S(1)} %select_convert_fusion.2), channel_id=1, source_target_pairs={{0,8},{4,12},{8,0},{12,4},{1,9},{5,13},{9,1},{13,5},{2,10},{6,14},... | collective-permute-start | bytes 442376 | tf_op jit(solution)/shard_map/ppermute | solution.py:101
  101.6 2.8 %collective-permute-done.9 = bf16[73728]{0:T(1024)(128)(2,1)S(1)} collective-permute-done((bf16[73728]{0:T(1024)(128)(2,1)S(1)}, bf16[73728]{0:T(1024)(128)(2,1)S(1)}, u32[]{:S(2)}, u32[]{:S(2)}) %collective-permute-start.9) | collective-permute-done | bytes 147488 | tf_op jit(solution)/shard_map/ppermute | solution.py:101
  104.5 2.5 %collective-permute-start.10 = (bf16[73728]{0:T(1024)(128)(2,1)S(1)}, bf16[73728]{0:T(1024)(128)(2,1)S(1)}, u32[]{:S(2)}, u32[]{:S(2)}) collective-permute-start(bf16[73728]{0:T(1024)(128)(2,1)S(1)} %add_convert_fusion.2), channel_id=1, source_target_pairs={{0,1},{1,0},{2,3},{3,2},{4,5},{5,4},{6,7},{7,6},{8,9},{9,8},{10,11... | collective-permute-start | bytes 442376 | tf_op jit(solution)/shard_map/ppermute | solution.py:101
  108.1 2.1 %collective-permute-done.10 = bf16[73728]{0:T(1024)(128)(2,1)S(1)} collective-permute-done((bf16[73728]{0:T(1024)(128)(2,1)S(1)}, bf16[73728]{0:T(1024)(128)(2,1)S(1)}, u32[]{:S(2)}, u32[]{:S(2)}) %collective-permute-start.10) | collective-permute-done | bytes 147488 | tf_op jit(solution)/shard_map/ppermute | solution.py:101
  110.2 3.1 %collective-permute-start.11 = (bf16[73728]{0:T(1024)(128)(2,1)S(1)}, bf16[73728]{0:T(1024)(128)(2,1)S(1)}, u32[]{:S(2)}, u32[]{:S(2)}) collective-permute-start(bf16[73728]{0:T(1024)(128)(2,1)S(1)} %add_convert_fusion.1), channel_id=1, source_target_pairs={{0,2},{1,3},{2,0},{3,1},{4,6},{5,7},{6,4},{7,5},{8,10},{9,11},{10,... | collective-permute-start | bytes 442376 | tf_op jit(solution)/shard_map/ppermute | solution.py:101
  113.3 4.7 %collective-permute-done.11 = bf16[73728]{0:T(1024)(128)(2,1)S(1)} collective-permute-done((bf16[73728]{0:T(1024)(128)(2,1)S(1)}, bf16[73728]{0:T(1024)(128)(2,1)S(1)}, u32[]{:S(2)}, u32[]{:S(2)}) %collective-permute-start.11) | collective-permute-done | bytes 147488 | tf_op jit(solution)/shard_map/ppermute | solution.py:101
  118.1 2.3 %collective-permute-start.12 = (bf16[73728]{0:T(1024)(128)(2,1)S(1)}, bf16[73728]{0:T(1024)(128)(2,1)S(1)}, u32[]{:S(2)}, u32[]{:S(2)}) collective-permute-start(bf16[73728]{0:T(1024)(128)(2,1)S(1)} %add_convert_fusion), channel_id=1, source_target_pairs={{0,8},{4,12},{8,0},{12,4},{1,9},{5,13},{9,1},{13,5},{2,10},{6,14},... | collective-permute-start | bytes 442376 | tf_op jit(solution)/shard_map/ppermute | solution.py:101
  120.5 3.0 %collective-permute-done.12 = bf16[73728]{0:T(1024)(128)(2,1)S(1)} collective-permute-done((bf16[73728]{0:T(1024)(128)(2,1)S(1)}, bf16[73728]{0:T(1024)(128)(2,1)S(1)}, u32[]{:S(2)}, u32[]{:S(2)}) %collective-permute-start.12) | collective-permute-done | bytes 147488 | tf_op jit(solution)/shard_map/ppermute | solution.py:101
  123.5 1.6 %collective-permute-start.13 = (bf16[147456]{0:T(1024)(128)(2,1)S(1)}, bf16[147456]{0:T(1024)(128)(2,1)S(1)}, u32[]{:S(2)}, u32[]{:S(2)}) collective-permute-start(bf16[147456]{0:T(1024)(128)(2,1)S(1)} %maximum_select_fusion.2), channel_id=1, source_target_pairs={{0,4},{4,0},{8,12},{12,8},{1,5},{5,1},{9,13},{13,9},{2,6},{6,2},{1... | collective-permute-start | bytes 884744 | tf_op jit(solution)/shard_map/ppermute | solution.py:101
  126.1 4.2 %collective-permute-done.13 = bf16[147456]{0:T(1024)(128)(2,1)S(1)} collective-permute-done((bf16[147456]{0:T(1024)(128)(2,1)S(1)}, bf16[147456]{0:T(1024)(128)(2,1)S(1)}, u32[]{:S(2)}, u32[]{:S(2)}) %collective-permute-start.13) | collective-permute-done | bytes 294944 | tf_op jit(solution)/shard_map/ppermute | solution.py:101
  (146 shorter events, 35.0 us)
Async XLA Ops:
  0.6 2.5 %copy-start = (bf16[4,16,32,128]{3,2,1,0:T(8,128)(2,1)S(1)}, bf16[4,16,32,128]{3,2,1,0:T(8,128)(2,1)}, u32[]{:S(2)}) copy-start(bf16[4,16,32,128]{3,2,1,0:T(8,128)(2,1)} %param.6) | copy-start | bytes 1572868
  0.6 1.8 %copy-start.10 = (bf16[2,3,3,128,128]{4,3,2,1,0:T(8,128)(2,1)S(1)}, bf16[2,3,3,128,128]{4,3,2,1,0:T(8,128)(2,1)}, u32[]{:S(2)}) copy-start(bf16[2,3,3,128,128]{4,3,2,1,0:T(8,128)(2,1)} %param.5) | copy-start | bytes 1769476
  0.7 1.9 %copy-start.14 = (s32[4]{0:T(128)S(1)}, s32[4]{0:T(128)}, u32[]{:S(2)}) copy-start(s32[4]{0:T(128)} %param.7) | copy-start | bytes 52
  1.9 2.1 %collective-permute-start = (bf16[2,16,32,128]{3,2,0,1:T(8,128)(2,1)S(1)}, bf16[2,16,32,128]{3,2,0,1:T(8,128)(2,1)S(1)}, u32[]{:S(2)}, u32[]{:S(2)}) collective-permute-start(bf16[2,16,32,128]{3,2,0,1:T(8,128)(2,1)S(1)} %bitcast.171), channel_id=1, source_target_pairs={{0,16},{16,0},{1,17},{17,1},{2,18},{18,2},{3,19},{19,3},{4,20},{20... | collective-permute-start | bytes 786440 | tf_op jit(solution)/shard_map/ppermute | solution.py:286
  2.4 20.9 %collective-permute-start.5 = (bf16[2,3,3,128,128]{4,3,2,1,0:T(8,128)(2,1)S(1)}, bf16[2,3,3,128,128]{4,3,2,1,0:T(8,128)(2,1)S(1)}, u32[]{:S(2)}, u32[]{:S(2)}) collective-permute-start(bf16[2,3,3,128,128]{4,3,2,1,0:T(8,128)(2,1)S(1)} %copy-done.10), channel_id=1, source_target_pairs={{0,16},{16,0},{1,17},{17,1},{2,18},{18,2},{3,19},{19,3},{4,20},{20... | collective-permute-start | bytes 1769480 | tf_op jit(solution)/shard_map/ppermute | solution.py:286
  4.1 12.7 %collective-permute-start.2 = (bf16[6,6,32,128]{3,2,0,1:T(8,128)(2,1)S(1)}, bf16[6,6,32,128]{3,2,0,1:T(8,128)(2,1)S(1)}, u32[]{:S(2)}, u32[]{:S(2)}) collective-permute-start(bf16[6,6,32,128]{3,2,0,1:T(8,128)(2,1)S(1)} %get-tuple-element.19), channel_id=1, source_target_pairs={{4,0},{5,1},{6,2},{7,3},{8,4},{9,5},{10,6},{11,7},{12,8},{13,9},{1... | collective-permute-start | bytes 884744 | tf_op jit(solution)/shard_map/ppermute | solution.py:43
  5.4 11.9 %collective-permute-start.1 = (bf16[6,6,32,128]{3,2,0,1:T(8,128)(2,1)S(1)}, bf16[6,6,32,128]{3,2,0,1:T(8,128)(2,1)S(1)}, u32[]{:S(2)}, u32[]{:S(2)}) collective-permute-start(bf16[6,6,32,128]{3,2,0,1:T(8,128)(2,1)S(1)} %get-tuple-element.18), channel_id=1, source_target_pairs={{0,4},{1,5},{2,6},{3,7},{4,8},{5,9},{6,10},{7,11},{8,12},{9,13},{1... | collective-permute-start | bytes 884744 | tf_op jit(solution)/shard_map/ppermute | solution.py:43
  17.5 11.1 %collective-permute-start.4 = (bf16[6,28,6,128]{3,2,0,1:T(8,128)(2,1)S(1)}, bf16[6,28,6,128]{3,2,0,1:T(8,128)(2,1)S(1)}, u32[]{:S(2)}, u32[]{:S(2)}) collective-permute-start(bf16[6,28,6,128]{3,2,0,1:T(8,128)(2,1)S(1)} %get-tuple-element.15), channel_id=1, source_target_pairs={{1,0},{2,1},{3,2},{5,4},{6,5},{7,6},{9,8},{10,9},{11,10},{13,12},{... | collective-permute-start | bytes 774152 | tf_op jit(solution)/shard_map/ppermute | solution.py:43
  18.8 11.0 %collective-permute-start.3 = (bf16[6,28,6,128]{3,2,0,1:T(8,128)(2,1)S(1)}, bf16[6,28,6,128]{3,2,0,1:T(8,128)(2,1)S(1)}, u32[]{:S(2)}, u32[]{:S(2)}) collective-permute-start(bf16[6,28,6,128]{3,2,0,1:T(8,128)(2,1)S(1)} %get-tuple-element.14), channel_id=1, source_target_pairs={{0,1},{1,2},{2,3},{4,5},{5,6},{6,7},{8,9},{9,10},{10,11},{12,13},{... | collective-permute-start | bytes 774152 | tf_op jit(solution)/shard_map/ppermute | solution.py:43
  23.4 5.1 %copy-start.1 = (bf16[2,3,3,128,128]{4,3,2,1,0:T(8,128)(2,1)}, bf16[2,3,3,128,128]{4,3,2,1,0:T(8,128)(2,1)S(1)}, u32[]{:S(2)}) copy-start(bf16[2,3,3,128,128]{4,3,2,1,0:T(8,128)(2,1)S(1)} %get-tuple-element.16) | copy-start | bytes 1769476
  23.5 11.9 %copy-start.3 = (bf16[2,3,3,128,128]{4,3,2,1,0:T(8,128)(2,1)}, bf16[2,3,3,128,128]{4,3,2,1,0:T(8,128)(2,1)S(1)}, u32[]{:S(2)}) copy-start(bf16[2,3,3,128,128]{4,3,2,1,0:T(8,128)(2,1)S(1)} %get-tuple-element.17) | copy-start | bytes 1769476
  34.1 1.2 copy-start.20
  39.5 3.5 %copy-start.5 = (bf16[28,2,44,128]{3,2,1,0:T(8,128)(2,1)S(1)}, bf16[28,2,44,128]{3,2,1,0:T(8,128)(2,1)}, u32[]{:S(2)}) copy-start(bf16[28,2,44,128]{3,2,1,0:T(8,128)(2,1)} %get-tuple-element.12) | copy-start | bytes 1892356
  43.2 1.3 copy-start.2
  43.2 1.3 copy-start.18
  51.8 1.1 copy-start.4
  51.8 1.1 copy-start.19
  55.5 1.1 copy-start.13
  67.4 1.1 copy-start.11
  69.9 1.8 %copy-start.9 = (bf16[28,44,2,128]{3,1,2,0:T(8,128)(2,1)S(1)}, bf16[28,44,2,128]{3,1,2,0:T(8,128)(2,1)}, u32[]{:S(2)}) copy-start(bf16[28,44,2,128]{3,1,2,0:T(8,128)(2,1)} %get-tuple-element.13) | copy-start | bytes 1892356
  75.3 2.0 %copy-start.8 = (bf16[28,44,2,128]{3,1,2,0:T(8,128)(2,1)S(1)}, bf16[28,44,2,128]{3,1,2,0:T(8,128)(2,1)}, u32[]{:S(2)}) copy-start(bf16[28,44,2,128]{3,1,2,0:T(8,128)(2,1)} %get-tuple-element.10) | copy-start | bytes 1892356
  80.2 3.2 %collective-permute-start.7 = (f32[2,3,3,128,128]{4,3,2,1,0:T(8,128)}, f32[2,3,3,128,128]{4,3,2,1,0:T(8,128)}, u32[]{:S(2)}, u32[]{:S(2)}) collective-permute-start(f32[2,3,3,128,128]{4,3,2,1,0:T(8,128)} %fusion.16), channel_id=1, source_target_pairs={{0,16},{16,0},{1,17},{17,1},{2,18},{18,2},{3,19},{19,3},{4,20},{20... | collective-permute-start | bytes 3538952 | tf_op jit(solution)/shard_map/ppermute | solution.py:286
  84.9 16.2 %copy-start.7 = (bf16[20,16,5,128]{3,1,2,0:T(8,128)(2,1)S(1)}, bf16[20,16,5,128]{3,1,2,0:T(8,128)(2,1)}, u32[]{:S(2)}) copy-start(bf16[20,16,5,128]{3,1,2,0:T(8,128)(2,1)} %copy-done.6) | copy-start | bytes 1228804
  85.0 12.3 %collective-permute-start.8 = (bf16[147456]{0:T(1024)(128)(2,1)S(1)}, bf16[147456]{0:T(1024)(128)(2,1)S(1)}, u32[]{:S(2)}, u32[]{:S(2)}) collective-permute-start(bf16[147456]{0:T(1024)(128)(2,1)S(1)} %bitcast.169), channel_id=1, source_target_pairs={{0,4},{4,0},{8,12},{12,8},{1,5},{5,1},{9,13},{13,9},{2,6},{6,2},{1... | collective-permute-start | bytes 884744 | tf_op jit(solution)/shard_map/ppermute | solution.py:101
  97.4 7.0 %collective-permute-start.9 = (bf16[73728]{0:T(1024)(128)(2,1)S(1)}, bf16[73728]{0:T(1024)(128)(2,1)S(1)}, u32[]{:S(2)}, u32[]{:S(2)}) collective-permute-start(bf16[73728]{0:T(1024)(128)(2,1)S(1)} %select_convert_fusion.2), channel_id=1, source_target_pairs={{0,8},{4,12},{8,0},{12,4},{1,9},{5,13},{9,1},{13,5},{2,10},{6,14},... | collective-permute-start | bytes 442376 | tf_op jit(solution)/shard_map/ppermute | solution.py:101
  101.2 5.8 %copy-start.12 = (bf16[2,3,3,128,128]{3,4,2,1,0:T(8,128)(2,1)S(1)}, bf16[2,3,3,128,128]{3,4,2,1,0:T(8,128)(2,1)}, u32[]{:S(2)}) copy-start(bf16[2,3,3,128,128]{3,4,2,1,0:T(8,128)(2,1)} %get-tuple-element.28) | copy-start | bytes 1769476
  101.3 5.8 %copy-start.15 = (pred[16,5]{0,1:T(8,128)(4,1)S(1)}, pred[16,5]{0,1:T(8,128)(4,1)}, u32[]{:S(2)}) copy-start(pred[16,5]{0,1:T(8,128)(4,1)} %constant.176) | copy-start | bytes 244
  104.5 5.7 %collective-permute-start.10 = (bf16[73728]{0:T(1024)(128)(2,1)S(1)}, bf16[73728]{0:T(1024)(128)(2,1)S(1)}, u32[]{:S(2)}, u32[]{:S(2)}) collective-permute-start(bf16[73728]{0:T(1024)(128)(2,1)S(1)} %add_convert_fusion.2), channel_id=1, source_target_pairs={{0,1},{1,0},{2,3},{3,2},{4,5},{5,4},{6,7},{7,6},{8,9},{9,8},{10,11... | collective-permute-start | bytes 442376 | tf_op jit(solution)/shard_map/ppermute | solution.py:101
  110.2 7.8 %collective-permute-start.11 = (bf16[73728]{0:T(1024)(128)(2,1)S(1)}, bf16[73728]{0:T(1024)(128)(2,1)S(1)}, u32[]{:S(2)}, u32[]{:S(2)}) collective-permute-start(bf16[73728]{0:T(1024)(128)(2,1)S(1)} %add_convert_fusion.1), channel_id=1, source_target_pairs={{0,2},{1,3},{2,0},{3,1},{4,6},{5,7},{6,4},{7,5},{8,10},{9,11},{10,... | collective-permute-start | bytes 442376 | tf_op jit(solution)/shard_map/ppermute | solution.py:101
  118.1 5.4 %collective-permute-start.12 = (bf16[73728]{0:T(1024)(128)(2,1)S(1)}, bf16[73728]{0:T(1024)(128)(2,1)S(1)}, u32[]{:S(2)}, u32[]{:S(2)}) collective-permute-start(bf16[73728]{0:T(1024)(128)(2,1)S(1)} %add_convert_fusion), channel_id=1, source_target_pairs={{0,8},{4,12},{8,0},{12,4},{1,9},{5,13},{9,1},{13,5},{2,10},{6,14},... | collective-permute-start | bytes 442376 | tf_op jit(solution)/shard_map/ppermute | solution.py:101
  120.4 4.7 %collective-permute-start.6 = (bf16[16,32,2,128]{3,0,1,2:T(8,128)(2,1)S(1)}, bf16[16,32,2,128]{3,0,1,2:T(8,128)(2,1)S(1)}, u32[]{:S(2)}, u32[]{:S(2)}) collective-permute-start(bf16[16,32,2,128]{3,0,1,2:T(8,128)(2,1)S(1)} %get-tuple-element.21), channel_id=1, source_target_pairs={{0,16},{16,0},{1,17},{17,1},{2,18},{18,2},{3,19},{19,3},{4,20},{20... | collective-permute-start | bytes 786440 | tf_op jit(solution)/shard_map/ppermute | solution.py:286
  123.5 6.8 %collective-permute-start.13 = (bf16[147456]{0:T(1024)(128)(2,1)S(1)}, bf16[147456]{0:T(1024)(128)(2,1)S(1)}, u32[]{:S(2)}, u32[]{:S(2)}) collective-permute-start(bf16[147456]{0:T(1024)(128)(2,1)S(1)} %maximum_select_fusion.2), channel_id=1, source_target_pairs={{0,4},{4,0},{8,12},{12,8},{1,5},{5,1},{9,13},{13,9},{2,6},{6,2},{1... | collective-permute-start | bytes 884744 | tf_op jit(solution)/shard_map/ppermute | solution.py:101
  (3 other events, 2.5 us)

commit v4 on v2

--- a/solution.py
+++ b/solution.py
@@ -290,7 +290,9 @@
 
     mine_terms = by_section(partials[0], partials[1], 0)
     other_terms = by_section(partials[1], partials[0], 0)
-    gathered = summed_over_tiles(mine_terms + swap(other_terms))
+    scale = 1.0 / batches
+    other_terms = swap((other_terms * scale).astype(jnp.bfloat16)).astype(jnp.float32)
+    gathered = summed_over_tiles(mine_terms * scale + other_terms)
     mine_back = by_section(results[0], results[1], 0)
     other_back = swap(by_section(results[1], results[0], 0))
     boundary = jnp.where(
@@ -298,7 +300,7 @@
         jnp.concatenate([mine_back, other_back], axis=0),
         jnp.concatenate([other_back, mine_back], axis=0),
     )
-    return (boundary[None], gathered / batches)
+    return (boundary[None], gathered)
 
 
 def solution(mesh):

time: 131 us -> 130 us (level)
    convert_element_type x0 -> x2, other arithmetic: none -> 2.11 us  [the longest x1 1.12 us: summed_over_tiles(): return current.astype(jnp.float32).reshape(grads.shape)]
where the time goes in v4:
time: 130 us; the launch traced here: 129 us
  waiting for transfers between devices  36.7 us (28%)
  starting transfers between devices  31.5 us (24%)
  other arithmetic  27.7 us (21%)
  matrix products  17 us (13%)
  local copies, waits for them, and re-layouts  14.6 us (11%)
  between operations  1.6 us (1%)
    ppermute x6, waiting for transfers between devices, exchange(): return lax.ppermute(values, axis, [(i, i ^ distance) for i in range(count)])  24 us
    ppermute x6, starting transfers between devices, exchange(): return lax.ppermute(values, axis, [(i, i ^ distance) for i in range(count)])  18.2 us
    ppermute x4, starting transfers between devices, from_neighbours(): parts.append(lax.ppermute(piece, AXES, pairs))  12.6 us
    ppermute x4, waiting for transfers between devices, from_neighbours(): parts.append(lax.ppermute(piece, AXES, pairs))  10.4 us
    conv_general_dilated x8, matrix products, convolve(): lax.conv_general_dilated(padded, kernel, (1, 1), 'VALID', dimension_numbe...  9.94 us
    convert_element_type x4, other arithmetic, local_split(): current = current.astype(jnp.bfloat16)  9.08 us
    convert_element_type x4, other arithmetic, section_chain(): signal = signal.astype(jnp.bfloat16)  8.96 us
    transpose x4, matrix products, kernel_terms(): return jnp.transpose(terms, (1, 2, 0, 3))  7.09 us
  transfers between devices with their start and end apart: 14, of which 11 were waited for; matrix products, arithmetic and copies ran while one was open for 5% of the time, Pallas kernels for 0%

profile of v4, /device:TPU:0, one launch (start us, length us, event | category | flops | bytes accessed | tf_op | source)
XLA Modules:
  0.0 129.1 jit_solution(3689044832767554921)
XLA Ops:
  5.4 5.4 %collective-permute-start.1 = (bf16[6,6,32,128]{3,2,0,1:T(8,128)(2,1)S(1)}, bf16[6,6,32,128]{3,2,0,1:T(8,128)(2,1)S(1)}, u32[]{:S(2)}, u32[]{:S(2)}) collective-permute-start(bf16[6,6,32,128]{3,2,0,1:T(8,128)(2,1)S(1)} %get-tuple-element.18), channel_id=1, source_target_pairs={{0,4},{1,5},{2,6},{3,7},{4,8},{5,9},{6,10},{7,11},{8,12},{9,13},{1... | collective-permute-start | bytes 884744 | tf_op jit(solution)/shard_map/ppermute | solution.py:43
  10.9 5.8 %collective-permute-done.2 = bf16[6,6,32,128]{3,2,0,1:T(8,128)(2,1)S(1)} collective-permute-done((bf16[6,6,32,128]{3,2,0,1:T(8,128)(2,1)S(1)}, bf16[6,6,32,128]{3,2,0,1:T(8,128)(2,1)S(1)}, u32[]{:S(2)}, u32[]{:S(2)}) %collective-permute-start.2) | collective-permute-done | bytes 294944 | tf_op jit(solution)/shard_map/ppermute | solution.py:43
  18.8 4.6 %collective-permute-start.3 = (bf16[6,28,6,128]{3,2,0,1:T(8,128)(2,1)S(1)}, bf16[6,28,6,128]{3,2,0,1:T(8,128)(2,1)S(1)}, u32[]{:S(2)}, u32[]{:S(2)}) collective-permute-start(bf16[6,28,6,128]{3,2,0,1:T(8,128)(2,1)S(1)} %get-tuple-element.14), channel_id=1, source_target_pairs={{0,1},{1,2},{2,3},{4,5},{5,6},{6,7},{8,9},{9,10},{10,11},{12,13},{... | collective-permute-start | bytes 774152 | tf_op jit(solution)/shard_map/ppermute | solution.py:43
  25.7 2.8 %collective-permute-done.4 = bf16[6,28,6,128]{3,2,0,1:T(8,128)(2,1)S(1)} collective-permute-done((bf16[6,28,6,128]{3,2,0,1:T(8,128)(2,1)S(1)}, bf16[6,28,6,128]{3,2,0,1:T(8,128)(2,1)S(1)}, u32[]{:S(2)}, u32[]{:S(2)}) %collective-permute-start.4) | collective-permute-done | bytes 258080 | tf_op jit(solution)/shard_map/ppermute | solution.py:43
  29.7 1.6 %pad_maximum_fusion.2 = (bf16[2,28,44,128]{3,2,0,1:T(8,128)(2,1)}, bf16[2,28,44,128]{3,2,0,1:T(8,128)(2,1)S(1)}) fusion(bf16[6,28,6,128]{3,2,0,1:T(8,128)(2,1)S(1)} %collective-permute-done.4, bf16[6,28,6,128]{3,2,0,1:T(8,128)(2,1)S(1)} %collective-permute-done.3, bf16[6,6,32,128]{3,2,0,1:T(8,128)(2,1)S(1)} %collective-permute-done.2, ...), kind=kLoop, calls=%fused_computation.66 | loop fusion | flops 8830976 | bytes 3153920 | tf_op jit(solution)/shard_map/concatenate | solution.py:44
  33.8 1.7 %fusion.1 = bf16[26,16,6,128]{3,1,2,0:T(8,128)(2,1)S(1)} fusion(bf16[28,2,8,8,128]{4,1,3,2,0:T(2,128)(2,1)S(1)} %fusion.16, pred[16,6]{0,1:T(8,128)(4,1)S(1)} %copy-done.26, bf16[2,3,3,128,128]{4,3,2,1,0:T(8,128)(2,1)S(1)} %get-tuple-element.17), kind=kOutput, calls=%fused_computation.6 | convolution fusion | flops 736739328 | bytes 1852416 | tf_op jit(solution)/shard_map/conv_general_dilated | solution.py:63
  35.9 1.7 %fusion.11 = bf16[26,2,42,128]{3,1,2,0:T(2,128)(2,1)S(1)} fusion(bf16[26,2,42,128]{3,2,1,0:T(8,128)(2,1)S(1)} %bitcast.138, pred[26,42]{1,0:T(8,128)(4,1)S(1)} %broadcast_and_fusion), kind=kLoop, calls=%fused_computation.35 | loop fusion | flops 279552 | bytes 1119300 | tf_op jit(solution)/shard_map/convert_element_type | solution.py:279
  37.6 1.7 %fusion.96 = bf16[2,26,42,128]{3,0,2,1:T(2,128)(2,1)S(1)} fusion(bf16[26,2,42,128]{3,2,1,0:T(8,128)(2,1)S(1)} %bitcast.139, pred[26,42]{1,0:T(8,128)(4,1)S(1)} %broadcast_and_fusion), kind=kLoop, calls=%fused_computation.191 | loop fusion | flops 279552 | bytes 1119300 | tf_op jit(solution)/shard_map/convert_element_type | solution.py:279
  42.6 2.8 %fusion.19 = bf16[22,2,38,128]{3,1,2,0:T(2,128)(2,1)S(1)} fusion(bf16[22,2,38,128]{3,0,2,1:T(8,128)(2,1)S(1)} %slice.149, pred[22,38]{1,0:T(8,128)(4,1)S(1)} %broadcast_and_fusion.2), kind=kLoop, calls=%fused_computation.47 | loop fusion | flops 214016 | bytes 856900 | tf_op jit(solution)/shard_map/convert_element_type | solution.py:279
  45.4 2.8 %fusion.95 = bf16[2,22,38,128]{3,0,2,1:T(2,128)(2,1)S(1)} fusion(bf16[22,2,38,128]{3,0,2,1:T(8,128)(2,1)S(1)} %slice.149, pred[22,38]{1,0:T(8,128)(4,1)S(1)} %broadcast_and_fusion.2), kind=kLoop, calls=%fused_computation.190 | loop fusion | flops 214016 | bytes 856900 | tf_op jit(solution)/shard_map/convert_element_type | solution.py:279
  49.3 1.6 %fusion.2 = bf16[24,16,6,128]{3,1,2,0:T(8,128)(2,1)S(1)} fusion(bf16[26,2,7,2,128]{4,2,1,3,0:T(8,128)(2,1)S(1)} %slice.136, bf16[26,2,8,6,128]{4,2,1,3,0:T(8,128)(2,1)S(1)} %copy.147, pred[16,6]{0,1:T(8,128)(4,1)S(1)} %copy-done.25, bf16[2,3,3,128,128]{4,3,2,1,0:T(8,128)(2,1)S(1)} %copy-done.8), kind=kOutput, calls=%fused_computation.8 | convolution fusion | flops 682622976 | bytes 1737728 | tf_op jit(solution)/shard_map/conv_general_dilated | solution.py:63
  52.1 2.1 %fusion.15 = bf16[2,24,40,128]{3,2,0,1:T(8,128)(2,1)S(1)} fusion(bf16[24,2,40,128]{3,0,2,1:T(8,128)(2,1)S(1)} %slice.138, bf16[6,28,6,128]{3,2,0,1:T(8,128)(2,1)S(1)} %copy-done.11, bf16[6,28,6,128]{3,2,0,1:T(8,128)(2,1)S(1)} %copy-done.13, bf16[6,6,32,128]{3,2,0,1:T(8,128)(2,1)S(1)} %copy-done.2, bf16[6,6,32,128]{3,2,0,1:T(8,128)(2,1)S(1)} %copy-done.4, ...), kind=kLoop, calls=%fused_computation.42 | loop fusion | flops 5160960 | bytes 2876352 | tf_op jit(solution)/shard_map/convert_element_type | solution.py:233
  57.0 2.9 %fusion.22 = bf16[2,22,38,128]{3,0,2,1:T(2,128)(2,1)S(1)} fusion(f32[22,2,38,128]{3,0,2,1:T(8,128)S(1)} %slice.141, pred[22,38]{1,0:T(8,128)(4,1)S(1)} %broadcast_and_fusion.2, bf16[2,26,42,128]{3,0,2,1:T(2,128)(2,1)S(1)} %fusion.96), kind=kLoop, calls=%fused_computation.51 | loop fusion | flops 1284096 | bytes 1712964 | tf_op jit(solution)/shard_map/convert_element_type | solution.py:233
  59.9 1.7 %convolution_bitcast_fusion.2 = f32[1,3,3,128,128]{4,3,2,1,0:T(8,128)S(1)} fusion(bf16[2,28,44,128]{3,2,0,1:T(8,128)(2,1)S(1)} %get-tuple-element.13, bf16[2,22,38,128]{3,0,2,1:T(2,128)(2,1)S(1)} %fusion.22), kind=kOutput, calls=%fused_computation.25 | convolution fusion | flops 301989888 | bytes 1540096 | tf_op jit(solution)/shard_map/transpose | solution.py:82
  65.4 2.0 %fusion.34 = bf16[20,2,36,128]{3,1,2,0:T(2,128)(2,1)S(1)} fusion(f32[20,2,36,128]{3,0,2,1:T(8,128)S(1)} %slice.145, pred[20,36]{1,0:T(8,128)(4,1)S(1)} %broadcast_and_fusion.3, bf16[20,2,36,128]{3,0,2,1:T(8,128)(2,1)S(1)} %slice.152), kind=kLoop, calls=%fused_computation.64 | loop fusion | flops 1290240 | bytes 1475280 | tf_op jit(solution)/shard_map/convert_element_type | solution.py:233
  69.8 1.8 %convolution_bitcast_fusion = f32[1,3,3,128,128]{4,3,2,1,0:T(8,128)S(1)} fusion(bf16[26,2,42,128]{3,1,2,0:T(2,128)(2,1)S(1)} %fusion.11, bf16[2,16,32,128]{3,2,0,1:T(8,128)(2,1)S(1)} %slice.165), kind=kOutput, calls=%fused_computation.23 | convolution fusion | flops 301989888 | bytes 1411072 | tf_op jit(solution)/shard_map/transpose | solution.py:82
  71.6 1.8 %convolution_bitcast_fusion.1 = f32[1,3,3,128,128]{4,3,2,1,0:T(8,128)S(1)} fusion(bf16[22,2,38,128]{3,1,2,0:T(2,128)(2,1)S(1)} %fusion.19, bf16[2,20,36,128]{3,0,2,1:T(2,128)(2,1)S(1)} %bitcast.161), kind=kOutput, calls=%fused_computation.24 | convolution fusion | flops 301989888 | bytes 1280000 | tf_op jit(solution)/shard_map/transpose | solution.py:82
  73.4 2.0 %fusion.54 = bf16[2,18,34,128]{3,0,2,1:T(2,128)(2,1)S(1)} fusion(f32[18,2,34,128]{3,0,2,1:T(8,128)S(1)} %slice.155, pred[18,34]{1,0:T(8,128)(4,1)S(1)} %broadcast_and_fusion.4, bf16[2,22,38,128]{3,0,2,1:T(2,128)(2,1)S(1)} %fusion.95), kind=kLoop, calls=%fused_computation.90 | loop fusion | flops 940032 | bytes 1253988 | tf_op jit(solution)/shard_map/convert_element_type | solution.py:233
  76.2 1.8 %convolution_bitcast_fusion.3 = f32[1,3,3,128,128]{4,3,2,1,0:T(8,128)S(1)} fusion(bf16[2,28,44,128]{3,2,0,1:T(8,128)(2,1)S(1)} %copy-done.9, bf16[2,18,34,128]{3,0,2,1:T(2,128)(2,1)S(1)} %fusion.54), kind=kOutput, calls=%fused_computation.26 | convolution fusion | flops 301989888 | bytes 1540096 | tf_op jit(solution)/shard_map/transpose | solution.py:82
  78.9 2.3 %collective-permute-done.7 = bf16[2,3,3,128,128]{4,3,2,1,0:T(8,128)(2,1)} collective-permute-done((bf16[2,3,3,128,128]{4,3,2,1,0:T(8,128)(2,1)}, bf16[2,3,3,128,128]{4,3,2,1,0:T(8,128)(2,1)}, u32[]{:S(2)}, u32[]{:S(2)}) %collective-permute-start.7) | collective-permute-done | bytes 589856 | tf_op jit(solution)/shard_map/ppermute | solution.py:250
  82.6 5.0 %collective-permute-start.8 = (bf16[147456]{0:T(1024)(128)(2,1)S(1)}, bf16[147456]{0:T(1024)(128)(2,1)S(1)}, u32[]{:S(2)}, u32[]{:S(2)}) collective-permute-start(bf16[147456]{0:T(1024)(128)(2,1)S(1)} %bitcast.168), channel_id=1, source_target_pairs={{0,4},{4,0},{8,12},{12,8},{1,5},{5,1},{9,13},{13,9},{2,6},{6,2},{1... | collective-permute-start | bytes 884744 | tf_op jit(solution)/shard_map/ppermute | solution.py:101
  87.7 7.3 %collective-permute-done.8 = bf16[147456]{0:T(1024)(128)(2,1)S(1)} collective-permute-done((bf16[147456]{0:T(1024)(128)(2,1)S(1)}, bf16[147456]{0:T(1024)(128)(2,1)S(1)}, u32[]{:S(2)}, u32[]{:S(2)}) %collective-permute-start.8) | collective-permute-done | bytes 294944 | tf_op jit(solution)/shard_map/ppermute | solution.py:101
  95.1 3.7 %collective-permute-start.9 = (bf16[73728]{0:T(1024)(128)(2,1)S(1)}, bf16[73728]{0:T(1024)(128)(2,1)S(1)}, u32[]{:S(2)}, u32[]{:S(2)}) collective-permute-start(bf16[73728]{0:T(1024)(128)(2,1)S(1)} %select_convert_fusion.2), channel_id=1, source_target_pairs={{0,8},{4,12},{8,0},{12,4},{1,9},{5,13},{9,1},{13,5},{2,10},{6,14},... | collective-permute-start | bytes 442376 | tf_op jit(solution)/shard_map/ppermute | solution.py:101
  98.8 3.3 %collective-permute-done.9 = bf16[73728]{0:T(1024)(128)(2,1)S(1)} collective-permute-done((bf16[73728]{0:T(1024)(128)(2,1)S(1)}, bf16[73728]{0:T(1024)(128)(2,1)S(1)}, u32[]{:S(2)}, u32[]{:S(2)}) %collective-permute-start.9) | collective-permute-done | bytes 147488 | tf_op jit(solution)/shard_map/ppermute | solution.py:101
  102.1 2.5 %collective-permute-start.10 = (bf16[73728]{0:T(1024)(128)(2,1)S(1)}, bf16[73728]{0:T(1024)(128)(2,1)S(1)}, u32[]{:S(2)}, u32[]{:S(2)}) collective-permute-start(bf16[73728]{0:T(1024)(128)(2,1)S(1)} %add_convert_fusion.2), channel_id=1, source_target_pairs={{0,1},{1,0},{2,3},{3,2},{4,5},{5,4},{6,7},{7,6},{8,9},{9,8},{10,11... | collective-permute-start | bytes 442376 | tf_op jit(solution)/shard_map/ppermute | solution.py:101
  105.2 2.6 %collective-permute-done.10 = bf16[73728]{0:T(1024)(128)(2,1)S(1)} collective-permute-done((bf16[73728]{0:T(1024)(128)(2,1)S(1)}, bf16[73728]{0:T(1024)(128)(2,1)S(1)}, u32[]{:S(2)}, u32[]{:S(2)}) %collective-permute-start.10) | collective-permute-done | bytes 147488 | tf_op jit(solution)/shard_map/ppermute | solution.py:101
  107.9 3.1 %collective-permute-start.11 = (bf16[73728]{0:T(1024)(128)(2,1)S(1)}, bf16[73728]{0:T(1024)(128)(2,1)S(1)}, u32[]{:S(2)}, u32[]{:S(2)}) collective-permute-start(bf16[73728]{0:T(1024)(128)(2,1)S(1)} %add_convert_fusion.1), channel_id=1, source_target_pairs={{0,2},{1,3},{2,0},{3,1},{4,6},{5,7},{6,4},{7,5},{8,10},{9,11},{10,... | collective-permute-start | bytes 442376 | tf_op jit(solution)/shard_map/ppermute | solution.py:101
  112.1 3.5 %collective-permute-done.11 = bf16[73728]{0:T(1024)(128)(2,1)S(1)} collective-permute-done((bf16[73728]{0:T(1024)(128)(2,1)S(1)}, bf16[73728]{0:T(1024)(128)(2,1)S(1)}, u32[]{:S(2)}, u32[]{:S(2)}) %collective-permute-start.11) | collective-permute-done | bytes 147488 | tf_op jit(solution)/shard_map/ppermute | solution.py:101
  115.7 2.3 %collective-permute-start.12 = (bf16[73728]{0:T(1024)(128)(2,1)S(1)}, bf16[73728]{0:T(1024)(128)(2,1)S(1)}, u32[]{:S(2)}, u32[]{:S(2)}) collective-permute-start(bf16[73728]{0:T(1024)(128)(2,1)S(1)} %add_convert_fusion), channel_id=1, source_target_pairs={{0,8},{4,12},{8,0},{12,4},{1,9},{5,13},{9,1},{13,5},{2,10},{6,14},... | collective-permute-start | bytes 442376 | tf_op jit(solution)/shard_map/ppermute | solution.py:101
  118.2 2.9 %collective-permute-done.12 = bf16[73728]{0:T(1024)(128)(2,1)S(1)} collective-permute-done((bf16[73728]{0:T(1024)(128)(2,1)S(1)}, bf16[73728]{0:T(1024)(128)(2,1)S(1)}, u32[]{:S(2)}, u32[]{:S(2)}) %collective-permute-start.12) | collective-permute-done | bytes 147488 | tf_op jit(solution)/shard_map/ppermute | solution.py:101
  121.2 1.6 %collective-permute-start.13 = (bf16[147456]{0:T(1024)(128)(2,1)S(1)}, bf16[147456]{0:T(1024)(128)(2,1)S(1)}, u32[]{:S(2)}, u32[]{:S(2)}) collective-permute-start(bf16[147456]{0:T(1024)(128)(2,1)S(1)} %maximum_select_fusion.2), channel_id=1, source_target_pairs={{0,4},{4,0},{8,12},{12,8},{1,5},{5,1},{9,13},{13,9},{2,6},{6,2},{1... | collective-permute-start | bytes 884744 | tf_op jit(solution)/shard_map/ppermute | solution.py:101
  123.7 4.3 %collective-permute-done.13 = bf16[147456]{0:T(1024)(128)(2,1)S(1)} collective-permute-done((bf16[147456]{0:T(1024)(128)(2,1)S(1)}, bf16[147456]{0:T(1024)(128)(2,1)S(1)}, u32[]{:S(2)}, u32[]{:S(2)}) %collective-permute-start.13) | collective-permute-done | bytes 294944 | tf_op jit(solution)/shard_map/ppermute | solution.py:101
  (159 shorter events, 34.3 us)
Async XLA Ops:
  0.6 2.5 %copy-start = (bf16[4,16,32,128]{3,2,1,0:T(8,128)(2,1)S(1)}, bf16[4,16,32,128]{3,2,1,0:T(8,128)(2,1)}, u32[]{:S(2)}) copy-start(bf16[4,16,32,128]{3,2,1,0:T(8,128)(2,1)} %param.6) | copy-start | bytes 1572868
  0.6 1.8 %copy-start.16 = (bf16[2,3,3,128,128]{4,3,2,1,0:T(8,128)(2,1)S(1)}, bf16[2,3,3,128,128]{4,3,2,1,0:T(8,128)(2,1)}, u32[]{:S(2)}) copy-start(bf16[2,3,3,128,128]{4,3,2,1,0:T(8,128)(2,1)} %param.5) | copy-start | bytes 1769476
  0.7 1.9 %copy-start.20 = (s32[4]{0:T(128)S(1)}, s32[4]{0:T(128)}, u32[]{:S(2)}) copy-start(s32[4]{0:T(128)} %param.7) | copy-start | bytes 52
  1.9 2.1 %collective-permute-start = (bf16[2,16,32,128]{3,2,0,1:T(8,128)(2,1)S(1)}, bf16[2,16,32,128]{3,2,0,1:T(8,128)(2,1)S(1)}, u32[]{:S(2)}, u32[]{:S(2)}) collective-permute-start(bf16[2,16,32,128]{3,2,0,1:T(8,128)(2,1)S(1)} %bitcast.170), channel_id=1, source_target_pairs={{0,16},{16,0},{1,17},{17,1},{2,18},{18,2},{3,19},{19,3},{4,20},{20... | collective-permute-start | bytes 786440 | tf_op jit(solution)/shard_map/ppermute | solution.py:250
  2.4 20.9 %collective-permute-start.5 = (bf16[2,3,3,128,128]{4,3,2,1,0:T(8,128)(2,1)S(1)}, bf16[2,3,3,128,128]{4,3,2,1,0:T(8,128)(2,1)}, u32[]{:S(2)}, u32[]{:S(2)}) collective-permute-start(bf16[2,3,3,128,128]{4,3,2,1,0:T(8,128)(2,1)S(1)} %copy-done.16), channel_id=1, source_target_pairs={{0,16},{16,0},{1,17},{17,1},{2,18},{18,2},{3,19},{19,3},{4,20},{20... | collective-permute-start | bytes 1769480 | tf_op jit(solution)/shard_map/ppermute | solution.py:250
  4.1 12.7 %collective-permute-start.2 = (bf16[6,6,32,128]{3,2,0,1:T(8,128)(2,1)S(1)}, bf16[6,6,32,128]{3,2,0,1:T(8,128)(2,1)S(1)}, u32[]{:S(2)}, u32[]{:S(2)}) collective-permute-start(bf16[6,6,32,128]{3,2,0,1:T(8,128)(2,1)S(1)} %get-tuple-element.19), channel_id=1, source_target_pairs={{4,0},{5,1},{6,2},{7,3},{8,4},{9,5},{10,6},{11,7},{12,8},{13,9},{1... | collective-permute-start | bytes 884744 | tf_op jit(solution)/shard_map/ppermute | solution.py:43
  5.4 11.9 %collective-permute-start.1 = (bf16[6,6,32,128]{3,2,0,1:T(8,128)(2,1)S(1)}, bf16[6,6,32,128]{3,2,0,1:T(8,128)(2,1)S(1)}, u32[]{:S(2)}, u32[]{:S(2)}) collective-permute-start(bf16[6,6,32,128]{3,2,0,1:T(8,128)(2,1)S(1)} %get-tuple-element.18), channel_id=1, source_target_pairs={{0,4},{1,5},{2,6},{3,7},{4,8},{5,9},{6,10},{7,11},{8,12},{9,13},{1... | collective-permute-start | bytes 884744 | tf_op jit(solution)/shard_map/ppermute | solution.py:43
  16.7 13.0 %copy-start.1 = (bf16[6,6,32,128]{3,2,0,1:T(8,128)(2,1)}, bf16[6,6,32,128]{3,2,0,1:T(8,128)(2,1)S(1)}, u32[]{:S(2)}) copy-start(bf16[6,6,32,128]{3,2,0,1:T(8,128)(2,1)S(1)} %collective-permute-done.2) | copy-start | bytes 884740
  17.3 12.4 %copy-start.3 = (bf16[6,6,32,128]{3,2,0,1:T(8,128)(2,1)}, bf16[6,6,32,128]{3,2,0,1:T(8,128)(2,1)S(1)}, u32[]{:S(2)}) copy-start(bf16[6,6,32,128]{3,2,0,1:T(8,128)(2,1)S(1)} %collective-permute-done.1) | copy-start | bytes 884740
  17.5 11.1 %collective-permute-start.4 = (bf16[6,28,6,128]{3,2,0,1:T(8,128)(2,1)S(1)}, bf16[6,28,6,128]{3,2,0,1:T(8,128)(2,1)S(1)}, u32[]{:S(2)}, u32[]{:S(2)}) collective-permute-start(bf16[6,28,6,128]{3,2,0,1:T(8,128)(2,1)S(1)} %get-tuple-element.15), channel_id=1, source_target_pairs={{1,0},{2,1},{3,2},{5,4},{6,5},{7,6},{9,8},{10,9},{11,10},{13,12},{... | collective-permute-start | bytes 774152 | tf_op jit(solution)/shard_map/ppermute | solution.py:43
  18.8 11.0 %collective-permute-start.3 = (bf16[6,28,6,128]{3,2,0,1:T(8,128)(2,1)S(1)}, bf16[6,28,6,128]{3,2,0,1:T(8,128)(2,1)S(1)}, u32[]{:S(2)}, u32[]{:S(2)}) collective-permute-start(bf16[6,28,6,128]{3,2,0,1:T(8,128)(2,1)S(1)} %get-tuple-element.14), channel_id=1, source_target_pairs={{0,1},{1,2},{2,3},{4,5},{5,6},{6,7},{8,9},{9,10},{10,11},{12,13},{... | collective-permute-start | bytes 774152 | tf_op jit(solution)/shard_map/ppermute | solution.py:43
  24.5 1.2 copy-start.5
  24.5 9.2 %copy-start.7 = (bf16[2,3,3,128,128]{4,3,2,1,0:T(8,128)(2,1)}, bf16[2,3,3,128,128]{4,3,2,1,0:T(8,128)(2,1)S(1)}, u32[]{:S(2)}) copy-start(bf16[2,3,3,128,128]{4,3,2,1,0:T(8,128)(2,1)S(1)} %get-tuple-element.17) | copy-start | bytes 1769476
  28.6 2.8 %copy-start.10 = (bf16[6,28,6,128]{3,2,0,1:T(8,128)(2,1)}, bf16[6,28,6,128]{3,2,0,1:T(8,128)(2,1)S(1)}, u32[]{:S(2)}) copy-start(bf16[6,28,6,128]{3,2,0,1:T(8,128)(2,1)S(1)} %collective-permute-done.4) | copy-start | bytes 774148
  29.7 1.7 %copy-start.12 = (bf16[6,28,6,128]{3,2,0,1:T(8,128)(2,1)}, bf16[6,28,6,128]{3,2,0,1:T(8,128)(2,1)S(1)}, u32[]{:S(2)}) copy-start(bf16[6,28,6,128]{3,2,0,1:T(8,128)(2,1)S(1)} %collective-permute-done.3) | copy-start | bytes 774148
  32.4 1.4 %copy-start.26 = (pred[16,6]{0,1:T(8,128)(4,1)S(1)}, pred[16,6]{0,1:T(8,128)(4,1)}, u32[]{:S(2)}) copy-start(pred[16,6]{0,1:T(8,128)(4,1)} %constant.180) | copy-start | bytes 292
  35.9 3.5 %copy-start.9 = (bf16[2,28,44,128]{3,2,0,1:T(8,128)(2,1)S(1)}, bf16[2,28,44,128]{3,2,0,1:T(8,128)(2,1)}, u32[]{:S(2)}) copy-start(bf16[2,28,44,128]{3,2,0,1:T(8,128)(2,1)} %get-tuple-element.12) | copy-start | bytes 1892356
  40.0 1.1 copy-start.6
  48.2 1.1 copy-start.8
  50.9 1.1 copy-start.11
  50.9 1.2 copy-start.13
  78.9 2.3 %collective-permute-start.7 = (bf16[2,3,3,128,128]{4,3,2,1,0:T(8,128)(2,1)}, bf16[2,3,3,128,128]{4,3,2,1,0:T(8,128)(2,1)}, u32[]{:S(2)}, u32[]{:S(2)}) collective-permute-start(bf16[2,3,3,128,128]{4,3,2,1,0:T(8,128)(2,1)} %multiply_convert_fusion), channel_id=1, source_target_pairs={{0,16},{16,0},{1,17},{17,1},{2,18},{18,2},{3,19},{19,3},{4,20},{20... | collective-permute-start | bytes 1769480 | tf_op jit(solution)/shard_map/ppermute | solution.py:250
  82.6 12.3 %collective-permute-start.8 = (bf16[147456]{0:T(1024)(128)(2,1)S(1)}, bf16[147456]{0:T(1024)(128)(2,1)S(1)}, u32[]{:S(2)}, u32[]{:S(2)}) collective-permute-start(bf16[147456]{0:T(1024)(128)(2,1)S(1)} %bitcast.168), channel_id=1, source_target_pairs={{0,4},{4,0},{8,12},{12,8},{1,5},{5,1},{9,13},{13,9},{2,6},{6,2},{1... | collective-permute-start | bytes 884744 | tf_op jit(solution)/shard_map/ppermute | solution.py:101
  95.0 9.8 %copy-start.15 = (bf16[2,18,34,128]{3,0,2,1:T(2,128)(2,1)S(1)}, bf16[2,18,34,128]{3,0,2,1:T(2,128)(2,1)}, u32[]{:S(2)}) copy-start(bf16[2,18,34,128]{3,0,2,1:T(2,128)(2,1)} %copy-done.14) | copy-start | bytes 940036
  95.1 7.0 %collective-permute-start.9 = (bf16[73728]{0:T(1024)(128)(2,1)S(1)}, bf16[73728]{0:T(1024)(128)(2,1)S(1)}, u32[]{:S(2)}, u32[]{:S(2)}) collective-permute-start(bf16[73728]{0:T(1024)(128)(2,1)S(1)} %select_convert_fusion.2), channel_id=1, source_target_pairs={{0,8},{4,12},{8,0},{12,4},{1,9},{5,13},{9,1},{13,5},{2,10},{6,14},... | collective-permute-start | bytes 442376 | tf_op jit(solution)/shard_map/ppermute | solution.py:101
  102.1 5.7 %collective-permute-start.10 = (bf16[73728]{0:T(1024)(128)(2,1)S(1)}, bf16[73728]{0:T(1024)(128)(2,1)S(1)}, u32[]{:S(2)}, u32[]{:S(2)}) collective-permute-start(bf16[73728]{0:T(1024)(128)(2,1)S(1)} %add_convert_fusion.2), channel_id=1, source_target_pairs={{0,1},{1,0},{2,3},{3,2},{4,5},{5,4},{6,7},{7,6},{8,9},{9,8},{10,11... | collective-permute-start | bytes 442376 | tf_op jit(solution)/shard_map/ppermute | solution.py:101
  104.8 6.1 %copy-start.18 = (bf16[2,3,3,128,128]{3,4,2,1,0:T(8,128)(2,1)S(1)}, bf16[2,3,3,128,128]{3,4,2,1,0:T(8,128)(2,1)}, u32[]{:S(2)}) copy-start(bf16[2,3,3,128,128]{3,4,2,1,0:T(8,128)(2,1)} %get-tuple-element.28) | copy-start | bytes 1769476
  104.8 6.1 %copy-start.21 = (pred[16,5]{0,1:T(8,128)(4,1)S(1)}, pred[16,5]{0,1:T(8,128)(4,1)}, u32[]{:S(2)}) copy-start(pred[16,5]{0,1:T(8,128)(4,1)} %constant.175) | copy-start | bytes 244
  107.9 7.8 %collective-permute-start.11 = (bf16[73728]{0:T(1024)(128)(2,1)S(1)}, bf16[73728]{0:T(1024)(128)(2,1)S(1)}, u32[]{:S(2)}, u32[]{:S(2)}) collective-permute-start(bf16[73728]{0:T(1024)(128)(2,1)S(1)} %add_convert_fusion.1), channel_id=1, source_target_pairs={{0,2},{1,3},{2,0},{3,1},{4,6},{5,7},{6,4},{7,5},{8,10},{9,11},{10,... | collective-permute-start | bytes 442376 | tf_op jit(solution)/shard_map/ppermute | solution.py:101
  115.7 5.4 %collective-permute-start.12 = (bf16[73728]{0:T(1024)(128)(2,1)S(1)}, bf16[73728]{0:T(1024)(128)(2,1)S(1)}, u32[]{:S(2)}, u32[]{:S(2)}) collective-permute-start(bf16[73728]{0:T(1024)(128)(2,1)S(1)} %add_convert_fusion), channel_id=1, source_target_pairs={{0,8},{4,12},{8,0},{12,4},{1,9},{5,13},{9,1},{13,5},{2,10},{6,14},... | collective-permute-start | bytes 442376 | tf_op jit(solution)/shard_map/ppermute | solution.py:101
  118.1 4.7 %collective-permute-start.6 = (bf16[2,16,32,128]{3,2,0,1:T(8,128)(2,1)S(1)}, bf16[2,16,32,128]{3,2,0,1:T(8,128)(2,1)S(1)}, u32[]{:S(2)}, u32[]{:S(2)}) collective-permute-start(bf16[2,16,32,128]{3,2,0,1:T(8,128)(2,1)S(1)} %get-tuple-element.21), channel_id=1, source_target_pairs={{0,16},{16,0},{1,17},{17,1},{2,18},{18,2},{3,19},{19,3},{4,20},{20... | collective-permute-start | bytes 786440 | tf_op jit(solution)/shard_map/ppermute | solution.py:250
  121.2 6.8 %collective-permute-start.13 = (bf16[147456]{0:T(1024)(128)(2,1)S(1)}, bf16[147456]{0:T(1024)(128)(2,1)S(1)}, u32[]{:S(2)}, u32[]{:S(2)}) collective-permute-start(bf16[147456]{0:T(1024)(128)(2,1)S(1)} %maximum_select_fusion.2), channel_id=1, source_target_pairs={{0,4},{4,0},{8,12},{12,8},{1,5},{5,1},{9,13},{13,9},{2,6},{6,2},{1... | collective-permute-start | bytes 884744 | tf_op jit(solution)/shard_map/ppermute | solution.py:101
  (9 other events, 8.7 us)

commit v5 on v4

--- a/solution.py
+++ b/solution.py
@@ -88,13 +88,12 @@
 
 def summed_over_tiles(grads):
     shape = sizes()
-
-    def distances(count):
-        found, distance = [], 1
-        while distance < count:
-            found.append(distance)
+    halving, doubling = [], []
+    for axis, dim in (("row", 1), ("col", 2)):
+        distance = 1
+        while distance < shape[dim]:
+            (halving if distance == 1 else doubling).append((axis, distance))
             distance *= 2
-        return found
 
     def exchange(values, axis, distance):
         count = lax.axis_size(axis)
@@ -102,25 +101,25 @@
 
     current = grads.reshape(-1)
     kept = []
-    for distance in distances(shape[1]):
+    for axis, distance in halving:
         half = current.shape[0] // 2
-        upper = (lax.axis_index("row") // distance) % 2 == 1
+        upper = (lax.axis_index(axis) // distance) % 2 == 1
         low, high = current[:half], current[half:]
         send = jnp.where(upper, low, high).astype(jnp.bfloat16)
         mine = jnp.where(upper, high, low).astype(jnp.bfloat16)
-        other = exchange(send, "row", distance)
+        other = exchange(send, axis, distance)
         current = mine.astype(jnp.float32) + other.astype(jnp.float32)
-        kept.append((distance, upper))
-    for distance in distances(shape[2]):
+        kept.append((axis, distance, upper))
+    for axis, distance in doubling:
         rounded = current.astype(jnp.bfloat16)
-        other = exchange(rounded, "col", distance)
-        upper = (lax.axis_index("col") // distance) % 2 == 1
+        other = exchange(rounded, axis, distance)
+        upper = (lax.axis_index(axis) // distance) % 2 == 1
         first = jnp.where(upper, other, rounded).astype(jnp.float32)
         second = jnp.where(upper, rounded, other).astype(jnp.float32)
         current = first + second
     current = current.astype(jnp.bfloat16)
-    for distance, upper in reversed(kept):
-        other = exchange(current, "row", distance)
+    for axis, distance, upper in reversed(kept):
+        other = exchange(current, axis, distance)
         current = jnp.where(
             upper, jnp.concatenate([other, current]), jnp.concatenate([current, other])
         )

time: 130 us -> 129 us (level)
  starting transfers between devices: 31.5 us -> 29.6 us
  waiting for transfers between devices: 36.7 us -> 38.5 us
    ppermute x6, starting transfers between devices: 18.2 us -> 16.3 us  [exchange(): return lax.ppermute(values, axis, [(i, i ^ distance) for i in range(count)])]
    ppermute x6, waiting for transfers between devices: 24 us -> 25.7 us  [exchange(): return lax.ppermute(values, axis, [(i, i ^ distance) for i in range(count)])]
where the time goes in v5:
time: 129 us
  waiting for transfers between devices  38.5 us (30%)
  starting transfers between devices  29.6 us (23%)
  other arithmetic  27.7 us (21%)
  matrix products  17 us (13%)
  local copies, waits for them, and re-layouts  14.6 us (11%)
  between operations  1.6 us (1%)
    ppermute x6, waiting for transfers between devices, exchange(): return lax.ppermute(values, axis, [(i, i ^ distance) for i in range(count)])  25.7 us
    ppermute x6, starting transfers between devices, exchange(): return lax.ppermute(values, axis, [(i, i ^ distance) for i in range(count)])  16.3 us
    ppermute x4, starting transfers between devices, from_neighbours(): parts.append(lax.ppermute(piece, AXES, pairs))  12.6 us
    ppermute x4, waiting for transfers between devices, from_neighbours(): parts.append(lax.ppermute(piece, AXES, pairs))  10.4 us
    conv_general_dilated x8, matrix products, convolve(): lax.conv_general_dilated(padded, kernel, (1, 1), 'VALID', dimension_numbe...  9.95 us
    convert_element_type x4, other arithmetic, local_split(): current = current.astype(jnp.bfloat16)  9.08 us
    convert_element_type x4, other arithmetic, section_chain(): signal = signal.astype(jnp.bfloat16)  8.96 us
    transpose x4, matrix products, kernel_terms(): return jnp.transpose(terms, (1, 2, 0, 3))  7.09 us
  transfers between devices with their start and end apart: 14, of which 11 were waited for; matrix products, arithmetic and copies ran while one was open for 5% of the time, Pallas kernels for 0%

profile of v5, /device:TPU:0, one launch (start us, length us, event | category | flops | bytes accessed | tf_op | source)
XLA Modules:
  0.0 129.0 jit_solution(15701813404293687602)
XLA Ops:
  5.4 5.4 %collective-permute-start.1 = (bf16[6,6,32,128]{3,2,0,1:T(8,128)(2,1)S(1)}, bf16[6,6,32,128]{3,2,0,1:T(8,128)(2,1)S(1)}, u32[]{:S(2)}, u32[]{:S(2)}) collective-permute-start(bf16[6,6,32,128]{3,2,0,1:T(8,128)(2,1)S(1)} %get-tuple-element.18), channel_id=1, source_target_pairs={{0,4},{1,5},{2,6},{3,7},{4,8},{5,9},{6,10},{7,11},{8,12},{9,13},{1... | collective-permute-start | bytes 884744 | tf_op jit(solution)/shard_map/ppermute | solution.py:43
  10.9 5.8 %collective-permute-done.2 = bf16[6,6,32,128]{3,2,0,1:T(8,128)(2,1)S(1)} collective-permute-done((bf16[6,6,32,128]{3,2,0,1:T(8,128)(2,1)S(1)}, bf16[6,6,32,128]{3,2,0,1:T(8,128)(2,1)S(1)}, u32[]{:S(2)}, u32[]{:S(2)}) %collective-permute-start.2) | collective-permute-done | bytes 294944 | tf_op jit(solution)/shard_map/ppermute | solution.py:43
  18.8 4.6 %collective-permute-start.3 = (bf16[6,28,6,128]{3,2,0,1:T(8,128)(2,1)S(1)}, bf16[6,28,6,128]{3,2,0,1:T(8,128)(2,1)S(1)}, u32[]{:S(2)}, u32[]{:S(2)}) collective-permute-start(bf16[6,28,6,128]{3,2,0,1:T(8,128)(2,1)S(1)} %get-tuple-element.14), channel_id=1, source_target_pairs={{0,1},{1,2},{2,3},{4,5},{5,6},{6,7},{8,9},{9,10},{10,11},{12,13},{... | collective-permute-start | bytes 774152 | tf_op jit(solution)/shard_map/ppermute | solution.py:43
  25.7 2.8 %collective-permute-done.4 = bf16[6,28,6,128]{3,2,0,1:T(8,128)(2,1)S(1)} collective-permute-done((bf16[6,28,6,128]{3,2,0,1:T(8,128)(2,1)S(1)}, bf16[6,28,6,128]{3,2,0,1:T(8,128)(2,1)S(1)}, u32[]{:S(2)}, u32[]{:S(2)}) %collective-permute-start.4) | collective-permute-done | bytes 258080 | tf_op jit(solution)/shard_map/ppermute | solution.py:43
  29.7 1.6 %pad_maximum_fusion.2 = (bf16[2,28,44,128]{3,2,0,1:T(8,128)(2,1)}, bf16[2,28,44,128]{3,2,0,1:T(8,128)(2,1)S(1)}) fusion(bf16[6,28,6,128]{3,2,0,1:T(8,128)(2,1)S(1)} %collective-permute-done.4, bf16[6,28,6,128]{3,2,0,1:T(8,128)(2,1)S(1)} %collective-permute-done.3, bf16[6,6,32,128]{3,2,0,1:T(8,128)(2,1)S(1)} %collective-permute-done.2, ...), kind=kLoop, calls=%fused_computation.66 | loop fusion | flops 8830976 | bytes 3153920 | tf_op jit(solution)/shard_map/concatenate | solution.py:44
  33.8 1.7 %fusion.1 = bf16[26,16,6,128]{3,1,2,0:T(8,128)(2,1)S(1)} fusion(bf16[28,2,8,8,128]{4,1,3,2,0:T(2,128)(2,1)S(1)} %fusion.16, pred[16,6]{0,1:T(8,128)(4,1)S(1)} %copy-done.26, bf16[2,3,3,128,128]{4,3,2,1,0:T(8,128)(2,1)S(1)} %get-tuple-element.17), kind=kOutput, calls=%fused_computation.6 | convolution fusion | flops 736739328 | bytes 1852416 | tf_op jit(solution)/shard_map/conv_general_dilated | solution.py:63
  35.9 1.7 %fusion.11 = bf16[26,2,42,128]{3,1,2,0:T(2,128)(2,1)S(1)} fusion(bf16[26,2,42,128]{3,2,1,0:T(8,128)(2,1)S(1)} %bitcast.138, pred[26,42]{1,0:T(8,128)(4,1)S(1)} %broadcast_and_fusion), kind=kLoop, calls=%fused_computation.35 | loop fusion | flops 279552 | bytes 1119300 | tf_op jit(solution)/shard_map/convert_element_type | solution.py:278
  37.6 1.7 %fusion.96 = bf16[2,26,42,128]{3,0,2,1:T(2,128)(2,1)S(1)} fusion(bf16[26,2,42,128]{3,2,1,0:T(8,128)(2,1)S(1)} %bitcast.139, pred[26,42]{1,0:T(8,128)(4,1)S(1)} %broadcast_and_fusion), kind=kLoop, calls=%fused_computation.191 | loop fusion | flops 279552 | bytes 1119300 | tf_op jit(solution)/shard_map/convert_element_type | solution.py:278
  42.6 2.8 %fusion.19 = bf16[22,2,38,128]{3,1,2,0:T(2,128)(2,1)S(1)} fusion(bf16[22,2,38,128]{3,0,2,1:T(8,128)(2,1)S(1)} %slice.149, pred[22,38]{1,0:T(8,128)(4,1)S(1)} %broadcast_and_fusion.2), kind=kLoop, calls=%fused_computation.47 | loop fusion | flops 214016 | bytes 856900 | tf_op jit(solution)/shard_map/convert_element_type | solution.py:278
  45.4 2.8 %fusion.95 = bf16[2,22,38,128]{3,0,2,1:T(2,128)(2,1)S(1)} fusion(bf16[22,2,38,128]{3,0,2,1:T(8,128)(2,1)S(1)} %slice.149, pred[22,38]{1,0:T(8,128)(4,1)S(1)} %broadcast_and_fusion.2), kind=kLoop, calls=%fused_computation.190 | loop fusion | flops 214016 | bytes 856900 | tf_op jit(solution)/shard_map/convert_element_type | solution.py:278
  49.3 1.6 %fusion.2 = bf16[24,16,6,128]{3,1,2,0:T(8,128)(2,1)S(1)} fusion(bf16[26,2,7,2,128]{4,2,1,3,0:T(8,128)(2,1)S(1)} %slice.136, bf16[26,2,8,6,128]{4,2,1,3,0:T(8,128)(2,1)S(1)} %copy.147, pred[16,6]{0,1:T(8,128)(4,1)S(1)} %copy-done.25, bf16[2,3,3,128,128]{4,3,2,1,0:T(8,128)(2,1)S(1)} %copy-done.8), kind=kOutput, calls=%fused_computation.8 | convolution fusion | flops 682622976 | bytes 1737728 | tf_op jit(solution)/shard_map/conv_general_dilated | solution.py:63
  52.1 2.1 %fusion.15 = bf16[2,24,40,128]{3,2,0,1:T(8,128)(2,1)S(1)} fusion(bf16[24,2,40,128]{3,0,2,1:T(8,128)(2,1)S(1)} %slice.138, bf16[6,28,6,128]{3,2,0,1:T(8,128)(2,1)S(1)} %copy-done.11, bf16[6,28,6,128]{3,2,0,1:T(8,128)(2,1)S(1)} %copy-done.13, bf16[6,6,32,128]{3,2,0,1:T(8,128)(2,1)S(1)} %copy-done.2, bf16[6,6,32,128]{3,2,0,1:T(8,128)(2,1)S(1)} %copy-done.4, ...), kind=kLoop, calls=%fused_computation.42 | loop fusion | flops 5160960 | bytes 2876352 | tf_op jit(solution)/shard_map/convert_element_type | solution.py:232
  57.0 2.9 %fusion.22 = bf16[2,22,38,128]{3,0,2,1:T(2,128)(2,1)S(1)} fusion(f32[22,2,38,128]{3,0,2,1:T(8,128)S(1)} %slice.141, pred[22,38]{1,0:T(8,128)(4,1)S(1)} %broadcast_and_fusion.2, bf16[2,26,42,128]{3,0,2,1:T(2,128)(2,1)S(1)} %fusion.96), kind=kLoop, calls=%fused_computation.51 | loop fusion | flops 1284096 | bytes 1712964 | tf_op jit(solution)/shard_map/convert_element_type | solution.py:232
  59.9 1.7 %convolution_bitcast_fusion.2 = f32[1,3,3,128,128]{4,3,2,1,0:T(8,128)S(1)} fusion(bf16[2,28,44,128]{3,2,0,1:T(8,128)(2,1)S(1)} %get-tuple-element.13, bf16[2,22,38,128]{3,0,2,1:T(2,128)(2,1)S(1)} %fusion.22), kind=kOutput, calls=%fused_computation.25 | convolution fusion | flops 301989888 | bytes 1540096 | tf_op jit(solution)/shard_map/transpose | solution.py:82
  65.4 2.0 %fusion.34 = bf16[20,2,36,128]{3,1,2,0:T(2,128)(2,1)S(1)} fusion(f32[20,2,36,128]{3,0,2,1:T(8,128)S(1)} %slice.145, pred[20,36]{1,0:T(8,128)(4,1)S(1)} %broadcast_and_fusion.3, bf16[20,2,36,128]{3,0,2,1:T(8,128)(2,1)S(1)} %slice.152), kind=kLoop, calls=%fused_computation.64 | loop fusion | flops 1290240 | bytes 1475280 | tf_op jit(solution)/shard_map/convert_element_type | solution.py:232
  69.8 1.8 %convolution_bitcast_fusion = f32[1,3,3,128,128]{4,3,2,1,0:T(8,128)S(1)} fusion(bf16[26,2,42,128]{3,1,2,0:T(2,128)(2,1)S(1)} %fusion.11, bf16[2,16,32,128]{3,2,0,1:T(8,128)(2,1)S(1)} %slice.165), kind=kOutput, calls=%fused_computation.23 | convolution fusion | flops 301989888 | bytes 1411072 | tf_op jit(solution)/shard_map/transpose | solution.py:82
  71.6 1.8 %convolution_bitcast_fusion.1 = f32[1,3,3,128,128]{4,3,2,1,0:T(8,128)S(1)} fusion(bf16[22,2,38,128]{3,1,2,0:T(2,128)(2,1)S(1)} %fusion.19, bf16[2,20,36,128]{3,0,2,1:T(2,128)(2,1)S(1)} %bitcast.161), kind=kOutput, calls=%fused_computation.24 | convolution fusion | flops 301989888 | bytes 1280000 | tf_op jit(solution)/shard_map/transpose | solution.py:82
  73.4 2.0 %fusion.54 = bf16[2,18,34,128]{3,0,2,1:T(2,128)(2,1)S(1)} fusion(f32[18,2,34,128]{3,0,2,1:T(8,128)S(1)} %slice.155, pred[18,34]{1,0:T(8,128)(4,1)S(1)} %broadcast_and_fusion.4, bf16[2,22,38,128]{3,0,2,1:T(2,128)(2,1)S(1)} %fusion.95), kind=kLoop, calls=%fused_computation.90 | loop fusion | flops 940032 | bytes 1253988 | tf_op jit(solution)/shard_map/convert_element_type | solution.py:232
  76.2 1.8 %convolution_bitcast_fusion.3 = f32[1,3,3,128,128]{4,3,2,1,0:T(8,128)S(1)} fusion(bf16[2,28,44,128]{3,2,0,1:T(8,128)(2,1)S(1)} %copy-done.9, bf16[2,18,34,128]{3,0,2,1:T(2,128)(2,1)S(1)} %fusion.54), kind=kOutput, calls=%fused_computation.26 | convolution fusion | flops 301989888 | bytes 1540096 | tf_op jit(solution)/shard_map/transpose | solution.py:82
  78.9 2.3 %collective-permute-done.7 = bf16[2,3,3,128,128]{4,3,2,1,0:T(8,128)(2,1)} collective-permute-done((bf16[2,3,3,128,128]{4,3,2,1,0:T(8,128)(2,1)}, bf16[2,3,3,128,128]{4,3,2,1,0:T(8,128)(2,1)}, u32[]{:S(2)}, u32[]{:S(2)}) %collective-permute-start.7) | collective-permute-done | bytes 589856 | tf_op jit(solution)/shard_map/ppermute | solution.py:249
  81.3 1.3 %convert_add_fusion = bf16[2,3,3,128,128]{4,3,2,1,0:T(8,128)(2,1)S(1)} fusion(bf16[2,3,3,128,128]{4,3,2,1,0:T(8,128)(2,1)} %collective-permute-done.7, f32[1,3,3,128,128]{4,3,2,1,0:T(8,128)S(1)} %convolution_bitcast_fusion, f32[1,3,3,128,128]{4,3,2,1,0:T(8,128)S(1)} %convolution_bitcast_fusion.2, f32[1,3,3,128,128]{4,3,2,1,0:T(8,128)S(1)} %convolution_bitcast_fusion.1, ...), kind=kLoop, calls=%fused_computation.30 | loop fusion | flops 2064384 | bytes 3538945 | tf_op jit(solution)/shard_map/add | solution.py:294
  82.6 5.0 %collective-permute-start.8 = (bf16[147456]{0:T(1024)(128)(2,1)S(1)}, bf16[147456]{0:T(1024)(128)(2,1)S(1)}, u32[]{:S(2)}, u32[]{:S(2)}) collective-permute-start(bf16[147456]{0:T(1024)(128)(2,1)S(1)} %bitcast.168), channel_id=1, source_target_pairs={{0,4},{4,0},{8,12},{12,8},{1,5},{5,1},{9,13},{13,9},{2,6},{6,2},{1... | collective-permute-start | bytes 884744 | tf_op jit(solution)/shard_map/ppermute | solution.py:100
  87.7 7.3 %collective-permute-done.8 = bf16[147456]{0:T(1024)(128)(2,1)S(1)} collective-permute-done((bf16[147456]{0:T(1024)(128)(2,1)S(1)}, bf16[147456]{0:T(1024)(128)(2,1)S(1)}, u32[]{:S(2)}, u32[]{:S(2)}) %collective-permute-start.8) | collective-permute-done | bytes 294944 | tf_op jit(solution)/shard_map/ppermute | solution.py:100
  95.1 2.5 %collective-permute-start.9 = (bf16[73728]{0:T(1024)(128)(2,1)S(1)}, bf16[73728]{0:T(1024)(128)(2,1)S(1)}, u32[]{:S(2)}, u32[]{:S(2)}) collective-permute-start(bf16[73728]{0:T(1024)(128)(2,1)S(1)} %select_convert_fusion.2), channel_id=1, source_target_pairs={{0,1},{1,0},{2,3},{3,2},{4,5},{5,4},{6,7},{7,6},{8,9},{9,8},{10,11... | collective-permute-start | bytes 442376 | tf_op jit(solution)/shard_map/ppermute | solution.py:100
  97.6 3.6 %collective-permute-done.9 = bf16[73728]{0:T(1024)(128)(2,1)S(1)} collective-permute-done((bf16[73728]{0:T(1024)(128)(2,1)S(1)}, bf16[73728]{0:T(1024)(128)(2,1)S(1)}, u32[]{:S(2)}, u32[]{:S(2)}) %collective-permute-start.9) | collective-permute-done | bytes 147488 | tf_op jit(solution)/shard_map/ppermute | solution.py:100
  101.2 3.4 %collective-permute-start.10 = (bf16[73728]{0:T(1024)(128)(2,1)S(1)}, bf16[73728]{0:T(1024)(128)(2,1)S(1)}, u32[]{:S(2)}, u32[]{:S(2)}) collective-permute-start(bf16[73728]{0:T(1024)(128)(2,1)S(1)} %add_convert_fusion.2), channel_id=1, source_target_pairs={{0,8},{4,12},{8,0},{12,4},{1,9},{5,13},{9,1},{13,5},{2,10},{6,14},... | collective-permute-start | bytes 442376 | tf_op jit(solution)/shard_map/ppermute | solution.py:100
  105.2 2.6 %collective-permute-done.10 = bf16[73728]{0:T(1024)(128)(2,1)S(1)} collective-permute-done((bf16[73728]{0:T(1024)(128)(2,1)S(1)}, bf16[73728]{0:T(1024)(128)(2,1)S(1)}, u32[]{:S(2)}, u32[]{:S(2)}) %collective-permute-start.10) | collective-permute-done | bytes 147488 | tf_op jit(solution)/shard_map/ppermute | solution.py:100
  107.9 2.9 %collective-permute-start.11 = (bf16[73728]{0:T(1024)(128)(2,1)S(1)}, bf16[73728]{0:T(1024)(128)(2,1)S(1)}, u32[]{:S(2)}, u32[]{:S(2)}) collective-permute-start(bf16[73728]{0:T(1024)(128)(2,1)S(1)} %add_convert_fusion.1), channel_id=1, source_target_pairs={{0,2},{1,3},{2,0},{3,1},{4,6},{5,7},{6,4},{7,5},{8,10},{9,11},{10,... | collective-permute-start | bytes 442376 | tf_op jit(solution)/shard_map/ppermute | solution.py:100
  112.0 3.7 %collective-permute-done.11 = bf16[73728]{0:T(1024)(128)(2,1)S(1)} collective-permute-done((bf16[73728]{0:T(1024)(128)(2,1)S(1)}, bf16[73728]{0:T(1024)(128)(2,1)S(1)}, u32[]{:S(2)}, u32[]{:S(2)}) %collective-permute-start.11) | collective-permute-done | bytes 147488 | tf_op jit(solution)/shard_map/ppermute | solution.py:100
  116.8 4.2 %collective-permute-done.12 = bf16[73728]{0:T(1024)(128)(2,1)S(1)} collective-permute-done((bf16[73728]{0:T(1024)(128)(2,1)S(1)}, bf16[73728]{0:T(1024)(128)(2,1)S(1)}, u32[]{:S(2)}, u32[]{:S(2)}) %collective-permute-start.12) | collective-permute-done | bytes 147488 | tf_op jit(solution)/shard_map/ppermute | solution.py:100
  121.0 1.5 %collective-permute-start.13 = (bf16[147456]{0:T(1024)(128)(2,1)S(1)}, bf16[147456]{0:T(1024)(128)(2,1)S(1)}, u32[]{:S(2)}, u32[]{:S(2)}) collective-permute-start(bf16[147456]{0:T(1024)(128)(2,1)S(1)} %maximum_select_fusion.2), channel_id=1, source_target_pairs={{0,4},{4,0},{8,12},{12,8},{1,5},{5,1},{9,13},{13,9},{2,6},{6,2},{1... | collective-permute-start | bytes 884744 | tf_op jit(solution)/shard_map/ppermute | solution.py:100
  123.5 4.4 %collective-permute-done.13 = bf16[147456]{0:T(1024)(128)(2,1)S(1)} collective-permute-done((bf16[147456]{0:T(1024)(128)(2,1)S(1)}, bf16[147456]{0:T(1024)(128)(2,1)S(1)}, u32[]{:S(2)}, u32[]{:S(2)}) %collective-permute-start.13) | collective-permute-done | bytes 294944 | tf_op jit(solution)/shard_map/ppermute | solution.py:100
  (159 shorter events, 33.9 us)
Async XLA Ops:
  0.6 2.5 %copy-start = (bf16[4,16,32,128]{3,2,1,0:T(8,128)(2,1)S(1)}, bf16[4,16,32,128]{3,2,1,0:T(8,128)(2,1)}, u32[]{:S(2)}) copy-start(bf16[4,16,32,128]{3,2,1,0:T(8,128)(2,1)} %param.6) | copy-start | bytes 1572868
  0.6 1.8 %copy-start.16 = (bf16[2,3,3,128,128]{4,3,2,1,0:T(8,128)(2,1)S(1)}, bf16[2,3,3,128,128]{4,3,2,1,0:T(8,128)(2,1)}, u32[]{:S(2)}) copy-start(bf16[2,3,3,128,128]{4,3,2,1,0:T(8,128)(2,1)} %param.5) | copy-start | bytes 1769476
  0.7 1.9 %copy-start.20 = (s32[4]{0:T(128)S(1)}, s32[4]{0:T(128)}, u32[]{:S(2)}) copy-start(s32[4]{0:T(128)} %param.7) | copy-start | bytes 52
  1.9 2.1 %collective-permute-start = (bf16[2,16,32,128]{3,2,0,1:T(8,128)(2,1)S(1)}, bf16[2,16,32,128]{3,2,0,1:T(8,128)(2,1)S(1)}, u32[]{:S(2)}, u32[]{:S(2)}) collective-permute-start(bf16[2,16,32,128]{3,2,0,1:T(8,128)(2,1)S(1)} %bitcast.170), channel_id=1, source_target_pairs={{0,16},{16,0},{1,17},{17,1},{2,18},{18,2},{3,19},{19,3},{4,20},{20... | collective-permute-start | bytes 786440 | tf_op jit(solution)/shard_map/ppermute | solution.py:249
  2.4 20.9 %collective-permute-start.5 = (bf16[2,3,3,128,128]{4,3,2,1,0:T(8,128)(2,1)S(1)}, bf16[2,3,3,128,128]{4,3,2,1,0:T(8,128)(2,1)}, u32[]{:S(2)}, u32[]{:S(2)}) collective-permute-start(bf16[2,3,3,128,128]{4,3,2,1,0:T(8,128)(2,1)S(1)} %copy-done.16), channel_id=1, source_target_pairs={{0,16},{16,0},{1,17},{17,1},{2,18},{18,2},{3,19},{19,3},{4,20},{20... | collective-permute-start | bytes 1769480 | tf_op jit(solution)/shard_map/ppermute | solution.py:249
  4.1 12.7 %collective-permute-start.2 = (bf16[6,6,32,128]{3,2,0,1:T(8,128)(2,1)S(1)}, bf16[6,6,32,128]{3,2,0,1:T(8,128)(2,1)S(1)}, u32[]{:S(2)}, u32[]{:S(2)}) collective-permute-start(bf16[6,6,32,128]{3,2,0,1:T(8,128)(2,1)S(1)} %get-tuple-element.19), channel_id=1, source_target_pairs={{4,0},{5,1},{6,2},{7,3},{8,4},{9,5},{10,6},{11,7},{12,8},{13,9},{1... | collective-permute-start | bytes 884744 | tf_op jit(solution)/shard_map/ppermute | solution.py:43
  5.4 11.9 %collective-permute-start.1 = (bf16[6,6,32,128]{3,2,0,1:T(8,128)(2,1)S(1)}, bf16[6,6,32,128]{3,2,0,1:T(8,128)(2,1)S(1)}, u32[]{:S(2)}, u32[]{:S(2)}) collective-permute-start(bf16[6,6,32,128]{3,2,0,1:T(8,128)(2,1)S(1)} %get-tuple-element.18), channel_id=1, source_target_pairs={{0,4},{1,5},{2,6},{3,7},{4,8},{5,9},{6,10},{7,11},{8,12},{9,13},{1... | collective-permute-start | bytes 884744 | tf_op jit(solution)/shard_map/ppermute | solution.py:43
  16.7 13.0 %copy-start.1 = (bf16[6,6,32,128]{3,2,0,1:T(8,128)(2,1)}, bf16[6,6,32,128]{3,2,0,1:T(8,128)(2,1)S(1)}, u32[]{:S(2)}) copy-start(bf16[6,6,32,128]{3,2,0,1:T(8,128)(2,1)S(1)} %collective-permute-done.2) | copy-start | bytes 884740
  17.3 12.4 %copy-start.3 = (bf16[6,6,32,128]{3,2,0,1:T(8,128)(2,1)}, bf16[6,6,32,128]{3,2,0,1:T(8,128)(2,1)S(1)}, u32[]{:S(2)}) copy-start(bf16[6,6,32,128]{3,2,0,1:T(8,128)(2,1)S(1)} %collective-permute-done.1) | copy-start | bytes 884740
  17.5 11.1 %collective-permute-start.4 = (bf16[6,28,6,128]{3,2,0,1:T(8,128)(2,1)S(1)}, bf16[6,28,6,128]{3,2,0,1:T(8,128)(2,1)S(1)}, u32[]{:S(2)}, u32[]{:S(2)}) collective-permute-start(bf16[6,28,6,128]{3,2,0,1:T(8,128)(2,1)S(1)} %get-tuple-element.15), channel_id=1, source_target_pairs={{1,0},{2,1},{3,2},{5,4},{6,5},{7,6},{9,8},{10,9},{11,10},{13,12},{... | collective-permute-start | bytes 774152 | tf_op jit(solution)/shard_map/ppermute | solution.py:43
  18.8 11.0 %collective-permute-start.3 = (bf16[6,28,6,128]{3,2,0,1:T(8,128)(2,1)S(1)}, bf16[6,28,6,128]{3,2,0,1:T(8,128)(2,1)S(1)}, u32[]{:S(2)}, u32[]{:S(2)}) collective-permute-start(bf16[6,28,6,128]{3,2,0,1:T(8,128)(2,1)S(1)} %get-tuple-element.14), channel_id=1, source_target_pairs={{0,1},{1,2},{2,3},{4,5},{5,6},{6,7},{8,9},{9,10},{10,11},{12,13},{... | collective-permute-start | bytes 774152 | tf_op jit(solution)/shard_map/ppermute | solution.py:43
  24.5 1.2 copy-start.5
  24.5 9.2 %copy-start.7 = (bf16[2,3,3,128,128]{4,3,2,1,0:T(8,128)(2,1)}, bf16[2,3,3,128,128]{4,3,2,1,0:T(8,128)(2,1)S(1)}, u32[]{:S(2)}) copy-start(bf16[2,3,3,128,128]{4,3,2,1,0:T(8,128)(2,1)S(1)} %get-tuple-element.17) | copy-start | bytes 1769476
  28.6 2.8 %copy-start.10 = (bf16[6,28,6,128]{3,2,0,1:T(8,128)(2,1)}, bf16[6,28,6,128]{3,2,0,1:T(8,128)(2,1)S(1)}, u32[]{:S(2)}) copy-start(bf16[6,28,6,128]{3,2,0,1:T(8,128)(2,1)S(1)} %collective-permute-done.4) | copy-start | bytes 774148
  29.7 1.7 %copy-start.12 = (bf16[6,28,6,128]{3,2,0,1:T(8,128)(2,1)}, bf16[6,28,6,128]{3,2,0,1:T(8,128)(2,1)S(1)}, u32[]{:S(2)}) copy-start(bf16[6,28,6,128]{3,2,0,1:T(8,128)(2,1)S(1)} %collective-permute-done.3) | copy-start | bytes 774148
  32.4 1.4 %copy-start.26 = (pred[16,6]{0,1:T(8,128)(4,1)S(1)}, pred[16,6]{0,1:T(8,128)(4,1)}, u32[]{:S(2)}) copy-start(pred[16,6]{0,1:T(8,128)(4,1)} %constant.180) | copy-start | bytes 292
  35.9 3.5 %copy-start.9 = (bf16[2,28,44,128]{3,2,0,1:T(8,128)(2,1)S(1)}, bf16[2,28,44,128]{3,2,0,1:T(8,128)(2,1)}, u32[]{:S(2)}) copy-start(bf16[2,28,44,128]{3,2,0,1:T(8,128)(2,1)} %get-tuple-element.12) | copy-start | bytes 1892356
  40.0 1.1 copy-start.6
  50.9 1.1 copy-start.11
  50.9 1.2 copy-start.13
  67.4 1.1 copy-start.17
  78.9 2.3 %collective-permute-start.7 = (bf16[2,3,3,128,128]{4,3,2,1,0:T(8,128)(2,1)}, bf16[2,3,3,128,128]{4,3,2,1,0:T(8,128)(2,1)}, u32[]{:S(2)}, u32[]{:S(2)}) collective-permute-start(bf16[2,3,3,128,128]{4,3,2,1,0:T(8,128)(2,1)} %multiply_convert_fusion), channel_id=1, source_target_pairs={{0,16},{16,0},{1,17},{17,1},{2,18},{18,2},{3,19},{19,3},{4,20},{20... | collective-permute-start | bytes 1769480 | tf_op jit(solution)/shard_map/ppermute | solution.py:249
  82.6 12.3 %collective-permute-start.8 = (bf16[147456]{0:T(1024)(128)(2,1)S(1)}, bf16[147456]{0:T(1024)(128)(2,1)S(1)}, u32[]{:S(2)}, u32[]{:S(2)}) collective-permute-start(bf16[147456]{0:T(1024)(128)(2,1)S(1)} %bitcast.168), channel_id=1, source_target_pairs={{0,4},{4,0},{8,12},{12,8},{1,5},{5,1},{9,13},{13,9},{2,6},{6,2},{1... | collective-permute-start | bytes 884744 | tf_op jit(solution)/shard_map/ppermute | solution.py:100
  95.0 9.8 %copy-start.15 = (bf16[2,18,34,128]{3,0,2,1:T(2,128)(2,1)S(1)}, bf16[2,18,34,128]{3,0,2,1:T(2,128)(2,1)}, u32[]{:S(2)}) copy-start(bf16[2,18,34,128]{3,0,2,1:T(2,128)(2,1)} %copy-done.14) | copy-start | bytes 940036
  95.1 6.1 %collective-permute-start.9 = (bf16[73728]{0:T(1024)(128)(2,1)S(1)}, bf16[73728]{0:T(1024)(128)(2,1)S(1)}, u32[]{:S(2)}, u32[]{:S(2)}) collective-permute-start(bf16[73728]{0:T(1024)(128)(2,1)S(1)} %select_convert_fusion.2), channel_id=1, source_target_pairs={{0,1},{1,0},{2,3},{3,2},{4,5},{5,4},{6,7},{7,6},{8,9},{9,8},{10,11... | collective-permute-start | bytes 442376 | tf_op jit(solution)/shard_map/ppermute | solution.py:100
  101.2 6.6 %collective-permute-start.10 = (bf16[73728]{0:T(1024)(128)(2,1)S(1)}, bf16[73728]{0:T(1024)(128)(2,1)S(1)}, u32[]{:S(2)}, u32[]{:S(2)}) collective-permute-start(bf16[73728]{0:T(1024)(128)(2,1)S(1)} %add_convert_fusion.2), channel_id=1, source_target_pairs={{0,8},{4,12},{8,0},{12,4},{1,9},{5,13},{9,1},{13,5},{2,10},{6,14},... | collective-permute-start | bytes 442376 | tf_op jit(solution)/shard_map/ppermute | solution.py:100
  104.8 6.0 %copy-start.18 = (bf16[2,3,3,128,128]{3,4,2,1,0:T(8,128)(2,1)S(1)}, bf16[2,3,3,128,128]{3,4,2,1,0:T(8,128)(2,1)}, u32[]{:S(2)}) copy-start(bf16[2,3,3,128,128]{3,4,2,1,0:T(8,128)(2,1)} %get-tuple-element.28) | copy-start | bytes 1769476
  104.8 6.0 %copy-start.21 = (pred[16,5]{0,1:T(8,128)(4,1)S(1)}, pred[16,5]{0,1:T(8,128)(4,1)}, u32[]{:S(2)}) copy-start(pred[16,5]{0,1:T(8,128)(4,1)} %constant.175) | copy-start | bytes 244
  107.9 7.8 %collective-permute-start.11 = (bf16[73728]{0:T(1024)(128)(2,1)S(1)}, bf16[73728]{0:T(1024)(128)(2,1)S(1)}, u32[]{:S(2)}, u32[]{:S(2)}) collective-permute-start(bf16[73728]{0:T(1024)(128)(2,1)S(1)} %add_convert_fusion.1), channel_id=1, source_target_pairs={{0,2},{1,3},{2,0},{3,1},{4,6},{5,7},{6,4},{7,5},{8,10},{9,11},{10,... | collective-permute-start | bytes 442376 | tf_op jit(solution)/shard_map/ppermute | solution.py:100
  115.8 5.2 %collective-permute-start.12 = (bf16[73728]{0:T(1024)(128)(2,1)S(1)}, bf16[73728]{0:T(1024)(128)(2,1)S(1)}, u32[]{:S(2)}, u32[]{:S(2)}) collective-permute-start(bf16[73728]{0:T(1024)(128)(2,1)S(1)} %add_convert_fusion), channel_id=1, source_target_pairs={{0,1},{1,0},{2,3},{3,2},{4,5},{5,4},{6,7},{7,6},{8,9},{9,8},{10,11... | collective-permute-start | bytes 442376 | tf_op jit(solution)/shard_map/ppermute | solution.py:100
  116.7 5.8 %collective-permute-start.6 = (bf16[2,16,32,128]{3,2,0,1:T(8,128)(2,1)S(1)}, bf16[2,16,32,128]{3,2,0,1:T(8,128)(2,1)S(1)}, u32[]{:S(2)}, u32[]{:S(2)}) collective-permute-start(bf16[2,16,32,128]{3,2,0,1:T(8,128)(2,1)S(1)} %get-tuple-element.21), channel_id=1, source_target_pairs={{0,16},{16,0},{1,17},{17,1},{2,18},{18,2},{3,19},{19,3},{4,20},{20... | collective-permute-start | bytes 786440 | tf_op jit(solution)/shard_map/ppermute | solution.py:249
  121.0 6.8 %collective-permute-start.13 = (bf16[147456]{0:T(1024)(128)(2,1)S(1)}, bf16[147456]{0:T(1024)(128)(2,1)S(1)}, u32[]{:S(2)}, u32[]{:S(2)}) collective-permute-start(bf16[147456]{0:T(1024)(128)(2,1)S(1)} %maximum_select_fusion.2), channel_id=1, source_target_pairs={{0,4},{4,0},{8,12},{12,8},{1,5},{5,1},{9,13},{13,9},{2,6},{6,2},{1... | collective-permute-start | bytes 884744 | tf_op jit(solution)/shard_map/ppermute | solution.py:100
  (9 other events, 8.7 us)

commit v6 on v5

--- a/solution.py
+++ b/solution.py
@@ -280,18 +280,19 @@
         flipped = jnp.transpose(section_kernels[s][:, ::-1, ::-1], (0, 1, 2, 4, 3))
         top_ext, signals = section_chain(top_ext, top_rim[s], inputs_list, rim, flipped)
         results[s] = crop(top_ext, top_rim[s] - layer_count)
-        partials[s] = jnp.stack(
-            [
-                kernel_terms(crop(inputs_list[layer_idx], rim - layer_idx - 1), signals[layer_idx])
-                for layer_idx in range(layer_count)
-            ]
-        )
-
-    mine_terms = by_section(partials[0], partials[1], 0)
-    other_terms = by_section(partials[1], partials[0], 0)
+        partials[s] = [
+            kernel_terms(crop(inputs_list[layer_idx], rim - layer_idx - 1), signals[layer_idx])
+            for layer_idx in range(layer_count)
+        ]
+
     scale = 1.0 / batches
-    other_terms = swap((other_terms * scale).astype(jnp.bfloat16)).astype(jnp.float32)
-    gathered = summed_over_tiles(mine_terms * scale + other_terms)
+    summed = []
+    for layer_idx in reversed(range(layer_count)):
+        mine_terms = by_section(partials[0][layer_idx], partials[1][layer_idx], 0)
+        other_terms = by_section(partials[1][layer_idx], partials[0][layer_idx], 0)
+        other_terms = swap((other_terms * scale).astype(jnp.bfloat16)).astype(jnp.float32)
+        summed.insert(0, summed_over_tiles(mine_terms * scale + other_terms))
+    gathered = jnp.stack(summed)
     mine_back = by_section(results[0], results[1], 0)
     other_back = swap(by_section(results[1], results[0], 0))
     boundary = jnp.where(

time: 129 us -> 123 us (0.953)
  waiting for transfers between devices: 38.5 us -> 24.1 us
  starting transfers between devices: 29.6 us -> 40 us
  other arithmetic: 27.7 us -> 25.8 us
    ppermute x6 -> x12, waiting for transfers between devices: 25.7 us -> 13.7 us  [exchange(): return lax.ppermute(values, axis, [(i, i ^ distance) for i in range(count)])]
    ppermute x6 -> x12, starting transfers between devices: 16.3 us -> 26.1 us  [exchange(): return lax.ppermute(values, axis, [(i, i ^ distance) for i in range(count)])]
    ppermute x4 -> x5, waiting for transfers between devices: 2.35 us -> 0.01 us  [swap(): return lax.ppermute(values, 'section', [(0, 1), (1, 0)])]
    convert_element_type x2 -> x0, other arithmetic: 2.11 us -> none  [the longest x1 1.12 us: summed_over_tiles(): return current.astype(jnp.float32).reshape(grads.shape)]
    unnamed x57 -> x51, local copies, waits for them, and re-layouts: 5.4 us -> 4.94 us
  transfers between devices with their start and end apart: 14 -> 21, of which waited for: 11 -> 12; matrix products, arithmetic and copies ran while one was open for 5% -> 9% of each run, Pallas kernels for 0% -> 0%
where the time goes in v6:
time: 123 us
  starting transfers between devices  40 us (33%)
  other arithmetic  25.8 us (21%)
  waiting for transfers between devices  24.1 us (20%)
  matrix products  17.1 us (14%)
  local copies, waits for them, and re-layouts  14.1 us (11%)
  between operations  1.7 us (1%)
    ppermute x12, starting transfers between devices, exchange(): return lax.ppermute(values, axis, [(i, i ^ distance) for i in range(count)])  26.1 us
    ppermute x12, waiting for transfers between devices, exchange(): return lax.ppermute(values, axis, [(i, i ^ distance) for i in range(count)])  13.7 us
    ppermute x4, starting transfers between devices, from_neighbours(): parts.append(lax.ppermute(piece, AXES, pairs))  12.6 us
    ppermute x4, waiting for transfers between devices, from_neighbours(): parts.append(lax.ppermute(piece, AXES, pairs))  10.4 us
    conv_general_dilated x8, matrix products, convolve(): lax.conv_general_dilated(padded, kernel, (1, 1), 'VALID', dimension_numbe...  9.95 us
    convert_element_type x4, other arithmetic, local_split(): current = current.astype(jnp.bfloat16)  9.08 us
    convert_element_type x4, other arithmetic, section_chain(): signal = signal.astype(jnp.bfloat16)  8.96 us
    transpose x4, matrix products, kernel_terms(): return jnp.transpose(terms, (1, 2, 0, 3))  7.12 us
  transfers between devices with their start and end apart: 21, of which 12 were waited for; matrix products, arithmetic and copies ran while one was open for 9% of the time, Pallas kernels for 0%

profile of v6, /device:TPU:0, one launch (start us, length us, event | category | flops | bytes accessed | tf_op | source)
XLA Modules:
  0.0 122.8 jit_solution(3343659442049824205)
XLA Ops:
  5.4 5.4 %collective-permute-start.1 = (bf16[6,6,32,128]{3,2,0,1:T(8,128)(2,1)S(1)}, bf16[6,6,32,128]{3,2,0,1:T(8,128)(2,1)S(1)}, u32[]{:S(2)}, u32[]{:S(2)}) collective-permute-start(bf16[6,6,32,128]{3,2,0,1:T(8,128)(2,1)S(1)} %get-tuple-element.18), channel_id=1, source_target_pairs={{0,4},{1,5},{2,6},{3,7},{4,8},{5,9},{6,10},{7,11},{8,12},{9,13},{1... | collective-permute-start | bytes 884744 | tf_op jit(solution)/shard_map/ppermute | solution.py:43
  11.0 5.8 %collective-permute-done.2 = bf16[6,6,32,128]{3,2,0,1:T(8,128)(2,1)S(1)} collective-permute-done((bf16[6,6,32,128]{3,2,0,1:T(8,128)(2,1)S(1)}, bf16[6,6,32,128]{3,2,0,1:T(8,128)(2,1)S(1)}, u32[]{:S(2)}, u32[]{:S(2)}) %collective-permute-start.2) | collective-permute-done | bytes 294944 | tf_op jit(solution)/shard_map/ppermute | solution.py:43
  18.8 4.6 %collective-permute-start.3 = (bf16[6,28,6,128]{3,2,0,1:T(8,128)(2,1)S(1)}, bf16[6,28,6,128]{3,2,0,1:T(8,128)(2,1)S(1)}, u32[]{:S(2)}, u32[]{:S(2)}) collective-permute-start(bf16[6,28,6,128]{3,2,0,1:T(8,128)(2,1)S(1)} %get-tuple-element.14), channel_id=1, source_target_pairs={{0,1},{1,2},{2,3},{4,5},{5,6},{6,7},{8,9},{9,10},{10,11},{12,13},{... | collective-permute-start | bytes 774152 | tf_op jit(solution)/shard_map/ppermute | solution.py:43
  25.8 2.8 %collective-permute-done.4 = bf16[6,28,6,128]{3,2,0,1:T(8,128)(2,1)S(1)} collective-permute-done((bf16[6,28,6,128]{3,2,0,1:T(8,128)(2,1)S(1)}, bf16[6,28,6,128]{3,2,0,1:T(8,128)(2,1)S(1)}, u32[]{:S(2)}, u32[]{:S(2)}) %collective-permute-start.4) | collective-permute-done | bytes 258080 | tf_op jit(solution)/shard_map/ppermute | solution.py:43
  29.8 1.6 %pad_maximum_fusion = (bf16[2,28,44,128]{3,2,0,1:T(8,128)(2,1)}, bf16[2,28,44,128]{3,2,0,1:T(8,128)(2,1)S(1)}) fusion(bf16[6,28,6,128]{3,2,0,1:T(8,128)(2,1)S(1)} %collective-permute-done.4, bf16[6,28,6,128]{3,2,0,1:T(8,128)(2,1)S(1)} %collective-permute-done.3, bf16[6,6,32,128]{3,2,0,1:T(8,128)(2,1)S(1)} %collective-permute-done.2, ...), kind=kLoop, calls=%fused_computation.58 | loop fusion | flops 8830976 | bytes 3153920 | tf_op jit(solution)/shard_map/concatenate | solution.py:44
  33.8 1.7 %fusion.1 = bf16[26,16,6,128]{3,1,2,0:T(8,128)(2,1)S(1)} fusion(bf16[28,2,8,8,128]{4,1,3,2,0:T(2,128)(2,1)S(1)} %fusion.16, pred[16,6]{0,1:T(8,128)(4,1)S(1)} %copy-done.23, bf16[2,3,3,128,128]{4,3,2,1,0:T(8,128)(2,1)S(1)} %get-tuple-element.17), kind=kOutput, calls=%fused_computation.6 | convolution fusion | flops 736739328 | bytes 1852416 | tf_op jit(solution)/shard_map/conv_general_dilated | solution.py:63
  36.0 1.7 %fusion.11 = bf16[26,2,42,128]{3,1,2,0:T(2,128)(2,1)S(1)} fusion(bf16[26,2,42,128]{3,2,1,0:T(8,128)(2,1)S(1)} %bitcast.129, pred[26,42]{1,0:T(8,128)(4,1)S(1)} %broadcast_and_fusion), kind=kLoop, calls=%fused_computation.27 | loop fusion | flops 279552 | bytes 1119300 | tf_op jit(solution)/shard_map/convert_element_type | solution.py:278
  37.7 1.7 %fusion.99 = bf16[2,26,42,128]{3,0,2,1:T(2,128)(2,1)S(1)} fusion(bf16[26,2,42,128]{3,2,1,0:T(8,128)(2,1)S(1)} %bitcast.130, pred[26,42]{1,0:T(8,128)(4,1)S(1)} %broadcast_and_fusion), kind=kLoop, calls=%fused_computation.201 | loop fusion | flops 279552 | bytes 1119300 | tf_op jit(solution)/shard_map/convert_element_type | solution.py:278
  42.6 2.8 %fusion.19 = bf16[22,2,38,128]{3,1,2,0:T(2,128)(2,1)S(1)} fusion(bf16[22,2,38,128]{3,0,2,1:T(8,128)(2,1)S(1)} %slice.163, pred[22,38]{1,0:T(8,128)(4,1)S(1)} %broadcast_and_fusion.2), kind=kLoop, calls=%fused_computation.39 | loop fusion | flops 214016 | bytes 856900 | tf_op jit(solution)/shard_map/convert_element_type | solution.py:278
  45.4 2.8 %fusion.98 = bf16[2,22,38,128]{3,0,2,1:T(2,128)(2,1)S(1)} fusion(bf16[22,2,38,128]{3,0,2,1:T(8,128)(2,1)S(1)} %slice.163, pred[22,38]{1,0:T(8,128)(4,1)S(1)} %broadcast_and_fusion.2), kind=kLoop, calls=%fused_computation.200 | loop fusion | flops 214016 | bytes 856900 | tf_op jit(solution)/shard_map/convert_element_type | solution.py:278
  49.3 1.6 %fusion.2 = bf16[24,16,6,128]{3,1,2,0:T(8,128)(2,1)S(1)} fusion(bf16[26,2,7,2,128]{4,2,1,3,0:T(8,128)(2,1)S(1)} %slice.150, bf16[26,2,8,6,128]{4,2,1,3,0:T(8,128)(2,1)S(1)} %copy.147, pred[16,6]{0,1:T(8,128)(4,1)S(1)} %copy-done.22, bf16[2,3,3,128,128]{4,3,2,1,0:T(8,128)(2,1)S(1)} %copy-done.8), kind=kOutput, calls=%fused_computation.8 | convolution fusion | flops 682622976 | bytes 1737728 | tf_op jit(solution)/shard_map/conv_general_dilated | solution.py:63
  52.2 2.1 %fusion.15 = bf16[2,24,40,128]{3,2,0,1:T(8,128)(2,1)S(1)} fusion(bf16[24,2,40,128]{3,0,2,1:T(8,128)(2,1)S(1)} %slice.152, bf16[6,28,6,128]{3,2,0,1:T(8,128)(2,1)S(1)} %copy-done.11, bf16[6,28,6,128]{3,2,0,1:T(8,128)(2,1)S(1)} %copy-done.13, bf16[6,6,32,128]{3,2,0,1:T(8,128)(2,1)S(1)} %copy-done.2, bf16[6,6,32,128]{3,2,0,1:T(8,128)(2,1)S(1)} %copy-done.4, ...), kind=kLoop, calls=%fused_computation.34 | loop fusion | flops 5160960 | bytes 2876352 | tf_op jit(solution)/shard_map/convert_element_type | solution.py:232
  57.0 2.9 %fusion.22 = bf16[2,22,38,128]{3,0,2,1:T(2,128)(2,1)S(1)} fusion(f32[22,2,38,128]{3,0,2,1:T(8,128)S(1)} %slice.155, pred[22,38]{1,0:T(8,128)(4,1)S(1)} %broadcast_and_fusion.2, bf16[2,26,42,128]{3,0,2,1:T(2,128)(2,1)S(1)} %fusion.99), kind=kLoop, calls=%fused_computation.43 | loop fusion | flops 1284096 | bytes 1712964 | tf_op jit(solution)/shard_map/convert_element_type | solution.py:232
  63.8 1.7 %fusion.34 = bf16[20,2,36,128]{3,1,2,0:T(2,128)(2,1)S(1)} fusion(f32[20,2,36,128]{3,0,2,1:T(8,128)S(1)} %slice.159, pred[20,36]{1,0:T(8,128)(4,1)S(1)} %broadcast_and_fusion.3, bf16[20,2,36,128]{3,0,2,1:T(8,128)(2,1)S(1)} %slice.166), kind=kLoop, calls=%fused_computation.56 | loop fusion | flops 1290240 | bytes 1475280 | tf_op jit(solution)/shard_map/convert_element_type | solution.py:232
  68.0 2.3 %fusion.56 = bf16[2,18,34,128]{3,0,2,1:T(2,128)(2,1)S(1)} fusion(f32[18,2,34,128]{3,0,2,1:T(8,128)S(1)} %slice.169, pred[18,34]{1,0:T(8,128)(4,1)S(1)} %broadcast_and_fusion.4, bf16[2,22,38,128]{3,0,2,1:T(2,128)(2,1)S(1)} %fusion.98), kind=kLoop, calls=%fused_computation.84 | loop fusion | flops 940032 | bytes 1253988 | tf_op jit(solution)/shard_map/convert_element_type | solution.py:232
  70.3 1.8 %fusion.52 = f32[3,3,128,128]{3,2,1,0:T(8,128)S(1)} fusion(bf16[2,28,44,128]{3,2,0,1:T(8,128)(2,1)S(1)} %copy-done.9, bf16[2,18,34,128]{3,0,2,1:T(2,128)(2,1)S(1)} %fusion.56), kind=kOutput, calls=%fused_computation.79 | convolution fusion | flops 301989888 | bytes 1540096 | tf_op jit(solution)/shard_map/transpose | solution.py:82
  74.2 1.8 %fusion.73 = f32[3,3,128,128]{3,2,1,0:T(8,128)S(1)} fusion(bf16[22,2,38,128]{3,1,2,0:T(2,128)(2,1)S(1)} %fusion.19, bf16[2,20,36,128]{3,0,2,1:T(2,128)(2,1)S(1)} %bitcast.156), kind=kOutput, calls=%fused_computation.141 | convolution fusion | flops 301989888 | bytes 1280000 | tf_op jit(solution)/shard_map/transpose | solution.py:82
  75.9 1.8 %multiply_convert_fusion = (bf16[3,3,128,128]{3,2,1,0:T(8,128)(2,1)S(1)}, f32[3,3,128,128]{3,2,1,0:T(8,128)S(1)}) fusion(f32[3,3,128,128]{3,2,1,0:T(8,128)S(1)} %fusion.73, pred[]{:T(512)S(6)} %eq.27, bf16[26,2,42,128]{3,1,2,0:T(2,128)(2,1)S(1)} %fusion.11, bf16[2,16,32,128]{3,2,0,1:T(8,128)(2,1)S(1)} %slice.183), kind=kOutput, calls=%fused_computation.87 | convolution fusion | flops 302432256 | bytes 2295809 | tf_op jit(solution)/shard_map/transpose | solution.py:82
  78.3 1.8 %multiply_convert_fusion.1 = (bf16[3,3,128,128]{3,2,1,0:T(8,128)(2,1)S(1)}, f32[3,3,128,128]{3,2,1,0:T(8,128)S(1)}) fusion(f32[3,3,128,128]{3,2,1,0:T(8,128)S(1)} %fusion.52, pred[]{:T(512)S(6)} %eq.27, bf16[2,22,38,128]{3,0,2,1:T(2,128)(2,1)S(1)} %fusion.22, bf16[2,28,44,128]{3,2,0,1:T(8,128)(2,1)S(1)} %get-tuple-element.13), kind=kOutput, calls=%fused_computation.89 | convolution fusion | flops 302432256 | bytes 2424833 | tf_op jit(solution)/shard_map/transpose | solution.py:82
  81.2 5.0 %collective-permute-start.15 = (bf16[73728]{0:T(1024)(128)(2,1)S(1)}, bf16[73728]{0:T(1024)(128)(2,1)S(1)}, u32[]{:S(2)}, u32[]{:S(2)}) collective-permute-start(bf16[73728]{0:T(1024)(128)(2,1)S(1)} %select_convert_fusion), channel_id=1, source_target_pairs={{0,4},{4,0},{8,12},{12,8},{1,5},{5,1},{9,13},{13,9},{2,6},{6,2},{1... | collective-permute-start | bytes 442376 | tf_op jit(solution)/shard_map/ppermute | solution.py:100
  86.9 4.0 %collective-permute-done.15 = bf16[73728]{0:T(1024)(128)(2,1)S(1)} collective-permute-done((bf16[73728]{0:T(1024)(128)(2,1)S(1)}, bf16[73728]{0:T(1024)(128)(2,1)S(1)}, u32[]{:S(2)}, u32[]{:S(2)}) %collective-permute-start.15) | collective-permute-done | bytes 147488 | tf_op jit(solution)/shard_map/ppermute | solution.py:100
  91.0 2.5 %collective-permute-start.16 = (bf16[36864]{0:T(1024)(128)(2,1)S(1)}, bf16[36864]{0:T(1024)(128)(2,1)S(1)}, u32[]{:S(2)}, u32[]{:S(2)}) collective-permute-start(bf16[36864]{0:T(1024)(128)(2,1)S(1)} %select_convert_fusion.4), channel_id=1, source_target_pairs={{0,1},{1,0},{2,3},{3,2},{4,5},{5,4},{6,7},{7,6},{8,9},{9,8},{10,11... | collective-permute-start | bytes 221192 | tf_op jit(solution)/shard_map/ppermute | solution.py:100
  94.0 2.5 %collective-permute-start.9 = (bf16[36864]{0:T(1024)(128)(2,1)S(1)}, bf16[36864]{0:T(1024)(128)(2,1)S(1)}, u32[]{:S(2)}, u32[]{:S(2)}) collective-permute-start(bf16[36864]{0:T(1024)(128)(2,1)S(1)} %select_convert_fusion.6), channel_id=1, source_target_pairs={{0,1},{1,0},{2,3},{3,2},{4,5},{5,4},{6,7},{7,6},{8,9},{9,8},{10,11... | collective-permute-start | bytes 221192 | tf_op jit(solution)/shard_map/ppermute | solution.py:100
  96.6 3.7 %collective-permute-start.17 = (bf16[36864]{0:T(1024)(128)(2,1)S(1)}, bf16[36864]{0:T(1024)(128)(2,1)S(1)}, u32[]{:S(2)}, u32[]{:S(2)}) collective-permute-start(bf16[36864]{0:T(1024)(128)(2,1)S(1)} %add_convert_fusion.2), channel_id=1, source_target_pairs={{0,8},{4,12},{8,0},{12,4},{1,9},{5,13},{9,1},{13,5},{2,10},{6,14},... | collective-permute-start | bytes 221192 | tf_op jit(solution)/shard_map/ppermute | solution.py:100
  100.3 2.3 %collective-permute-start.10 = (bf16[36864]{0:T(1024)(128)(2,1)S(1)}, bf16[36864]{0:T(1024)(128)(2,1)S(1)}, u32[]{:S(2)}, u32[]{:S(2)}) collective-permute-start(bf16[36864]{0:T(1024)(128)(2,1)S(1)} %add_convert_fusion.5), channel_id=1, source_target_pairs={{0,8},{4,12},{8,0},{12,4},{1,9},{5,13},{9,1},{13,5},{2,10},{6,14},... | collective-permute-start | bytes 221192 | tf_op jit(solution)/shard_map/ppermute | solution.py:100
  103.0 2.7 %collective-permute-start.18 = (bf16[36864]{0:T(1024)(128)(2,1)S(1)}, bf16[36864]{0:T(1024)(128)(2,1)S(1)}, u32[]{:S(2)}, u32[]{:S(2)}) collective-permute-start(bf16[36864]{0:T(1024)(128)(2,1)S(1)} %add_convert_fusion.1), channel_id=1, source_target_pairs={{0,2},{1,3},{2,0},{3,1},{4,6},{5,7},{6,4},{7,5},{8,10},{9,11},{10,... | collective-permute-start | bytes 221192 | tf_op jit(solution)/shard_map/ppermute | solution.py:100
  105.7 2.3 %collective-permute-start.11 = (bf16[36864]{0:T(1024)(128)(2,1)S(1)}, bf16[36864]{0:T(1024)(128)(2,1)S(1)}, u32[]{:S(2)}, u32[]{:S(2)}) collective-permute-start(bf16[36864]{0:T(1024)(128)(2,1)S(1)} %add_convert_fusion.4), channel_id=1, source_target_pairs={{0,2},{1,3},{2,0},{3,1},{4,6},{5,7},{6,4},{7,5},{8,10},{9,11},{10,... | collective-permute-start | bytes 221192 | tf_op jit(solution)/shard_map/ppermute | solution.py:100
  108.0 2.3 %collective-permute-done.18 = bf16[36864]{0:T(1024)(128)(2,1)S(1)} collective-permute-done((bf16[36864]{0:T(1024)(128)(2,1)S(1)}, bf16[36864]{0:T(1024)(128)(2,1)S(1)}, u32[]{:S(2)}, u32[]{:S(2)}) %collective-permute-start.18) | collective-permute-done | bytes 73760 | tf_op jit(solution)/shard_map/ppermute | solution.py:100
  111.2 1.7 %collective-permute-start.12 = (bf16[36864]{0:T(1024)(128)(2,1)S(1)}, bf16[36864]{0:T(1024)(128)(2,1)S(1)}, u32[]{:S(2)}, u32[]{:S(2)}) collective-permute-start(bf16[36864]{0:T(1024)(128)(2,1)S(1)} %add_convert_fusion.3), channel_id=1, source_target_pairs={{0,1},{1,0},{2,3},{3,2},{4,5},{5,4},{6,7},{7,6},{8,9},{9,8},{10,11... | collective-permute-start | bytes 221192 | tf_op jit(solution)/shard_map/ppermute | solution.py:100
  112.9 1.9 %collective-permute-done.19 = bf16[36864]{0:T(1024)(128)(2,1)S(1)} collective-permute-done((bf16[36864]{0:T(1024)(128)(2,1)S(1)}, bf16[36864]{0:T(1024)(128)(2,1)S(1)}, u32[]{:S(2)}, u32[]{:S(2)}) %collective-permute-start.19) | collective-permute-done | bytes 73760 | tf_op jit(solution)/shard_map/ppermute | solution.py:100
  114.9 1.6 %collective-permute-start.20 = (bf16[73728]{0:T(1024)(128)(2,1)S(1)}, bf16[73728]{0:T(1024)(128)(2,1)S(1)}, u32[]{:S(2)}, u32[]{:S(2)}) collective-permute-start(bf16[73728]{0:T(1024)(128)(2,1)S(1)} %maximum_select_fusion.4), channel_id=1, source_target_pairs={{0,4},{4,0},{8,12},{12,8},{1,5},{5,1},{9,13},{13,9},{2,6},{6,2},{1... | collective-permute-start | bytes 442376 | tf_op jit(solution)/shard_map/ppermute | solution.py:100
  117.2 2.9 %collective-permute-done.20 = bf16[73728]{0:T(1024)(128)(2,1)S(1)} collective-permute-done((bf16[73728]{0:T(1024)(128)(2,1)S(1)}, bf16[73728]{0:T(1024)(128)(2,1)S(1)}, u32[]{:S(2)}, u32[]{:S(2)}) %collective-permute-start.20) | collective-permute-done | bytes 147488 | tf_op jit(solution)/shard_map/ppermute | solution.py:100
  (176 shorter events, 36.9 us)
Async XLA Ops:
  0.6 2.6 %copy-start = (bf16[4,16,32,128]{3,2,1,0:T(8,128)(2,1)S(1)}, bf16[4,16,32,128]{3,2,1,0:T(8,128)(2,1)}, u32[]{:S(2)}) copy-start(bf16[4,16,32,128]{3,2,1,0:T(8,128)(2,1)} %param.6) | copy-start | bytes 1572868
  0.6 1.8 %copy-start.14 = (bf16[2,3,3,128,128]{4,3,2,1,0:T(8,128)(2,1)S(1)}, bf16[2,3,3,128,128]{4,3,2,1,0:T(8,128)(2,1)}, u32[]{:S(2)}) copy-start(bf16[2,3,3,128,128]{4,3,2,1,0:T(8,128)(2,1)} %param.5) | copy-start | bytes 1769476
  0.7 1.9 %copy-start.17 = (s32[4]{0:T(128)S(1)}, s32[4]{0:T(128)}, u32[]{:S(2)}) copy-start(s32[4]{0:T(128)} %param.7) | copy-start | bytes 52
  1.9 2.2 %collective-permute-start = (bf16[2,16,32,128]{3,2,0,1:T(8,128)(2,1)S(1)}, bf16[2,16,32,128]{3,2,0,1:T(8,128)(2,1)S(1)}, u32[]{:S(2)}, u32[]{:S(2)}) collective-permute-start(bf16[2,16,32,128]{3,2,0,1:T(8,128)(2,1)S(1)} %bitcast.163), channel_id=1, source_target_pairs={{0,16},{16,0},{1,17},{17,1},{2,18},{18,2},{3,19},{19,3},{4,20},{20... | collective-permute-start | bytes 786440 | tf_op jit(solution)/shard_map/ppermute | solution.py:249
  2.4 21.0 %collective-permute-start.5 = (bf16[2,3,3,128,128]{4,3,2,1,0:T(8,128)(2,1)S(1)}, bf16[2,3,3,128,128]{4,3,2,1,0:T(8,128)(2,1)}, u32[]{:S(2)}, u32[]{:S(2)}) collective-permute-start(bf16[2,3,3,128,128]{4,3,2,1,0:T(8,128)(2,1)S(1)} %copy-done.14), channel_id=1, source_target_pairs={{0,16},{16,0},{1,17},{17,1},{2,18},{18,2},{3,19},{19,3},{4,20},{20... | collective-permute-start | bytes 1769480 | tf_op jit(solution)/shard_map/ppermute | solution.py:249
  4.1 12.7 %collective-permute-start.2 = (bf16[6,6,32,128]{3,2,0,1:T(8,128)(2,1)S(1)}, bf16[6,6,32,128]{3,2,0,1:T(8,128)(2,1)S(1)}, u32[]{:S(2)}, u32[]{:S(2)}) collective-permute-start(bf16[6,6,32,128]{3,2,0,1:T(8,128)(2,1)S(1)} %get-tuple-element.19), channel_id=1, source_target_pairs={{4,0},{5,1},{6,2},{7,3},{8,4},{9,5},{10,6},{11,7},{12,8},{13,9},{1... | collective-permute-start | bytes 884744 | tf_op jit(solution)/shard_map/ppermute | solution.py:43
  5.4 11.9 %collective-permute-start.1 = (bf16[6,6,32,128]{3,2,0,1:T(8,128)(2,1)S(1)}, bf16[6,6,32,128]{3,2,0,1:T(8,128)(2,1)S(1)}, u32[]{:S(2)}, u32[]{:S(2)}) collective-permute-start(bf16[6,6,32,128]{3,2,0,1:T(8,128)(2,1)S(1)} %get-tuple-element.18), channel_id=1, source_target_pairs={{0,4},{1,5},{2,6},{3,7},{4,8},{5,9},{6,10},{7,11},{8,12},{9,13},{1... | collective-permute-start | bytes 884744 | tf_op jit(solution)/shard_map/ppermute | solution.py:43
  16.8 13.0 %copy-start.1 = (bf16[6,6,32,128]{3,2,0,1:T(8,128)(2,1)}, bf16[6,6,32,128]{3,2,0,1:T(8,128)(2,1)S(1)}, u32[]{:S(2)}) copy-start(bf16[6,6,32,128]{3,2,0,1:T(8,128)(2,1)S(1)} %collective-permute-done.2) | copy-start | bytes 884740
  17.4 12.4 %copy-start.3 = (bf16[6,6,32,128]{3,2,0,1:T(8,128)(2,1)}, bf16[6,6,32,128]{3,2,0,1:T(8,128)(2,1)S(1)}, u32[]{:S(2)}) copy-start(bf16[6,6,32,128]{3,2,0,1:T(8,128)(2,1)S(1)} %collective-permute-done.1) | copy-start | bytes 884740
  17.5 11.1 %collective-permute-start.4 = (bf16[6,28,6,128]{3,2,0,1:T(8,128)(2,1)S(1)}, bf16[6,28,6,128]{3,2,0,1:T(8,128)(2,1)S(1)}, u32[]{:S(2)}, u32[]{:S(2)}) collective-permute-start(bf16[6,28,6,128]{3,2,0,1:T(8,128)(2,1)S(1)} %get-tuple-element.15), channel_id=1, source_target_pairs={{1,0},{2,1},{3,2},{5,4},{6,5},{7,6},{9,8},{10,9},{11,10},{13,12},{... | collective-permute-start | bytes 774152 | tf_op jit(solution)/shard_map/ppermute | solution.py:43
  18.8 11.0 %collective-permute-start.3 = (bf16[6,28,6,128]{3,2,0,1:T(8,128)(2,1)S(1)}, bf16[6,28,6,128]{3,2,0,1:T(8,128)(2,1)S(1)}, u32[]{:S(2)}, u32[]{:S(2)}) collective-permute-start(bf16[6,28,6,128]{3,2,0,1:T(8,128)(2,1)S(1)} %get-tuple-element.14), channel_id=1, source_target_pairs={{0,1},{1,2},{2,3},{4,5},{5,6},{6,7},{8,9},{9,10},{10,11},{12,13},{... | collective-permute-start | bytes 774152 | tf_op jit(solution)/shard_map/ppermute | solution.py:43
  24.6 9.2 %copy-start.7 = (bf16[2,3,3,128,128]{4,3,2,1,0:T(8,128)(2,1)}, bf16[2,3,3,128,128]{4,3,2,1,0:T(8,128)(2,1)S(1)}, u32[]{:S(2)}) copy-start(bf16[2,3,3,128,128]{4,3,2,1,0:T(8,128)(2,1)S(1)} %get-tuple-element.17) | copy-start | bytes 1769476
  28.6 2.8 %copy-start.10 = (bf16[6,28,6,128]{3,2,0,1:T(8,128)(2,1)}, bf16[6,28,6,128]{3,2,0,1:T(8,128)(2,1)S(1)}, u32[]{:S(2)}) copy-start(bf16[6,28,6,128]{3,2,0,1:T(8,128)(2,1)S(1)} %collective-permute-done.4) | copy-start | bytes 774148
  29.8 1.7 %copy-start.12 = (bf16[6,28,6,128]{3,2,0,1:T(8,128)(2,1)}, bf16[6,28,6,128]{3,2,0,1:T(8,128)(2,1)S(1)}, u32[]{:S(2)}) copy-start(bf16[6,28,6,128]{3,2,0,1:T(8,128)(2,1)S(1)} %collective-permute-done.3) | copy-start | bytes 774148
  32.4 1.4 %copy-start.23 = (pred[16,6]{0,1:T(8,128)(4,1)S(1)}, pred[16,6]{0,1:T(8,128)(4,1)}, u32[]{:S(2)}) copy-start(pred[16,6]{0,1:T(8,128)(4,1)} %constant.196) | copy-start | bytes 292
  36.0 3.5 %copy-start.9 = (bf16[2,28,44,128]{3,2,0,1:T(8,128)(2,1)S(1)}, bf16[2,28,44,128]{3,2,0,1:T(8,128)(2,1)}, u32[]{:S(2)}) copy-start(bf16[2,28,44,128]{3,2,0,1:T(8,128)(2,1)} %get-tuple-element.12) | copy-start | bytes 1892356
  50.9 1.2 %copy-start.13 = (bf16[6,28,6,128]{3,2,0,1:T(8,128)(2,1)S(1)}, bf16[6,28,6,128]{3,2,0,1:T(8,128)(2,1)}, u32[]{:S(2)}) copy-start(bf16[6,28,6,128]{3,2,0,1:T(8,128)(2,1)} %copy-done.12) | copy-start | bytes 774148
  74.1 6.1 %collective-permute-start.6 = (bf16[2,16,32,128]{3,2,0,1:T(8,128)(2,1)S(1)}, bf16[2,16,32,128]{3,2,0,1:T(8,128)(2,1)S(1)}, u32[]{:S(2)}, u32[]{:S(2)}) collective-permute-start(bf16[2,16,32,128]{3,2,0,1:T(8,128)(2,1)S(1)} %get-tuple-element.21), channel_id=1, source_target_pairs={{0,16},{16,0},{1,17},{17,1},{2,18},{18,2},{3,19},{19,3},{4,20},{20... | collective-permute-start | bytes 786440 | tf_op jit(solution)/shard_map/ppermute | solution.py:249
  77.7 3.3 %collective-permute-start.14 = (bf16[3,3,128,128]{3,2,1,0:T(8,128)(2,1)S(1)}, bf16[3,3,128,128]{3,2,1,0:T(8,128)(2,1)S(1)}, u32[]{:S(2)}, u32[]{:S(2)}) collective-permute-start(bf16[3,3,128,128]{3,2,1,0:T(8,128)(2,1)S(1)} %get-tuple-element.26), channel_id=1, source_target_pairs={{0,16},{16,0},{1,17},{17,1},{2,18},{18,2},{3,19},{19,3},{4,20},{20... | collective-permute-start | bytes 884744 | tf_op jit(solution)/shard_map/ppermute | solution.py:249
  80.1 6.2 %collective-permute-start.7 = (bf16[3,3,128,128]{3,2,1,0:T(8,128)(2,1)S(1)}, bf16[3,3,128,128]{3,2,1,0:T(8,128)(2,1)S(1)}, u32[]{:S(2)}, u32[]{:S(2)}) collective-permute-start(bf16[3,3,128,128]{3,2,1,0:T(8,128)(2,1)S(1)} %get-tuple-element.28), channel_id=1, source_target_pairs={{0,16},{16,0},{1,17},{17,1},{2,18},{18,2},{3,19},{19,3},{4,20},{20... | collective-permute-start | bytes 884744 | tf_op jit(solution)/shard_map/ppermute | solution.py:249
  81.2 9.7 %collective-permute-start.15 = (bf16[73728]{0:T(1024)(128)(2,1)S(1)}, bf16[73728]{0:T(1024)(128)(2,1)S(1)}, u32[]{:S(2)}, u32[]{:S(2)}) collective-permute-start(bf16[73728]{0:T(1024)(128)(2,1)S(1)} %select_convert_fusion), channel_id=1, source_target_pairs={{0,4},{4,0},{8,12},{12,8},{1,5},{5,1},{9,13},{13,9},{2,6},{6,2},{1... | collective-permute-start | bytes 442376 | tf_op jit(solution)/shard_map/ppermute | solution.py:100
  86.4 7.5 %collective-permute-start.8 = (bf16[73728]{0:T(1024)(128)(2,1)S(1)}, bf16[73728]{0:T(1024)(128)(2,1)S(1)}, u32[]{:S(2)}, u32[]{:S(2)}) collective-permute-start(bf16[73728]{0:T(1024)(128)(2,1)S(1)} %select_convert_fusion.2), channel_id=1, source_target_pairs={{0,4},{4,0},{8,12},{12,8},{1,5},{5,1},{9,13},{13,9},{2,6},{6,2},{1... | collective-permute-start | bytes 442376 | tf_op jit(solution)/shard_map/ppermute | solution.py:100
  91.0 5.5 %collective-permute-start.16 = (bf16[36864]{0:T(1024)(128)(2,1)S(1)}, bf16[36864]{0:T(1024)(128)(2,1)S(1)}, u32[]{:S(2)}, u32[]{:S(2)}) collective-permute-start(bf16[36864]{0:T(1024)(128)(2,1)S(1)} %select_convert_fusion.4), channel_id=1, source_target_pairs={{0,1},{1,0},{2,3},{3,2},{4,5},{5,4},{6,7},{7,6},{8,9},{9,8},{10,11... | collective-permute-start | bytes 221192 | tf_op jit(solution)/shard_map/ppermute | solution.py:100
  94.0 6.3 %collective-permute-start.9 = (bf16[36864]{0:T(1024)(128)(2,1)S(1)}, bf16[36864]{0:T(1024)(128)(2,1)S(1)}, u32[]{:S(2)}, u32[]{:S(2)}) collective-permute-start(bf16[36864]{0:T(1024)(128)(2,1)S(1)} %select_convert_fusion.6), channel_id=1, source_target_pairs={{0,1},{1,0},{2,3},{3,2},{4,5},{5,4},{6,7},{7,6},{8,9},{9,8},{10,11... | collective-permute-start | bytes 221192 | tf_op jit(solution)/shard_map/ppermute | solution.py:100
  96.6 6.4 %collective-permute-start.17 = (bf16[36864]{0:T(1024)(128)(2,1)S(1)}, bf16[36864]{0:T(1024)(128)(2,1)S(1)}, u32[]{:S(2)}, u32[]{:S(2)}) collective-permute-start(bf16[36864]{0:T(1024)(128)(2,1)S(1)} %add_convert_fusion.2), channel_id=1, source_target_pairs={{0,8},{4,12},{8,0},{12,4},{1,9},{5,13},{9,1},{13,5},{2,10},{6,14},... | collective-permute-start | bytes 221192 | tf_op jit(solution)/shard_map/ppermute | solution.py:100
  100.3 5.4 %collective-permute-start.10 = (bf16[36864]{0:T(1024)(128)(2,1)S(1)}, bf16[36864]{0:T(1024)(128)(2,1)S(1)}, u32[]{:S(2)}, u32[]{:S(2)}) collective-permute-start(bf16[36864]{0:T(1024)(128)(2,1)S(1)} %add_convert_fusion.5), channel_id=1, source_target_pairs={{0,8},{4,12},{8,0},{12,4},{1,9},{5,13},{9,1},{13,5},{2,10},{6,14},... | collective-permute-start | bytes 221192 | tf_op jit(solution)/shard_map/ppermute | solution.py:100
  103.0 7.3 %collective-permute-start.18 = (bf16[36864]{0:T(1024)(128)(2,1)S(1)}, bf16[36864]{0:T(1024)(128)(2,1)S(1)}, u32[]{:S(2)}, u32[]{:S(2)}) collective-permute-start(bf16[36864]{0:T(1024)(128)(2,1)S(1)} %add_convert_fusion.1), channel_id=1, source_target_pairs={{0,2},{1,3},{2,0},{3,1},{4,6},{5,7},{6,4},{7,5},{8,10},{9,11},{10,... | collective-permute-start | bytes 221192 | tf_op jit(solution)/shard_map/ppermute | solution.py:100
  105.7 5.4 %collective-permute-start.11 = (bf16[36864]{0:T(1024)(128)(2,1)S(1)}, bf16[36864]{0:T(1024)(128)(2,1)S(1)}, u32[]{:S(2)}, u32[]{:S(2)}) collective-permute-start(bf16[36864]{0:T(1024)(128)(2,1)S(1)} %add_convert_fusion.4), channel_id=1, source_target_pairs={{0,2},{1,3},{2,0},{3,1},{4,6},{5,7},{6,4},{7,5},{8,10},{9,11},{10,... | collective-permute-start | bytes 221192 | tf_op jit(solution)/shard_map/ppermute | solution.py:100
  110.4 4.4 %collective-permute-start.19 = (bf16[36864]{0:T(1024)(128)(2,1)S(1)}, bf16[36864]{0:T(1024)(128)(2,1)S(1)}, u32[]{:S(2)}, u32[]{:S(2)}) collective-permute-start(bf16[36864]{0:T(1024)(128)(2,1)S(1)} %add_convert_fusion), channel_id=1, source_target_pairs={{0,1},{1,0},{2,3},{3,2},{4,5},{5,4},{6,7},{7,6},{8,9},{9,8},{10,11... | collective-permute-start | bytes 221192 | tf_op jit(solution)/shard_map/ppermute | solution.py:100
  111.2 5.2 %collective-permute-start.12 = (bf16[36864]{0:T(1024)(128)(2,1)S(1)}, bf16[36864]{0:T(1024)(128)(2,1)S(1)}, u32[]{:S(2)}, u32[]{:S(2)}) collective-permute-start(bf16[36864]{0:T(1024)(128)(2,1)S(1)} %add_convert_fusion.3), channel_id=1, source_target_pairs={{0,1},{1,0},{2,3},{3,2},{4,5},{5,4},{6,7},{7,6},{8,9},{9,8},{10,11... | collective-permute-start | bytes 221192 | tf_op jit(solution)/shard_map/ppermute | solution.py:100
  114.9 5.2 %collective-permute-start.20 = (bf16[73728]{0:T(1024)(128)(2,1)S(1)}, bf16[73728]{0:T(1024)(128)(2,1)S(1)}, u32[]{:S(2)}, u32[]{:S(2)}) collective-permute-start(bf16[73728]{0:T(1024)(128)(2,1)S(1)} %maximum_select_fusion.4), channel_id=1, source_target_pairs={{0,4},{4,0},{8,12},{12,8},{1,5},{5,1},{9,13},{13,9},{2,6},{6,2},{1... | collective-permute-start | bytes 442376 | tf_op jit(solution)/shard_map/ppermute | solution.py:100
  116.5 5.2 %collective-permute-start.13 = (bf16[73728]{0:T(1024)(128)(2,1)S(1)}, bf16[73728]{0:T(1024)(128)(2,1)S(1)}, u32[]{:S(2)}, u32[]{:S(2)}) collective-permute-start(bf16[73728]{0:T(1024)(128)(2,1)S(1)} %maximum_select_fusion.3), channel_id=1, source_target_pairs={{0,4},{4,0},{8,12},{12,8},{1,5},{5,1},{9,13},{13,9},{2,6},{6,2},{1... | collective-permute-start | bytes 442376 | tf_op jit(solution)/shard_map/ppermute | solution.py:100
  (13 other events, 13.2 us)

commit v7 on v5

--- a/solution.py
+++ b/solution.py
@@ -217,7 +217,7 @@
     return (boundary[None], kernel_grad)
 
 
-def section_chain(top_ext, top_width, inputs_list, rim, flipped_kernels):
+def section_chain(top_ext, top_width, inputs_list, rim, flipped_kernels, early=None):
     layer_count = len(flipped_kernels)
     tile_rows = inputs_list[0].shape[1] - 2 * rim
     tile_cols = inputs_list[0].shape[2] - 2 * rim
@@ -231,7 +231,12 @@
         signal = jnp.where(inside_mask(tile_rows, tile_cols, width), signal, 0.0)
         signal = signal.astype(jnp.bfloat16)
         signals[layer_idx] = crop(signal, width)
+        if early is not None and layer_idx == layer_count - 1:
+            started = early(signals[layer_idx])
+            signal, started = lax.optimization_barrier((signal, started))
         gradient = convolve(signal, flipped_kernels[layer_idx])
+    if early is not None:
+        return gradient.astype(jnp.bfloat16), signals, started
     return gradient.astype(jnp.bfloat16), signals
 
 
@@ -264,6 +269,14 @@
     stacked = with_rim(jnp.concatenate(stacked, axis=0), rims[1], 0, range(2))
     firsts = [crop(stacked[:half], rims[1] - rims[0]), stacked[half : 2 * half]]
     top_ext = crop(stacked[2 * half :], rims[1] - top_rim[1])
+
+    scale = 1.0 / batches
+
+    def sum_input(section_one, section_zero):
+        mine_terms = by_section(section_zero, section_one, 0)
+        other_terms = by_section(section_one, section_zero, 0)
+        other_terms = swap((other_terms * scale).astype(jnp.bfloat16)).astype(jnp.float32)
+        return mine_terms * scale + other_terms
 
     results, partials = [None, None], [None, None]
     for s in (1, 0):
@@ -278,20 +291,27 @@
             current = current.astype(jnp.bfloat16)
             inputs_list.append(current)
         flipped = jnp.transpose(section_kernels[s][:, ::-1, ::-1], (0, 1, 2, 4, 3))
-        top_ext, signals = section_chain(top_ext, top_rim[s], inputs_list, rim, flipped)
+
+        def product(layer_idx, signal, inputs_list=inputs_list, rim=rim):
+            return kernel_terms(crop(inputs_list[layer_idx], rim - layer_idx - 1), signal)
+
+        if s == 1:
+            top_ext, signals = section_chain(top_ext, top_rim[s], inputs_list, rim, flipped)
+            partials[s] = [product(l, signals[l]) for l in range(layer_count)]
+        else:
+            top_ext, signals, early_total = section_chain(
+                top_ext,
+                top_rim[s],
+                inputs_list,
+                rim,
+                flipped,
+                lambda signal: sum_input(partials[1][-1], product(layer_count - 1, signal)),
+            )
+            partials[s] = [product(l, signals[l]) for l in range(layer_count - 1)] + [None]
         results[s] = crop(top_ext, top_rim[s] - layer_count)
-        partials[s] = jnp.stack(
-            [
-                kernel_terms(crop(inputs_list[layer_idx], rim - layer_idx - 1), signals[layer_idx])
-                for layer_idx in range(layer_count)
-            ]
-        )
-
-    mine_terms = by_section(partials[0], partials[1], 0)
-    other_terms = by_section(partials[1], partials[0], 0)
-    scale = 1.0 / batches
-    other_terms = swap((other_terms * scale).astype(jnp.bfloat16)).astype(jnp.float32)
-    gathered = summed_over_tiles(mine_terms * scale + other_terms)
+
+    summed = [summed_over_tiles(sum_input(partials[1][l], partials[0][l])) for l in range(layer_count - 1)]
+    gathered = jnp.stack(summed + [summed_over_tiles(early_total)])
     mine_back = by_section(results[0], results[1], 0)
     other_back = swap(by_section(results[1], results[0], 0))
     boundary = jnp.where(

time: 129 us -> 129 us (level)
  starting transfers between devices: 29.6 us -> 25 us
  waiting for transfers between devices: 38.5 us -> 42.1 us
    ppermute x4, waiting for transfers between devices: 10.4 us -> 20.4 us  [from_neighbours(): parts.append(lax.ppermute(piece, AXES, pairs))]
    ppermute x6 -> x12, waiting for transfers between devices: 25.7 us -> 21.7 us  [exchange(): return lax.ppermute(values, axis, [(i, i ^ distance) for i in range(count)])]
    ppermute x6 -> x12, starting transfers between devices: 16.3 us -> 12.8 us  [exchange(): return lax.ppermute(values, axis, [(i, i ^ distance) for i in range(count)])]
    ppermute x4 -> x5, waiting for transfers between devices: 2.35 us -> 0.01 us  [swap(): return lax.ppermute(values, 'section', [(0, 1), (1, 0)])]
    convert_element_type x2 -> x0, other arithmetic: 2.11 us -> none  [the longest x1 1.12 us: summed_over_tiles(): return current.astype(jnp.float32).reshape(grads.shape)]
    ppermute x4, starting transfers between devices: 12.6 us -> 10.9 us  [from_neighbours(): parts.append(lax.ppermute(piece, AXES, pairs))]
    slice x0 -> x1, other arithmetic: none -> 1.65 us  [local_split(): firsts = [crop(stacked[:half], rims[1] - rims[0]), stacked[half:2 * half]]]
    concatenate x1 -> x0, other arithmetic: 1.65 us -> none  [from_neighbours(): return jnp.concatenate(parts, axis=dim)]
  transfers between devices with their start and end apart: 14 -> 21, of which waited for: 11 -> 15; matrix products, arithmetic and copies ran while one was open for 5% -> 8% of each run, Pallas kernels for 0% -> 0%
where the time goes in v7:
time: 129 us; the launch traced here: 128 us
  waiting for transfers between devices  42.1 us (33%)
  other arithmetic  27 us (21%)
  starting transfers between devices  25 us (19%)
  matrix products  18 us (14%)
  local copies, waits for them, and re-layouts  14.5 us (11%)
  between operations  1.78 us (1%)
    ppermute x12, waiting for transfers between devices, exchange(): return lax.ppermute(values, axis, [(i, i ^ distance) for i in range(count)])  21.7 us
    ppermute x4, waiting for transfers between devices, from_neighbours(): parts.append(lax.ppermute(piece, AXES, pairs))  20.4 us
    ppermute x12, starting transfers between devices, exchange(): return lax.ppermute(values, axis, [(i, i ^ distance) for i in range(count)])  12.8 us
    ppermute x4, starting transfers between devices, from_neighbours(): parts.append(lax.ppermute(piece, AXES, pairs))  10.9 us
    conv_general_dilated x8, matrix products, convolve(): lax.conv_general_dilated(padded, kernel, (1, 1), 'VALID', dimension_numbe...  9.93 us
    convert_element_type x4, other arithmetic, local_split(): current = current.astype(jnp.bfloat16)  9.3 us
    convert_element_type x4, other arithmetic, section_chain(): signal = signal.astype(jnp.bfloat16)  8.67 us
    transpose x4, matrix products, kernel_terms(): return jnp.transpose(terms, (1, 2, 0, 3))  8.06 us
  transfers between devices with their start and end apart: 21, of which 15 were waited for; matrix products, arithmetic and copies ran while one was open for 8% of the time, Pallas kernels for 0%

profile of v7, /device:TPU:0, one launch (start us, length us, event | category | flops | bytes accessed | tf_op | source)
XLA Modules:
  0.0 128.4 jit_solution(16030429664059967813)
XLA Ops:
  4.0 4.8 %collective-permute-start.1 = (bf16[6,6,32,128]{3,2,0,1:T(8,128)(2,1)S(1)}, bf16[6,6,32,128]{3,2,0,1:T(8,128)(2,1)S(1)}, u32[]{:S(2)}, u32[]{:S(2)}) collective-permute-start(bf16[6,6,32,128]{3,2,0,1:T(8,128)(2,1)S(1)} %get-tuple-element.22), channel_id=1, source_target_pairs={{0,4},{1,5},{2,6},{3,7},{4,8},{5,9},{6,10},{7,11},{8,12},{9,13},{1... | collective-permute-start | bytes 884744 | tf_op jit(solution)/shard_map/ppermute | solution.py:43
  10.2 5.1 %collective-permute-done.1 = bf16[6,6,32,128]{3,2,0,1:T(8,128)(2,1)S(1)} collective-permute-done((bf16[6,6,32,128]{3,2,0,1:T(8,128)(2,1)S(1)}, bf16[6,6,32,128]{3,2,0,1:T(8,128)(2,1)S(1)}, u32[]{:S(2)}, u32[]{:S(2)}) %collective-permute-start.1) | collective-permute-done | bytes 294944 | tf_op jit(solution)/shard_map/ppermute | solution.py:43
  15.3 8.3 %collective-permute-done.2 = bf16[6,6,32,128]{3,2,0,1:T(8,128)(2,1)S(1)} collective-permute-done((bf16[6,6,32,128]{3,2,0,1:T(8,128)(2,1)S(1)}, bf16[6,6,32,128]{3,2,0,1:T(8,128)(2,1)S(1)}, u32[]{:S(2)}, u32[]{:S(2)}) %collective-permute-start.2) | collective-permute-done | bytes 294944 | tf_op jit(solution)/shard_map/ppermute | solution.py:43
  23.7 3.5 %collective-permute-start.3 = (bf16[6,28,6,128]{3,2,0,1:T(8,128)(2,1)S(1)}, bf16[6,28,6,128]{3,2,0,1:T(8,128)(2,1)S(1)}, u32[]{:S(2)}, u32[]{:S(2)}) collective-permute-start(bf16[6,28,6,128]{3,2,0,1:T(8,128)(2,1)S(1)} %get-tuple-element.18), channel_id=1, source_target_pairs={{0,1},{1,2},{2,3},{4,5},{5,6},{6,7},{8,9},{9,10},{10,11},{12,13},{... | collective-permute-start | bytes 774152 | tf_op jit(solution)/shard_map/ppermute | solution.py:43
  30.9 3.0 %collective-permute-done.3 = bf16[6,28,6,128]{3,2,0,1:T(8,128)(2,1)S(1)} collective-permute-done((bf16[6,28,6,128]{3,2,0,1:T(8,128)(2,1)S(1)}, bf16[6,28,6,128]{3,2,0,1:T(8,128)(2,1)S(1)}, u32[]{:S(2)}, u32[]{:S(2)}) %collective-permute-start.3) | collective-permute-done | bytes 258080 | tf_op jit(solution)/shard_map/ppermute | solution.py:43
  33.9 4.1 %collective-permute-done.4 = bf16[6,28,6,128]{3,2,0,1:T(8,128)(2,1)S(1)} collective-permute-done((bf16[6,28,6,128]{3,2,0,1:T(8,128)(2,1)S(1)}, bf16[6,28,6,128]{3,2,0,1:T(8,128)(2,1)S(1)}, u32[]{:S(2)}, u32[]{:S(2)}) %collective-permute-start.4) | collective-permute-done | bytes 258080 | tf_op jit(solution)/shard_map/ppermute | solution.py:43
  38.1 1.6 %pad_maximum_fusion.6 = (bf16[2,28,44,128]{3,2,0,1:T(8,128)(2,1)S(1)}, bf16[2,28,44,128]{3,2,0,1:T(8,128)(2,1)}) fusion(bf16[6,28,6,128]{3,2,0,1:T(8,128)(2,1)S(1)} %collective-permute-done.4, bf16[6,28,6,128]{3,2,0,1:T(8,128)(2,1)S(1)} %collective-permute-done.3, bf16[6,6,32,128]{3,2,0,1:T(8,128)(2,1)S(1)} %collective-permute-done.2, ...), kind=kLoop, calls=%fused_computation.63 | loop fusion | flops 8830976 | bytes 3153920 | tf_op jit(solution)/shard_map/slice | solution.py:270
  41.9 1.7 %fusion.1 = bf16[26,16,6,128]{3,1,2,0:T(8,128)(2,1)S(1)} fusion(bf16[28,2,8,8,128]{4,1,3,2,0:T(2,128)(2,1)S(1)} %fusion.15, pred[16,6]{0,1:T(8,128)(4,1)S(1)} %copy-done.32, bf16[2,3,3,128,128]{4,3,2,1,0:T(8,128)(2,1)S(1)} %get-tuple-element.20), kind=kOutput, calls=%fused_computation.7 | convolution fusion | flops 736739328 | bytes 1852416 | tf_op jit(solution)/shard_map/conv_general_dilated | solution.py:63
  44.0 1.7 %fusion.10 = bf16[26,2,42,128]{3,1,2,0:T(2,128)(2,1)S(1)} fusion(bf16[26,2,42,128]{3,2,1,0:T(8,128)(2,1)S(1)} %bitcast.131, pred[26,42]{1,0:T(8,128)(4,1)S(1)} %broadcast_and_fusion), kind=kLoop, calls=%fused_computation.26 | loop fusion | flops 279552 | bytes 1119300 | tf_op jit(solution)/shard_map/convert_element_type | solution.py:291
  45.8 1.7 %fusion.92 = bf16[2,26,42,128]{3,0,2,1:T(2,128)(2,1)S(1)} fusion(bf16[26,2,42,128]{3,2,1,0:T(8,128)(2,1)S(1)} %bitcast.132, pred[26,42]{1,0:T(8,128)(4,1)S(1)} %broadcast_and_fusion), kind=kLoop, calls=%fused_computation.195 | loop fusion | flops 279552 | bytes 1119300 | tf_op jit(solution)/shard_map/convert_element_type | solution.py:291
  51.4 1.9 %fusion.14 = bf16[2,24,40,128]{3,2,0,1:T(8,128)(2,1)S(1)} fusion(bf16[24,2,40,128]{3,0,2,1:T(8,128)(2,1)S(1)} %slice.152, bf16[6,28,6,128]{3,2,0,1:T(8,128)(2,1)S(1)} %copy-done.19, bf16[6,28,6,128]{3,2,0,1:T(8,128)(2,1)S(1)} %copy-done.17, bf16[6,6,32,128]{3,2,0,1:T(8,128)(2,1)S(1)} %copy-done.4, bf16[6,6,32,128]{3,2,0,1:T(8,128)(2,1)S(1)} %copy-done.2, ...), kind=kLoop, calls=%fused_computation.33 | loop fusion | flops 5160960 | bytes 2876352 | tf_op jit(solution)/shard_map/convert_element_type | solution.py:232
  56.0 3.1 %fusion.21 = bf16[2,22,38,128]{3,0,2,1:T(2,128)(2,1)S(1)} fusion(f32[22,2,38,128]{3,0,2,1:T(8,128)S(1)} %slice.155, pred[22,38]{1,0:T(8,128)(4,1)S(1)} %broadcast_and_fusion.2, bf16[2,26,42,128]{3,0,2,1:T(2,128)(2,1)S(1)} %fusion.92), kind=kLoop, calls=%fused_computation.42 | loop fusion | flops 1284096 | bytes 1712964 | tf_op jit(solution)/shard_map/convert_element_type | solution.py:232
  65.4 2.8 %fusion.18 = bf16[22,2,38,128]{3,1,2,0:T(2,128)(2,1)S(1)} fusion(bf16[22,2,38,128]{3,0,2,1:T(8,128)(2,1)S(1)} %slice.163, pred[22,38]{1,0:T(8,128)(4,1)S(1)} %broadcast_and_fusion.2), kind=kLoop, calls=%fused_computation.38 | loop fusion | flops 214016 | bytes 856900 | tf_op jit(solution)/shard_map/convert_element_type | solution.py:291
  70.0 1.7 %fusion.66 = bf16[2,20,36,128]{3,0,2,1:T(2,128)(2,1)S(1)} fusion(bf16[20,2,36,128]{3,0,2,1:T(8,128)(2,1)S(1)} %slice.166, f32[20,2,36,128]{3,0,2,1:T(8,128)S(1)} %slice.159, pred[20,36]{1,0:T(8,128)(4,1)S(1)} %broadcast_and_fusion.3), kind=kLoop, calls=%fused_computation.104 | loop fusion | flops 1290240 | bytes 1475280 | tf_op jit(solution)/shard_map/convert_element_type | solution.py:232
  71.8 1.8 %fusion.69 = f32[3,3,128,128]{3,2,1,0:T(8,128)S(1)} fusion(bf16[22,2,38,128]{3,1,2,0:T(2,128)(2,1)S(1)} %fusion.18, bf16[2,20,36,128]{3,0,2,1:T(2,128)(2,1)S(1)} %fusion.66), kind=kOutput, calls=%fused_computation.138 | convolution fusion | flops 301989888 | bytes 1280000 | tf_op jit(solution)/shard_map/transpose | solution.py:82
  73.6 2.8 %multiply_convert_fusion.1 = (bf16[3,3,128,128]{3,2,1,0:T(8,128)(2,1)}, f32[3,3,128,128]{3,2,1,0:T(8,128)}) fusion(f32[3,3,128,128]{3,2,1,0:T(8,128)S(1)} %fusion.69, pred[]{:T(512)S(6)} %eq.27, bf16[26,2,42,128]{3,1,2,0:T(2,128)(2,1)S(1)} %fusion.10, bf16[2,16,32,128]{3,2,0,1:T(8,128)(2,1)S(1)} %slice.168), kind=kOutput, calls=%fused_computation.89 | convolution fusion | flops 302432256 | bytes 2295809 | tf_op jit(solution)/shard_map/transpose | solution.py:82
  76.7 3.0 %fusion.91 = bf16[2,22,38,128]{3,0,2,1:T(2,128)(2,1)S(1)} fusion(bf16[22,2,38,128]{3,0,2,1:T(8,128)(2,1)S(1)} %slice.163, pred[22,38]{1,0:T(8,128)(4,1)S(1)} %broadcast_and_fusion.2), kind=kLoop, calls=%fused_computation.194 | loop fusion | flops 214016 | bytes 856900 | tf_op jit(solution)/shard_map/convert_element_type | solution.py:291
  83.3 2.0 %fusion.55 = bf16[2,18,34,128]{3,0,2,1:T(2,128)(2,1)S(1)} fusion(f32[18,2,34,128]{3,0,2,1:T(8,128)S(1)} %slice.171, pred[18,34]{1,0:T(8,128)(4,1)S(1)} %broadcast_and_fusion.4, bf16[2,22,38,128]{3,0,2,1:T(2,128)(2,1)S(1)} %fusion.91), kind=kLoop, calls=%fused_computation.83 | loop fusion | flops 940032 | bytes 1253988 | tf_op jit(solution)/shard_map/convert_element_type | solution.py:232
  85.3 1.8 %fusion.51 = f32[3,3,128,128]{3,2,1,0:T(8,128)S(1)} fusion(bf16[2,28,44,128]{3,2,0,1:T(8,128)(2,1)S(1)} %copy-done.9, bf16[2,18,34,128]{3,0,2,1:T(2,128)(2,1)S(1)} %fusion.55), kind=kOutput, calls=%fused_computation.78 | convolution fusion | flops 301989888 | bytes 1540096 | tf_op jit(solution)/shard_map/transpose | solution.py:82
  87.1 1.8 %multiply_convert_fusion = (bf16[3,3,128,128]{3,2,1,0:T(8,128)(2,1)S(1)}, f32[3,3,128,128]{3,2,1,0:T(8,128)S(1)}) fusion(f32[3,3,128,128]{3,2,1,0:T(8,128)S(1)} %fusion.51, pred[]{:T(512)S(6)} %eq.27, bf16[2,22,38,128]{3,0,2,1:T(2,128)(2,1)S(1)} %copy-done.11, bf16[2,28,44,128]{3,2,0,1:T(8,128)(2,1)S(1)} %get-tuple-element.16), kind=kOutput, calls=%fused_computation.86 | convolution fusion | flops 302432256 | bytes 2424833 | tf_op jit(solution)/shard_map/transpose | solution.py:82
  89.5 1.6 %collective-permute-start.15 = (bf16[73728]{0:T(1024)(128)(2,1)S(1)}, bf16[73728]{0:T(1024)(128)(2,1)S(1)}, u32[]{:S(2)}, u32[]{:S(2)}) collective-permute-start(bf16[73728]{0:T(1024)(128)(2,1)S(1)} %select_convert_fusion), channel_id=1, source_target_pairs={{0,4},{4,0},{8,12},{12,8},{1,5},{5,1},{9,13},{13,9},{2,6},{6,2},{1... | collective-permute-start | bytes 442376 | tf_op jit(solution)/shard_map/ppermute | solution.py:100
  92.7 2.6 %collective-permute-done.15 = bf16[73728]{0:T(1024)(128)(2,1)S(1)} collective-permute-done((bf16[73728]{0:T(1024)(128)(2,1)S(1)}, bf16[73728]{0:T(1024)(128)(2,1)S(1)}, u32[]{:S(2)}, u32[]{:S(2)}) %collective-permute-start.15) | collective-permute-done | bytes 147488 | tf_op jit(solution)/shard_map/ppermute | solution.py:100
  95.4 1.6 %collective-permute-start.16 = (bf16[36864]{0:T(1024)(128)(2,1)S(1)}, bf16[36864]{0:T(1024)(128)(2,1)S(1)}, u32[]{:S(2)}, u32[]{:S(2)}) collective-permute-start(bf16[36864]{0:T(1024)(128)(2,1)S(1)} %select_convert_fusion.4), channel_id=1, source_target_pairs={{0,1},{1,0},{2,3},{3,2},{4,5},{5,4},{6,7},{7,6},{8,9},{9,8},{10,11... | collective-permute-start | bytes 221192 | tf_op jit(solution)/shard_map/ppermute | solution.py:100
  97.2 1.6 %collective-permute-start.9 = (bf16[73728]{0:T(1024)(128)(2,1)S(1)}, bf16[73728]{0:T(1024)(128)(2,1)S(1)}, u32[]{:S(2)}, u32[]{:S(2)}) collective-permute-start(bf16[73728]{0:T(1024)(128)(2,1)S(1)} %select_convert_fusion.2), channel_id=1, source_target_pairs={{0,4},{4,0},{8,12},{12,8},{1,5},{5,1},{9,13},{13,9},{2,6},{6,2},{1... | collective-permute-start | bytes 442376 | tf_op jit(solution)/shard_map/ppermute | solution.py:100
  99.9 2.5 %collective-permute-done.9 = bf16[73728]{0:T(1024)(128)(2,1)S(1)} collective-permute-done((bf16[73728]{0:T(1024)(128)(2,1)S(1)}, bf16[73728]{0:T(1024)(128)(2,1)S(1)}, u32[]{:S(2)}, u32[]{:S(2)}) %collective-permute-start.9) | collective-permute-done | bytes 147488 | tf_op jit(solution)/shard_map/ppermute | solution.py:100
  103.9 3.0 %collective-permute-done.10 = bf16[36864]{0:T(1024)(128)(2,1)S(1)} collective-permute-done((bf16[36864]{0:T(1024)(128)(2,1)S(1)}, bf16[36864]{0:T(1024)(128)(2,1)S(1)}, u32[]{:S(2)}, u32[]{:S(2)}) %collective-permute-start.10) | collective-permute-done | bytes 73760 | tf_op jit(solution)/shard_map/ppermute | solution.py:100
  107.1 2.2 %collective-permute-start.18 = (bf16[36864]{0:T(1024)(128)(2,1)S(1)}, bf16[36864]{0:T(1024)(128)(2,1)S(1)}, u32[]{:S(2)}, u32[]{:S(2)}) collective-permute-start(bf16[36864]{0:T(1024)(128)(2,1)S(1)} %add_convert_fusion.1), channel_id=1, source_target_pairs={{0,2},{1,3},{2,0},{3,1},{4,6},{5,7},{6,4},{7,5},{8,10},{9,11},{10,... | collective-permute-start | bytes 221192 | tf_op jit(solution)/shard_map/ppermute | solution.py:100
  109.2 2.1 %collective-permute-done.11 = bf16[36864]{0:T(1024)(128)(2,1)S(1)} collective-permute-done((bf16[36864]{0:T(1024)(128)(2,1)S(1)}, bf16[36864]{0:T(1024)(128)(2,1)S(1)}, u32[]{:S(2)}, u32[]{:S(2)}) %collective-permute-start.11) | collective-permute-done | bytes 73760 | tf_op jit(solution)/shard_map/ppermute | solution.py:100
  114.6 2.9 %collective-permute-done.12 = bf16[36864]{0:T(1024)(128)(2,1)S(1)} collective-permute-done((bf16[36864]{0:T(1024)(128)(2,1)S(1)}, bf16[36864]{0:T(1024)(128)(2,1)S(1)}, u32[]{:S(2)}, u32[]{:S(2)}) %collective-permute-start.12) | collective-permute-done | bytes 73760 | tf_op jit(solution)/shard_map/ppermute | solution.py:100
  118.6 1.6 %collective-permute-start.20 = (bf16[73728]{0:T(1024)(128)(2,1)S(1)}, bf16[73728]{0:T(1024)(128)(2,1)S(1)}, u32[]{:S(2)}, u32[]{:S(2)}) collective-permute-start(bf16[73728]{0:T(1024)(128)(2,1)S(1)} %maximum_select_fusion.4), channel_id=1, source_target_pairs={{0,4},{4,0},{8,12},{12,8},{1,5},{5,1},{9,13},{13,9},{2,6},{6,2},{1... | collective-permute-start | bytes 442376 | tf_op jit(solution)/shard_map/ppermute | solution.py:100
  120.2 1.8 %collective-permute-done.13 = bf16[36864]{0:T(1024)(128)(2,1)S(1)} collective-permute-done((bf16[36864]{0:T(1024)(128)(2,1)S(1)}, bf16[36864]{0:T(1024)(128)(2,1)S(1)}, u32[]{:S(2)}, u32[]{:S(2)}) %collective-permute-start.13) | collective-permute-done | bytes 73760 | tf_op jit(solution)/shard_map/ppermute | solution.py:100
  124.2 3.0 %collective-permute-done.14 = bf16[73728]{0:T(1024)(128)(2,1)S(1)} collective-permute-done((bf16[73728]{0:T(1024)(128)(2,1)S(1)}, bf16[73728]{0:T(1024)(128)(2,1)S(1)}, u32[]{:S(2)}, u32[]{:S(2)}) %collective-permute-start.14) | collective-permute-done | bytes 147488 | tf_op jit(solution)/shard_map/ppermute | solution.py:100
  (194 shorter events, 42.2 us)
Async XLA Ops:
  0.6 2.5 %copy-start = (bf16[4,16,32,128]{3,2,1,0:T(8,128)(2,1)S(1)}, bf16[4,16,32,128]{3,2,1,0:T(8,128)(2,1)}, u32[]{:S(2)}) copy-start(bf16[4,16,32,128]{3,2,1,0:T(8,128)(2,1)} %param.6) | copy-start | bytes 1572868
  1.9 2.0 %collective-permute-start = (bf16[2,16,32,128]{3,2,0,1:T(8,128)(2,1)S(1)}, bf16[2,16,32,128]{3,2,0,1:T(8,128)(2,1)S(1)}, u32[]{:S(2)}, u32[]{:S(2)}) collective-permute-start(bf16[2,16,32,128]{3,2,0,1:T(8,128)(2,1)S(1)} %bitcast.166), channel_id=1, source_target_pairs={{0,16},{16,0},{1,17},{17,1},{2,18},{18,2},{3,19},{19,3},{4,20},{20... | collective-permute-start | bytes 786440 | tf_op jit(solution)/shard_map/ppermute | solution.py:254
  2.4 26.1 %collective-permute-start.5 = (bf16[2,3,3,128,128]{4,3,2,1,0:T(8,128)(2,1)S(1)}, bf16[2,3,3,128,128]{4,3,2,1,0:T(8,128)(2,1)}, u32[]{:S(2)}, u32[]{:S(2)}) collective-permute-start(bf16[2,3,3,128,128]{4,3,2,1,0:T(8,128)(2,1)S(1)} %copy-done.20), channel_id=1, source_target_pairs={{0,16},{16,0},{1,17},{17,1},{2,18},{18,2},{3,19},{19,3},{4,20},{20... | collective-permute-start | bytes 1769480 | tf_op jit(solution)/shard_map/ppermute | solution.py:254
  4.0 11.3 %collective-permute-start.1 = (bf16[6,6,32,128]{3,2,0,1:T(8,128)(2,1)S(1)}, bf16[6,6,32,128]{3,2,0,1:T(8,128)(2,1)S(1)}, u32[]{:S(2)}, u32[]{:S(2)}) collective-permute-start(bf16[6,6,32,128]{3,2,0,1:T(8,128)(2,1)S(1)} %get-tuple-element.22), channel_id=1, source_target_pairs={{0,4},{1,5},{2,6},{3,7},{4,8},{5,9},{6,10},{7,11},{8,12},{9,13},{1... | collective-permute-start | bytes 884744 | tf_op jit(solution)/shard_map/ppermute | solution.py:43
  8.8 14.7 %collective-permute-start.2 = (bf16[6,6,32,128]{3,2,0,1:T(8,128)(2,1)S(1)}, bf16[6,6,32,128]{3,2,0,1:T(8,128)(2,1)S(1)}, u32[]{:S(2)}, u32[]{:S(2)}) collective-permute-start(bf16[6,6,32,128]{3,2,0,1:T(8,128)(2,1)S(1)} %get-tuple-element.23), channel_id=1, source_target_pairs={{4,0},{5,1},{6,2},{7,3},{8,4},{9,5},{10,6},{11,7},{12,8},{13,9},{1... | collective-permute-start | bytes 884744 | tf_op jit(solution)/shard_map/ppermute | solution.py:43
  15.3 22.7 %copy-start.1 = (bf16[6,6,32,128]{3,2,0,1:T(8,128)(2,1)}, bf16[6,6,32,128]{3,2,0,1:T(8,128)(2,1)S(1)}, u32[]{:S(2)}) copy-start(bf16[6,6,32,128]{3,2,0,1:T(8,128)(2,1)S(1)} %collective-permute-done.1) | copy-start | bytes 884740
  23.6 14.5 %copy-start.3 = (bf16[6,6,32,128]{3,2,0,1:T(8,128)(2,1)}, bf16[6,6,32,128]{3,2,0,1:T(8,128)(2,1)S(1)}, u32[]{:S(2)}) copy-start(bf16[6,6,32,128]{3,2,0,1:T(8,128)(2,1)S(1)} %collective-permute-done.2) | copy-start | bytes 884740
  23.7 10.2 %collective-permute-start.3 = (bf16[6,28,6,128]{3,2,0,1:T(8,128)(2,1)S(1)}, bf16[6,28,6,128]{3,2,0,1:T(8,128)(2,1)S(1)}, u32[]{:S(2)}, u32[]{:S(2)}) collective-permute-start(bf16[6,28,6,128]{3,2,0,1:T(8,128)(2,1)S(1)} %get-tuple-element.18), channel_id=1, source_target_pairs={{0,1},{1,2},{2,3},{4,5},{5,6},{6,7},{8,9},{9,10},{10,11},{12,13},{... | collective-permute-start | bytes 774152 | tf_op jit(solution)/shard_map/ppermute | solution.py:43
  27.2 10.8 %collective-permute-start.4 = (bf16[6,28,6,128]{3,2,0,1:T(8,128)(2,1)S(1)}, bf16[6,28,6,128]{3,2,0,1:T(8,128)(2,1)S(1)}, u32[]{:S(2)}, u32[]{:S(2)}) collective-permute-start(bf16[6,28,6,128]{3,2,0,1:T(8,128)(2,1)S(1)} %get-tuple-element.19), channel_id=1, source_target_pairs={{1,0},{2,1},{3,2},{5,4},{6,5},{7,6},{9,8},{10,9},{11,10},{13,12},{... | collective-permute-start | bytes 774152 | tf_op jit(solution)/shard_map/ppermute | solution.py:43
  29.7 12.2 %copy-start.7 = (bf16[2,3,3,128,128]{4,3,2,1,0:T(8,128)(2,1)}, bf16[2,3,3,128,128]{4,3,2,1,0:T(8,128)(2,1)S(1)}, u32[]{:S(2)}) copy-start(bf16[2,3,3,128,128]{4,3,2,1,0:T(8,128)(2,1)S(1)} %get-tuple-element.20) | copy-start | bytes 1769476
  33.9 5.8 %copy-start.16 = (bf16[6,28,6,128]{3,2,0,1:T(8,128)(2,1)}, bf16[6,28,6,128]{3,2,0,1:T(8,128)(2,1)S(1)}, u32[]{:S(2)}) copy-start(bf16[6,28,6,128]{3,2,0,1:T(8,128)(2,1)S(1)} %collective-permute-done.3) | copy-start | bytes 774148
  73.5 2.8 %copy-start.22 = (f32[3,3,128,128]{3,2,1,0:T(8,128)}, f32[3,3,128,128]{3,2,1,0:T(8,128)S(1)}, u32[]{:S(2)}) copy-start(f32[3,3,128,128]{3,2,1,0:T(8,128)S(1)} %fusion.69) | copy-start | bytes 1769476
  73.6 2.9 %copy-start.13 = (bf16[20,16,5,128]{3,1,2,0:T(8,128)(2,1)S(1)}, bf16[20,16,5,128]{3,1,2,0:T(8,128)(2,1)}, u32[]{:S(2)}) copy-start(bf16[20,16,5,128]{3,1,2,0:T(8,128)(2,1)} %copy-done.12) | copy-start | bytes 1228804
  76.3 3.4 %collective-permute-start.6 = (bf16[3,3,128,128]{3,2,1,0:T(8,128)(2,1)}, bf16[3,3,128,128]{3,2,1,0:T(8,128)(2,1)}, u32[]{:S(2)}, u32[]{:S(2)}) collective-permute-start(bf16[3,3,128,128]{3,2,1,0:T(8,128)(2,1)} %get-tuple-element.30), channel_id=1, source_target_pairs={{0,16},{16,0},{1,17},{17,1},{2,18},{18,2},{3,19},{19,3},{4,20},{20... | collective-permute-start | bytes 884744 | tf_op jit(solution)/shard_map/ppermute | solution.py:254
  76.5 3.2 %copy-start.23 = (f32[3,3,128,128]{3,2,1,0:T(8,128)S(1)}, f32[3,3,128,128]{3,2,1,0:T(8,128)}, u32[]{:S(2)}) copy-start(f32[3,3,128,128]{3,2,1,0:T(8,128)} %copy-done.22) | copy-start | bytes 1769476
  76.6 3.2 %copy-start.24 = (f32[3,3,128,128]{3,2,1,0:T(8,128)S(1)}, f32[3,3,128,128]{3,2,1,0:T(8,128)}, u32[]{:S(2)}) copy-start(f32[3,3,128,128]{3,2,1,0:T(8,128)} %get-tuple-element.31) | copy-start | bytes 1769476
  76.7 4.2 %copy-start.15 = (bf16[2,20,36,128]{3,0,2,1:T(2,128)(2,1)S(1)}, bf16[2,20,36,128]{3,0,2,1:T(2,128)(2,1)}, u32[]{:S(2)}) copy-start(bf16[2,20,36,128]{3,0,2,1:T(2,128)(2,1)} %copy-done.14) | copy-start | bytes 1105924
  88.9 2.5 %copy-start.27 = (pred[16,5]{0,1:T(8,128)(4,1)S(1)}, pred[16,5]{0,1:T(8,128)(4,1)}, u32[]{:S(2)}) copy-start(pred[16,5]{0,1:T(8,128)(4,1)} %constant.191) | copy-start | bytes 244
  88.9 8.1 %collective-permute-start.8 = (bf16[3,3,128,128]{3,2,1,0:T(8,128)(2,1)S(1)}, bf16[3,3,128,128]{3,2,1,0:T(8,128)(2,1)S(1)}, u32[]{:S(2)}, u32[]{:S(2)}) collective-permute-start(bf16[3,3,128,128]{3,2,1,0:T(8,128)(2,1)S(1)} %get-tuple-element.32), channel_id=1, source_target_pairs={{0,16},{16,0},{1,17},{17,1},{2,18},{18,2},{3,19},{19,3},{4,20},{20... | collective-permute-start | bytes 884744 | tf_op jit(solution)/shard_map/ppermute | solution.py:254
  89.5 5.8 %collective-permute-start.15 = (bf16[73728]{0:T(1024)(128)(2,1)S(1)}, bf16[73728]{0:T(1024)(128)(2,1)S(1)}, u32[]{:S(2)}, u32[]{:S(2)}) collective-permute-start(bf16[73728]{0:T(1024)(128)(2,1)S(1)} %select_convert_fusion), channel_id=1, source_target_pairs={{0,4},{4,0},{8,12},{12,8},{1,5},{5,1},{9,13},{13,9},{2,6},{6,2},{1... | collective-permute-start | bytes 442376 | tf_op jit(solution)/shard_map/ppermute | solution.py:100
  92.6 10.4 %collective-permute-start.7 = (bf16[2,16,32,128]{3,2,0,1:T(8,128)(2,1)S(1)}, bf16[2,16,32,128]{3,2,0,1:T(8,128)(2,1)S(1)}, u32[]{:S(2)}, u32[]{:S(2)}) collective-permute-start(bf16[2,16,32,128]{3,2,0,1:T(8,128)(2,1)S(1)} %get-tuple-element.25), channel_id=1, source_target_pairs={{0,16},{16,0},{1,17},{17,1},{2,18},{18,2},{3,19},{19,3},{4,20},{20... | collective-permute-start | bytes 786440 | tf_op jit(solution)/shard_map/ppermute | solution.py:254
  95.4 4.4 %collective-permute-start.16 = (bf16[36864]{0:T(1024)(128)(2,1)S(1)}, bf16[36864]{0:T(1024)(128)(2,1)S(1)}, u32[]{:S(2)}, u32[]{:S(2)}) collective-permute-start(bf16[36864]{0:T(1024)(128)(2,1)S(1)} %select_convert_fusion.4), channel_id=1, source_target_pairs={{0,1},{1,0},{2,3},{3,2},{4,5},{5,4},{6,7},{7,6},{8,9},{9,8},{10,11... | collective-permute-start | bytes 221192 | tf_op jit(solution)/shard_map/ppermute | solution.py:100
  97.2 5.2 %collective-permute-start.9 = (bf16[73728]{0:T(1024)(128)(2,1)S(1)}, bf16[73728]{0:T(1024)(128)(2,1)S(1)}, u32[]{:S(2)}, u32[]{:S(2)}) collective-permute-start(bf16[73728]{0:T(1024)(128)(2,1)S(1)} %select_convert_fusion.2), channel_id=1, source_target_pairs={{0,4},{4,0},{8,12},{12,8},{1,5},{5,1},{9,13},{13,9},{2,6},{6,2},{1... | collective-permute-start | bytes 442376 | tf_op jit(solution)/shard_map/ppermute | solution.py:100
  99.9 7.2 %collective-permute-start.17 = (bf16[36864]{0:T(1024)(128)(2,1)S(1)}, bf16[36864]{0:T(1024)(128)(2,1)S(1)}, u32[]{:S(2)}, u32[]{:S(2)}) collective-permute-start(bf16[36864]{0:T(1024)(128)(2,1)S(1)} %add_convert_fusion.2), channel_id=1, source_target_pairs={{0,8},{4,12},{8,0},{12,4},{1,9},{5,13},{9,1},{13,5},{2,10},{6,14},... | collective-permute-start | bytes 221192 | tf_op jit(solution)/shard_map/ppermute | solution.py:100
  102.5 4.4 %collective-permute-start.10 = (bf16[36864]{0:T(1024)(128)(2,1)S(1)}, bf16[36864]{0:T(1024)(128)(2,1)S(1)}, u32[]{:S(2)}, u32[]{:S(2)}) collective-permute-start(bf16[36864]{0:T(1024)(128)(2,1)S(1)} %select_convert_fusion.6), channel_id=1, source_target_pairs={{0,1},{1,0},{2,3},{3,2},{4,5},{5,4},{6,7},{7,6},{8,9},{9,8},{10,11... | collective-permute-start | bytes 221192 | tf_op jit(solution)/shard_map/ppermute | solution.py:100
  106.9 4.4 %collective-permute-start.11 = (bf16[36864]{0:T(1024)(128)(2,1)S(1)}, bf16[36864]{0:T(1024)(128)(2,1)S(1)}, u32[]{:S(2)}, u32[]{:S(2)}) collective-permute-start(bf16[36864]{0:T(1024)(128)(2,1)S(1)} %add_convert_fusion.5), channel_id=1, source_target_pairs={{0,8},{4,12},{8,0},{12,4},{1,9},{5,13},{9,1},{13,5},{2,10},{6,14},... | collective-permute-start | bytes 221192 | tf_op jit(solution)/shard_map/ppermute | solution.py:100
  107.1 6.7 %collective-permute-start.18 = (bf16[36864]{0:T(1024)(128)(2,1)S(1)}, bf16[36864]{0:T(1024)(128)(2,1)S(1)}, u32[]{:S(2)}, u32[]{:S(2)}) collective-permute-start(bf16[36864]{0:T(1024)(128)(2,1)S(1)} %add_convert_fusion.1), channel_id=1, source_target_pairs={{0,2},{1,3},{2,0},{3,1},{4,6},{5,7},{6,4},{7,5},{8,10},{9,11},{10,... | collective-permute-start | bytes 221192 | tf_op jit(solution)/shard_map/ppermute | solution.py:100
  111.4 6.1 %collective-permute-start.12 = (bf16[36864]{0:T(1024)(128)(2,1)S(1)}, bf16[36864]{0:T(1024)(128)(2,1)S(1)}, u32[]{:S(2)}, u32[]{:S(2)}) collective-permute-start(bf16[36864]{0:T(1024)(128)(2,1)S(1)} %add_convert_fusion.4), channel_id=1, source_target_pairs={{0,2},{1,3},{2,0},{3,1},{4,6},{5,7},{6,4},{7,5},{8,10},{9,11},{10,... | collective-permute-start | bytes 221192 | tf_op jit(solution)/shard_map/ppermute | solution.py:100
  113.8 4.8 %collective-permute-start.19 = (bf16[36864]{0:T(1024)(128)(2,1)S(1)}, bf16[36864]{0:T(1024)(128)(2,1)S(1)}, u32[]{:S(2)}, u32[]{:S(2)}) collective-permute-start(bf16[36864]{0:T(1024)(128)(2,1)S(1)} %add_convert_fusion), channel_id=1, source_target_pairs={{0,1},{1,0},{2,3},{3,2},{4,5},{5,4},{6,7},{7,6},{8,9},{9,8},{10,11... | collective-permute-start | bytes 221192 | tf_op jit(solution)/shard_map/ppermute | solution.py:100
  117.5 4.4 %collective-permute-start.13 = (bf16[36864]{0:T(1024)(128)(2,1)S(1)}, bf16[36864]{0:T(1024)(128)(2,1)S(1)}, u32[]{:S(2)}, u32[]{:S(2)}) collective-permute-start(bf16[36864]{0:T(1024)(128)(2,1)S(1)} %add_convert_fusion.3), channel_id=1, source_target_pairs={{0,1},{1,0},{2,3},{3,2},{4,5},{5,4},{6,7},{7,6},{8,9},{9,8},{10,11... | collective-permute-start | bytes 221192 | tf_op jit(solution)/shard_map/ppermute | solution.py:100
  118.6 5.5 %collective-permute-start.20 = (bf16[73728]{0:T(1024)(128)(2,1)S(1)}, bf16[73728]{0:T(1024)(128)(2,1)S(1)}, u32[]{:S(2)}, u32[]{:S(2)}) collective-permute-start(bf16[73728]{0:T(1024)(128)(2,1)S(1)} %maximum_select_fusion.4), channel_id=1, source_target_pairs={{0,4},{4,0},{8,12},{12,8},{1,5},{5,1},{9,13},{13,9},{2,6},{6,2},{1... | collective-permute-start | bytes 442376 | tf_op jit(solution)/shard_map/ppermute | solution.py:100
  122.0 5.2 %collective-permute-start.14 = (bf16[73728]{0:T(1024)(128)(2,1)S(1)}, bf16[73728]{0:T(1024)(128)(2,1)S(1)}, u32[]{:S(2)}, u32[]{:S(2)}) collective-permute-start(bf16[73728]{0:T(1024)(128)(2,1)S(1)} %maximum_select_fusion.3), channel_id=1, source_target_pairs={{0,4},{4,0},{8,12},{12,8},{1,5},{5,1},{9,13},{13,9},{2,6},{6,2},{1... | collective-permute-start | bytes 442376 | tf_op jit(solution)/shard_map/ppermute | solution.py:100
  (22 other events, 27.5 us)

commit v8 on v6

--- a/solution.py
+++ b/solution.py
@@ -261,7 +261,13 @@
     rims = [r + layer_count for r in top_rim]
     group_cotangent = lax.dynamic_slice_in_dim(top_cotangent, section_index * half, half, 0)
     stacked = [by_section(mine, theirs, s) for s in range(2)] + [group_cotangent]
-    stacked = with_rim(jnp.concatenate(stacked, axis=0), rims[1], 0, range(2))
+    stacked = jnp.concatenate(stacked, axis=0)
+    middle = stacked.shape[0] // 2
+    stacked = jnp.concatenate(
+        [with_rim(stacked[:middle], rims[1], 0, range(2)),
+         with_rim(stacked[middle:], rims[1], 0, range(2))],
+        axis=0,
+    )
     firsts = [crop(stacked[:half], rims[1] - rims[0]), stacked[half : 2 * half]]
     top_ext = crop(stacked[2 * half :], rims[1] - top_rim[1])
 

time: 123 us -> 125 us (1.016)
  starting transfers between devices: 40 us -> 46 us
  waiting for transfers between devices: 24.1 us -> 19.6 us
  local copies, waits for them, and re-layouts: 14.1 us -> 12.5 us
  other arithmetic: 25.8 us -> 27.4 us
    ppermute x4 -> x8, starting transfers between devices: 12.6 us -> 25.2 us  [from_neighbours(): parts.append(lax.ppermute(piece, AXES, pairs))]
    ppermute x4 -> x8, waiting for transfers between devices: 10.4 us -> 2.82 us  [from_neighbours(): parts.append(lax.ppermute(piece, AXES, pairs))]
    ppermute x12, starting transfers between devices: 26.1 us -> 19.4 us  [exchange(): return lax.ppermute(values, axis, [(i, i ^ distance) for i in range(count)])]
    ppermute x12, waiting for transfers between devices: 13.7 us -> 16.7 us  [exchange(): return lax.ppermute(values, axis, [(i, i ^ distance) for i in range(count)])]
    unnamed x51 -> x43, local copies, waits for them, and re-layouts: 4.94 us -> 4.44 us
  transfers between devices with their start and end apart: 21 -> 25, of which waited for: 12 -> 11; matrix products, arithmetic and copies ran while one was open for 9% -> 12% of each run, Pallas kernels for 0% -> 0%
where the time goes in v8:
time: 125 us; the launch traced here: 124 us
  starting transfers between devices  46 us (37%)
  other arithmetic  27.4 us (22%)
  waiting for transfers between devices  19.6 us (16%)
  matrix products  17 us (14%)
  local copies, waits for them, and re-layouts  12.5 us (10%)
  between operations  1.79 us (1%)
    ppermute x8, starting transfers between devices, from_neighbours(): parts.append(lax.ppermute(piece, AXES, pairs))  25.2 us
    ppermute x12, starting transfers between devices, exchange(): return lax.ppermute(values, axis, [(i, i ^ distance) for i in range(count)])  19.4 us
    ppermute x12, waiting for transfers between devices, exchange(): return lax.ppermute(values, axis, [(i, i ^ distance) for i in range(count)])  16.7 us
    conv_general_dilated x8, matrix products, convolve(): lax.conv_general_dilated(padded, kernel, (1, 1), 'VALID', dimension_numbe...  9.91 us
    convert_element_type x4, other arithmetic, local_split(): current = current.astype(jnp.bfloat16)  9.08 us
    convert_element_type x4, other arithmetic, section_chain(): signal = signal.astype(jnp.bfloat16)  8.13 us
    transpose x4, matrix products, kernel_terms(): return jnp.transpose(terms, (1, 2, 0, 3))  7.11 us
    unnamed x43, local copies, waits for them, and re-layouts  4.44 us
  transfers between devices with their start and end apart: 25, of which 11 were waited for; matrix products, arithmetic and copies ran while one was open for 12% of the time, Pallas kernels for 0%

profile of v8, /device:TPU:0, one launch (start us, length us, event | category | flops | bytes accessed | tf_op | source)
XLA Modules:
  0.0 124.2 jit_solution(3551021665625063574)
XLA Ops:
  5.9 5.4 %collective-permute-start.5 = (bf16[3,6,32,128]{3,2,0,1:T(8,128)(2,1)S(1)}, bf16[3,6,32,128]{3,2,0,1:T(8,128)(2,1)S(1)}, u32[]{:S(2)}, u32[]{:S(2)}) collective-permute-start(bf16[3,6,32,128]{3,2,0,1:T(8,128)(2,1)S(1)} %get-tuple-element.22), channel_id=1, source_target_pairs={{0,4},{1,5},{2,6},{3,7},{4,8},{5,9},{6,10},{7,11},{8,12},{9,13},{1... | collective-permute-start | bytes 442376 | tf_op jit(solution)/shard_map/ppermute | solution.py:43
  12.7 5.4 %collective-permute-start.1 = (bf16[3,6,32,128]{3,2,0,1:T(8,128)(2,1)S(1)}, bf16[3,6,32,128]{3,2,0,1:T(8,128)(2,1)S(1)}, u32[]{:S(2)}, u32[]{:S(2)}) collective-permute-start(bf16[3,6,32,128]{3,2,0,1:T(8,128)(2,1)S(1)} %get-tuple-element.31), channel_id=1, source_target_pairs={{0,4},{1,5},{2,6},{3,7},{4,8},{5,9},{6,10},{7,11},{8,12},{9,13},{1... | collective-permute-start | bytes 442376 | tf_op jit(solution)/shard_map/ppermute | solution.py:43
  19.7 4.6 %collective-permute-start.7 = (bf16[3,28,6,128]{3,2,0,1:T(8,128)(2,1)S(1)}, bf16[3,28,6,128]{3,2,0,1:T(8,128)(2,1)S(1)}, u32[]{:S(2)}, u32[]{:S(2)}) collective-permute-start(bf16[3,28,6,128]{3,2,0,1:T(8,128)(2,1)S(1)} %get-tuple-element.16), channel_id=1, source_target_pairs={{0,1},{1,2},{2,3},{4,5},{5,6},{6,7},{8,9},{9,10},{10,11},{12,13},{... | collective-permute-start | bytes 387080 | tf_op jit(solution)/shard_map/ppermute | solution.py:43
  25.7 4.6 %collective-permute-start.3 = (bf16[3,28,6,128]{3,2,0,1:T(8,128)(2,1)S(1)}, bf16[3,28,6,128]{3,2,0,1:T(8,128)(2,1)S(1)}, u32[]{:S(2)}, u32[]{:S(2)}) collective-permute-start(bf16[3,28,6,128]{3,2,0,1:T(8,128)(2,1)S(1)} %get-tuple-element.18), channel_id=1, source_target_pairs={{0,1},{1,2},{2,3},{4,5},{5,6},{6,7},{8,9},{9,10},{10,11},{12,13},{... | collective-permute-start | bytes 387080 | tf_op jit(solution)/shard_map/ppermute | solution.py:43
  31.7 1.5 %collective-permute-done.3 = bf16[3,28,6,128]{3,2,0,1:T(8,128)(2,1)S(1)} collective-permute-done((bf16[3,28,6,128]{3,2,0,1:T(8,128)(2,1)S(1)}, bf16[3,28,6,128]{3,2,0,1:T(8,128)(2,1)S(1)}, u32[]{:S(2)}, u32[]{:S(2)}) %collective-permute-start.3) | collective-permute-done | bytes 129056 | tf_op jit(solution)/shard_map/ppermute | solution.py:43
  33.1 1.7 %pad_maximum_fusion = (bf16[2,28,44,128]{3,2,0,1:T(8,128)(2,1)S(1)}, bf16[2,28,44,128]{3,2,0,1:T(8,128)(2,1)S(1)}) fusion(bf16[3,28,6,128]{3,2,0,1:T(8,128)(2,1)S(1)} %collective-permute-done.8, bf16[3,28,6,128]{3,2,0,1:T(8,128)(2,1)S(1)} %collective-permute-done.7, bf16[3,6,32,128]{3,2,0,1:T(8,128)(2,1)S(1)} %collective-permute-done.6, ...), kind=kLoop, calls=%fused_computation.58 | loop fusion | flops 9461760 | bytes 3153920 | tf_op jit(solution)/shard_map/concatenate | solution.py:44
  36.8 1.6 %fusion.29 = bf16[28,2,8,7,128]{4,1,3,2,0:T(2,128)(2,1)} fusion(bf16[28,2,7,2,128]{4,1,3,2,0:T(2,128)(2,1)S(1)} %slice.195, bf16[28,2,8,5,128]{4,1,3,2,0:T(2,128)(2,1)S(1)} %bitcast.137), kind=kLoop, calls=%fused_computation.49 | loop fusion | flops 2408448 | bytes 1576960 | tf_op jit(solution)/shard_map/conv_general_dilated | solution.py:63
  39.4 2.2 %broadcast_select_fusion = (bf16[2,3,3,128,128]{4,3,2,1,0:T(8,128)(2,1)}, bf16[2,3,3,128,128]{4,3,2,1,0:T(8,128)(2,1)S(1)}) fusion(bf16[2,3,3,128,128]{4,3,2,1,0:T(8,128)(2,1)} %param.5, bf16[2,3,3,128,128]{4,3,2,1,0:T(8,128)(2,1)} %collective-permute-done.9, pred[]{:T(512)S(6)} %eq.27, pred[]{:T(512)S(6)} %eq.54), kind=kLoop, calls=%fused_computation.98 | loop fusion | flops 589824 | bytes 2359298 | tf_op jit(solution)/shard_map/jit(_where)/select_n | solution.py:252
  41.6 1.7 %fusion.1 = bf16[26,16,6,128]{3,1,2,0:T(8,128)(2,1)S(1)} fusion(bf16[28,2,8,8,128]{4,1,3,2,0:T(2,128)(2,1)S(1)} %fusion.16, pred[16,6]{0,1:T(8,128)(4,1)S(1)} %copy-done.19, bf16[2,3,3,128,128]{4,3,2,1,0:T(8,128)(2,1)S(1)} %get-tuple-element.13), kind=kOutput, calls=%fused_computation.6 | convolution fusion | flops 736739328 | bytes 1852416 | tf_op jit(solution)/shard_map/conv_general_dilated | solution.py:63
  43.7 1.7 %fusion.11 = bf16[26,2,42,128]{3,1,2,0:T(2,128)(2,1)S(1)} fusion(bf16[26,2,42,128]{3,2,1,0:T(8,128)(2,1)S(1)} %bitcast.129, pred[26,42]{1,0:T(8,128)(4,1)S(1)} %broadcast_and_fusion), kind=kLoop, calls=%fused_computation.27 | loop fusion | flops 279552 | bytes 1119300 | tf_op jit(solution)/shard_map/convert_element_type | solution.py:284
  45.5 1.7 %fusion.102 = bf16[2,26,42,128]{3,0,2,1:T(2,128)(2,1)S(1)} fusion(bf16[26,2,42,128]{3,2,1,0:T(8,128)(2,1)S(1)} %bitcast.130, pred[26,42]{1,0:T(8,128)(4,1)S(1)} %broadcast_and_fusion), kind=kLoop, calls=%fused_computation.219 | loop fusion | flops 279552 | bytes 1119300 | tf_op jit(solution)/shard_map/convert_element_type | solution.py:284
  49.8 2.8 %fusion.19 = bf16[22,2,38,128]{3,1,2,0:T(2,128)(2,1)S(1)} fusion(bf16[22,2,38,128]{3,0,2,1:T(8,128)(2,1)S(1)} %slice.197, pred[22,38]{1,0:T(8,128)(4,1)S(1)} %broadcast_and_fusion.2), kind=kLoop, calls=%fused_computation.39 | loop fusion | flops 214016 | bytes 856900 | tf_op jit(solution)/shard_map/convert_element_type | solution.py:284
  52.6 2.8 %fusion.101 = bf16[2,22,38,128]{3,0,2,1:T(2,128)(2,1)S(1)} fusion(bf16[22,2,38,128]{3,0,2,1:T(8,128)(2,1)S(1)} %slice.197, pred[22,38]{1,0:T(8,128)(4,1)S(1)} %broadcast_and_fusion.2), kind=kLoop, calls=%fused_computation.218 | loop fusion | flops 214016 | bytes 856900 | tf_op jit(solution)/shard_map/convert_element_type | solution.py:284
  56.1 1.6 %fusion.2 = bf16[24,16,6,128]{3,1,2,0:T(8,128)(2,1)S(1)} fusion(bf16[26,2,7,2,128]{4,2,1,3,0:T(8,128)(2,1)S(1)} %slice.184, bf16[26,2,8,6,128]{4,2,1,3,0:T(8,128)(2,1)S(1)} %copy.147, pred[16,6]{0,1:T(8,128)(4,1)S(1)} %copy-done.18, bf16[2,3,3,128,128]{4,3,2,1,0:T(8,128)(2,1)S(1)} %copy-done.3), kind=kOutput, calls=%fused_computation.8 | convolution fusion | flops 682622976 | bytes 1737728 | tf_op jit(solution)/shard_map/conv_general_dilated | solution.py:63
  61.9 3.1 %fusion.22 = bf16[2,22,38,128]{3,0,2,1:T(2,128)(2,1)S(1)} fusion(f32[22,2,38,128]{3,0,2,1:T(8,128)S(1)} %slice.189, pred[22,38]{1,0:T(8,128)(4,1)S(1)} %broadcast_and_fusion.2, bf16[2,26,42,128]{3,0,2,1:T(2,128)(2,1)S(1)} %fusion.102), kind=kLoop, calls=%fused_computation.43 | loop fusion | flops 1284096 | bytes 1712964 | tf_op jit(solution)/shard_map/convert_element_type | solution.py:232
  69.5 1.7 %fusion.34 = bf16[20,2,36,128]{3,1,2,0:T(2,128)(2,1)S(1)} fusion(f32[20,2,36,128]{3,0,2,1:T(8,128)S(1)} %slice.193, pred[20,36]{1,0:T(8,128)(4,1)S(1)} %copy-done.12, bf16[20,2,36,128]{3,0,2,1:T(8,128)(2,1)S(1)} %slice.200), kind=kLoop, calls=%fused_computation.56 | loop fusion | flops 1290240 | bytes 1475280 | tf_op jit(solution)/shard_map/convert_element_type | solution.py:232
  73.2 2.0 %fusion.57 = bf16[2,18,34,128]{3,0,2,1:T(2,128)(2,1)S(1)} fusion(f32[18,2,34,128]{3,0,2,1:T(8,128)S(1)} %slice.203, pred[18,34]{1,0:T(8,128)(4,1)S(1)} %broadcast_and_fusion.4, bf16[2,22,38,128]{3,0,2,1:T(2,128)(2,1)S(1)} %fusion.101), kind=kLoop, calls=%fused_computation.90 | loop fusion | flops 940032 | bytes 1253988 | tf_op jit(solution)/shard_map/convert_element_type | solution.py:232
  75.3 1.7 %fusion.53 = f32[3,3,128,128]{3,2,1,0:T(8,128)S(1)} fusion(bf16[2,28,44,128]{3,2,0,1:T(8,128)(2,1)S(1)} %copy-done.5, bf16[2,18,34,128]{3,0,2,1:T(2,128)(2,1)S(1)} %fusion.57), kind=kOutput, calls=%fused_computation.85 | convolution fusion | flops 301989888 | bytes 1540096 | tf_op jit(solution)/shard_map/transpose | solution.py:82
  79.1 1.8 %fusion.76 = f32[3,3,128,128]{3,2,1,0:T(8,128)S(1)} fusion(bf16[22,2,38,128]{3,1,2,0:T(2,128)(2,1)S(1)} %fusion.19, bf16[2,20,36,128]{3,0,2,1:T(2,128)(2,1)S(1)} %bitcast.156), kind=kOutput, calls=%fused_computation.149 | convolution fusion | flops 301989888 | bytes 1280000 | tf_op jit(solution)/shard_map/transpose | solution.py:82
  80.9 1.8 %multiply_convert_fusion = (bf16[3,3,128,128]{3,2,1,0:T(8,128)(2,1)S(1)}, f32[3,3,128,128]{3,2,1,0:T(8,128)S(1)}) fusion(f32[3,3,128,128]{3,2,1,0:T(8,128)S(1)} %fusion.76, pred[]{:T(512)S(6)} %eq.27, bf16[26,2,42,128]{3,1,2,0:T(2,128)(2,1)S(1)} %fusion.11, bf16[2,16,32,128]{3,2,0,1:T(8,128)(2,1)S(1)} %slice.217), kind=kOutput, calls=%fused_computation.93 | convolution fusion | flops 302432256 | bytes 2295809 | tf_op jit(solution)/shard_map/transpose | solution.py:82
  83.2 1.8 %multiply_convert_fusion.1 = (bf16[3,3,128,128]{3,2,1,0:T(8,128)(2,1)S(1)}, f32[3,3,128,128]{3,2,1,0:T(8,128)S(1)}) fusion(f32[3,3,128,128]{3,2,1,0:T(8,128)S(1)} %fusion.53, pred[]{:T(512)S(6)} %eq.27, bf16[2,22,38,128]{3,0,2,1:T(2,128)(2,1)S(1)} %fusion.22, bf16[2,28,44,128]{3,2,0,1:T(8,128)(2,1)S(1)} %get-tuple-element.15), kind=kOutput, calls=%fused_computation.95 | convolution fusion | flops 302432256 | bytes 2424833 | tf_op jit(solution)/shard_map/transpose | solution.py:82
  86.2 3.0 %collective-permute-start.19 = (bf16[73728]{0:T(1024)(128)(2,1)S(1)}, bf16[73728]{0:T(1024)(128)(2,1)S(1)}, u32[]{:S(2)}, u32[]{:S(2)}) collective-permute-start(bf16[73728]{0:T(1024)(128)(2,1)S(1)} %select_convert_fusion), channel_id=1, source_target_pairs={{0,4},{4,0},{8,12},{12,8},{1,5},{5,1},{9,13},{13,9},{2,6},{6,2},{1... | collective-permute-start | bytes 442376 | tf_op jit(solution)/shard_map/ppermute | solution.py:100
  89.8 4.1 %collective-permute-done.19 = bf16[73728]{0:T(1024)(128)(2,1)S(1)} collective-permute-done((bf16[73728]{0:T(1024)(128)(2,1)S(1)}, bf16[73728]{0:T(1024)(128)(2,1)S(1)}, u32[]{:S(2)}, u32[]{:S(2)}) %collective-permute-start.19) | collective-permute-done | bytes 147488 | tf_op jit(solution)/shard_map/ppermute | solution.py:100
  93.9 2.5 %collective-permute-start.20 = (bf16[36864]{0:T(1024)(128)(2,1)S(1)}, bf16[36864]{0:T(1024)(128)(2,1)S(1)}, u32[]{:S(2)}, u32[]{:S(2)}) collective-permute-start(bf16[36864]{0:T(1024)(128)(2,1)S(1)} %select_convert_fusion.4), channel_id=1, source_target_pairs={{0,1},{1,0},{2,3},{3,2},{4,5},{5,4},{6,7},{7,6},{8,9},{9,8},{10,11... | collective-permute-start | bytes 221192 | tf_op jit(solution)/shard_map/ppermute | solution.py:100
  96.9 2.5 %collective-permute-start.13 = (bf16[36864]{0:T(1024)(128)(2,1)S(1)}, bf16[36864]{0:T(1024)(128)(2,1)S(1)}, u32[]{:S(2)}, u32[]{:S(2)}) collective-permute-start(bf16[36864]{0:T(1024)(128)(2,1)S(1)} %select_convert_fusion.6), channel_id=1, source_target_pairs={{0,1},{1,0},{2,3},{3,2},{4,5},{5,4},{6,7},{7,6},{8,9},{9,8},{10,11... | collective-permute-start | bytes 221192 | tf_op jit(solution)/shard_map/ppermute | solution.py:100
  104.0 2.8 %collective-permute-start.22 = (bf16[36864]{0:T(1024)(128)(2,1)S(1)}, bf16[36864]{0:T(1024)(128)(2,1)S(1)}, u32[]{:S(2)}, u32[]{:S(2)}) collective-permute-start(bf16[36864]{0:T(1024)(128)(2,1)S(1)} %add_convert_fusion.1), channel_id=1, source_target_pairs={{0,2},{1,3},{2,0},{3,1},{4,6},{5,7},{6,4},{7,5},{8,10},{9,11},{10,... | collective-permute-start | bytes 221192 | tf_op jit(solution)/shard_map/ppermute | solution.py:100
  106.9 2.5 %collective-permute-start.15 = (bf16[36864]{0:T(1024)(128)(2,1)S(1)}, bf16[36864]{0:T(1024)(128)(2,1)S(1)}, u32[]{:S(2)}, u32[]{:S(2)}) collective-permute-start(bf16[36864]{0:T(1024)(128)(2,1)S(1)} %add_convert_fusion.4), channel_id=1, source_target_pairs={{0,2},{1,3},{2,0},{3,1},{4,6},{5,7},{6,4},{7,5},{8,10},{9,11},{10,... | collective-permute-start | bytes 221192 | tf_op jit(solution)/shard_map/ppermute | solution.py:100
  109.3 2.3 %collective-permute-done.22 = bf16[36864]{0:T(1024)(128)(2,1)S(1)} collective-permute-done((bf16[36864]{0:T(1024)(128)(2,1)S(1)}, bf16[36864]{0:T(1024)(128)(2,1)S(1)}, u32[]{:S(2)}, u32[]{:S(2)}) %collective-permute-start.22) | collective-permute-done | bytes 73760 | tf_op jit(solution)/shard_map/ppermute | solution.py:100
  113.9 2.2 %collective-permute-done.23 = bf16[36864]{0:T(1024)(128)(2,1)S(1)} collective-permute-done((bf16[36864]{0:T(1024)(128)(2,1)S(1)}, bf16[36864]{0:T(1024)(128)(2,1)S(1)}, u32[]{:S(2)}, u32[]{:S(2)}) %collective-permute-start.23) | collective-permute-done | bytes 73760 | tf_op jit(solution)/shard_map/ppermute | solution.py:100
  116.1 1.7 %collective-permute-start.24 = (bf16[73728]{0:T(1024)(128)(2,1)S(1)}, bf16[73728]{0:T(1024)(128)(2,1)S(1)}, u32[]{:S(2)}, u32[]{:S(2)}) collective-permute-start(bf16[73728]{0:T(1024)(128)(2,1)S(1)} %maximum_select_fusion.4), channel_id=1, source_target_pairs={{0,4},{4,0},{8,12},{12,8},{1,5},{5,1},{9,13},{13,9},{2,6},{6,2},{1... | collective-permute-start | bytes 442376 | tf_op jit(solution)/shard_map/ppermute | solution.py:100
  118.9 2.4 %collective-permute-done.24 = bf16[73728]{0:T(1024)(128)(2,1)S(1)} collective-permute-done((bf16[73728]{0:T(1024)(128)(2,1)S(1)}, bf16[73728]{0:T(1024)(128)(2,1)S(1)}, u32[]{:S(2)}, u32[]{:S(2)}) %collective-permute-start.24) | collective-permute-done | bytes 147488 | tf_op jit(solution)/shard_map/ppermute | solution.py:100
  121.4 1.6 %collective-permute-done.17 = bf16[73728]{0:T(1024)(128)(2,1)S(1)} collective-permute-done((bf16[73728]{0:T(1024)(128)(2,1)S(1)}, bf16[73728]{0:T(1024)(128)(2,1)S(1)}, u32[]{:S(2)}, u32[]{:S(2)}) %collective-permute-start.17) | collective-permute-done | bytes 147488 | tf_op jit(solution)/shard_map/ppermute | solution.py:100
  (178 shorter events, 41.7 us)
Async XLA Ops:
  0.6 3.0 %copy-start = (bf16[4,16,32,128]{3,2,1,0:T(8,128)(2,1)S(1)}, bf16[4,16,32,128]{3,2,1,0:T(8,128)(2,1)}, u32[]{:S(2)}) copy-start(bf16[4,16,32,128]{3,2,1,0:T(8,128)(2,1)} %param.6) | copy-start | bytes 1572868
  1.8 2.7 %collective-permute-start = (bf16[2,16,32,128]{3,2,0,1:T(8,128)(2,1)S(1)}, bf16[2,16,32,128]{3,2,0,1:T(8,128)(2,1)S(1)}, u32[]{:S(2)}, u32[]{:S(2)}) collective-permute-start(bf16[2,16,32,128]{3,2,0,1:T(8,128)(2,1)S(1)} %bitcast.163), channel_id=1, source_target_pairs={{0,16},{16,0},{1,17},{17,1},{2,18},{18,2},{3,19},{19,3},{4,20},{20... | collective-permute-start | bytes 786440 | tf_op jit(solution)/shard_map/ppermute | solution.py:249
  2.4 37.0 %collective-permute-start.9 = (bf16[2,3,3,128,128]{4,3,2,1,0:T(8,128)(2,1)}, bf16[2,3,3,128,128]{4,3,2,1,0:T(8,128)(2,1)}, u32[]{:S(2)}, u32[]{:S(2)}) collective-permute-start(bf16[2,3,3,128,128]{4,3,2,1,0:T(8,128)(2,1)} %param.5), channel_id=1, source_target_pairs={{0,16},{16,0},{1,17},{17,1},{2,18},{18,2},{3,19},{19,3},{4,20},{20... | collective-permute-start | bytes 1769480 | tf_op jit(solution)/shard_map/ppermute | solution.py:249
  4.6 13.7 %collective-permute-start.6 = (bf16[3,6,32,128]{3,2,0,1:T(8,128)(2,1)S(1)}, bf16[3,6,32,128]{3,2,0,1:T(8,128)(2,1)S(1)}, u32[]{:S(2)}, u32[]{:S(2)}) collective-permute-start(bf16[3,6,32,128]{3,2,0,1:T(8,128)(2,1)S(1)} %get-tuple-element.23), channel_id=1, source_target_pairs={{4,0},{5,1},{6,2},{7,3},{8,4},{9,5},{10,6},{11,7},{12,8},{13,9},{1... | collective-permute-start | bytes 442376 | tf_op jit(solution)/shard_map/ppermute | solution.py:43
  5.9 12.4 %collective-permute-start.5 = (bf16[3,6,32,128]{3,2,0,1:T(8,128)(2,1)S(1)}, bf16[3,6,32,128]{3,2,0,1:T(8,128)(2,1)S(1)}, u32[]{:S(2)}, u32[]{:S(2)}) collective-permute-start(bf16[3,6,32,128]{3,2,0,1:T(8,128)(2,1)S(1)} %get-tuple-element.22), channel_id=1, source_target_pairs={{0,4},{1,5},{2,6},{3,7},{4,8},{5,9},{6,10},{7,11},{8,12},{9,13},{1... | collective-permute-start | bytes 442376 | tf_op jit(solution)/shard_map/ppermute | solution.py:43
  11.4 12.8 %collective-permute-start.2 = (bf16[3,6,32,128]{3,2,0,1:T(8,128)(2,1)S(1)}, bf16[3,6,32,128]{3,2,0,1:T(8,128)(2,1)S(1)}, u32[]{:S(2)}, u32[]{:S(2)}) collective-permute-start(bf16[3,6,32,128]{3,2,0,1:T(8,128)(2,1)S(1)} %get-tuple-element.30), channel_id=1, source_target_pairs={{4,0},{5,1},{6,2},{7,3},{8,4},{9,5},{10,6},{11,7},{12,8},{13,9},{1... | collective-permute-start | bytes 442376 | tf_op jit(solution)/shard_map/ppermute | solution.py:43
  12.7 11.5 %collective-permute-start.1 = (bf16[3,6,32,128]{3,2,0,1:T(8,128)(2,1)S(1)}, bf16[3,6,32,128]{3,2,0,1:T(8,128)(2,1)S(1)}, u32[]{:S(2)}, u32[]{:S(2)}) collective-permute-start(bf16[3,6,32,128]{3,2,0,1:T(8,128)(2,1)S(1)} %get-tuple-element.31), channel_id=1, source_target_pairs={{0,4},{1,5},{2,6},{3,7},{4,8},{5,9},{6,10},{7,11},{8,12},{9,13},{1... | collective-permute-start | bytes 442376 | tf_op jit(solution)/shard_map/ppermute | solution.py:43
  18.3 13.4 %copy-start.11 = (bf16[3,6,32,128]{3,2,0,1:T(8,128)(2,1)}, bf16[3,6,32,128]{3,2,0,1:T(8,128)(2,1)S(1)}, u32[]{:S(2)}) copy-start(bf16[3,6,32,128]{3,2,0,1:T(8,128)(2,1)S(1)} %collective-permute-done.5) | copy-start | bytes 442372
  18.4 11.9 %collective-permute-start.8 = (bf16[3,28,6,128]{3,2,0,1:T(8,128)(2,1)S(1)}, bf16[3,28,6,128]{3,2,0,1:T(8,128)(2,1)S(1)}, u32[]{:S(2)}, u32[]{:S(2)}) collective-permute-start(bf16[3,28,6,128]{3,2,0,1:T(8,128)(2,1)S(1)} %get-tuple-element.17), channel_id=1, source_target_pairs={{1,0},{2,1},{3,2},{5,4},{6,5},{7,6},{9,8},{10,9},{11,10},{13,12},{... | collective-permute-start | bytes 387080 | tf_op jit(solution)/shard_map/ppermute | solution.py:43
  19.7 10.6 %collective-permute-start.7 = (bf16[3,28,6,128]{3,2,0,1:T(8,128)(2,1)S(1)}, bf16[3,28,6,128]{3,2,0,1:T(8,128)(2,1)S(1)}, u32[]{:S(2)}, u32[]{:S(2)}) collective-permute-start(bf16[3,28,6,128]{3,2,0,1:T(8,128)(2,1)S(1)} %get-tuple-element.16), channel_id=1, source_target_pairs={{0,1},{1,2},{2,3},{4,5},{5,6},{6,7},{8,9},{9,10},{10,11},{12,13},{... | collective-permute-start | bytes 387080 | tf_op jit(solution)/shard_map/ppermute | solution.py:43
  24.4 7.3 %collective-permute-start.4 = (bf16[3,28,6,128]{3,2,0,1:T(8,128)(2,1)S(1)}, bf16[3,28,6,128]{3,2,0,1:T(8,128)(2,1)S(1)}, u32[]{:S(2)}, u32[]{:S(2)}) collective-permute-start(bf16[3,28,6,128]{3,2,0,1:T(8,128)(2,1)S(1)} %get-tuple-element.19), channel_id=1, source_target_pairs={{1,0},{2,1},{3,2},{5,4},{6,5},{7,6},{9,8},{10,9},{11,10},{13,12},{... | collective-permute-start | bytes 387080 | tf_op jit(solution)/shard_map/ppermute | solution.py:43
  25.7 7.5 %collective-permute-start.3 = (bf16[3,28,6,128]{3,2,0,1:T(8,128)(2,1)S(1)}, bf16[3,28,6,128]{3,2,0,1:T(8,128)(2,1)S(1)}, u32[]{:S(2)}, u32[]{:S(2)}) collective-permute-start(bf16[3,28,6,128]{3,2,0,1:T(8,128)(2,1)S(1)} %get-tuple-element.18), channel_id=1, source_target_pairs={{0,1},{1,2},{2,3},{4,5},{5,6},{6,7},{8,9},{9,10},{10,11},{12,13},{... | collective-permute-start | bytes 387080 | tf_op jit(solution)/shard_map/ppermute | solution.py:43
  31.7 3.1 %copy-start.7 = (bf16[3,28,6,128]{3,2,0,1:T(8,128)(2,1)}, bf16[3,28,6,128]{3,2,0,1:T(8,128)(2,1)S(1)}, u32[]{:S(2)}) copy-start(bf16[3,28,6,128]{3,2,0,1:T(8,128)(2,1)S(1)} %collective-permute-done.4) | copy-start | bytes 387076
  39.4 2.2 %copy-start.19 = (pred[16,6]{0,1:T(8,128)(4,1)S(1)}, pred[16,6]{0,1:T(8,128)(4,1)}, u32[]{:S(2)}) copy-start(pred[16,6]{0,1:T(8,128)(4,1)} %constant.196) | copy-start | bytes 292
  43.7 3.5 %copy-start.1 = (bf16[2,3,3,128,128]{4,3,2,1,0:T(8,128)(2,1)S(1)}, bf16[2,3,3,128,128]{4,3,2,1,0:T(8,128)(2,1)}, u32[]{:S(2)}) copy-start(bf16[2,3,3,128,128]{4,3,2,1,0:T(8,128)(2,1)} %get-tuple-element.12) | copy-start | bytes 1769476
  43.7 3.5 %copy-start.3 = (bf16[2,3,3,128,128]{4,3,2,1,0:T(8,128)(2,1)S(1)}, bf16[2,3,3,128,128]{4,3,2,1,0:T(8,128)(2,1)}, u32[]{:S(2)}) copy-start(bf16[2,3,3,128,128]{4,3,2,1,0:T(8,128)(2,1)} %copy-done.2) | copy-start | bytes 1769476
  73.1 2.1 %copy-start.5 = (bf16[2,28,44,128]{3,2,0,1:T(8,128)(2,1)S(1)}, bf16[2,28,44,128]{3,2,0,1:T(8,128)(2,1)}, u32[]{:S(2)}) copy-start(bf16[2,28,44,128]{3,2,0,1:T(8,128)(2,1)} %copy-done.4) | copy-start | bytes 1892356
  79.0 6.1 %collective-permute-start.10 = (bf16[2,16,32,128]{3,2,0,1:T(8,128)(2,1)S(1)}, bf16[2,16,32,128]{3,2,0,1:T(8,128)(2,1)S(1)}, u32[]{:S(2)}, u32[]{:S(2)}) collective-permute-start(bf16[2,16,32,128]{3,2,0,1:T(8,128)(2,1)S(1)} %get-tuple-element.21), channel_id=1, source_target_pairs={{0,16},{16,0},{1,17},{17,1},{2,18},{18,2},{3,19},{19,3},{4,20},{20... | collective-permute-start | bytes 786440 | tf_op jit(solution)/shard_map/ppermute | solution.py:249
  82.7 3.3 %collective-permute-start.18 = (bf16[3,3,128,128]{3,2,1,0:T(8,128)(2,1)S(1)}, bf16[3,3,128,128]{3,2,1,0:T(8,128)(2,1)S(1)}, u32[]{:S(2)}, u32[]{:S(2)}) collective-permute-start(bf16[3,3,128,128]{3,2,1,0:T(8,128)(2,1)S(1)} %get-tuple-element.34), channel_id=1, source_target_pairs={{0,16},{16,0},{1,17},{17,1},{2,18},{18,2},{3,19},{19,3},{4,20},{20... | collective-permute-start | bytes 884744 | tf_op jit(solution)/shard_map/ppermute | solution.py:249
  85.0 4.1 %collective-permute-start.11 = (bf16[3,3,128,128]{3,2,1,0:T(8,128)(2,1)S(1)}, bf16[3,3,128,128]{3,2,1,0:T(8,128)(2,1)S(1)}, u32[]{:S(2)}, u32[]{:S(2)}) collective-permute-start(bf16[3,3,128,128]{3,2,1,0:T(8,128)(2,1)S(1)} %get-tuple-element.36), channel_id=1, source_target_pairs={{0,16},{16,0},{1,17},{17,1},{2,18},{18,2},{3,19},{19,3},{4,20},{20... | collective-permute-start | bytes 884744 | tf_op jit(solution)/shard_map/ppermute | solution.py:249
  86.2 7.7 %collective-permute-start.19 = (bf16[73728]{0:T(1024)(128)(2,1)S(1)}, bf16[73728]{0:T(1024)(128)(2,1)S(1)}, u32[]{:S(2)}, u32[]{:S(2)}) collective-permute-start(bf16[73728]{0:T(1024)(128)(2,1)S(1)} %select_convert_fusion), channel_id=1, source_target_pairs={{0,4},{4,0},{8,12},{12,8},{1,5},{5,1},{9,13},{13,9},{2,6},{6,2},{1... | collective-permute-start | bytes 442376 | tf_op jit(solution)/shard_map/ppermute | solution.py:100
  89.3 7.5 %collective-permute-start.12 = (bf16[73728]{0:T(1024)(128)(2,1)S(1)}, bf16[73728]{0:T(1024)(128)(2,1)S(1)}, u32[]{:S(2)}, u32[]{:S(2)}) collective-permute-start(bf16[73728]{0:T(1024)(128)(2,1)S(1)} %select_convert_fusion.2), channel_id=1, source_target_pairs={{0,4},{4,0},{8,12},{12,8},{1,5},{5,1},{9,13},{13,9},{2,6},{6,2},{1... | collective-permute-start | bytes 442376 | tf_op jit(solution)/shard_map/ppermute | solution.py:100
  93.9 5.5 %collective-permute-start.20 = (bf16[36864]{0:T(1024)(128)(2,1)S(1)}, bf16[36864]{0:T(1024)(128)(2,1)S(1)}, u32[]{:S(2)}, u32[]{:S(2)}) collective-permute-start(bf16[36864]{0:T(1024)(128)(2,1)S(1)} %select_convert_fusion.4), channel_id=1, source_target_pairs={{0,1},{1,0},{2,3},{3,2},{4,5},{5,4},{6,7},{7,6},{8,9},{9,8},{10,11... | collective-permute-start | bytes 221192 | tf_op jit(solution)/shard_map/ppermute | solution.py:100
  96.9 4.9 %collective-permute-start.13 = (bf16[36864]{0:T(1024)(128)(2,1)S(1)}, bf16[36864]{0:T(1024)(128)(2,1)S(1)}, u32[]{:S(2)}, u32[]{:S(2)}) collective-permute-start(bf16[36864]{0:T(1024)(128)(2,1)S(1)} %select_convert_fusion.6), channel_id=1, source_target_pairs={{0,1},{1,0},{2,3},{3,2},{4,5},{5,4},{6,7},{7,6},{8,9},{9,8},{10,11... | collective-permute-start | bytes 221192 | tf_op jit(solution)/shard_map/ppermute | solution.py:100
  99.5 4.5 %collective-permute-start.21 = (bf16[36864]{0:T(1024)(128)(2,1)S(1)}, bf16[36864]{0:T(1024)(128)(2,1)S(1)}, u32[]{:S(2)}, u32[]{:S(2)}) collective-permute-start(bf16[36864]{0:T(1024)(128)(2,1)S(1)} %add_convert_fusion.2), channel_id=1, source_target_pairs={{0,8},{4,12},{8,0},{12,4},{1,9},{5,13},{9,1},{13,5},{2,10},{6,14},... | collective-permute-start | bytes 221192 | tf_op jit(solution)/shard_map/ppermute | solution.py:100
  101.8 5.0 %collective-permute-start.14 = (bf16[36864]{0:T(1024)(128)(2,1)S(1)}, bf16[36864]{0:T(1024)(128)(2,1)S(1)}, u32[]{:S(2)}, u32[]{:S(2)}) collective-permute-start(bf16[36864]{0:T(1024)(128)(2,1)S(1)} %add_convert_fusion.5), channel_id=1, source_target_pairs={{0,8},{4,12},{8,0},{12,4},{1,9},{5,13},{9,1},{13,5},{2,10},{6,14},... | collective-permute-start | bytes 221192 | tf_op jit(solution)/shard_map/ppermute | solution.py:100
  104.0 7.6 %collective-permute-start.22 = (bf16[36864]{0:T(1024)(128)(2,1)S(1)}, bf16[36864]{0:T(1024)(128)(2,1)S(1)}, u32[]{:S(2)}, u32[]{:S(2)}) collective-permute-start(bf16[36864]{0:T(1024)(128)(2,1)S(1)} %add_convert_fusion.1), channel_id=1, source_target_pairs={{0,2},{1,3},{2,0},{3,1},{4,6},{5,7},{6,4},{7,5},{8,10},{9,11},{10,... | collective-permute-start | bytes 221192 | tf_op jit(solution)/shard_map/ppermute | solution.py:100
  106.9 6.3 %collective-permute-start.15 = (bf16[36864]{0:T(1024)(128)(2,1)S(1)}, bf16[36864]{0:T(1024)(128)(2,1)S(1)}, u32[]{:S(2)}, u32[]{:S(2)}) collective-permute-start(bf16[36864]{0:T(1024)(128)(2,1)S(1)} %add_convert_fusion.4), channel_id=1, source_target_pairs={{0,2},{1,3},{2,0},{3,1},{4,6},{5,7},{6,4},{7,5},{8,10},{9,11},{10,... | collective-permute-start | bytes 221192 | tf_op jit(solution)/shard_map/ppermute | solution.py:100
  111.7 4.4 %collective-permute-start.23 = (bf16[36864]{0:T(1024)(128)(2,1)S(1)}, bf16[36864]{0:T(1024)(128)(2,1)S(1)}, u32[]{:S(2)}, u32[]{:S(2)}) collective-permute-start(bf16[36864]{0:T(1024)(128)(2,1)S(1)} %add_convert_fusion), channel_id=1, source_target_pairs={{0,1},{1,0},{2,3},{3,2},{4,5},{5,4},{6,7},{7,6},{8,9},{9,8},{10,11... | collective-permute-start | bytes 221192 | tf_op jit(solution)/shard_map/ppermute | solution.py:100
  113.2 4.6 %collective-permute-start.16 = (bf16[36864]{0:T(1024)(128)(2,1)S(1)}, bf16[36864]{0:T(1024)(128)(2,1)S(1)}, u32[]{:S(2)}, u32[]{:S(2)}) collective-permute-start(bf16[36864]{0:T(1024)(128)(2,1)S(1)} %add_convert_fusion.3), channel_id=1, source_target_pairs={{0,1},{1,0},{2,3},{3,2},{4,5},{5,4},{6,7},{7,6},{8,9},{9,8},{10,11... | collective-permute-start | bytes 221192 | tf_op jit(solution)/shard_map/ppermute | solution.py:100
  116.1 5.2 %collective-permute-start.24 = (bf16[73728]{0:T(1024)(128)(2,1)S(1)}, bf16[73728]{0:T(1024)(128)(2,1)S(1)}, u32[]{:S(2)}, u32[]{:S(2)}) collective-permute-start(bf16[73728]{0:T(1024)(128)(2,1)S(1)} %maximum_select_fusion.4), channel_id=1, source_target_pairs={{0,4},{4,0},{8,12},{12,8},{1,5},{5,1},{9,13},{13,9},{2,6},{6,2},{1... | collective-permute-start | bytes 442376 | tf_op jit(solution)/shard_map/ppermute | solution.py:100
  117.8 5.2 %collective-permute-start.17 = (bf16[73728]{0:T(1024)(128)(2,1)S(1)}, bf16[73728]{0:T(1024)(128)(2,1)S(1)}, u32[]{:S(2)}, u32[]{:S(2)}) collective-permute-start(bf16[73728]{0:T(1024)(128)(2,1)S(1)} %maximum_select_fusion.3), channel_id=1, source_target_pairs={{0,4},{4,0},{8,12},{12,8},{1,5},{5,1},{9,13},{13,9},{2,6},{6,2},{1... | collective-permute-start | bytes 442376 | tf_op jit(solution)/shard_map/ppermute | solution.py:100
  (13 other events, 13.9 us)

commit v9 on v6

--- a/solution.py
+++ b/solution.py
@@ -92,7 +92,7 @@
     for axis, dim in (("row", 1), ("col", 2)):
         distance = 1
         while distance < shape[dim]:
-            (halving if distance == 1 else doubling).append((axis, distance))
+            (halving if axis == "row" else doubling).append((axis, distance))
             distance *= 2
 
     def exchange(values, axis, distance):

time: 123 us -> 124 us (level)
  starting transfers between devices: 40 us -> 41.9 us
  waiting for transfers between devices: 24.1 us -> 22.5 us
    ppermute x12, starting transfers between devices: 26.1 us -> 28 us  [exchange(): return lax.ppermute(values, axis, [(i, i ^ distance) for i in range(count)])]
    ppermute x12, waiting for transfers between devices: 13.7 us -> 12.1 us  [exchange(): return lax.ppermute(values, axis, [(i, i ^ distance) for i in range(count)])]
  transfers between devices with their start and end apart: 21 -> 21, of which waited for: 12 -> 11; matrix products, arithmetic and copies ran while one was open for 9% -> 9% of each run, Pallas kernels for 0% -> 0%
where the time goes in v9:
time: 124 us; the launch traced here: 123 us
  starting transfers between devices  41.9 us (34%)
  other arithmetic  25.8 us (21%)
  waiting for transfers between devices  22.5 us (18%)
  matrix products  17.1 us (14%)
  local copies, waits for them, and re-layouts  14.1 us (11%)
  between operations  1.7 us (1%)
    ppermute x12, starting transfers between devices, exchange(): return lax.ppermute(values, axis, [(i, i ^ distance) for i in range(count)])  28 us
    ppermute x4, starting transfers between devices, from_neighbours(): parts.append(lax.ppermute(piece, AXES, pairs))  12.6 us
    ppermute x12, waiting for transfers between devices, exchange(): return lax.ppermute(values, axis, [(i, i ^ distance) for i in range(count)])  12.1 us
    ppermute x4, waiting for transfers between devices, from_neighbours(): parts.append(lax.ppermute(piece, AXES, pairs))  10.4 us
    conv_general_dilated x8, matrix products, convolve(): lax.conv_general_dilated(padded, kernel, (1, 1), 'VALID', dimension_numbe...  9.95 us
    convert_element_type x4, other arithmetic, local_split(): current = current.astype(jnp.bfloat16)  9.08 us
    convert_element_type x4, other arithmetic, section_chain(): signal = signal.astype(jnp.bfloat16)  8.96 us
    transpose x4, matrix products, kernel_terms(): return jnp.transpose(terms, (1, 2, 0, 3))  7.12 us
  transfers between devices with their start and end apart: 21, of which 11 were waited for; matrix products, arithmetic and copies ran while one was open for 9% of the time, Pallas kernels for 0%

profile of v9, /device:TPU:0, one launch (start us, length us, event | category | flops | bytes accessed | tf_op | source)
XLA Modules:
  0.0 123.1 jit_solution(8050700783339498461)
XLA Ops:
  5.4 5.4 %collective-permute-start.1 = (bf16[6,6,32,128]{3,2,0,1:T(8,128)(2,1)S(1)}, bf16[6,6,32,128]{3,2,0,1:T(8,128)(2,1)S(1)}, u32[]{:S(2)}, u32[]{:S(2)}) collective-permute-start(bf16[6,6,32,128]{3,2,0,1:T(8,128)(2,1)S(1)} %get-tuple-element.18), channel_id=1, source_target_pairs={{0,4},{1,5},{2,6},{3,7},{4,8},{5,9},{6,10},{7,11},{8,12},{9,13},{1... | collective-permute-start | bytes 884744 | tf_op jit(solution)/shard_map/ppermute | solution.py:43
  11.0 5.8 %collective-permute-done.2 = bf16[6,6,32,128]{3,2,0,1:T(8,128)(2,1)S(1)} collective-permute-done((bf16[6,6,32,128]{3,2,0,1:T(8,128)(2,1)S(1)}, bf16[6,6,32,128]{3,2,0,1:T(8,128)(2,1)S(1)}, u32[]{:S(2)}, u32[]{:S(2)}) %collective-permute-start.2) | collective-permute-done | bytes 294944 | tf_op jit(solution)/shard_map/ppermute | solution.py:43
  18.8 4.6 %collective-permute-start.3 = (bf16[6,28,6,128]{3,2,0,1:T(8,128)(2,1)S(1)}, bf16[6,28,6,128]{3,2,0,1:T(8,128)(2,1)S(1)}, u32[]{:S(2)}, u32[]{:S(2)}) collective-permute-start(bf16[6,28,6,128]{3,2,0,1:T(8,128)(2,1)S(1)} %get-tuple-element.14), channel_id=1, source_target_pairs={{0,1},{1,2},{2,3},{4,5},{5,6},{6,7},{8,9},{9,10},{10,11},{12,13},{... | collective-permute-start | bytes 774152 | tf_op jit(solution)/shard_map/ppermute | solution.py:43
  25.8 2.8 %collective-permute-done.4 = bf16[6,28,6,128]{3,2,0,1:T(8,128)(2,1)S(1)} collective-permute-done((bf16[6,28,6,128]{3,2,0,1:T(8,128)(2,1)S(1)}, bf16[6,28,6,128]{3,2,0,1:T(8,128)(2,1)S(1)}, u32[]{:S(2)}, u32[]{:S(2)}) %collective-permute-start.4) | collective-permute-done | bytes 258080 | tf_op jit(solution)/shard_map/ppermute | solution.py:43
  29.8 1.6 %pad_maximum_fusion = (bf16[2,28,44,128]{3,2,0,1:T(8,128)(2,1)}, bf16[2,28,44,128]{3,2,0,1:T(8,128)(2,1)S(1)}) fusion(bf16[6,28,6,128]{3,2,0,1:T(8,128)(2,1)S(1)} %collective-permute-done.4, bf16[6,28,6,128]{3,2,0,1:T(8,128)(2,1)S(1)} %collective-permute-done.3, bf16[6,6,32,128]{3,2,0,1:T(8,128)(2,1)S(1)} %collective-permute-done.2, ...), kind=kLoop, calls=%fused_computation.58 | loop fusion | flops 8830976 | bytes 3153920 | tf_op jit(solution)/shard_map/concatenate | solution.py:44
  33.8 1.7 %fusion.1 = bf16[26,16,6,128]{3,1,2,0:T(8,128)(2,1)S(1)} fusion(bf16[28,2,8,8,128]{4,1,3,2,0:T(2,128)(2,1)S(1)} %fusion.16, pred[16,6]{0,1:T(8,128)(4,1)S(1)} %copy-done.23, bf16[2,3,3,128,128]{4,3,2,1,0:T(8,128)(2,1)S(1)} %get-tuple-element.17), kind=kOutput, calls=%fused_computation.6 | convolution fusion | flops 736739328 | bytes 1852416 | tf_op jit(solution)/shard_map/conv_general_dilated | solution.py:63
  36.0 1.7 %fusion.11 = bf16[26,2,42,128]{3,1,2,0:T(2,128)(2,1)S(1)} fusion(bf16[26,2,42,128]{3,2,1,0:T(8,128)(2,1)S(1)} %bitcast.129, pred[26,42]{1,0:T(8,128)(4,1)S(1)} %broadcast_and_fusion), kind=kLoop, calls=%fused_computation.27 | loop fusion | flops 279552 | bytes 1119300 | tf_op jit(solution)/shard_map/convert_element_type | solution.py:278
  37.7 1.7 %fusion.99 = bf16[2,26,42,128]{3,0,2,1:T(2,128)(2,1)S(1)} fusion(bf16[26,2,42,128]{3,2,1,0:T(8,128)(2,1)S(1)} %bitcast.130, pred[26,42]{1,0:T(8,128)(4,1)S(1)} %broadcast_and_fusion), kind=kLoop, calls=%fused_computation.201 | loop fusion | flops 279552 | bytes 1119300 | tf_op jit(solution)/shard_map/convert_element_type | solution.py:278
  42.6 2.8 %fusion.19 = bf16[22,2,38,128]{3,1,2,0:T(2,128)(2,1)S(1)} fusion(bf16[22,2,38,128]{3,0,2,1:T(8,128)(2,1)S(1)} %slice.163, pred[22,38]{1,0:T(8,128)(4,1)S(1)} %broadcast_and_fusion.2), kind=kLoop, calls=%fused_computation.39 | loop fusion | flops 214016 | bytes 856900 | tf_op jit(solution)/shard_map/convert_element_type | solution.py:278
  45.4 2.8 %fusion.98 = bf16[2,22,38,128]{3,0,2,1:T(2,128)(2,1)S(1)} fusion(bf16[22,2,38,128]{3,0,2,1:T(8,128)(2,1)S(1)} %slice.163, pred[22,38]{1,0:T(8,128)(4,1)S(1)} %broadcast_and_fusion.2), kind=kLoop, calls=%fused_computation.200 | loop fusion | flops 214016 | bytes 856900 | tf_op jit(solution)/shard_map/convert_element_type | solution.py:278
  49.3 1.6 %fusion.2 = bf16[24,16,6,128]{3,1,2,0:T(8,128)(2,1)S(1)} fusion(bf16[26,2,7,2,128]{4,2,1,3,0:T(8,128)(2,1)S(1)} %slice.150, bf16[26,2,8,6,128]{4,2,1,3,0:T(8,128)(2,1)S(1)} %copy.147, pred[16,6]{0,1:T(8,128)(4,1)S(1)} %copy-done.22, bf16[2,3,3,128,128]{4,3,2,1,0:T(8,128)(2,1)S(1)} %copy-done.8), kind=kOutput, calls=%fused_computation.8 | convolution fusion | flops 682622976 | bytes 1737728 | tf_op jit(solution)/shard_map/conv_general_dilated | solution.py:63
  52.2 2.1 %fusion.15 = bf16[2,24,40,128]{3,2,0,1:T(8,128)(2,1)S(1)} fusion(bf16[24,2,40,128]{3,0,2,1:T(8,128)(2,1)S(1)} %slice.152, bf16[6,28,6,128]{3,2,0,1:T(8,128)(2,1)S(1)} %copy-done.11, bf16[6,28,6,128]{3,2,0,1:T(8,128)(2,1)S(1)} %copy-done.13, bf16[6,6,32,128]{3,2,0,1:T(8,128)(2,1)S(1)} %copy-done.2, bf16[6,6,32,128]{3,2,0,1:T(8,128)(2,1)S(1)} %copy-done.4, ...), kind=kLoop, calls=%fused_computation.34 | loop fusion | flops 5160960 | bytes 2876352 | tf_op jit(solution)/shard_map/convert_element_type | solution.py:232
  57.0 2.9 %fusion.22 = bf16[2,22,38,128]{3,0,2,1:T(2,128)(2,1)S(1)} fusion(f32[22,2,38,128]{3,0,2,1:T(8,128)S(1)} %slice.155, pred[22,38]{1,0:T(8,128)(4,1)S(1)} %broadcast_and_fusion.2, bf16[2,26,42,128]{3,0,2,1:T(2,128)(2,1)S(1)} %fusion.99), kind=kLoop, calls=%fused_computation.43 | loop fusion | flops 1284096 | bytes 1712964 | tf_op jit(solution)/shard_map/convert_element_type | solution.py:232
  63.8 1.7 %fusion.34 = bf16[20,2,36,128]{3,1,2,0:T(2,128)(2,1)S(1)} fusion(f32[20,2,36,128]{3,0,2,1:T(8,128)S(1)} %slice.159, pred[20,36]{1,0:T(8,128)(4,1)S(1)} %broadcast_and_fusion.3, bf16[20,2,36,128]{3,0,2,1:T(8,128)(2,1)S(1)} %slice.166), kind=kLoop, calls=%fused_computation.56 | loop fusion | flops 1290240 | bytes 1475280 | tf_op jit(solution)/shard_map/convert_element_type | solution.py:232
  68.0 2.3 %fusion.56 = bf16[2,18,34,128]{3,0,2,1:T(2,128)(2,1)S(1)} fusion(f32[18,2,34,128]{3,0,2,1:T(8,128)S(1)} %slice.169, pred[18,34]{1,0:T(8,128)(4,1)S(1)} %broadcast_and_fusion.4, bf16[2,22,38,128]{3,0,2,1:T(2,128)(2,1)S(1)} %fusion.98), kind=kLoop, calls=%fused_computation.84 | loop fusion | flops 940032 | bytes 1253988 | tf_op jit(solution)/shard_map/convert_element_type | solution.py:232
  70.3 1.8 %fusion.52 = f32[3,3,128,128]{3,2,1,0:T(8,128)S(1)} fusion(bf16[2,28,44,128]{3,2,0,1:T(8,128)(2,1)S(1)} %copy-done.9, bf16[2,18,34,128]{3,0,2,1:T(2,128)(2,1)S(1)} %fusion.56), kind=kOutput, calls=%fused_computation.79 | convolution fusion | flops 301989888 | bytes 1540096 | tf_op jit(solution)/shard_map/transpose | solution.py:82
  74.2 1.8 %fusion.73 = f32[3,3,128,128]{3,2,1,0:T(8,128)S(1)} fusion(bf16[22,2,38,128]{3,1,2,0:T(2,128)(2,1)S(1)} %fusion.19, bf16[2,20,36,128]{3,0,2,1:T(2,128)(2,1)S(1)} %bitcast.156), kind=kOutput, calls=%fused_computation.141 | convolution fusion | flops 301989888 | bytes 1280000 | tf_op jit(solution)/shard_map/transpose | solution.py:82
  75.9 1.8 %multiply_convert_fusion = (bf16[3,3,128,128]{3,2,1,0:T(8,128)(2,1)S(1)}, f32[3,3,128,128]{3,2,1,0:T(8,128)S(1)}) fusion(f32[3,3,128,128]{3,2,1,0:T(8,128)S(1)} %fusion.73, pred[]{:T(512)S(6)} %eq.27, bf16[26,2,42,128]{3,1,2,0:T(2,128)(2,1)S(1)} %fusion.11, bf16[2,16,32,128]{3,2,0,1:T(8,128)(2,1)S(1)} %slice.183), kind=kOutput, calls=%fused_computation.87 | convolution fusion | flops 302432256 | bytes 2295809 | tf_op jit(solution)/shard_map/transpose | solution.py:82
  78.3 1.8 %multiply_convert_fusion.1 = (bf16[3,3,128,128]{3,2,1,0:T(8,128)(2,1)S(1)}, f32[3,3,128,128]{3,2,1,0:T(8,128)S(1)}) fusion(f32[3,3,128,128]{3,2,1,0:T(8,128)S(1)} %fusion.52, pred[]{:T(512)S(6)} %eq.27, bf16[2,22,38,128]{3,0,2,1:T(2,128)(2,1)S(1)} %fusion.22, bf16[2,28,44,128]{3,2,0,1:T(8,128)(2,1)S(1)} %get-tuple-element.13), kind=kOutput, calls=%fused_computation.89 | convolution fusion | flops 302432256 | bytes 2424833 | tf_op jit(solution)/shard_map/transpose | solution.py:82
  81.2 5.0 %collective-permute-start.15 = (bf16[73728]{0:T(1024)(128)(2,1)S(1)}, bf16[73728]{0:T(1024)(128)(2,1)S(1)}, u32[]{:S(2)}, u32[]{:S(2)}) collective-permute-start(bf16[73728]{0:T(1024)(128)(2,1)S(1)} %select_convert_fusion), channel_id=1, source_target_pairs={{0,4},{4,0},{8,12},{12,8},{1,5},{5,1},{9,13},{13,9},{2,6},{6,2},{1... | collective-permute-start | bytes 442376 | tf_op jit(solution)/shard_map/ppermute | solution.py:100
  86.9 4.0 %collective-permute-done.15 = bf16[73728]{0:T(1024)(128)(2,1)S(1)} collective-permute-done((bf16[73728]{0:T(1024)(128)(2,1)S(1)}, bf16[73728]{0:T(1024)(128)(2,1)S(1)}, u32[]{:S(2)}, u32[]{:S(2)}) %collective-permute-start.15) | collective-permute-done | bytes 147488 | tf_op jit(solution)/shard_map/ppermute | solution.py:100
  91.0 4.0 %collective-permute-start.16 = (bf16[36864]{0:T(1024)(128)(2,1)S(1)}, bf16[36864]{0:T(1024)(128)(2,1)S(1)}, u32[]{:S(2)}, u32[]{:S(2)}) collective-permute-start(bf16[36864]{0:T(1024)(128)(2,1)S(1)} %select_convert_fusion.4), channel_id=1, source_target_pairs={{0,8},{4,12},{8,0},{12,4},{1,9},{5,13},{9,1},{13,5},{2,10},{6,14},... | collective-permute-start | bytes 221192 | tf_op jit(solution)/shard_map/ppermute | solution.py:100
  95.1 2.6 %collective-permute-start.9 = (bf16[36864]{0:T(1024)(128)(2,1)S(1)}, bf16[36864]{0:T(1024)(128)(2,1)S(1)}, u32[]{:S(2)}, u32[]{:S(2)}) collective-permute-start(bf16[36864]{0:T(1024)(128)(2,1)S(1)} %select_convert_fusion.6), channel_id=1, source_target_pairs={{0,8},{4,12},{8,0},{12,4},{1,9},{5,13},{9,1},{13,5},{2,10},{6,14},... | collective-permute-start | bytes 221192 | tf_op jit(solution)/shard_map/ppermute | solution.py:100
  97.7 2.5 %collective-permute-start.17 = (bf16[36864]{0:T(1024)(128)(2,1)S(1)}, bf16[36864]{0:T(1024)(128)(2,1)S(1)}, u32[]{:S(2)}, u32[]{:S(2)}) collective-permute-start(bf16[36864]{0:T(1024)(128)(2,1)S(1)} %add_convert_fusion.2), channel_id=1, source_target_pairs={{0,1},{1,0},{2,3},{3,2},{4,5},{5,4},{6,7},{7,6},{8,9},{9,8},{10,11... | collective-permute-start | bytes 221192 | tf_op jit(solution)/shard_map/ppermute | solution.py:100
  100.3 2.3 %collective-permute-start.10 = (bf16[36864]{0:T(1024)(128)(2,1)S(1)}, bf16[36864]{0:T(1024)(128)(2,1)S(1)}, u32[]{:S(2)}, u32[]{:S(2)}) collective-permute-start(bf16[36864]{0:T(1024)(128)(2,1)S(1)} %add_convert_fusion.5), channel_id=1, source_target_pairs={{0,1},{1,0},{2,3},{3,2},{4,5},{5,4},{6,7},{7,6},{8,9},{9,8},{10,11... | collective-permute-start | bytes 221192 | tf_op jit(solution)/shard_map/ppermute | solution.py:100
  103.0 3.3 %collective-permute-start.18 = (bf16[36864]{0:T(1024)(128)(2,1)S(1)}, bf16[36864]{0:T(1024)(128)(2,1)S(1)}, u32[]{:S(2)}, u32[]{:S(2)}) collective-permute-start(bf16[36864]{0:T(1024)(128)(2,1)S(1)} %add_convert_fusion.1), channel_id=1, source_target_pairs={{0,2},{1,3},{2,0},{3,1},{4,6},{5,7},{6,4},{7,5},{8,10},{9,11},{10,... | collective-permute-start | bytes 221192 | tf_op jit(solution)/shard_map/ppermute | solution.py:100
  106.4 1.7 %collective-permute-start.11 = (bf16[36864]{0:T(1024)(128)(2,1)S(1)}, bf16[36864]{0:T(1024)(128)(2,1)S(1)}, u32[]{:S(2)}, u32[]{:S(2)}) collective-permute-start(bf16[36864]{0:T(1024)(128)(2,1)S(1)} %add_convert_fusion.4), channel_id=1, source_target_pairs={{0,2},{1,3},{2,0},{3,1},{4,6},{5,7},{6,4},{7,5},{8,10},{9,11},{10,... | collective-permute-start | bytes 221192 | tf_op jit(solution)/shard_map/ppermute | solution.py:100
  108.1 2.4 %collective-permute-done.18 = bf16[36864]{0:T(1024)(128)(2,1)S(1)} collective-permute-done((bf16[36864]{0:T(1024)(128)(2,1)S(1)}, bf16[36864]{0:T(1024)(128)(2,1)S(1)}, u32[]{:S(2)}, u32[]{:S(2)}) %collective-permute-start.18) | collective-permute-done | bytes 73760 | tf_op jit(solution)/shard_map/ppermute | solution.py:100
  110.5 1.7 %collective-permute-start.19 = (bf16[36864]{0:T(1024)(128)(2,1)S(1)}, bf16[36864]{0:T(1024)(128)(2,1)S(1)}, u32[]{:S(2)}, u32[]{:S(2)}) collective-permute-start(bf16[36864]{0:T(1024)(128)(2,1)S(1)} %add_convert_fusion), channel_id=1, source_target_pairs={{0,8},{4,12},{8,0},{12,4},{1,9},{5,13},{9,1},{13,5},{2,10},{6,14},... | collective-permute-start | bytes 221192 | tf_op jit(solution)/shard_map/ppermute | solution.py:100
  115.0 1.6 %collective-permute-start.20 = (bf16[73728]{0:T(1024)(128)(2,1)S(1)}, bf16[73728]{0:T(1024)(128)(2,1)S(1)}, u32[]{:S(2)}, u32[]{:S(2)}) collective-permute-start(bf16[73728]{0:T(1024)(128)(2,1)S(1)} %maximum_select_fusion.4), channel_id=1, source_target_pairs={{0,4},{4,0},{8,12},{12,8},{1,5},{5,1},{9,13},{13,9},{2,6},{6,2},{1... | collective-permute-start | bytes 442376 | tf_op jit(solution)/shard_map/ppermute | solution.py:100
  118.3 1.9 %collective-permute-done.20 = bf16[73728]{0:T(1024)(128)(2,1)S(1)} collective-permute-done((bf16[73728]{0:T(1024)(128)(2,1)S(1)}, bf16[73728]{0:T(1024)(128)(2,1)S(1)}, u32[]{:S(2)}, u32[]{:S(2)}) %collective-permute-start.20) | collective-permute-done | bytes 147488 | tf_op jit(solution)/shard_map/ppermute | solution.py:100
  120.3 1.6 %collective-permute-done.13 = bf16[73728]{0:T(1024)(128)(2,1)S(1)} collective-permute-done((bf16[73728]{0:T(1024)(128)(2,1)S(1)}, bf16[73728]{0:T(1024)(128)(2,1)S(1)}, u32[]{:S(2)}, u32[]{:S(2)}) %collective-permute-start.13) | collective-permute-done | bytes 147488 | tf_op jit(solution)/shard_map/ppermute | solution.py:100
  (176 shorter events, 37.9 us)
Async XLA Ops:
  0.6 2.6 %copy-start = (bf16[4,16,32,128]{3,2,1,0:T(8,128)(2,1)S(1)}, bf16[4,16,32,128]{3,2,1,0:T(8,128)(2,1)}, u32[]{:S(2)}) copy-start(bf16[4,16,32,128]{3,2,1,0:T(8,128)(2,1)} %param.6) | copy-start | bytes 1572868
  0.6 1.8 %copy-start.14 = (bf16[2,3,3,128,128]{4,3,2,1,0:T(8,128)(2,1)S(1)}, bf16[2,3,3,128,128]{4,3,2,1,0:T(8,128)(2,1)}, u32[]{:S(2)}) copy-start(bf16[2,3,3,128,128]{4,3,2,1,0:T(8,128)(2,1)} %param.5) | copy-start | bytes 1769476
  0.7 1.9 %copy-start.17 = (s32[4]{0:T(128)S(1)}, s32[4]{0:T(128)}, u32[]{:S(2)}) copy-start(s32[4]{0:T(128)} %param.7) | copy-start | bytes 52
  1.9 2.2 %collective-permute-start = (bf16[2,16,32,128]{3,2,0,1:T(8,128)(2,1)S(1)}, bf16[2,16,32,128]{3,2,0,1:T(8,128)(2,1)S(1)}, u32[]{:S(2)}, u32[]{:S(2)}) collective-permute-start(bf16[2,16,32,128]{3,2,0,1:T(8,128)(2,1)S(1)} %bitcast.163), channel_id=1, source_target_pairs={{0,16},{16,0},{1,17},{17,1},{2,18},{18,2},{3,19},{19,3},{4,20},{20... | collective-permute-start | bytes 786440 | tf_op jit(solution)/shard_map/ppermute | solution.py:249
  2.4 21.0 %collective-permute-start.5 = (bf16[2,3,3,128,128]{4,3,2,1,0:T(8,128)(2,1)S(1)}, bf16[2,3,3,128,128]{4,3,2,1,0:T(8,128)(2,1)}, u32[]{:S(2)}, u32[]{:S(2)}) collective-permute-start(bf16[2,3,3,128,128]{4,3,2,1,0:T(8,128)(2,1)S(1)} %copy-done.14), channel_id=1, source_target_pairs={{0,16},{16,0},{1,17},{17,1},{2,18},{18,2},{3,19},{19,3},{4,20},{20... | collective-permute-start | bytes 1769480 | tf_op jit(solution)/shard_map/ppermute | solution.py:249
  4.1 12.7 %collective-permute-start.2 = (bf16[6,6,32,128]{3,2,0,1:T(8,128)(2,1)S(1)}, bf16[6,6,32,128]{3,2,0,1:T(8,128)(2,1)S(1)}, u32[]{:S(2)}, u32[]{:S(2)}) collective-permute-start(bf16[6,6,32,128]{3,2,0,1:T(8,128)(2,1)S(1)} %get-tuple-element.19), channel_id=1, source_target_pairs={{4,0},{5,1},{6,2},{7,3},{8,4},{9,5},{10,6},{11,7},{12,8},{13,9},{1... | collective-permute-start | bytes 884744 | tf_op jit(solution)/shard_map/ppermute | solution.py:43
  5.4 11.9 %collective-permute-start.1 = (bf16[6,6,32,128]{3,2,0,1:T(8,128)(2,1)S(1)}, bf16[6,6,32,128]{3,2,0,1:T(8,128)(2,1)S(1)}, u32[]{:S(2)}, u32[]{:S(2)}) collective-permute-start(bf16[6,6,32,128]{3,2,0,1:T(8,128)(2,1)S(1)} %get-tuple-element.18), channel_id=1, source_target_pairs={{0,4},{1,5},{2,6},{3,7},{4,8},{5,9},{6,10},{7,11},{8,12},{9,13},{1... | collective-permute-start | bytes 884744 | tf_op jit(solution)/shard_map/ppermute | solution.py:43
  16.8 13.0 %copy-start.1 = (bf16[6,6,32,128]{3,2,0,1:T(8,128)(2,1)}, bf16[6,6,32,128]{3,2,0,1:T(8,128)(2,1)S(1)}, u32[]{:S(2)}) copy-start(bf16[6,6,32,128]{3,2,0,1:T(8,128)(2,1)S(1)} %collective-permute-done.2) | copy-start | bytes 884740
  17.4 12.4 %copy-start.3 = (bf16[6,6,32,128]{3,2,0,1:T(8,128)(2,1)}, bf16[6,6,32,128]{3,2,0,1:T(8,128)(2,1)S(1)}, u32[]{:S(2)}) copy-start(bf16[6,6,32,128]{3,2,0,1:T(8,128)(2,1)S(1)} %collective-permute-done.1) | copy-start | bytes 884740
  17.5 11.1 %collective-permute-start.4 = (bf16[6,28,6,128]{3,2,0,1:T(8,128)(2,1)S(1)}, bf16[6,28,6,128]{3,2,0,1:T(8,128)(2,1)S(1)}, u32[]{:S(2)}, u32[]{:S(2)}) collective-permute-start(bf16[6,28,6,128]{3,2,0,1:T(8,128)(2,1)S(1)} %get-tuple-element.15), channel_id=1, source_target_pairs={{1,0},{2,1},{3,2},{5,4},{6,5},{7,6},{9,8},{10,9},{11,10},{13,12},{... | collective-permute-start | bytes 774152 | tf_op jit(solution)/shard_map/ppermute | solution.py:43
  18.8 11.0 %collective-permute-start.3 = (bf16[6,28,6,128]{3,2,0,1:T(8,128)(2,1)S(1)}, bf16[6,28,6,128]{3,2,0,1:T(8,128)(2,1)S(1)}, u32[]{:S(2)}, u32[]{:S(2)}) collective-permute-start(bf16[6,28,6,128]{3,2,0,1:T(8,128)(2,1)S(1)} %get-tuple-element.14), channel_id=1, source_target_pairs={{0,1},{1,2},{2,3},{4,5},{5,6},{6,7},{8,9},{9,10},{10,11},{12,13},{... | collective-permute-start | bytes 774152 | tf_op jit(solution)/shard_map/ppermute | solution.py:43
  24.6 9.2 %copy-start.7 = (bf16[2,3,3,128,128]{4,3,2,1,0:T(8,128)(2,1)}, bf16[2,3,3,128,128]{4,3,2,1,0:T(8,128)(2,1)S(1)}, u32[]{:S(2)}) copy-start(bf16[2,3,3,128,128]{4,3,2,1,0:T(8,128)(2,1)S(1)} %get-tuple-element.17) | copy-start | bytes 1769476
  28.6 2.8 %copy-start.10 = (bf16[6,28,6,128]{3,2,0,1:T(8,128)(2,1)}, bf16[6,28,6,128]{3,2,0,1:T(8,128)(2,1)S(1)}, u32[]{:S(2)}) copy-start(bf16[6,28,6,128]{3,2,0,1:T(8,128)(2,1)S(1)} %collective-permute-done.4) | copy-start | bytes 774148
  29.8 1.7 %copy-start.12 = (bf16[6,28,6,128]{3,2,0,1:T(8,128)(2,1)}, bf16[6,28,6,128]{3,2,0,1:T(8,128)(2,1)S(1)}, u32[]{:S(2)}) copy-start(bf16[6,28,6,128]{3,2,0,1:T(8,128)(2,1)S(1)} %collective-permute-done.3) | copy-start | bytes 774148
  32.4 1.4 %copy-start.23 = (pred[16,6]{0,1:T(8,128)(4,1)S(1)}, pred[16,6]{0,1:T(8,128)(4,1)}, u32[]{:S(2)}) copy-start(pred[16,6]{0,1:T(8,128)(4,1)} %constant.196) | copy-start | bytes 292
  36.0 3.5 %copy-start.9 = (bf16[2,28,44,128]{3,2,0,1:T(8,128)(2,1)S(1)}, bf16[2,28,44,128]{3,2,0,1:T(8,128)(2,1)}, u32[]{:S(2)}) copy-start(bf16[2,28,44,128]{3,2,0,1:T(8,128)(2,1)} %get-tuple-element.12) | copy-start | bytes 1892356
  50.9 1.2 %copy-start.13 = (bf16[6,28,6,128]{3,2,0,1:T(8,128)(2,1)S(1)}, bf16[6,28,6,128]{3,2,0,1:T(8,128)(2,1)}, u32[]{:S(2)}) copy-start(bf16[6,28,6,128]{3,2,0,1:T(8,128)(2,1)} %copy-done.12) | copy-start | bytes 774148
  74.1 6.1 %collective-permute-start.6 = (bf16[2,16,32,128]{3,2,0,1:T(8,128)(2,1)S(1)}, bf16[2,16,32,128]{3,2,0,1:T(8,128)(2,1)S(1)}, u32[]{:S(2)}, u32[]{:S(2)}) collective-permute-start(bf16[2,16,32,128]{3,2,0,1:T(8,128)(2,1)S(1)} %get-tuple-element.21), channel_id=1, source_target_pairs={{0,16},{16,0},{1,17},{17,1},{2,18},{18,2},{3,19},{19,3},{4,20},{20... | collective-permute-start | bytes 786440 | tf_op jit(solution)/shard_map/ppermute | solution.py:249
  77.7 3.3 %collective-permute-start.14 = (bf16[3,3,128,128]{3,2,1,0:T(8,128)(2,1)S(1)}, bf16[3,3,128,128]{3,2,1,0:T(8,128)(2,1)S(1)}, u32[]{:S(2)}, u32[]{:S(2)}) collective-permute-start(bf16[3,3,128,128]{3,2,1,0:T(8,128)(2,1)S(1)} %get-tuple-element.26), channel_id=1, source_target_pairs={{0,16},{16,0},{1,17},{17,1},{2,18},{18,2},{3,19},{19,3},{4,20},{20... | collective-permute-start | bytes 884744 | tf_op jit(solution)/shard_map/ppermute | solution.py:249
  80.1 6.2 %collective-permute-start.7 = (bf16[3,3,128,128]{3,2,1,0:T(8,128)(2,1)S(1)}, bf16[3,3,128,128]{3,2,1,0:T(8,128)(2,1)S(1)}, u32[]{:S(2)}, u32[]{:S(2)}) collective-permute-start(bf16[3,3,128,128]{3,2,1,0:T(8,128)(2,1)S(1)} %get-tuple-element.28), channel_id=1, source_target_pairs={{0,16},{16,0},{1,17},{17,1},{2,18},{18,2},{3,19},{19,3},{4,20},{20... | collective-permute-start | bytes 884744 | tf_op jit(solution)/shard_map/ppermute | solution.py:249
  81.2 9.7 %collective-permute-start.15 = (bf16[73728]{0:T(1024)(128)(2,1)S(1)}, bf16[73728]{0:T(1024)(128)(2,1)S(1)}, u32[]{:S(2)}, u32[]{:S(2)}) collective-permute-start(bf16[73728]{0:T(1024)(128)(2,1)S(1)} %select_convert_fusion), channel_id=1, source_target_pairs={{0,4},{4,0},{8,12},{12,8},{1,5},{5,1},{9,13},{13,9},{2,6},{6,2},{1... | collective-permute-start | bytes 442376 | tf_op jit(solution)/shard_map/ppermute | solution.py:100
  86.4 8.6 %collective-permute-start.8 = (bf16[73728]{0:T(1024)(128)(2,1)S(1)}, bf16[73728]{0:T(1024)(128)(2,1)S(1)}, u32[]{:S(2)}, u32[]{:S(2)}) collective-permute-start(bf16[73728]{0:T(1024)(128)(2,1)S(1)} %select_convert_fusion.2), channel_id=1, source_target_pairs={{0,4},{4,0},{8,12},{12,8},{1,5},{5,1},{9,13},{13,9},{2,6},{6,2},{1... | collective-permute-start | bytes 442376 | tf_op jit(solution)/shard_map/ppermute | solution.py:100
  91.0 6.7 %collective-permute-start.16 = (bf16[36864]{0:T(1024)(128)(2,1)S(1)}, bf16[36864]{0:T(1024)(128)(2,1)S(1)}, u32[]{:S(2)}, u32[]{:S(2)}) collective-permute-start(bf16[36864]{0:T(1024)(128)(2,1)S(1)} %select_convert_fusion.4), channel_id=1, source_target_pairs={{0,8},{4,12},{8,0},{12,4},{1,9},{5,13},{9,1},{13,5},{2,10},{6,14},... | collective-permute-start | bytes 221192 | tf_op jit(solution)/shard_map/ppermute | solution.py:100
  95.1 5.2 %collective-permute-start.9 = (bf16[36864]{0:T(1024)(128)(2,1)S(1)}, bf16[36864]{0:T(1024)(128)(2,1)S(1)}, u32[]{:S(2)}, u32[]{:S(2)}) collective-permute-start(bf16[36864]{0:T(1024)(128)(2,1)S(1)} %select_convert_fusion.6), channel_id=1, source_target_pairs={{0,8},{4,12},{8,0},{12,4},{1,9},{5,13},{9,1},{13,5},{2,10},{6,14},... | collective-permute-start | bytes 221192 | tf_op jit(solution)/shard_map/ppermute | solution.py:100
  97.7 5.3 %collective-permute-start.17 = (bf16[36864]{0:T(1024)(128)(2,1)S(1)}, bf16[36864]{0:T(1024)(128)(2,1)S(1)}, u32[]{:S(2)}, u32[]{:S(2)}) collective-permute-start(bf16[36864]{0:T(1024)(128)(2,1)S(1)} %add_convert_fusion.2), channel_id=1, source_target_pairs={{0,1},{1,0},{2,3},{3,2},{4,5},{5,4},{6,7},{7,6},{8,9},{9,8},{10,11... | collective-permute-start | bytes 221192 | tf_op jit(solution)/shard_map/ppermute | solution.py:100
  100.3 6.1 %collective-permute-start.10 = (bf16[36864]{0:T(1024)(128)(2,1)S(1)}, bf16[36864]{0:T(1024)(128)(2,1)S(1)}, u32[]{:S(2)}, u32[]{:S(2)}) collective-permute-start(bf16[36864]{0:T(1024)(128)(2,1)S(1)} %add_convert_fusion.5), channel_id=1, source_target_pairs={{0,1},{1,0},{2,3},{3,2},{4,5},{5,4},{6,7},{7,6},{8,9},{9,8},{10,11... | collective-permute-start | bytes 221192 | tf_op jit(solution)/shard_map/ppermute | solution.py:100
  103.0 7.5 %collective-permute-start.18 = (bf16[36864]{0:T(1024)(128)(2,1)S(1)}, bf16[36864]{0:T(1024)(128)(2,1)S(1)}, u32[]{:S(2)}, u32[]{:S(2)}) collective-permute-start(bf16[36864]{0:T(1024)(128)(2,1)S(1)} %add_convert_fusion.1), channel_id=1, source_target_pairs={{0,2},{1,3},{2,0},{3,1},{4,6},{5,7},{6,4},{7,5},{8,10},{9,11},{10,... | collective-permute-start | bytes 221192 | tf_op jit(solution)/shard_map/ppermute | solution.py:100
  106.4 5.8 %collective-permute-start.11 = (bf16[36864]{0:T(1024)(128)(2,1)S(1)}, bf16[36864]{0:T(1024)(128)(2,1)S(1)}, u32[]{:S(2)}, u32[]{:S(2)}) collective-permute-start(bf16[36864]{0:T(1024)(128)(2,1)S(1)} %add_convert_fusion.4), channel_id=1, source_target_pairs={{0,2},{1,3},{2,0},{3,1},{4,6},{5,7},{6,4},{7,5},{8,10},{9,11},{10,... | collective-permute-start | bytes 221192 | tf_op jit(solution)/shard_map/ppermute | solution.py:100
  110.5 4.4 %collective-permute-start.19 = (bf16[36864]{0:T(1024)(128)(2,1)S(1)}, bf16[36864]{0:T(1024)(128)(2,1)S(1)}, u32[]{:S(2)}, u32[]{:S(2)}) collective-permute-start(bf16[36864]{0:T(1024)(128)(2,1)S(1)} %add_convert_fusion), channel_id=1, source_target_pairs={{0,8},{4,12},{8,0},{12,4},{1,9},{5,13},{9,1},{13,5},{2,10},{6,14},... | collective-permute-start | bytes 221192 | tf_op jit(solution)/shard_map/ppermute | solution.py:100
  112.2 4.4 %collective-permute-start.12 = (bf16[36864]{0:T(1024)(128)(2,1)S(1)}, bf16[36864]{0:T(1024)(128)(2,1)S(1)}, u32[]{:S(2)}, u32[]{:S(2)}) collective-permute-start(bf16[36864]{0:T(1024)(128)(2,1)S(1)} %add_convert_fusion.3), channel_id=1, source_target_pairs={{0,8},{4,12},{8,0},{12,4},{1,9},{5,13},{9,1},{13,5},{2,10},{6,14},... | collective-permute-start | bytes 221192 | tf_op jit(solution)/shard_map/ppermute | solution.py:100
  115.0 5.2 %collective-permute-start.20 = (bf16[73728]{0:T(1024)(128)(2,1)S(1)}, bf16[73728]{0:T(1024)(128)(2,1)S(1)}, u32[]{:S(2)}, u32[]{:S(2)}) collective-permute-start(bf16[73728]{0:T(1024)(128)(2,1)S(1)} %maximum_select_fusion.4), channel_id=1, source_target_pairs={{0,4},{4,0},{8,12},{12,8},{1,5},{5,1},{9,13},{13,9},{2,6},{6,2},{1... | collective-permute-start | bytes 442376 | tf_op jit(solution)/shard_map/ppermute | solution.py:100
  116.7 5.2 %collective-permute-start.13 = (bf16[73728]{0:T(1024)(128)(2,1)S(1)}, bf16[73728]{0:T(1024)(128)(2,1)S(1)}, u32[]{:S(2)}, u32[]{:S(2)}) collective-permute-start(bf16[73728]{0:T(1024)(128)(2,1)S(1)} %maximum_select_fusion.3), channel_id=1, source_target_pairs={{0,4},{4,0},{8,12},{12,8},{1,5},{5,1},{9,13},{13,9},{2,6},{6,2},{1... | collective-permute-start | bytes 442376 | tf_op jit(solution)/shard_map/ppermute | solution.py:100
  (13 other events, 13.2 us)

commit v10 on v6

--- a/solution.py
+++ b/solution.py
@@ -286,13 +286,11 @@
         ]
 
     scale = 1.0 / batches
-    summed = []
-    for layer_idx in reversed(range(layer_count)):
-        mine_terms = by_section(partials[0][layer_idx], partials[1][layer_idx], 0)
-        other_terms = by_section(partials[1][layer_idx], partials[0][layer_idx], 0)
-        other_terms = swap((other_terms * scale).astype(jnp.bfloat16)).astype(jnp.float32)
-        summed.insert(0, summed_over_tiles(mine_terms * scale + other_terms))
-    gathered = jnp.stack(summed)
+    mine_terms = by_section(jnp.stack(partials[0]), jnp.stack(partials[1]), 0)
+    other_terms = by_section(jnp.stack(partials[1]), jnp.stack(partials[0]), 0)
+    other_terms = swap((other_terms * scale).astype(jnp.bfloat16)).astype(jnp.float32)
+    total = mine_terms * scale + other_terms
+    gathered = jnp.stack([summed_over_tiles(total[layer_idx]) for layer_idx in range(layer_count)])
     mine_back = by_section(results[0], results[1], 0)
     other_back = swap(by_section(results[1], results[0], 0))
     boundary = jnp.where(

time: 123 us -> 128 us (1.041)
  other arithmetic: 25.8 us -> 28.9 us
    ppermute x5 -> x4, waiting for transfers between devices: 0.01 us -> 2.03 us  [swap(): return lax.ppermute(values, 'section', [(0, 1), (1, 0)])]
  transfers between devices with their start and end apart: 21 -> 20, of which waited for: 12 -> 11; matrix products, arithmetic and copies ran while one was open for 9% -> 5% of each run, Pallas kernels for 0% -> 0%
where the time goes in v10:
time: 128 us; the launch traced here: 127 us
  starting transfers between devices  40.8 us (32%)
  other arithmetic  28.9 us (23%)
  waiting for transfers between devices  25 us (20%)
  matrix products  17 us (13%)
  local copies, waits for them, and re-layouts  14.2 us (11%)
  between operations  1.61 us (1%)
    ppermute x12, starting transfers between devices, exchange(): return lax.ppermute(values, axis, [(i, i ^ distance) for i in range(count)])  27 us
    ppermute x4, starting transfers between devices, from_neighbours(): parts.append(lax.ppermute(piece, AXES, pairs))  12.6 us
    ppermute x12, waiting for transfers between devices, exchange(): return lax.ppermute(values, axis, [(i, i ^ distance) for i in range(count)])  12.6 us
    ppermute x4, waiting for transfers between devices, from_neighbours(): parts.append(lax.ppermute(piece, AXES, pairs))  10.4 us
    conv_general_dilated x8, matrix products, convolve(): lax.conv_general_dilated(padded, kernel, (1, 1), 'VALID', dimension_numbe...  9.94 us
    convert_element_type x4, other arithmetic, local_split(): current = current.astype(jnp.bfloat16)  9.08 us
    convert_element_type x4, other arithmetic, section_chain(): signal = signal.astype(jnp.bfloat16)  8.96 us
    transpose x4, matrix products, kernel_terms(): return jnp.transpose(terms, (1, 2, 0, 3))  7.02 us
  transfers between devices with their start and end apart: 20, of which 11 were waited for; matrix products, arithmetic and copies ran while one was open for 5% of the time, Pallas kernels for 0%

profile of v10, /device:TPU:0, one launch (start us, length us, event | category | flops | bytes accessed | tf_op | source)
XLA Modules:
  0.0 127.5 jit_solution(15350486680885123132)
XLA Ops:
  5.4 5.4 %collective-permute-start.1 = (bf16[6,6,32,128]{3,2,0,1:T(8,128)(2,1)S(1)}, bf16[6,6,32,128]{3,2,0,1:T(8,128)(2,1)S(1)}, u32[]{:S(2)}, u32[]{:S(2)}) collective-permute-start(bf16[6,6,32,128]{3,2,0,1:T(8,128)(2,1)S(1)} %get-tuple-element.18), channel_id=1, source_target_pairs={{0,4},{1,5},{2,6},{3,7},{4,8},{5,9},{6,10},{7,11},{8,12},{9,13},{1... | collective-permute-start | bytes 884744 | tf_op jit(solution)/shard_map/ppermute | solution.py:43
  10.9 5.8 %collective-permute-done.2 = bf16[6,6,32,128]{3,2,0,1:T(8,128)(2,1)S(1)} collective-permute-done((bf16[6,6,32,128]{3,2,0,1:T(8,128)(2,1)S(1)}, bf16[6,6,32,128]{3,2,0,1:T(8,128)(2,1)S(1)}, u32[]{:S(2)}, u32[]{:S(2)}) %collective-permute-start.2) | collective-permute-done | bytes 294944 | tf_op jit(solution)/shard_map/ppermute | solution.py:43
  18.8 4.6 %collective-permute-start.3 = (bf16[6,28,6,128]{3,2,0,1:T(8,128)(2,1)S(1)}, bf16[6,28,6,128]{3,2,0,1:T(8,128)(2,1)S(1)}, u32[]{:S(2)}, u32[]{:S(2)}) collective-permute-start(bf16[6,28,6,128]{3,2,0,1:T(8,128)(2,1)S(1)} %get-tuple-element.14), channel_id=1, source_target_pairs={{0,1},{1,2},{2,3},{4,5},{5,6},{6,7},{8,9},{9,10},{10,11},{12,13},{... | collective-permute-start | bytes 774152 | tf_op jit(solution)/shard_map/ppermute | solution.py:43
  25.7 2.8 %collective-permute-done.4 = bf16[6,28,6,128]{3,2,0,1:T(8,128)(2,1)S(1)} collective-permute-done((bf16[6,28,6,128]{3,2,0,1:T(8,128)(2,1)S(1)}, bf16[6,28,6,128]{3,2,0,1:T(8,128)(2,1)S(1)}, u32[]{:S(2)}, u32[]{:S(2)}) %collective-permute-start.4) | collective-permute-done | bytes 258080 | tf_op jit(solution)/shard_map/ppermute | solution.py:43
  29.7 1.6 %pad_maximum_fusion.2 = (bf16[2,28,44,128]{3,2,0,1:T(8,128)(2,1)}, bf16[2,28,44,128]{3,2,0,1:T(8,128)(2,1)S(1)}) fusion(bf16[6,28,6,128]{3,2,0,1:T(8,128)(2,1)S(1)} %collective-permute-done.4, bf16[6,28,6,128]{3,2,0,1:T(8,128)(2,1)S(1)} %collective-permute-done.3, bf16[6,6,32,128]{3,2,0,1:T(8,128)(2,1)S(1)} %collective-permute-done.2, ...), kind=kLoop, calls=%fused_computation.66 | loop fusion | flops 8830976 | bytes 3153920 | tf_op jit(solution)/shard_map/concatenate | solution.py:44
  33.8 1.7 %fusion.1 = bf16[26,16,6,128]{3,1,2,0:T(8,128)(2,1)S(1)} fusion(bf16[28,2,8,8,128]{4,1,3,2,0:T(2,128)(2,1)S(1)} %fusion.16, pred[16,6]{0,1:T(8,128)(4,1)S(1)} %copy-done.23, bf16[2,3,3,128,128]{4,3,2,1,0:T(8,128)(2,1)S(1)} %get-tuple-element.17), kind=kOutput, calls=%fused_computation.6 | convolution fusion | flops 736739328 | bytes 1852416 | tf_op jit(solution)/shard_map/conv_general_dilated | solution.py:63
  35.9 1.7 %fusion.11 = bf16[26,2,42,128]{3,1,2,0:T(2,128)(2,1)S(1)} fusion(bf16[26,2,42,128]{3,2,1,0:T(8,128)(2,1)S(1)} %bitcast.137, pred[26,42]{1,0:T(8,128)(4,1)S(1)} %broadcast_and_fusion), kind=kLoop, calls=%fused_computation.35 | loop fusion | flops 279552 | bytes 1119300 | tf_op jit(solution)/shard_map/convert_element_type | solution.py:278
  37.6 1.7 %fusion.96 = bf16[2,26,42,128]{3,0,2,1:T(2,128)(2,1)S(1)} fusion(bf16[26,2,42,128]{3,2,1,0:T(8,128)(2,1)S(1)} %bitcast.138, pred[26,42]{1,0:T(8,128)(4,1)S(1)} %broadcast_and_fusion), kind=kLoop, calls=%fused_computation.202 | loop fusion | flops 279552 | bytes 1119300 | tf_op jit(solution)/shard_map/convert_element_type | solution.py:278
  42.6 2.8 %fusion.19 = bf16[22,2,38,128]{3,1,2,0:T(2,128)(2,1)S(1)} fusion(bf16[22,2,38,128]{3,0,2,1:T(8,128)(2,1)S(1)} %slice.171, pred[22,38]{1,0:T(8,128)(4,1)S(1)} %broadcast_and_fusion.2), kind=kLoop, calls=%fused_computation.47 | loop fusion | flops 214016 | bytes 856900 | tf_op jit(solution)/shard_map/convert_element_type | solution.py:278
  45.4 2.8 %fusion.95 = bf16[2,22,38,128]{3,0,2,1:T(2,128)(2,1)S(1)} fusion(bf16[22,2,38,128]{3,0,2,1:T(8,128)(2,1)S(1)} %slice.171, pred[22,38]{1,0:T(8,128)(4,1)S(1)} %broadcast_and_fusion.2), kind=kLoop, calls=%fused_computation.201 | loop fusion | flops 214016 | bytes 856900 | tf_op jit(solution)/shard_map/convert_element_type | solution.py:278
  49.3 1.6 %fusion.2 = bf16[24,16,6,128]{3,1,2,0:T(8,128)(2,1)S(1)} fusion(bf16[26,2,7,2,128]{4,2,1,3,0:T(8,128)(2,1)S(1)} %slice.158, bf16[26,2,8,6,128]{4,2,1,3,0:T(8,128)(2,1)S(1)} %copy.147, pred[16,6]{0,1:T(8,128)(4,1)S(1)} %copy-done.22, bf16[2,3,3,128,128]{4,3,2,1,0:T(8,128)(2,1)S(1)} %copy-done.8), kind=kOutput, calls=%fused_computation.8 | convolution fusion | flops 682622976 | bytes 1737728 | tf_op jit(solution)/shard_map/conv_general_dilated | solution.py:63
  52.1 2.1 %fusion.15 = bf16[2,24,40,128]{3,2,0,1:T(8,128)(2,1)S(1)} fusion(bf16[24,2,40,128]{3,0,2,1:T(8,128)(2,1)S(1)} %slice.160, bf16[6,28,6,128]{3,2,0,1:T(8,128)(2,1)S(1)} %copy-done.11, bf16[6,28,6,128]{3,2,0,1:T(8,128)(2,1)S(1)} %copy-done.13, bf16[6,6,32,128]{3,2,0,1:T(8,128)(2,1)S(1)} %copy-done.2, bf16[6,6,32,128]{3,2,0,1:T(8,128)(2,1)S(1)} %copy-done.4, ...), kind=kLoop, calls=%fused_computation.42 | loop fusion | flops 5160960 | bytes 2876352 | tf_op jit(solution)/shard_map/convert_element_type | solution.py:232
  56.9 2.9 %fusion.22 = bf16[2,22,38,128]{3,0,2,1:T(2,128)(2,1)S(1)} fusion(f32[22,2,38,128]{3,0,2,1:T(8,128)S(1)} %slice.163, pred[22,38]{1,0:T(8,128)(4,1)S(1)} %broadcast_and_fusion.2, bf16[2,26,42,128]{3,0,2,1:T(2,128)(2,1)S(1)} %fusion.96), kind=kLoop, calls=%fused_computation.51 | loop fusion | flops 1284096 | bytes 1712964 | tf_op jit(solution)/shard_map/convert_element_type | solution.py:232
  61.9 1.7 %convolution_bitcast_fusion.2 = f32[1,3,3,128,128]{4,3,2,1,0:T(8,128)S(1)} fusion(bf16[2,28,44,128]{3,2,0,1:T(8,128)(2,1)S(1)} %get-tuple-element.13, bf16[2,22,38,128]{3,0,2,1:T(2,128)(2,1)S(1)} %fusion.22), kind=kOutput, calls=%fused_computation.25 | convolution fusion | flops 301989888 | bytes 1540096 | tf_op jit(solution)/shard_map/transpose | solution.py:82
  65.5 1.7 %fusion.34 = bf16[20,2,36,128]{3,1,2,0:T(2,128)(2,1)S(1)} fusion(f32[20,2,36,128]{3,0,2,1:T(8,128)S(1)} %slice.167, pred[20,36]{1,0:T(8,128)(4,1)S(1)} %broadcast_and_fusion.3, bf16[20,2,36,128]{3,0,2,1:T(8,128)(2,1)S(1)} %slice.174), kind=kLoop, calls=%fused_computation.64 | loop fusion | flops 1290240 | bytes 1475280 | tf_op jit(solution)/shard_map/convert_element_type | solution.py:232
  69.7 2.3 %fusion.54 = bf16[2,18,34,128]{3,0,2,1:T(2,128)(2,1)S(1)} fusion(f32[18,2,34,128]{3,0,2,1:T(8,128)S(1)} %slice.177, pred[18,34]{1,0:T(8,128)(4,1)S(1)} %broadcast_and_fusion.4, bf16[2,22,38,128]{3,0,2,1:T(2,128)(2,1)S(1)} %fusion.95), kind=kLoop, calls=%fused_computation.90 | loop fusion | flops 940032 | bytes 1253988 | tf_op jit(solution)/shard_map/convert_element_type | solution.py:232
  72.0 1.8 %convolution_bitcast_fusion.3 = f32[1,3,3,128,128]{4,3,2,1,0:T(8,128)S(1)} fusion(bf16[2,28,44,128]{3,2,0,1:T(8,128)(2,1)S(1)} %copy-done.9, bf16[2,18,34,128]{3,0,2,1:T(2,128)(2,1)S(1)} %fusion.54), kind=kOutput, calls=%fused_computation.26 | convolution fusion | flops 301989888 | bytes 1540096 | tf_op jit(solution)/shard_map/transpose | solution.py:82
  75.6 1.8 %convolution_bitcast_fusion = f32[1,3,3,128,128]{4,3,2,1,0:T(8,128)S(1)} fusion(bf16[26,2,42,128]{3,1,2,0:T(2,128)(2,1)S(1)} %fusion.11, bf16[2,16,32,128]{3,2,0,1:T(8,128)(2,1)S(1)} %slice.187), kind=kOutput, calls=%fused_computation.23 | convolution fusion | flops 301989888 | bytes 1411072 | tf_op jit(solution)/shard_map/transpose | solution.py:82
  77.4 1.7 %convolution_bitcast_fusion.1 = f32[1,3,3,128,128]{4,3,2,1,0:T(8,128)S(1)} fusion(bf16[22,2,38,128]{3,1,2,0:T(2,128)(2,1)S(1)} %fusion.19, bf16[2,20,36,128]{3,0,2,1:T(2,128)(2,1)S(1)} %bitcast.164), kind=kOutput, calls=%fused_computation.24 | convolution fusion | flops 301989888 | bytes 1280000 | tf_op jit(solution)/shard_map/transpose | solution.py:82
  80.8 2.0 %collective-permute-done.6 = bf16[2,16,32,128]{3,2,0,1:T(8,128)(2,1)} collective-permute-done((bf16[2,16,32,128]{3,2,0,1:T(8,128)(2,1)S(1)}, bf16[2,16,32,128]{3,2,0,1:T(8,128)(2,1)}, u32[]{:S(2)}, u32[]{:S(2)}) %collective-permute-start.6) | collective-permute-done | bytes 262176 | tf_op jit(solution)/shard_map/ppermute | solution.py:249
  86.2 5.0 %collective-permute-start.14 = (bf16[73728]{0:T(1024)(128)(2,1)S(1)}, bf16[73728]{0:T(1024)(128)(2,1)S(1)}, u32[]{:S(2)}, u32[]{:S(2)}) collective-permute-start(bf16[73728]{0:T(1024)(128)(2,1)S(1)} %select_convert_fusion), channel_id=1, source_target_pairs={{0,4},{4,0},{8,12},{12,8},{1,5},{5,1},{9,13},{13,9},{2,6},{6,2},{1... | collective-permute-start | bytes 442376 | tf_op jit(solution)/shard_map/ppermute | solution.py:100
  91.3 4.6 %collective-permute-done.14 = bf16[73728]{0:T(1024)(128)(2,1)S(1)} collective-permute-done((bf16[73728]{0:T(1024)(128)(2,1)S(1)}, bf16[73728]{0:T(1024)(128)(2,1)S(1)}, u32[]{:S(2)}, u32[]{:S(2)}) %collective-permute-start.14) | collective-permute-done | bytes 147488 | tf_op jit(solution)/shard_map/ppermute | solution.py:100
  96.0 2.5 %collective-permute-start.15 = (bf16[36864]{0:T(1024)(128)(2,1)S(1)}, bf16[36864]{0:T(1024)(128)(2,1)S(1)}, u32[]{:S(2)}, u32[]{:S(2)}) collective-permute-start(bf16[36864]{0:T(1024)(128)(2,1)S(1)} %select_convert_fusion.4), channel_id=1, source_target_pairs={{0,1},{1,0},{2,3},{3,2},{4,5},{5,4},{6,7},{7,6},{8,9},{9,8},{10,11... | collective-permute-start | bytes 221192 | tf_op jit(solution)/shard_map/ppermute | solution.py:100
  98.6 2.5 %collective-permute-start.9 = (bf16[36864]{0:T(1024)(128)(2,1)S(1)}, bf16[36864]{0:T(1024)(128)(2,1)S(1)}, u32[]{:S(2)}, u32[]{:S(2)}) collective-permute-start(bf16[36864]{0:T(1024)(128)(2,1)S(1)} %select_convert_fusion.6), channel_id=1, source_target_pairs={{0,1},{1,0},{2,3},{3,2},{4,5},{5,4},{6,7},{7,6},{8,9},{9,8},{10,11... | collective-permute-start | bytes 221192 | tf_op jit(solution)/shard_map/ppermute | solution.py:100
  101.2 3.7 %collective-permute-start.16 = (bf16[36864]{0:T(1024)(128)(2,1)S(1)}, bf16[36864]{0:T(1024)(128)(2,1)S(1)}, u32[]{:S(2)}, u32[]{:S(2)}) collective-permute-start(bf16[36864]{0:T(1024)(128)(2,1)S(1)} %add_convert_fusion.2), channel_id=1, source_target_pairs={{0,8},{4,12},{8,0},{12,4},{1,9},{5,13},{9,1},{13,5},{2,10},{6,14},... | collective-permute-start | bytes 221192 | tf_op jit(solution)/shard_map/ppermute | solution.py:100
  104.9 2.3 %collective-permute-start.10 = (bf16[36864]{0:T(1024)(128)(2,1)S(1)}, bf16[36864]{0:T(1024)(128)(2,1)S(1)}, u32[]{:S(2)}, u32[]{:S(2)}) collective-permute-start(bf16[36864]{0:T(1024)(128)(2,1)S(1)} %add_convert_fusion.5), channel_id=1, source_target_pairs={{0,8},{4,12},{8,0},{12,4},{1,9},{5,13},{9,1},{13,5},{2,10},{6,14},... | collective-permute-start | bytes 221192 | tf_op jit(solution)/shard_map/ppermute | solution.py:100
  108.0 3.0 %collective-permute-start.17 = (bf16[36864]{0:T(1024)(128)(2,1)S(1)}, bf16[36864]{0:T(1024)(128)(2,1)S(1)}, u32[]{:S(2)}, u32[]{:S(2)}) collective-permute-start(bf16[36864]{0:T(1024)(128)(2,1)S(1)} %add_convert_fusion.1), channel_id=1, source_target_pairs={{0,2},{1,3},{2,0},{3,1},{4,6},{5,7},{6,4},{7,5},{8,10},{9,11},{10,... | collective-permute-start | bytes 221192 | tf_op jit(solution)/shard_map/ppermute | solution.py:100
  111.1 1.6 %collective-permute-start.11 = (bf16[36864]{0:T(1024)(128)(2,1)S(1)}, bf16[36864]{0:T(1024)(128)(2,1)S(1)}, u32[]{:S(2)}, u32[]{:S(2)}) collective-permute-start(bf16[36864]{0:T(1024)(128)(2,1)S(1)} %add_convert_fusion.4), channel_id=1, source_target_pairs={{0,2},{1,3},{2,0},{3,1},{4,6},{5,7},{6,4},{7,5},{8,10},{9,11},{10,... | collective-permute-start | bytes 221192 | tf_op jit(solution)/shard_map/ppermute | solution.py:100
  112.6 2.3 %collective-permute-done.17 = bf16[36864]{0:T(1024)(128)(2,1)S(1)} collective-permute-done((bf16[36864]{0:T(1024)(128)(2,1)S(1)}, bf16[36864]{0:T(1024)(128)(2,1)S(1)}, u32[]{:S(2)}, u32[]{:S(2)}) %collective-permute-start.17) | collective-permute-done | bytes 73760 | tf_op jit(solution)/shard_map/ppermute | solution.py:100
  115.0 1.6 %collective-permute-start.18 = (bf16[36864]{0:T(1024)(128)(2,1)S(1)}, bf16[36864]{0:T(1024)(128)(2,1)S(1)}, u32[]{:S(2)}, u32[]{:S(2)}) collective-permute-start(bf16[36864]{0:T(1024)(128)(2,1)S(1)} %add_convert_fusion), channel_id=1, source_target_pairs={{0,1},{1,0},{2,3},{3,2},{4,5},{5,4},{6,7},{7,6},{8,9},{9,8},{10,11... | collective-permute-start | bytes 221192 | tf_op jit(solution)/shard_map/ppermute | solution.py:100
  119.4 1.6 %collective-permute-start.19 = (bf16[73728]{0:T(1024)(128)(2,1)S(1)}, bf16[73728]{0:T(1024)(128)(2,1)S(1)}, u32[]{:S(2)}, u32[]{:S(2)}) collective-permute-start(bf16[73728]{0:T(1024)(128)(2,1)S(1)} %maximum_select_fusion.4), channel_id=1, source_target_pairs={{0,4},{4,0},{8,12},{12,8},{1,5},{5,1},{9,13},{13,9},{2,6},{6,2},{1... | collective-permute-start | bytes 442376 | tf_op jit(solution)/shard_map/ppermute | solution.py:100
  122.6 2.0 %collective-permute-done.19 = bf16[73728]{0:T(1024)(128)(2,1)S(1)} collective-permute-done((bf16[73728]{0:T(1024)(128)(2,1)S(1)}, bf16[73728]{0:T(1024)(128)(2,1)S(1)}, u32[]{:S(2)}, u32[]{:S(2)}) %collective-permute-start.19) | collective-permute-done | bytes 147488 | tf_op jit(solution)/shard_map/ppermute | solution.py:100
  (175 shorter events, 42.4 us)
Async XLA Ops:
  0.6 2.5 %copy-start = (bf16[4,16,32,128]{3,2,1,0:T(8,128)(2,1)S(1)}, bf16[4,16,32,128]{3,2,1,0:T(8,128)(2,1)}, u32[]{:S(2)}) copy-start(bf16[4,16,32,128]{3,2,1,0:T(8,128)(2,1)} %param.6) | copy-start | bytes 1572868
  0.6 1.8 %copy-start.14 = (bf16[2,3,3,128,128]{4,3,2,1,0:T(8,128)(2,1)S(1)}, bf16[2,3,3,128,128]{4,3,2,1,0:T(8,128)(2,1)}, u32[]{:S(2)}) copy-start(bf16[2,3,3,128,128]{4,3,2,1,0:T(8,128)(2,1)} %param.5) | copy-start | bytes 1769476
  0.7 1.9 %copy-start.17 = (s32[4]{0:T(128)S(1)}, s32[4]{0:T(128)}, u32[]{:S(2)}) copy-start(s32[4]{0:T(128)} %param.7) | copy-start | bytes 52
  1.9 2.1 %collective-permute-start = (bf16[2,16,32,128]{3,2,0,1:T(8,128)(2,1)S(1)}, bf16[2,16,32,128]{3,2,0,1:T(8,128)(2,1)S(1)}, u32[]{:S(2)}, u32[]{:S(2)}) collective-permute-start(bf16[2,16,32,128]{3,2,0,1:T(8,128)(2,1)S(1)} %bitcast.171), channel_id=1, source_target_pairs={{0,16},{16,0},{1,17},{17,1},{2,18},{18,2},{3,19},{19,3},{4,20},{20... | collective-permute-start | bytes 786440 | tf_op jit(solution)/shard_map/ppermute | solution.py:249
  2.4 20.9 %collective-permute-start.5 = (bf16[2,3,3,128,128]{4,3,2,1,0:T(8,128)(2,1)S(1)}, bf16[2,3,3,128,128]{4,3,2,1,0:T(8,128)(2,1)}, u32[]{:S(2)}, u32[]{:S(2)}) collective-permute-start(bf16[2,3,3,128,128]{4,3,2,1,0:T(8,128)(2,1)S(1)} %copy-done.14), channel_id=1, source_target_pairs={{0,16},{16,0},{1,17},{17,1},{2,18},{18,2},{3,19},{19,3},{4,20},{20... | collective-permute-start | bytes 1769480 | tf_op jit(solution)/shard_map/ppermute | solution.py:249
  4.1 12.7 %collective-permute-start.2 = (bf16[6,6,32,128]{3,2,0,1:T(8,128)(2,1)S(1)}, bf16[6,6,32,128]{3,2,0,1:T(8,128)(2,1)S(1)}, u32[]{:S(2)}, u32[]{:S(2)}) collective-permute-start(bf16[6,6,32,128]{3,2,0,1:T(8,128)(2,1)S(1)} %get-tuple-element.19), channel_id=1, source_target_pairs={{4,0},{5,1},{6,2},{7,3},{8,4},{9,5},{10,6},{11,7},{12,8},{13,9},{1... | collective-permute-start | bytes 884744 | tf_op jit(solution)/shard_map/ppermute | solution.py:43
  5.4 11.9 %collective-permute-start.1 = (bf16[6,6,32,128]{3,2,0,1:T(8,128)(2,1)S(1)}, bf16[6,6,32,128]{3,2,0,1:T(8,128)(2,1)S(1)}, u32[]{:S(2)}, u32[]{:S(2)}) collective-permute-start(bf16[6,6,32,128]{3,2,0,1:T(8,128)(2,1)S(1)} %get-tuple-element.18), channel_id=1, source_target_pairs={{0,4},{1,5},{2,6},{3,7},{4,8},{5,9},{6,10},{7,11},{8,12},{9,13},{1... | collective-permute-start | bytes 884744 | tf_op jit(solution)/shard_map/ppermute | solution.py:43
  16.7 13.0 %copy-start.1 = (bf16[6,6,32,128]{3,2,0,1:T(8,128)(2,1)}, bf16[6,6,32,128]{3,2,0,1:T(8,128)(2,1)S(1)}, u32[]{:S(2)}) copy-start(bf16[6,6,32,128]{3,2,0,1:T(8,128)(2,1)S(1)} %collective-permute-done.2) | copy-start | bytes 884740
  17.3 12.4 %copy-start.3 = (bf16[6,6,32,128]{3,2,0,1:T(8,128)(2,1)}, bf16[6,6,32,128]{3,2,0,1:T(8,128)(2,1)S(1)}, u32[]{:S(2)}) copy-start(bf16[6,6,32,128]{3,2,0,1:T(8,128)(2,1)S(1)} %collective-permute-done.1) | copy-start | bytes 884740
  17.5 11.1 %collective-permute-start.4 = (bf16[6,28,6,128]{3,2,0,1:T(8,128)(2,1)S(1)}, bf16[6,28,6,128]{3,2,0,1:T(8,128)(2,1)S(1)}, u32[]{:S(2)}, u32[]{:S(2)}) collective-permute-start(bf16[6,28,6,128]{3,2,0,1:T(8,128)(2,1)S(1)} %get-tuple-element.15), channel_id=1, source_target_pairs={{1,0},{2,1},{3,2},{5,4},{6,5},{7,6},{9,8},{10,9},{11,10},{13,12},{... | collective-permute-start | bytes 774152 | tf_op jit(solution)/shard_map/ppermute | solution.py:43
  18.8 11.0 %collective-permute-start.3 = (bf16[6,28,6,128]{3,2,0,1:T(8,128)(2,1)S(1)}, bf16[6,28,6,128]{3,2,0,1:T(8,128)(2,1)S(1)}, u32[]{:S(2)}, u32[]{:S(2)}) collective-permute-start(bf16[6,28,6,128]{3,2,0,1:T(8,128)(2,1)S(1)} %get-tuple-element.14), channel_id=1, source_target_pairs={{0,1},{1,2},{2,3},{4,5},{5,6},{6,7},{8,9},{9,10},{10,11},{12,13},{... | collective-permute-start | bytes 774152 | tf_op jit(solution)/shard_map/ppermute | solution.py:43
  24.5 1.2 copy-start.5
  24.5 9.2 %copy-start.7 = (bf16[2,3,3,128,128]{4,3,2,1,0:T(8,128)(2,1)}, bf16[2,3,3,128,128]{4,3,2,1,0:T(8,128)(2,1)S(1)}, u32[]{:S(2)}) copy-start(bf16[2,3,3,128,128]{4,3,2,1,0:T(8,128)(2,1)S(1)} %get-tuple-element.17) | copy-start | bytes 1769476
  28.6 2.8 %copy-start.10 = (bf16[6,28,6,128]{3,2,0,1:T(8,128)(2,1)}, bf16[6,28,6,128]{3,2,0,1:T(8,128)(2,1)S(1)}, u32[]{:S(2)}) copy-start(bf16[6,28,6,128]{3,2,0,1:T(8,128)(2,1)S(1)} %collective-permute-done.4) | copy-start | bytes 774148
  29.7 1.7 %copy-start.12 = (bf16[6,28,6,128]{3,2,0,1:T(8,128)(2,1)}, bf16[6,28,6,128]{3,2,0,1:T(8,128)(2,1)S(1)}, u32[]{:S(2)}) copy-start(bf16[6,28,6,128]{3,2,0,1:T(8,128)(2,1)S(1)} %collective-permute-done.3) | copy-start | bytes 774148
  32.4 1.4 %copy-start.23 = (pred[16,6]{0,1:T(8,128)(4,1)S(1)}, pred[16,6]{0,1:T(8,128)(4,1)}, u32[]{:S(2)}) copy-start(pred[16,6]{0,1:T(8,128)(4,1)} %constant.196) | copy-start | bytes 292
  35.9 3.5 %copy-start.9 = (bf16[2,28,44,128]{3,2,0,1:T(8,128)(2,1)S(1)}, bf16[2,28,44,128]{3,2,0,1:T(8,128)(2,1)}, u32[]{:S(2)}) copy-start(bf16[2,28,44,128]{3,2,0,1:T(8,128)(2,1)} %get-tuple-element.12) | copy-start | bytes 1892356
  50.9 1.2 copy-start.13
  80.1 4.7 %collective-permute-start.7 = (bf16[2,3,3,128,128]{4,3,2,1,0:T(8,128)(2,1)}, bf16[2,3,3,128,128]{4,3,2,1,0:T(8,128)(2,1)}, u32[]{:S(2)}, u32[]{:S(2)}) collective-permute-start(bf16[2,3,3,128,128]{4,3,2,1,0:T(8,128)(2,1)} %multiply_convert_fusion), channel_id=1, source_target_pairs={{0,16},{16,0},{1,17},{17,1},{2,18},{18,2},{3,19},{19,3},{4,20},{20... | collective-permute-start | bytes 1769480 | tf_op jit(solution)/shard_map/ppermute | solution.py:249
  80.2 2.6 %collective-permute-start.6 = (bf16[2,16,32,128]{3,2,0,1:T(8,128)(2,1)S(1)}, bf16[2,16,32,128]{3,2,0,1:T(8,128)(2,1)}, u32[]{:S(2)}, u32[]{:S(2)}) collective-permute-start(bf16[2,16,32,128]{3,2,0,1:T(8,128)(2,1)S(1)} %get-tuple-element.21), channel_id=1, source_target_pairs={{0,16},{16,0},{1,17},{17,1},{2,18},{18,2},{3,19},{19,3},{4,20},{20... | collective-permute-start | bytes 786440 | tf_op jit(solution)/shard_map/ppermute | solution.py:249
  86.2 9.7 %collective-permute-start.14 = (bf16[73728]{0:T(1024)(128)(2,1)S(1)}, bf16[73728]{0:T(1024)(128)(2,1)S(1)}, u32[]{:S(2)}, u32[]{:S(2)}) collective-permute-start(bf16[73728]{0:T(1024)(128)(2,1)S(1)} %select_convert_fusion), channel_id=1, source_target_pairs={{0,4},{4,0},{8,12},{12,8},{1,5},{5,1},{9,13},{13,9},{2,6},{6,2},{1... | collective-permute-start | bytes 442376 | tf_op jit(solution)/shard_map/ppermute | solution.py:100
  91.2 7.3 %collective-permute-start.8 = (bf16[73728]{0:T(1024)(128)(2,1)S(1)}, bf16[73728]{0:T(1024)(128)(2,1)S(1)}, u32[]{:S(2)}, u32[]{:S(2)}) collective-permute-start(bf16[73728]{0:T(1024)(128)(2,1)S(1)} %select_convert_fusion.2), channel_id=1, source_target_pairs={{0,4},{4,0},{8,12},{12,8},{1,5},{5,1},{9,13},{13,9},{2,6},{6,2},{1... | collective-permute-start | bytes 442376 | tf_op jit(solution)/shard_map/ppermute | solution.py:100
  96.0 5.2 %collective-permute-start.15 = (bf16[36864]{0:T(1024)(128)(2,1)S(1)}, bf16[36864]{0:T(1024)(128)(2,1)S(1)}, u32[]{:S(2)}, u32[]{:S(2)}) collective-permute-start(bf16[36864]{0:T(1024)(128)(2,1)S(1)} %select_convert_fusion.4), channel_id=1, source_target_pairs={{0,1},{1,0},{2,3},{3,2},{4,5},{5,4},{6,7},{7,6},{8,9},{9,8},{10,11... | collective-permute-start | bytes 221192 | tf_op jit(solution)/shard_map/ppermute | solution.py:100
  98.6 6.3 %collective-permute-start.9 = (bf16[36864]{0:T(1024)(128)(2,1)S(1)}, bf16[36864]{0:T(1024)(128)(2,1)S(1)}, u32[]{:S(2)}, u32[]{:S(2)}) collective-permute-start(bf16[36864]{0:T(1024)(128)(2,1)S(1)} %select_convert_fusion.6), channel_id=1, source_target_pairs={{0,1},{1,0},{2,3},{3,2},{4,5},{5,4},{6,7},{7,6},{8,9},{9,8},{10,11... | collective-permute-start | bytes 221192 | tf_op jit(solution)/shard_map/ppermute | solution.py:100
  101.2 6.8 %collective-permute-start.16 = (bf16[36864]{0:T(1024)(128)(2,1)S(1)}, bf16[36864]{0:T(1024)(128)(2,1)S(1)}, u32[]{:S(2)}, u32[]{:S(2)}) collective-permute-start(bf16[36864]{0:T(1024)(128)(2,1)S(1)} %add_convert_fusion.2), channel_id=1, source_target_pairs={{0,8},{4,12},{8,0},{12,4},{1,9},{5,13},{9,1},{13,5},{2,10},{6,14},... | collective-permute-start | bytes 221192 | tf_op jit(solution)/shard_map/ppermute | solution.py:100
  104.9 6.1 %collective-permute-start.10 = (bf16[36864]{0:T(1024)(128)(2,1)S(1)}, bf16[36864]{0:T(1024)(128)(2,1)S(1)}, u32[]{:S(2)}, u32[]{:S(2)}) collective-permute-start(bf16[36864]{0:T(1024)(128)(2,1)S(1)} %add_convert_fusion.5), channel_id=1, source_target_pairs={{0,8},{4,12},{8,0},{12,4},{1,9},{5,13},{9,1},{13,5},{2,10},{6,14},... | collective-permute-start | bytes 221192 | tf_op jit(solution)/shard_map/ppermute | solution.py:100
  108.0 6.9 %collective-permute-start.17 = (bf16[36864]{0:T(1024)(128)(2,1)S(1)}, bf16[36864]{0:T(1024)(128)(2,1)S(1)}, u32[]{:S(2)}, u32[]{:S(2)}) collective-permute-start(bf16[36864]{0:T(1024)(128)(2,1)S(1)} %add_convert_fusion.1), channel_id=1, source_target_pairs={{0,2},{1,3},{2,0},{3,1},{4,6},{5,7},{6,4},{7,5},{8,10},{9,11},{10,... | collective-permute-start | bytes 221192 | tf_op jit(solution)/shard_map/ppermute | solution.py:100
  111.1 5.5 %collective-permute-start.11 = (bf16[36864]{0:T(1024)(128)(2,1)S(1)}, bf16[36864]{0:T(1024)(128)(2,1)S(1)}, u32[]{:S(2)}, u32[]{:S(2)}) collective-permute-start(bf16[36864]{0:T(1024)(128)(2,1)S(1)} %add_convert_fusion.4), channel_id=1, source_target_pairs={{0,2},{1,3},{2,0},{3,1},{4,6},{5,7},{6,4},{7,5},{8,10},{9,11},{10,... | collective-permute-start | bytes 221192 | tf_op jit(solution)/shard_map/ppermute | solution.py:100
  115.0 4.4 %collective-permute-start.18 = (bf16[36864]{0:T(1024)(128)(2,1)S(1)}, bf16[36864]{0:T(1024)(128)(2,1)S(1)}, u32[]{:S(2)}, u32[]{:S(2)}) collective-permute-start(bf16[36864]{0:T(1024)(128)(2,1)S(1)} %add_convert_fusion), channel_id=1, source_target_pairs={{0,1},{1,0},{2,3},{3,2},{4,5},{5,4},{6,7},{7,6},{8,9},{9,8},{10,11... | collective-permute-start | bytes 221192 | tf_op jit(solution)/shard_map/ppermute | solution.py:100
  116.6 4.4 %collective-permute-start.12 = (bf16[36864]{0:T(1024)(128)(2,1)S(1)}, bf16[36864]{0:T(1024)(128)(2,1)S(1)}, u32[]{:S(2)}, u32[]{:S(2)}) collective-permute-start(bf16[36864]{0:T(1024)(128)(2,1)S(1)} %add_convert_fusion.3), channel_id=1, source_target_pairs={{0,1},{1,0},{2,3},{3,2},{4,5},{5,4},{6,7},{7,6},{8,9},{9,8},{10,11... | collective-permute-start | bytes 221192 | tf_op jit(solution)/shard_map/ppermute | solution.py:100
  119.4 5.2 %collective-permute-start.19 = (bf16[73728]{0:T(1024)(128)(2,1)S(1)}, bf16[73728]{0:T(1024)(128)(2,1)S(1)}, u32[]{:S(2)}, u32[]{:S(2)}) collective-permute-start(bf16[73728]{0:T(1024)(128)(2,1)S(1)} %maximum_select_fusion.4), channel_id=1, source_target_pairs={{0,4},{4,0},{8,12},{12,8},{1,5},{5,1},{9,13},{13,9},{2,6},{6,2},{1... | collective-permute-start | bytes 442376 | tf_op jit(solution)/shard_map/ppermute | solution.py:100
  121.1 5.2 %collective-permute-start.13 = (bf16[73728]{0:T(1024)(128)(2,1)S(1)}, bf16[73728]{0:T(1024)(128)(2,1)S(1)}, u32[]{:S(2)}, u32[]{:S(2)}) collective-permute-start(bf16[73728]{0:T(1024)(128)(2,1)S(1)} %maximum_select_fusion.3), channel_id=1, source_target_pairs={{0,4},{4,0},{8,12},{12,8},{1,5},{5,1},{9,13},{13,9},{2,6},{6,2},{1... | collective-permute-start | bytes 442376 | tf_op jit(solution)/shard_map/ppermute | solution.py:100
  (12 other events, 11.9 us)

commit v11 on v6

--- a/solution.py
+++ b/solution.py
@@ -287,11 +287,11 @@
 
     scale = 1.0 / batches
     summed = []
-    for layer_idx in reversed(range(layer_count)):
+    for layer_idx in range(layer_count):
         mine_terms = by_section(partials[0][layer_idx], partials[1][layer_idx], 0)
         other_terms = by_section(partials[1][layer_idx], partials[0][layer_idx], 0)
         other_terms = swap((other_terms * scale).astype(jnp.bfloat16)).astype(jnp.float32)
-        summed.insert(0, summed_over_tiles(mine_terms * scale + other_terms))
+        summed.append(summed_over_tiles(mine_terms * scale + other_terms))
     gathered = jnp.stack(summed)
     mine_back = by_section(results[0], results[1], 0)
     other_back = swap(by_section(results[1], results[0], 0))

time: 123 us -> 123 us (level)
  no operation moved by 1% of the time
where the time goes in v11:
time: 123 us
  starting transfers between devices  40 us (33%)
  other arithmetic  25.8 us (21%)
  waiting for transfers between devices  24.1 us (20%)
  matrix products  17.1 us (14%)
  local copies, waits for them, and re-layouts  14.1 us (11%)
  between operations  1.7 us (1%)
    ppermute x12, starting transfers between devices, exchange(): return lax.ppermute(values, axis, [(i, i ^ distance) for i in range(count)])  26.1 us
    ppermute x12, waiting for transfers between devices, exchange(): return lax.ppermute(values, axis, [(i, i ^ distance) for i in range(count)])  13.7 us
    ppermute x4, starting transfers between devices, from_neighbours(): parts.append(lax.ppermute(piece, AXES, pairs))  12.6 us
    ppermute x4, waiting for transfers between devices, from_neighbours(): parts.append(lax.ppermute(piece, AXES, pairs))  10.4 us
    conv_general_dilated x8, matrix products, convolve(): lax.conv_general_dilated(padded, kernel, (1, 1), 'VALID', dimension_numbe...  9.95 us
    convert_element_type x4, other arithmetic, local_split(): current = current.astype(jnp.bfloat16)  9.08 us
    convert_element_type x4, other arithmetic, section_chain(): signal = signal.astype(jnp.bfloat16)  8.96 us
    transpose x4, matrix products, kernel_terms(): return jnp.transpose(terms, (1, 2, 0, 3))  7.12 us
  transfers between devices with their start and end apart: 21, of which 12 were waited for; matrix products, arithmetic and copies ran while one was open for 9% of the time, Pallas kernels for 0%

profile of v11, /device:TPU:0, one launch (start us, length us, event | category | flops | bytes accessed | tf_op | source)
XLA Modules:
  0.0 122.8 jit_solution(3343659442049824205)
XLA Ops:
  5.4 5.4 %collective-permute-start.1 = (bf16[6,6,32,128]{3,2,0,1:T(8,128)(2,1)S(1)}, bf16[6,6,32,128]{3,2,0,1:T(8,128)(2,1)S(1)}, u32[]{:S(2)}, u32[]{:S(2)}) collective-permute-start(bf16[6,6,32,128]{3,2,0,1:T(8,128)(2,1)S(1)} %get-tuple-element.18), channel_id=1, source_target_pairs={{0,4},{1,5},{2,6},{3,7},{4,8},{5,9},{6,10},{7,11},{8,12},{9,13},{1... | collective-permute-start | bytes 884744 | tf_op jit(solution)/shard_map/ppermute | solution.py:43
  11.0 5.8 %collective-permute-done.2 = bf16[6,6,32,128]{3,2,0,1:T(8,128)(2,1)S(1)} collective-permute-done((bf16[6,6,32,128]{3,2,0,1:T(8,128)(2,1)S(1)}, bf16[6,6,32,128]{3,2,0,1:T(8,128)(2,1)S(1)}, u32[]{:S(2)}, u32[]{:S(2)}) %collective-permute-start.2) | collective-permute-done | bytes 294944 | tf_op jit(solution)/shard_map/ppermute | solution.py:43
  18.8 4.6 %collective-permute-start.3 = (bf16[6,28,6,128]{3,2,0,1:T(8,128)(2,1)S(1)}, bf16[6,28,6,128]{3,2,0,1:T(8,128)(2,1)S(1)}, u32[]{:S(2)}, u32[]{:S(2)}) collective-permute-start(bf16[6,28,6,128]{3,2,0,1:T(8,128)(2,1)S(1)} %get-tuple-element.14), channel_id=1, source_target_pairs={{0,1},{1,2},{2,3},{4,5},{5,6},{6,7},{8,9},{9,10},{10,11},{12,13},{... | collective-permute-start | bytes 774152 | tf_op jit(solution)/shard_map/ppermute | solution.py:43
  25.8 2.8 %collective-permute-done.4 = bf16[6,28,6,128]{3,2,0,1:T(8,128)(2,1)S(1)} collective-permute-done((bf16[6,28,6,128]{3,2,0,1:T(8,128)(2,1)S(1)}, bf16[6,28,6,128]{3,2,0,1:T(8,128)(2,1)S(1)}, u32[]{:S(2)}, u32[]{:S(2)}) %collective-permute-start.4) | collective-permute-done | bytes 258080 | tf_op jit(solution)/shard_map/ppermute | solution.py:43
  29.8 1.6 %pad_maximum_fusion = (bf16[2,28,44,128]{3,2,0,1:T(8,128)(2,1)}, bf16[2,28,44,128]{3,2,0,1:T(8,128)(2,1)S(1)}) fusion(bf16[6,28,6,128]{3,2,0,1:T(8,128)(2,1)S(1)} %collective-permute-done.4, bf16[6,28,6,128]{3,2,0,1:T(8,128)(2,1)S(1)} %collective-permute-done.3, bf16[6,6,32,128]{3,2,0,1:T(8,128)(2,1)S(1)} %collective-permute-done.2, ...), kind=kLoop, calls=%fused_computation.58 | loop fusion | flops 8830976 | bytes 3153920 | tf_op jit(solution)/shard_map/concatenate | solution.py:44
  33.8 1.7 %fusion.1 = bf16[26,16,6,128]{3,1,2,0:T(8,128)(2,1)S(1)} fusion(bf16[28,2,8,8,128]{4,1,3,2,0:T(2,128)(2,1)S(1)} %fusion.16, pred[16,6]{0,1:T(8,128)(4,1)S(1)} %copy-done.23, bf16[2,3,3,128,128]{4,3,2,1,0:T(8,128)(2,1)S(1)} %get-tuple-element.17), kind=kOutput, calls=%fused_computation.6 | convolution fusion | flops 736739328 | bytes 1852416 | tf_op jit(solution)/shard_map/conv_general_dilated | solution.py:63
  36.0 1.7 %fusion.11 = bf16[26,2,42,128]{3,1,2,0:T(2,128)(2,1)S(1)} fusion(bf16[26,2,42,128]{3,2,1,0:T(8,128)(2,1)S(1)} %bitcast.129, pred[26,42]{1,0:T(8,128)(4,1)S(1)} %broadcast_and_fusion), kind=kLoop, calls=%fused_computation.27 | loop fusion | flops 279552 | bytes 1119300 | tf_op jit(solution)/shard_map/convert_element_type | solution.py:278
  37.7 1.7 %fusion.99 = bf16[2,26,42,128]{3,0,2,1:T(2,128)(2,1)S(1)} fusion(bf16[26,2,42,128]{3,2,1,0:T(8,128)(2,1)S(1)} %bitcast.130, pred[26,42]{1,0:T(8,128)(4,1)S(1)} %broadcast_and_fusion), kind=kLoop, calls=%fused_computation.201 | loop fusion | flops 279552 | bytes 1119300 | tf_op jit(solution)/shard_map/convert_element_type | solution.py:278
  42.6 2.8 %fusion.19 = bf16[22,2,38,128]{3,1,2,0:T(2,128)(2,1)S(1)} fusion(bf16[22,2,38,128]{3,0,2,1:T(8,128)(2,1)S(1)} %slice.163, pred[22,38]{1,0:T(8,128)(4,1)S(1)} %broadcast_and_fusion.2), kind=kLoop, calls=%fused_computation.39 | loop fusion | flops 214016 | bytes 856900 | tf_op jit(solution)/shard_map/convert_element_type | solution.py:278
  45.4 2.8 %fusion.98 = bf16[2,22,38,128]{3,0,2,1:T(2,128)(2,1)S(1)} fusion(bf16[22,2,38,128]{3,0,2,1:T(8,128)(2,1)S(1)} %slice.163, pred[22,38]{1,0:T(8,128)(4,1)S(1)} %broadcast_and_fusion.2), kind=kLoop, calls=%fused_computation.200 | loop fusion | flops 214016 | bytes 856900 | tf_op jit(solution)/shard_map/convert_element_type | solution.py:278
  49.3 1.6 %fusion.2 = bf16[24,16,6,128]{3,1,2,0:T(8,128)(2,1)S(1)} fusion(bf16[26,2,7,2,128]{4,2,1,3,0:T(8,128)(2,1)S(1)} %slice.150, bf16[26,2,8,6,128]{4,2,1,3,0:T(8,128)(2,1)S(1)} %copy.147, pred[16,6]{0,1:T(8,128)(4,1)S(1)} %copy-done.22, bf16[2,3,3,128,128]{4,3,2,1,0:T(8,128)(2,1)S(1)} %copy-done.8), kind=kOutput, calls=%fused_computation.8 | convolution fusion | flops 682622976 | bytes 1737728 | tf_op jit(solution)/shard_map/conv_general_dilated | solution.py:63
  52.2 2.1 %fusion.15 = bf16[2,24,40,128]{3,2,0,1:T(8,128)(2,1)S(1)} fusion(bf16[24,2,40,128]{3,0,2,1:T(8,128)(2,1)S(1)} %slice.152, bf16[6,28,6,128]{3,2,0,1:T(8,128)(2,1)S(1)} %copy-done.11, bf16[6,28,6,128]{3,2,0,1:T(8,128)(2,1)S(1)} %copy-done.13, bf16[6,6,32,128]{3,2,0,1:T(8,128)(2,1)S(1)} %copy-done.2, bf16[6,6,32,128]{3,2,0,1:T(8,128)(2,1)S(1)} %copy-done.4, ...), kind=kLoop, calls=%fused_computation.34 | loop fusion | flops 5160960 | bytes 2876352 | tf_op jit(solution)/shard_map/convert_element_type | solution.py:232
  57.0 2.9 %fusion.22 = bf16[2,22,38,128]{3,0,2,1:T(2,128)(2,1)S(1)} fusion(f32[22,2,38,128]{3,0,2,1:T(8,128)S(1)} %slice.155, pred[22,38]{1,0:T(8,128)(4,1)S(1)} %broadcast_and_fusion.2, bf16[2,26,42,128]{3,0,2,1:T(2,128)(2,1)S(1)} %fusion.99), kind=kLoop, calls=%fused_computation.43 | loop fusion | flops 1284096 | bytes 1712964 | tf_op jit(solution)/shard_map/convert_element_type | solution.py:232
  63.8 1.7 %fusion.34 = bf16[20,2,36,128]{3,1,2,0:T(2,128)(2,1)S(1)} fusion(f32[20,2,36,128]{3,0,2,1:T(8,128)S(1)} %slice.159, pred[20,36]{1,0:T(8,128)(4,1)S(1)} %broadcast_and_fusion.3, bf16[20,2,36,128]{3,0,2,1:T(8,128)(2,1)S(1)} %slice.166), kind=kLoop, calls=%fused_computation.56 | loop fusion | flops 1290240 | bytes 1475280 | tf_op jit(solution)/shard_map/convert_element_type | solution.py:232
  68.0 2.3 %fusion.56 = bf16[2,18,34,128]{3,0,2,1:T(2,128)(2,1)S(1)} fusion(f32[18,2,34,128]{3,0,2,1:T(8,128)S(1)} %slice.169, pred[18,34]{1,0:T(8,128)(4,1)S(1)} %broadcast_and_fusion.4, bf16[2,22,38,128]{3,0,2,1:T(2,128)(2,1)S(1)} %fusion.98), kind=kLoop, calls=%fused_computation.84 | loop fusion | flops 940032 | bytes 1253988 | tf_op jit(solution)/shard_map/convert_element_type | solution.py:232
  70.3 1.8 %fusion.52 = f32[3,3,128,128]{3,2,1,0:T(8,128)S(1)} fusion(bf16[2,28,44,128]{3,2,0,1:T(8,128)(2,1)S(1)} %copy-done.9, bf16[2,18,34,128]{3,0,2,1:T(2,128)(2,1)S(1)} %fusion.56), kind=kOutput, calls=%fused_computation.79 | convolution fusion | flops 301989888 | bytes 1540096 | tf_op jit(solution)/shard_map/transpose | solution.py:82
  74.2 1.8 %fusion.73 = f32[3,3,128,128]{3,2,1,0:T(8,128)S(1)} fusion(bf16[22,2,38,128]{3,1,2,0:T(2,128)(2,1)S(1)} %fusion.19, bf16[2,20,36,128]{3,0,2,1:T(2,128)(2,1)S(1)} %bitcast.156), kind=kOutput, calls=%fused_computation.141 | convolution fusion | flops 301989888 | bytes 1280000 | tf_op jit(solution)/shard_map/transpose | solution.py:82
  75.9 1.8 %multiply_convert_fusion = (bf16[3,3,128,128]{3,2,1,0:T(8,128)(2,1)S(1)}, f32[3,3,128,128]{3,2,1,0:T(8,128)S(1)}) fusion(f32[3,3,128,128]{3,2,1,0:T(8,128)S(1)} %fusion.73, pred[]{:T(512)S(6)} %eq.27, bf16[26,2,42,128]{3,1,2,0:T(2,128)(2,1)S(1)} %fusion.11, bf16[2,16,32,128]{3,2,0,1:T(8,128)(2,1)S(1)} %slice.183), kind=kOutput, calls=%fused_computation.87 | convolution fusion | flops 302432256 | bytes 2295809 | tf_op jit(solution)/shard_map/transpose | solution.py:82
  78.3 1.8 %multiply_convert_fusion.1 = (bf16[3,3,128,128]{3,2,1,0:T(8,128)(2,1)S(1)}, f32[3,3,128,128]{3,2,1,0:T(8,128)S(1)}) fusion(f32[3,3,128,128]{3,2,1,0:T(8,128)S(1)} %fusion.52, pred[]{:T(512)S(6)} %eq.27, bf16[2,22,38,128]{3,0,2,1:T(2,128)(2,1)S(1)} %fusion.22, bf16[2,28,44,128]{3,2,0,1:T(8,128)(2,1)S(1)} %get-tuple-element.13), kind=kOutput, calls=%fused_computation.89 | convolution fusion | flops 302432256 | bytes 2424833 | tf_op jit(solution)/shard_map/transpose | solution.py:82
  81.2 5.0 %collective-permute-start.15 = (bf16[73728]{0:T(1024)(128)(2,1)S(1)}, bf16[73728]{0:T(1024)(128)(2,1)S(1)}, u32[]{:S(2)}, u32[]{:S(2)}) collective-permute-start(bf16[73728]{0:T(1024)(128)(2,1)S(1)} %select_convert_fusion), channel_id=1, source_target_pairs={{0,4},{4,0},{8,12},{12,8},{1,5},{5,1},{9,13},{13,9},{2,6},{6,2},{1... | collective-permute-start | bytes 442376 | tf_op jit(solution)/shard_map/ppermute | solution.py:100
  86.9 4.0 %collective-permute-done.15 = bf16[73728]{0:T(1024)(128)(2,1)S(1)} collective-permute-done((bf16[73728]{0:T(1024)(128)(2,1)S(1)}, bf16[73728]{0:T(1024)(128)(2,1)S(1)}, u32[]{:S(2)}, u32[]{:S(2)}) %collective-permute-start.15) | collective-permute-done | bytes 147488 | tf_op jit(solution)/shard_map/ppermute | solution.py:100
  91.0 2.5 %collective-permute-start.16 = (bf16[36864]{0:T(1024)(128)(2,1)S(1)}, bf16[36864]{0:T(1024)(128)(2,1)S(1)}, u32[]{:S(2)}, u32[]{:S(2)}) collective-permute-start(bf16[36864]{0:T(1024)(128)(2,1)S(1)} %select_convert_fusion.4), channel_id=1, source_target_pairs={{0,1},{1,0},{2,3},{3,2},{4,5},{5,4},{6,7},{7,6},{8,9},{9,8},{10,11... | collective-permute-start | bytes 221192 | tf_op jit(solution)/shard_map/ppermute | solution.py:100
  94.0 2.5 %collective-permute-start.9 = (bf16[36864]{0:T(1024)(128)(2,1)S(1)}, bf16[36864]{0:T(1024)(128)(2,1)S(1)}, u32[]{:S(2)}, u32[]{:S(2)}) collective-permute-start(bf16[36864]{0:T(1024)(128)(2,1)S(1)} %select_convert_fusion.6), channel_id=1, source_target_pairs={{0,1},{1,0},{2,3},{3,2},{4,5},{5,4},{6,7},{7,6},{8,9},{9,8},{10,11... | collective-permute-start | bytes 221192 | tf_op jit(solution)/shard_map/ppermute | solution.py:100
  96.6 3.7 %collective-permute-start.17 = (bf16[36864]{0:T(1024)(128)(2,1)S(1)}, bf16[36864]{0:T(1024)(128)(2,1)S(1)}, u32[]{:S(2)}, u32[]{:S(2)}) collective-permute-start(bf16[36864]{0:T(1024)(128)(2,1)S(1)} %add_convert_fusion.2), channel_id=1, source_target_pairs={{0,8},{4,12},{8,0},{12,4},{1,9},{5,13},{9,1},{13,5},{2,10},{6,14},... | collective-permute-start | bytes 221192 | tf_op jit(solution)/shard_map/ppermute | solution.py:100
  100.3 2.3 %collective-permute-start.10 = (bf16[36864]{0:T(1024)(128)(2,1)S(1)}, bf16[36864]{0:T(1024)(128)(2,1)S(1)}, u32[]{:S(2)}, u32[]{:S(2)}) collective-permute-start(bf16[36864]{0:T(1024)(128)(2,1)S(1)} %add_convert_fusion.5), channel_id=1, source_target_pairs={{0,8},{4,12},{8,0},{12,4},{1,9},{5,13},{9,1},{13,5},{2,10},{6,14},... | collective-permute-start | bytes 221192 | tf_op jit(solution)/shard_map/ppermute | solution.py:100
  103.0 2.7 %collective-permute-start.18 = (bf16[36864]{0:T(1024)(128)(2,1)S(1)}, bf16[36864]{0:T(1024)(128)(2,1)S(1)}, u32[]{:S(2)}, u32[]{:S(2)}) collective-permute-start(bf16[36864]{0:T(1024)(128)(2,1)S(1)} %add_convert_fusion.1), channel_id=1, source_target_pairs={{0,2},{1,3},{2,0},{3,1},{4,6},{5,7},{6,4},{7,5},{8,10},{9,11},{10,... | collective-permute-start | bytes 221192 | tf_op jit(solution)/shard_map/ppermute | solution.py:100
  105.7 2.3 %collective-permute-start.11 = (bf16[36864]{0:T(1024)(128)(2,1)S(1)}, bf16[36864]{0:T(1024)(128)(2,1)S(1)}, u32[]{:S(2)}, u32[]{:S(2)}) collective-permute-start(bf16[36864]{0:T(1024)(128)(2,1)S(1)} %add_convert_fusion.4), channel_id=1, source_target_pairs={{0,2},{1,3},{2,0},{3,1},{4,6},{5,7},{6,4},{7,5},{8,10},{9,11},{10,... | collective-permute-start | bytes 221192 | tf_op jit(solution)/shard_map/ppermute | solution.py:100
  108.0 2.3 %collective-permute-done.18 = bf16[36864]{0:T(1024)(128)(2,1)S(1)} collective-permute-done((bf16[36864]{0:T(1024)(128)(2,1)S(1)}, bf16[36864]{0:T(1024)(128)(2,1)S(1)}, u32[]{:S(2)}, u32[]{:S(2)}) %collective-permute-start.18) | collective-permute-done | bytes 73760 | tf_op jit(solution)/shard_map/ppermute | solution.py:100
  111.2 1.7 %collective-permute-start.12 = (bf16[36864]{0:T(1024)(128)(2,1)S(1)}, bf16[36864]{0:T(1024)(128)(2,1)S(1)}, u32[]{:S(2)}, u32[]{:S(2)}) collective-permute-start(bf16[36864]{0:T(1024)(128)(2,1)S(1)} %add_convert_fusion.3), channel_id=1, source_target_pairs={{0,1},{1,0},{2,3},{3,2},{4,5},{5,4},{6,7},{7,6},{8,9},{9,8},{10,11... | collective-permute-start | bytes 221192 | tf_op jit(solution)/shard_map/ppermute | solution.py:100
  112.9 1.9 %collective-permute-done.19 = bf16[36864]{0:T(1024)(128)(2,1)S(1)} collective-permute-done((bf16[36864]{0:T(1024)(128)(2,1)S(1)}, bf16[36864]{0:T(1024)(128)(2,1)S(1)}, u32[]{:S(2)}, u32[]{:S(2)}) %collective-permute-start.19) | collective-permute-done | bytes 73760 | tf_op jit(solution)/shard_map/ppermute | solution.py:100
  114.9 1.6 %collective-permute-start.20 = (bf16[73728]{0:T(1024)(128)(2,1)S(1)}, bf16[73728]{0:T(1024)(128)(2,1)S(1)}, u32[]{:S(2)}, u32[]{:S(2)}) collective-permute-start(bf16[73728]{0:T(1024)(128)(2,1)S(1)} %maximum_select_fusion.4), channel_id=1, source_target_pairs={{0,4},{4,0},{8,12},{12,8},{1,5},{5,1},{9,13},{13,9},{2,6},{6,2},{1... | collective-permute-start | bytes 442376 | tf_op jit(solution)/shard_map/ppermute | solution.py:100
  117.2 2.9 %collective-permute-done.20 = bf16[73728]{0:T(1024)(128)(2,1)S(1)} collective-permute-done((bf16[73728]{0:T(1024)(128)(2,1)S(1)}, bf16[73728]{0:T(1024)(128)(2,1)S(1)}, u32[]{:S(2)}, u32[]{:S(2)}) %collective-permute-start.20) | collective-permute-done | bytes 147488 | tf_op jit(solution)/shard_map/ppermute | solution.py:100
  (176 shorter events, 36.9 us)
Async XLA Ops:
  0.6 2.6 %copy-start = (bf16[4,16,32,128]{3,2,1,0:T(8,128)(2,1)S(1)}, bf16[4,16,32,128]{3,2,1,0:T(8,128)(2,1)}, u32[]{:S(2)}) copy-start(bf16[4,16,32,128]{3,2,1,0:T(8,128)(2,1)} %param.6) | copy-start | bytes 1572868
  0.6 1.8 %copy-start.14 = (bf16[2,3,3,128,128]{4,3,2,1,0:T(8,128)(2,1)S(1)}, bf16[2,3,3,128,128]{4,3,2,1,0:T(8,128)(2,1)}, u32[]{:S(2)}) copy-start(bf16[2,3,3,128,128]{4,3,2,1,0:T(8,128)(2,1)} %param.5) | copy-start | bytes 1769476
  0.7 1.9 %copy-start.17 = (s32[4]{0:T(128)S(1)}, s32[4]{0:T(128)}, u32[]{:S(2)}) copy-start(s32[4]{0:T(128)} %param.7) | copy-start | bytes 52
  1.9 2.2 %collective-permute-start = (bf16[2,16,32,128]{3,2,0,1:T(8,128)(2,1)S(1)}, bf16[2,16,32,128]{3,2,0,1:T(8,128)(2,1)S(1)}, u32[]{:S(2)}, u32[]{:S(2)}) collective-permute-start(bf16[2,16,32,128]{3,2,0,1:T(8,128)(2,1)S(1)} %bitcast.163), channel_id=1, source_target_pairs={{0,16},{16,0},{1,17},{17,1},{2,18},{18,2},{3,19},{19,3},{4,20},{20... | collective-permute-start | bytes 786440 | tf_op jit(solution)/shard_map/ppermute | solution.py:249
  2.4 21.0 %collective-permute-start.5 = (bf16[2,3,3,128,128]{4,3,2,1,0:T(8,128)(2,1)S(1)}, bf16[2,3,3,128,128]{4,3,2,1,0:T(8,128)(2,1)}, u32[]{:S(2)}, u32[]{:S(2)}) collective-permute-start(bf16[2,3,3,128,128]{4,3,2,1,0:T(8,128)(2,1)S(1)} %copy-done.14), channel_id=1, source_target_pairs={{0,16},{16,0},{1,17},{17,1},{2,18},{18,2},{3,19},{19,3},{4,20},{20... | collective-permute-start | bytes 1769480 | tf_op jit(solution)/shard_map/ppermute | solution.py:249
  4.1 12.7 %collective-permute-start.2 = (bf16[6,6,32,128]{3,2,0,1:T(8,128)(2,1)S(1)}, bf16[6,6,32,128]{3,2,0,1:T(8,128)(2,1)S(1)}, u32[]{:S(2)}, u32[]{:S(2)}) collective-permute-start(bf16[6,6,32,128]{3,2,0,1:T(8,128)(2,1)S(1)} %get-tuple-element.19), channel_id=1, source_target_pairs={{4,0},{5,1},{6,2},{7,3},{8,4},{9,5},{10,6},{11,7},{12,8},{13,9},{1... | collective-permute-start | bytes 884744 | tf_op jit(solution)/shard_map/ppermute | solution.py:43
  5.4 11.9 %collective-permute-start.1 = (bf16[6,6,32,128]{3,2,0,1:T(8,128)(2,1)S(1)}, bf16[6,6,32,128]{3,2,0,1:T(8,128)(2,1)S(1)}, u32[]{:S(2)}, u32[]{:S(2)}) collective-permute-start(bf16[6,6,32,128]{3,2,0,1:T(8,128)(2,1)S(1)} %get-tuple-element.18), channel_id=1, source_target_pairs={{0,4},{1,5},{2,6},{3,7},{4,8},{5,9},{6,10},{7,11},{8,12},{9,13},{1... | collective-permute-start | bytes 884744 | tf_op jit(solution)/shard_map/ppermute | solution.py:43
  16.8 13.0 %copy-start.1 = (bf16[6,6,32,128]{3,2,0,1:T(8,128)(2,1)}, bf16[6,6,32,128]{3,2,0,1:T(8,128)(2,1)S(1)}, u32[]{:S(2)}) copy-start(bf16[6,6,32,128]{3,2,0,1:T(8,128)(2,1)S(1)} %collective-permute-done.2) | copy-start | bytes 884740
  17.4 12.4 %copy-start.3 = (bf16[6,6,32,128]{3,2,0,1:T(8,128)(2,1)}, bf16[6,6,32,128]{3,2,0,1:T(8,128)(2,1)S(1)}, u32[]{:S(2)}) copy-start(bf16[6,6,32,128]{3,2,0,1:T(8,128)(2,1)S(1)} %collective-permute-done.1) | copy-start | bytes 884740
  17.5 11.1 %collective-permute-start.4 = (bf16[6,28,6,128]{3,2,0,1:T(8,128)(2,1)S(1)}, bf16[6,28,6,128]{3,2,0,1:T(8,128)(2,1)S(1)}, u32[]{:S(2)}, u32[]{:S(2)}) collective-permute-start(bf16[6,28,6,128]{3,2,0,1:T(8,128)(2,1)S(1)} %get-tuple-element.15), channel_id=1, source_target_pairs={{1,0},{2,1},{3,2},{5,4},{6,5},{7,6},{9,8},{10,9},{11,10},{13,12},{... | collective-permute-start | bytes 774152 | tf_op jit(solution)/shard_map/ppermute | solution.py:43
  18.8 11.0 %collective-permute-start.3 = (bf16[6,28,6,128]{3,2,0,1:T(8,128)(2,1)S(1)}, bf16[6,28,6,128]{3,2,0,1:T(8,128)(2,1)S(1)}, u32[]{:S(2)}, u32[]{:S(2)}) collective-permute-start(bf16[6,28,6,128]{3,2,0,1:T(8,128)(2,1)S(1)} %get-tuple-element.14), channel_id=1, source_target_pairs={{0,1},{1,2},{2,3},{4,5},{5,6},{6,7},{8,9},{9,10},{10,11},{12,13},{... | collective-permute-start | bytes 774152 | tf_op jit(solution)/shard_map/ppermute | solution.py:43
  24.6 9.2 %copy-start.7 = (bf16[2,3,3,128,128]{4,3,2,1,0:T(8,128)(2,1)}, bf16[2,3,3,128,128]{4,3,2,1,0:T(8,128)(2,1)S(1)}, u32[]{:S(2)}) copy-start(bf16[2,3,3,128,128]{4,3,2,1,0:T(8,128)(2,1)S(1)} %get-tuple-element.17) | copy-start | bytes 1769476
  28.6 2.8 %copy-start.10 = (bf16[6,28,6,128]{3,2,0,1:T(8,128)(2,1)}, bf16[6,28,6,128]{3,2,0,1:T(8,128)(2,1)S(1)}, u32[]{:S(2)}) copy-start(bf16[6,28,6,128]{3,2,0,1:T(8,128)(2,1)S(1)} %collective-permute-done.4) | copy-start | bytes 774148
  29.8 1.7 %copy-start.12 = (bf16[6,28,6,128]{3,2,0,1:T(8,128)(2,1)}, bf16[6,28,6,128]{3,2,0,1:T(8,128)(2,1)S(1)}, u32[]{:S(2)}) copy-start(bf16[6,28,6,128]{3,2,0,1:T(8,128)(2,1)S(1)} %collective-permute-done.3) | copy-start | bytes 774148
  32.4 1.4 %copy-start.23 = (pred[16,6]{0,1:T(8,128)(4,1)S(1)}, pred[16,6]{0,1:T(8,128)(4,1)}, u32[]{:S(2)}) copy-start(pred[16,6]{0,1:T(8,128)(4,1)} %constant.196) | copy-start | bytes 292
  36.0 3.5 %copy-start.9 = (bf16[2,28,44,128]{3,2,0,1:T(8,128)(2,1)S(1)}, bf16[2,28,44,128]{3,2,0,1:T(8,128)(2,1)}, u32[]{:S(2)}) copy-start(bf16[2,28,44,128]{3,2,0,1:T(8,128)(2,1)} %get-tuple-element.12) | copy-start | bytes 1892356
  50.9 1.2 %copy-start.13 = (bf16[6,28,6,128]{3,2,0,1:T(8,128)(2,1)S(1)}, bf16[6,28,6,128]{3,2,0,1:T(8,128)(2,1)}, u32[]{:S(2)}) copy-start(bf16[6,28,6,128]{3,2,0,1:T(8,128)(2,1)} %copy-done.12) | copy-start | bytes 774148
  74.1 6.1 %collective-permute-start.6 = (bf16[2,16,32,128]{3,2,0,1:T(8,128)(2,1)S(1)}, bf16[2,16,32,128]{3,2,0,1:T(8,128)(2,1)S(1)}, u32[]{:S(2)}, u32[]{:S(2)}) collective-permute-start(bf16[2,16,32,128]{3,2,0,1:T(8,128)(2,1)S(1)} %get-tuple-element.21), channel_id=1, source_target_pairs={{0,16},{16,0},{1,17},{17,1},{2,18},{18,2},{3,19},{19,3},{4,20},{20... | collective-permute-start | bytes 786440 | tf_op jit(solution)/shard_map/ppermute | solution.py:249
  77.7 3.3 %collective-permute-start.14 = (bf16[3,3,128,128]{3,2,1,0:T(8,128)(2,1)S(1)}, bf16[3,3,128,128]{3,2,1,0:T(8,128)(2,1)S(1)}, u32[]{:S(2)}, u32[]{:S(2)}) collective-permute-start(bf16[3,3,128,128]{3,2,1,0:T(8,128)(2,1)S(1)} %get-tuple-element.26), channel_id=1, source_target_pairs={{0,16},{16,0},{1,17},{17,1},{2,18},{18,2},{3,19},{19,3},{4,20},{20... | collective-permute-start | bytes 884744 | tf_op jit(solution)/shard_map/ppermute | solution.py:249
  80.1 6.2 %collective-permute-start.7 = (bf16[3,3,128,128]{3,2,1,0:T(8,128)(2,1)S(1)}, bf16[3,3,128,128]{3,2,1,0:T(8,128)(2,1)S(1)}, u32[]{:S(2)}, u32[]{:S(2)}) collective-permute-start(bf16[3,3,128,128]{3,2,1,0:T(8,128)(2,1)S(1)} %get-tuple-element.28), channel_id=1, source_target_pairs={{0,16},{16,0},{1,17},{17,1},{2,18},{18,2},{3,19},{19,3},{4,20},{20... | collective-permute-start | bytes 884744 | tf_op jit(solution)/shard_map/ppermute | solution.py:249
  81.2 9.7 %collective-permute-start.15 = (bf16[73728]{0:T(1024)(128)(2,1)S(1)}, bf16[73728]{0:T(1024)(128)(2,1)S(1)}, u32[]{:S(2)}, u32[]{:S(2)}) collective-permute-start(bf16[73728]{0:T(1024)(128)(2,1)S(1)} %select_convert_fusion), channel_id=1, source_target_pairs={{0,4},{4,0},{8,12},{12,8},{1,5},{5,1},{9,13},{13,9},{2,6},{6,2},{1... | collective-permute-start | bytes 442376 | tf_op jit(solution)/shard_map/ppermute | solution.py:100
  86.4 7.5 %collective-permute-start.8 = (bf16[73728]{0:T(1024)(128)(2,1)S(1)}, bf16[73728]{0:T(1024)(128)(2,1)S(1)}, u32[]{:S(2)}, u32[]{:S(2)}) collective-permute-start(bf16[73728]{0:T(1024)(128)(2,1)S(1)} %select_convert_fusion.2), channel_id=1, source_target_pairs={{0,4},{4,0},{8,12},{12,8},{1,5},{5,1},{9,13},{13,9},{2,6},{6,2},{1... | collective-permute-start | bytes 442376 | tf_op jit(solution)/shard_map/ppermute | solution.py:100
  91.0 5.5 %collective-permute-start.16 = (bf16[36864]{0:T(1024)(128)(2,1)S(1)}, bf16[36864]{0:T(1024)(128)(2,1)S(1)}, u32[]{:S(2)}, u32[]{:S(2)}) collective-permute-start(bf16[36864]{0:T(1024)(128)(2,1)S(1)} %select_convert_fusion.4), channel_id=1, source_target_pairs={{0,1},{1,0},{2,3},{3,2},{4,5},{5,4},{6,7},{7,6},{8,9},{9,8},{10,11... | collective-permute-start | bytes 221192 | tf_op jit(solution)/shard_map/ppermute | solution.py:100
  94.0 6.3 %collective-permute-start.9 = (bf16[36864]{0:T(1024)(128)(2,1)S(1)}, bf16[36864]{0:T(1024)(128)(2,1)S(1)}, u32[]{:S(2)}, u32[]{:S(2)}) collective-permute-start(bf16[36864]{0:T(1024)(128)(2,1)S(1)} %select_convert_fusion.6), channel_id=1, source_target_pairs={{0,1},{1,0},{2,3},{3,2},{4,5},{5,4},{6,7},{7,6},{8,9},{9,8},{10,11... | collective-permute-start | bytes 221192 | tf_op jit(solution)/shard_map/ppermute | solution.py:100
  96.6 6.4 %collective-permute-start.17 = (bf16[36864]{0:T(1024)(128)(2,1)S(1)}, bf16[36864]{0:T(1024)(128)(2,1)S(1)}, u32[]{:S(2)}, u32[]{:S(2)}) collective-permute-start(bf16[36864]{0:T(1024)(128)(2,1)S(1)} %add_convert_fusion.2), channel_id=1, source_target_pairs={{0,8},{4,12},{8,0},{12,4},{1,9},{5,13},{9,1},{13,5},{2,10},{6,14},... | collective-permute-start | bytes 221192 | tf_op jit(solution)/shard_map/ppermute | solution.py:100
  100.3 5.4 %collective-permute-start.10 = (bf16[36864]{0:T(1024)(128)(2,1)S(1)}, bf16[36864]{0:T(1024)(128)(2,1)S(1)}, u32[]{:S(2)}, u32[]{:S(2)}) collective-permute-start(bf16[36864]{0:T(1024)(128)(2,1)S(1)} %add_convert_fusion.5), channel_id=1, source_target_pairs={{0,8},{4,12},{8,0},{12,4},{1,9},{5,13},{9,1},{13,5},{2,10},{6,14},... | collective-permute-start | bytes 221192 | tf_op jit(solution)/shard_map/ppermute | solution.py:100
  103.0 7.3 %collective-permute-start.18 = (bf16[36864]{0:T(1024)(128)(2,1)S(1)}, bf16[36864]{0:T(1024)(128)(2,1)S(1)}, u32[]{:S(2)}, u32[]{:S(2)}) collective-permute-start(bf16[36864]{0:T(1024)(128)(2,1)S(1)} %add_convert_fusion.1), channel_id=1, source_target_pairs={{0,2},{1,3},{2,0},{3,1},{4,6},{5,7},{6,4},{7,5},{8,10},{9,11},{10,... | collective-permute-start | bytes 221192 | tf_op jit(solution)/shard_map/ppermute | solution.py:100
  105.7 5.4 %collective-permute-start.11 = (bf16[36864]{0:T(1024)(128)(2,1)S(1)}, bf16[36864]{0:T(1024)(128)(2,1)S(1)}, u32[]{:S(2)}, u32[]{:S(2)}) collective-permute-start(bf16[36864]{0:T(1024)(128)(2,1)S(1)} %add_convert_fusion.4), channel_id=1, source_target_pairs={{0,2},{1,3},{2,0},{3,1},{4,6},{5,7},{6,4},{7,5},{8,10},{9,11},{10,... | collective-permute-start | bytes 221192 | tf_op jit(solution)/shard_map/ppermute | solution.py:100
  110.4 4.4 %collective-permute-start.19 = (bf16[36864]{0:T(1024)(128)(2,1)S(1)}, bf16[36864]{0:T(1024)(128)(2,1)S(1)}, u32[]{:S(2)}, u32[]{:S(2)}) collective-permute-start(bf16[36864]{0:T(1024)(128)(2,1)S(1)} %add_convert_fusion), channel_id=1, source_target_pairs={{0,1},{1,0},{2,3},{3,2},{4,5},{5,4},{6,7},{7,6},{8,9},{9,8},{10,11... | collective-permute-start | bytes 221192 | tf_op jit(solution)/shard_map/ppermute | solution.py:100
  111.2 5.2 %collective-permute-start.12 = (bf16[36864]{0:T(1024)(128)(2,1)S(1)}, bf16[36864]{0:T(1024)(128)(2,1)S(1)}, u32[]{:S(2)}, u32[]{:S(2)}) collective-permute-start(bf16[36864]{0:T(1024)(128)(2,1)S(1)} %add_convert_fusion.3), channel_id=1, source_target_pairs={{0,1},{1,0},{2,3},{3,2},{4,5},{5,4},{6,7},{7,6},{8,9},{9,8},{10,11... | collective-permute-start | bytes 221192 | tf_op jit(solution)/shard_map/ppermute | solution.py:100
  114.9 5.2 %collective-permute-start.20 = (bf16[73728]{0:T(1024)(128)(2,1)S(1)}, bf16[73728]{0:T(1024)(128)(2,1)S(1)}, u32[]{:S(2)}, u32[]{:S(2)}) collective-permute-start(bf16[73728]{0:T(1024)(128)(2,1)S(1)} %maximum_select_fusion.4), channel_id=1, source_target_pairs={{0,4},{4,0},{8,12},{12,8},{1,5},{5,1},{9,13},{13,9},{2,6},{6,2},{1... | collective-permute-start | bytes 442376 | tf_op jit(solution)/shard_map/ppermute | solution.py:100
  116.5 5.2 %collective-permute-start.13 = (bf16[73728]{0:T(1024)(128)(2,1)S(1)}, bf16[73728]{0:T(1024)(128)(2,1)S(1)}, u32[]{:S(2)}, u32[]{:S(2)}) collective-permute-start(bf16[73728]{0:T(1024)(128)(2,1)S(1)} %maximum_select_fusion.3), channel_id=1, source_target_pairs={{0,4},{4,0},{8,12},{12,8},{1,5},{5,1},{9,13},{13,9},{2,6},{6,2},{1... | collective-permute-start | bytes 442376 | tf_op jit(solution)/shard_map/ppermute | solution.py:100
  (13 other events, 13.2 us)

commit v12 on v11

--- a/solution.py
+++ b/solution.py
@@ -113,10 +113,7 @@
     for axis, distance in doubling:
         rounded = current.astype(jnp.bfloat16)
         other = exchange(rounded, axis, distance)
-        upper = (lax.axis_index(axis) // distance) % 2 == 1
-        first = jnp.where(upper, other, rounded).astype(jnp.float32)
-        second = jnp.where(upper, rounded, other).astype(jnp.float32)
-        current = first + second
+        current = rounded.astype(jnp.float32) + other.astype(jnp.float32)
     current = current.astype(jnp.bfloat16)
     for axis, distance, upper in reversed(kept):
         other = exchange(current, axis, distance)

time: 123 us -> 123 us (level)
  no operation moved by 1% of the time
where the time goes in v12:
time: 123 us
  starting transfers between devices  40.1 us (33%)
  other arithmetic  25.7 us (21%)
  waiting for transfers between devices  24.1 us (20%)
  matrix products  17.1 us (14%)
  local copies, waits for them, and re-layouts  14.1 us (11%)
  between operations  1.66 us (1%)
    ppermute x12, starting transfers between devices, exchange(): return lax.ppermute(values, axis, [(i, i ^ distance) for i in range(count)])  26.1 us
    ppermute x12, waiting for transfers between devices, exchange(): return lax.ppermute(values, axis, [(i, i ^ distance) for i in range(count)])  13.7 us
    ppermute x4, starting transfers between devices, from_neighbours(): parts.append(lax.ppermute(piece, AXES, pairs))  12.6 us
    ppermute x4, waiting for transfers between devices, from_neighbours(): parts.append(lax.ppermute(piece, AXES, pairs))  10.4 us
    conv_general_dilated x8, matrix products, convolve(): lax.conv_general_dilated(padded, kernel, (1, 1), 'VALID', dimension_numbe...  9.95 us
    convert_element_type x4, other arithmetic, local_split(): current = current.astype(jnp.bfloat16)  9.08 us
    convert_element_type x4, other arithmetic, section_chain(): signal = signal.astype(jnp.bfloat16)  8.96 us
    transpose x4, matrix products, kernel_terms(): return jnp.transpose(terms, (1, 2, 0, 3))  7.12 us
  transfers between devices with their start and end apart: 21, of which 12 were waited for; matrix products, arithmetic and copies ran while one was open for 9% of the time, Pallas kernels for 0%

profile of v12, /device:TPU:0, one launch (start us, length us, event | category | flops | bytes accessed | tf_op | source)
XLA Modules:
  0.0 122.8 jit_solution(1362670269526718534)
XLA Ops:
  5.4 5.4 %collective-permute-start.1 = (bf16[6,6,32,128]{3,2,0,1:T(8,128)(2,1)S(1)}, bf16[6,6,32,128]{3,2,0,1:T(8,128)(2,1)S(1)}, u32[]{:S(2)}, u32[]{:S(2)}) collective-permute-start(bf16[6,6,32,128]{3,2,0,1:T(8,128)(2,1)S(1)} %get-tuple-element.18), channel_id=1, source_target_pairs={{0,4},{1,5},{2,6},{3,7},{4,8},{5,9},{6,10},{7,11},{8,12},{9,13},{1... | collective-permute-start | bytes 884744 | tf_op jit(solution)/shard_map/ppermute | solution.py:43
  10.9 5.8 %collective-permute-done.2 = bf16[6,6,32,128]{3,2,0,1:T(8,128)(2,1)S(1)} collective-permute-done((bf16[6,6,32,128]{3,2,0,1:T(8,128)(2,1)S(1)}, bf16[6,6,32,128]{3,2,0,1:T(8,128)(2,1)S(1)}, u32[]{:S(2)}, u32[]{:S(2)}) %collective-permute-start.2) | collective-permute-done | bytes 294944 | tf_op jit(solution)/shard_map/ppermute | solution.py:43
  18.8 4.6 %collective-permute-start.3 = (bf16[6,28,6,128]{3,2,0,1:T(8,128)(2,1)S(1)}, bf16[6,28,6,128]{3,2,0,1:T(8,128)(2,1)S(1)}, u32[]{:S(2)}, u32[]{:S(2)}) collective-permute-start(bf16[6,28,6,128]{3,2,0,1:T(8,128)(2,1)S(1)} %get-tuple-element.14), channel_id=1, source_target_pairs={{0,1},{1,2},{2,3},{4,5},{5,6},{6,7},{8,9},{9,10},{10,11},{12,13},{... | collective-permute-start | bytes 774152 | tf_op jit(solution)/shard_map/ppermute | solution.py:43
  25.7 2.8 %collective-permute-done.4 = bf16[6,28,6,128]{3,2,0,1:T(8,128)(2,1)S(1)} collective-permute-done((bf16[6,28,6,128]{3,2,0,1:T(8,128)(2,1)S(1)}, bf16[6,28,6,128]{3,2,0,1:T(8,128)(2,1)S(1)}, u32[]{:S(2)}, u32[]{:S(2)}) %collective-permute-start.4) | collective-permute-done | bytes 258080 | tf_op jit(solution)/shard_map/ppermute | solution.py:43
  29.8 1.6 %pad_maximum_fusion = (bf16[2,28,44,128]{3,2,0,1:T(8,128)(2,1)}, bf16[2,28,44,128]{3,2,0,1:T(8,128)(2,1)S(1)}) fusion(bf16[6,28,6,128]{3,2,0,1:T(8,128)(2,1)S(1)} %collective-permute-done.4, bf16[6,28,6,128]{3,2,0,1:T(8,128)(2,1)S(1)} %collective-permute-done.3, bf16[6,6,32,128]{3,2,0,1:T(8,128)(2,1)S(1)} %collective-permute-done.2, ...), kind=kLoop, calls=%fused_computation.58 | loop fusion | flops 8830976 | bytes 3153920 | tf_op jit(solution)/shard_map/concatenate | solution.py:44
  33.8 1.7 %fusion.1 = bf16[26,16,6,128]{3,1,2,0:T(8,128)(2,1)S(1)} fusion(bf16[28,2,8,8,128]{4,1,3,2,0:T(2,128)(2,1)S(1)} %fusion.16, pred[16,6]{0,1:T(8,128)(4,1)S(1)} %copy-done.23, bf16[2,3,3,128,128]{4,3,2,1,0:T(8,128)(2,1)S(1)} %get-tuple-element.17), kind=kOutput, calls=%fused_computation.6 | convolution fusion | flops 736739328 | bytes 1852416 | tf_op jit(solution)/shard_map/conv_general_dilated | solution.py:63
  35.9 1.7 %fusion.11 = bf16[26,2,42,128]{3,1,2,0:T(2,128)(2,1)S(1)} fusion(bf16[26,2,42,128]{3,2,1,0:T(8,128)(2,1)S(1)} %bitcast.129, pred[26,42]{1,0:T(8,128)(4,1)S(1)} %broadcast_and_fusion), kind=kLoop, calls=%fused_computation.27 | loop fusion | flops 279552 | bytes 1119300 | tf_op jit(solution)/shard_map/convert_element_type | solution.py:275
  37.7 1.7 %fusion.99 = bf16[2,26,42,128]{3,0,2,1:T(2,128)(2,1)S(1)} fusion(bf16[26,2,42,128]{3,2,1,0:T(8,128)(2,1)S(1)} %bitcast.130, pred[26,42]{1,0:T(8,128)(4,1)S(1)} %broadcast_and_fusion), kind=kLoop, calls=%fused_computation.201 | loop fusion | flops 279552 | bytes 1119300 | tf_op jit(solution)/shard_map/convert_element_type | solution.py:275
  42.6 2.8 %fusion.19 = bf16[22,2,38,128]{3,1,2,0:T(2,128)(2,1)S(1)} fusion(bf16[22,2,38,128]{3,0,2,1:T(8,128)(2,1)S(1)} %slice.163, pred[22,38]{1,0:T(8,128)(4,1)S(1)} %broadcast_and_fusion.2), kind=kLoop, calls=%fused_computation.39 | loop fusion | flops 214016 | bytes 856900 | tf_op jit(solution)/shard_map/convert_element_type | solution.py:275
  45.4 2.8 %fusion.98 = bf16[2,22,38,128]{3,0,2,1:T(2,128)(2,1)S(1)} fusion(bf16[22,2,38,128]{3,0,2,1:T(8,128)(2,1)S(1)} %slice.163, pred[22,38]{1,0:T(8,128)(4,1)S(1)} %broadcast_and_fusion.2), kind=kLoop, calls=%fused_computation.200 | loop fusion | flops 214016 | bytes 856900 | tf_op jit(solution)/shard_map/convert_element_type | solution.py:275
  49.3 1.6 %fusion.2 = bf16[24,16,6,128]{3,1,2,0:T(8,128)(2,1)S(1)} fusion(bf16[26,2,7,2,128]{4,2,1,3,0:T(8,128)(2,1)S(1)} %slice.150, bf16[26,2,8,6,128]{4,2,1,3,0:T(8,128)(2,1)S(1)} %copy.147, pred[16,6]{0,1:T(8,128)(4,1)S(1)} %copy-done.22, bf16[2,3,3,128,128]{4,3,2,1,0:T(8,128)(2,1)S(1)} %copy-done.8), kind=kOutput, calls=%fused_computation.8 | convolution fusion | flops 682622976 | bytes 1737728 | tf_op jit(solution)/shard_map/conv_general_dilated | solution.py:63
  52.1 2.1 %fusion.15 = bf16[2,24,40,128]{3,2,0,1:T(8,128)(2,1)S(1)} fusion(bf16[24,2,40,128]{3,0,2,1:T(8,128)(2,1)S(1)} %slice.152, bf16[6,28,6,128]{3,2,0,1:T(8,128)(2,1)S(1)} %copy-done.11, bf16[6,28,6,128]{3,2,0,1:T(8,128)(2,1)S(1)} %copy-done.13, bf16[6,6,32,128]{3,2,0,1:T(8,128)(2,1)S(1)} %copy-done.2, bf16[6,6,32,128]{3,2,0,1:T(8,128)(2,1)S(1)} %copy-done.4, ...), kind=kLoop, calls=%fused_computation.34 | loop fusion | flops 5160960 | bytes 2876352 | tf_op jit(solution)/shard_map/convert_element_type | solution.py:229
  56.9 2.9 %fusion.22 = bf16[2,22,38,128]{3,0,2,1:T(2,128)(2,1)S(1)} fusion(f32[22,2,38,128]{3,0,2,1:T(8,128)S(1)} %slice.155, pred[22,38]{1,0:T(8,128)(4,1)S(1)} %broadcast_and_fusion.2, bf16[2,26,42,128]{3,0,2,1:T(2,128)(2,1)S(1)} %fusion.99), kind=kLoop, calls=%fused_computation.43 | loop fusion | flops 1284096 | bytes 1712964 | tf_op jit(solution)/shard_map/convert_element_type | solution.py:229
  63.8 1.7 %fusion.34 = bf16[20,2,36,128]{3,1,2,0:T(2,128)(2,1)S(1)} fusion(f32[20,2,36,128]{3,0,2,1:T(8,128)S(1)} %slice.159, pred[20,36]{1,0:T(8,128)(4,1)S(1)} %broadcast_and_fusion.3, bf16[20,2,36,128]{3,0,2,1:T(8,128)(2,1)S(1)} %slice.166), kind=kLoop, calls=%fused_computation.56 | loop fusion | flops 1290240 | bytes 1475280 | tf_op jit(solution)/shard_map/convert_element_type | solution.py:229
  67.9 2.3 %fusion.56 = bf16[2,18,34,128]{3,0,2,1:T(2,128)(2,1)S(1)} fusion(f32[18,2,34,128]{3,0,2,1:T(8,128)S(1)} %slice.169, pred[18,34]{1,0:T(8,128)(4,1)S(1)} %broadcast_and_fusion.4, bf16[2,22,38,128]{3,0,2,1:T(2,128)(2,1)S(1)} %fusion.98), kind=kLoop, calls=%fused_computation.84 | loop fusion | flops 940032 | bytes 1253988 | tf_op jit(solution)/shard_map/convert_element_type | solution.py:229
  70.2 1.8 %fusion.52 = f32[3,3,128,128]{3,2,1,0:T(8,128)S(1)} fusion(bf16[2,28,44,128]{3,2,0,1:T(8,128)(2,1)S(1)} %copy-done.9, bf16[2,18,34,128]{3,0,2,1:T(2,128)(2,1)S(1)} %fusion.56), kind=kOutput, calls=%fused_computation.79 | convolution fusion | flops 301989888 | bytes 1540096 | tf_op jit(solution)/shard_map/transpose | solution.py:82
  74.1 1.8 %fusion.73 = f32[3,3,128,128]{3,2,1,0:T(8,128)S(1)} fusion(bf16[22,2,38,128]{3,1,2,0:T(2,128)(2,1)S(1)} %fusion.19, bf16[2,20,36,128]{3,0,2,1:T(2,128)(2,1)S(1)} %bitcast.156), kind=kOutput, calls=%fused_computation.141 | convolution fusion | flops 301989888 | bytes 1280000 | tf_op jit(solution)/shard_map/transpose | solution.py:82
  75.9 1.8 %multiply_convert_fusion = (bf16[3,3,128,128]{3,2,1,0:T(8,128)(2,1)S(1)}, f32[3,3,128,128]{3,2,1,0:T(8,128)S(1)}) fusion(f32[3,3,128,128]{3,2,1,0:T(8,128)S(1)} %fusion.73, pred[]{:T(512)S(6)} %eq.19, bf16[26,2,42,128]{3,1,2,0:T(2,128)(2,1)S(1)} %fusion.11, bf16[2,16,32,128]{3,2,0,1:T(8,128)(2,1)S(1)} %slice.183), kind=kOutput, calls=%fused_computation.87 | convolution fusion | flops 302432256 | bytes 2295809 | tf_op jit(solution)/shard_map/transpose | solution.py:82
  78.2 1.8 %multiply_convert_fusion.1 = (bf16[3,3,128,128]{3,2,1,0:T(8,128)(2,1)S(1)}, f32[3,3,128,128]{3,2,1,0:T(8,128)S(1)}) fusion(f32[3,3,128,128]{3,2,1,0:T(8,128)S(1)} %fusion.52, pred[]{:T(512)S(6)} %eq.19, bf16[2,22,38,128]{3,0,2,1:T(2,128)(2,1)S(1)} %fusion.22, bf16[2,28,44,128]{3,2,0,1:T(8,128)(2,1)S(1)} %get-tuple-element.13), kind=kOutput, calls=%fused_computation.89 | convolution fusion | flops 302432256 | bytes 2424833 | tf_op jit(solution)/shard_map/transpose | solution.py:82
  81.2 5.0 %collective-permute-start.15 = (bf16[73728]{0:T(1024)(128)(2,1)S(1)}, bf16[73728]{0:T(1024)(128)(2,1)S(1)}, u32[]{:S(2)}, u32[]{:S(2)}) collective-permute-start(bf16[73728]{0:T(1024)(128)(2,1)S(1)} %select_convert_fusion), channel_id=1, source_target_pairs={{0,4},{4,0},{8,12},{12,8},{1,5},{5,1},{9,13},{13,9},{2,6},{6,2},{1... | collective-permute-start | bytes 442376 | tf_op jit(solution)/shard_map/ppermute | solution.py:100
  86.8 4.0 %collective-permute-done.15 = bf16[73728]{0:T(1024)(128)(2,1)S(1)} collective-permute-done((bf16[73728]{0:T(1024)(128)(2,1)S(1)}, bf16[73728]{0:T(1024)(128)(2,1)S(1)}, u32[]{:S(2)}, u32[]{:S(2)}) %collective-permute-start.15) | collective-permute-done | bytes 147488 | tf_op jit(solution)/shard_map/ppermute | solution.py:100
  91.0 2.5 %collective-permute-start.16 = (bf16[36864]{0:T(1024)(128)(2,1)S(1)}, bf16[36864]{0:T(1024)(128)(2,1)S(1)}, u32[]{:S(2)}, u32[]{:S(2)}) collective-permute-start(bf16[36864]{0:T(1024)(128)(2,1)S(1)} %select_convert_fusion.4), channel_id=1, source_target_pairs={{0,1},{1,0},{2,3},{3,2},{4,5},{5,4},{6,7},{7,6},{8,9},{9,8},{10,11... | collective-permute-start | bytes 221192 | tf_op jit(solution)/shard_map/ppermute | solution.py:100
  93.9 2.5 %collective-permute-start.9 = (bf16[36864]{0:T(1024)(128)(2,1)S(1)}, bf16[36864]{0:T(1024)(128)(2,1)S(1)}, u32[]{:S(2)}, u32[]{:S(2)}) collective-permute-start(bf16[36864]{0:T(1024)(128)(2,1)S(1)} %select_convert_fusion.6), channel_id=1, source_target_pairs={{0,1},{1,0},{2,3},{3,2},{4,5},{5,4},{6,7},{7,6},{8,9},{9,8},{10,11... | collective-permute-start | bytes 221192 | tf_op jit(solution)/shard_map/ppermute | solution.py:100
  96.5 3.7 %collective-permute-start.17 = (bf16[36864]{0:T(1024)(128)(2,1)S(1)}, bf16[36864]{0:T(1024)(128)(2,1)S(1)}, u32[]{:S(2)}, u32[]{:S(2)}) collective-permute-start(bf16[36864]{0:T(1024)(128)(2,1)S(1)} %add_convert_fusion.2), channel_id=1, source_target_pairs={{0,8},{4,12},{8,0},{12,4},{1,9},{5,13},{9,1},{13,5},{2,10},{6,14},... | collective-permute-start | bytes 221192 | tf_op jit(solution)/shard_map/ppermute | solution.py:100
  100.3 2.3 %collective-permute-start.10 = (bf16[36864]{0:T(1024)(128)(2,1)S(1)}, bf16[36864]{0:T(1024)(128)(2,1)S(1)}, u32[]{:S(2)}, u32[]{:S(2)}) collective-permute-start(bf16[36864]{0:T(1024)(128)(2,1)S(1)} %add_convert_fusion.5), channel_id=1, source_target_pairs={{0,8},{4,12},{8,0},{12,4},{1,9},{5,13},{9,1},{13,5},{2,10},{6,14},... | collective-permute-start | bytes 221192 | tf_op jit(solution)/shard_map/ppermute | solution.py:100
  103.0 2.7 %collective-permute-start.18 = (bf16[36864]{0:T(1024)(128)(2,1)S(1)}, bf16[36864]{0:T(1024)(128)(2,1)S(1)}, u32[]{:S(2)}, u32[]{:S(2)}) collective-permute-start(bf16[36864]{0:T(1024)(128)(2,1)S(1)} %add_convert_fusion.1), channel_id=1, source_target_pairs={{0,2},{1,3},{2,0},{3,1},{4,6},{5,7},{6,4},{7,5},{8,10},{9,11},{10,... | collective-permute-start | bytes 221192 | tf_op jit(solution)/shard_map/ppermute | solution.py:100
  105.7 2.3 %collective-permute-start.11 = (bf16[36864]{0:T(1024)(128)(2,1)S(1)}, bf16[36864]{0:T(1024)(128)(2,1)S(1)}, u32[]{:S(2)}, u32[]{:S(2)}) collective-permute-start(bf16[36864]{0:T(1024)(128)(2,1)S(1)} %add_convert_fusion.4), channel_id=1, source_target_pairs={{0,2},{1,3},{2,0},{3,1},{4,6},{5,7},{6,4},{7,5},{8,10},{9,11},{10,... | collective-permute-start | bytes 221192 | tf_op jit(solution)/shard_map/ppermute | solution.py:100
  108.0 2.3 %collective-permute-done.18 = bf16[36864]{0:T(1024)(128)(2,1)S(1)} collective-permute-done((bf16[36864]{0:T(1024)(128)(2,1)S(1)}, bf16[36864]{0:T(1024)(128)(2,1)S(1)}, u32[]{:S(2)}, u32[]{:S(2)}) %collective-permute-start.18) | collective-permute-done | bytes 73760 | tf_op jit(solution)/shard_map/ppermute | solution.py:100
  111.1 1.7 %collective-permute-start.12 = (bf16[36864]{0:T(1024)(128)(2,1)S(1)}, bf16[36864]{0:T(1024)(128)(2,1)S(1)}, u32[]{:S(2)}, u32[]{:S(2)}) collective-permute-start(bf16[36864]{0:T(1024)(128)(2,1)S(1)} %add_convert_fusion.3), channel_id=1, source_target_pairs={{0,1},{1,0},{2,3},{3,2},{4,5},{5,4},{6,7},{7,6},{8,9},{9,8},{10,11... | collective-permute-start | bytes 221192 | tf_op jit(solution)/shard_map/ppermute | solution.py:100
  112.8 1.9 %collective-permute-done.19 = bf16[36864]{0:T(1024)(128)(2,1)S(1)} collective-permute-done((bf16[36864]{0:T(1024)(128)(2,1)S(1)}, bf16[36864]{0:T(1024)(128)(2,1)S(1)}, u32[]{:S(2)}, u32[]{:S(2)}) %collective-permute-start.19) | collective-permute-done | bytes 73760 | tf_op jit(solution)/shard_map/ppermute | solution.py:100
  114.8 1.6 %collective-permute-start.20 = (bf16[73728]{0:T(1024)(128)(2,1)S(1)}, bf16[73728]{0:T(1024)(128)(2,1)S(1)}, u32[]{:S(2)}, u32[]{:S(2)}) collective-permute-start(bf16[73728]{0:T(1024)(128)(2,1)S(1)} %maximum_select_fusion.4), channel_id=1, source_target_pairs={{0,4},{4,0},{8,12},{12,8},{1,5},{5,1},{9,13},{13,9},{2,6},{6,2},{1... | collective-permute-start | bytes 442376 | tf_op jit(solution)/shard_map/ppermute | solution.py:100
  117.1 2.9 %collective-permute-done.20 = bf16[73728]{0:T(1024)(128)(2,1)S(1)} collective-permute-done((bf16[73728]{0:T(1024)(128)(2,1)S(1)}, bf16[73728]{0:T(1024)(128)(2,1)S(1)}, u32[]{:S(2)}, u32[]{:S(2)}) %collective-permute-start.20) | collective-permute-done | bytes 147488 | tf_op jit(solution)/shard_map/ppermute | solution.py:100
  (176 shorter events, 36.9 us)
Async XLA Ops:
  0.6 2.5 %copy-start = (bf16[4,16,32,128]{3,2,1,0:T(8,128)(2,1)S(1)}, bf16[4,16,32,128]{3,2,1,0:T(8,128)(2,1)}, u32[]{:S(2)}) copy-start(bf16[4,16,32,128]{3,2,1,0:T(8,128)(2,1)} %param.6) | copy-start | bytes 1572868
  0.6 1.8 %copy-start.14 = (bf16[2,3,3,128,128]{4,3,2,1,0:T(8,128)(2,1)S(1)}, bf16[2,3,3,128,128]{4,3,2,1,0:T(8,128)(2,1)}, u32[]{:S(2)}) copy-start(bf16[2,3,3,128,128]{4,3,2,1,0:T(8,128)(2,1)} %param.5) | copy-start | bytes 1769476
  0.7 1.9 %copy-start.17 = (s32[4]{0:T(128)S(1)}, s32[4]{0:T(128)}, u32[]{:S(2)}) copy-start(s32[4]{0:T(128)} %param.7) | copy-start | bytes 52
  1.9 2.1 %collective-permute-start = (bf16[2,16,32,128]{3,2,0,1:T(8,128)(2,1)S(1)}, bf16[2,16,32,128]{3,2,0,1:T(8,128)(2,1)S(1)}, u32[]{:S(2)}, u32[]{:S(2)}) collective-permute-start(bf16[2,16,32,128]{3,2,0,1:T(8,128)(2,1)S(1)} %bitcast.163), channel_id=1, source_target_pairs={{0,16},{16,0},{1,17},{17,1},{2,18},{18,2},{3,19},{19,3},{4,20},{20... | collective-permute-start | bytes 786440 | tf_op jit(solution)/shard_map/ppermute | solution.py:246
  2.4 20.9 %collective-permute-start.5 = (bf16[2,3,3,128,128]{4,3,2,1,0:T(8,128)(2,1)S(1)}, bf16[2,3,3,128,128]{4,3,2,1,0:T(8,128)(2,1)}, u32[]{:S(2)}, u32[]{:S(2)}) collective-permute-start(bf16[2,3,3,128,128]{4,3,2,1,0:T(8,128)(2,1)S(1)} %copy-done.14), channel_id=1, source_target_pairs={{0,16},{16,0},{1,17},{17,1},{2,18},{18,2},{3,19},{19,3},{4,20},{20... | collective-permute-start | bytes 1769480 | tf_op jit(solution)/shard_map/ppermute | solution.py:246
  4.1 12.7 %collective-permute-start.2 = (bf16[6,6,32,128]{3,2,0,1:T(8,128)(2,1)S(1)}, bf16[6,6,32,128]{3,2,0,1:T(8,128)(2,1)S(1)}, u32[]{:S(2)}, u32[]{:S(2)}) collective-permute-start(bf16[6,6,32,128]{3,2,0,1:T(8,128)(2,1)S(1)} %get-tuple-element.19), channel_id=1, source_target_pairs={{4,0},{5,1},{6,2},{7,3},{8,4},{9,5},{10,6},{11,7},{12,8},{13,9},{1... | collective-permute-start | bytes 884744 | tf_op jit(solution)/shard_map/ppermute | solution.py:43
  5.4 11.9 %collective-permute-start.1 = (bf16[6,6,32,128]{3,2,0,1:T(8,128)(2,1)S(1)}, bf16[6,6,32,128]{3,2,0,1:T(8,128)(2,1)S(1)}, u32[]{:S(2)}, u32[]{:S(2)}) collective-permute-start(bf16[6,6,32,128]{3,2,0,1:T(8,128)(2,1)S(1)} %get-tuple-element.18), channel_id=1, source_target_pairs={{0,4},{1,5},{2,6},{3,7},{4,8},{5,9},{6,10},{7,11},{8,12},{9,13},{1... | collective-permute-start | bytes 884744 | tf_op jit(solution)/shard_map/ppermute | solution.py:43
  16.8 13.0 %copy-start.1 = (bf16[6,6,32,128]{3,2,0,1:T(8,128)(2,1)}, bf16[6,6,32,128]{3,2,0,1:T(8,128)(2,1)S(1)}, u32[]{:S(2)}) copy-start(bf16[6,6,32,128]{3,2,0,1:T(8,128)(2,1)S(1)} %collective-permute-done.2) | copy-start | bytes 884740
  17.3 12.4 %copy-start.3 = (bf16[6,6,32,128]{3,2,0,1:T(8,128)(2,1)}, bf16[6,6,32,128]{3,2,0,1:T(8,128)(2,1)S(1)}, u32[]{:S(2)}) copy-start(bf16[6,6,32,128]{3,2,0,1:T(8,128)(2,1)S(1)} %collective-permute-done.1) | copy-start | bytes 884740
  17.5 11.1 %collective-permute-start.4 = (bf16[6,28,6,128]{3,2,0,1:T(8,128)(2,1)S(1)}, bf16[6,28,6,128]{3,2,0,1:T(8,128)(2,1)S(1)}, u32[]{:S(2)}, u32[]{:S(2)}) collective-permute-start(bf16[6,28,6,128]{3,2,0,1:T(8,128)(2,1)S(1)} %get-tuple-element.15), channel_id=1, source_target_pairs={{1,0},{2,1},{3,2},{5,4},{6,5},{7,6},{9,8},{10,9},{11,10},{13,12},{... | collective-permute-start | bytes 774152 | tf_op jit(solution)/shard_map/ppermute | solution.py:43
  18.8 11.0 %collective-permute-start.3 = (bf16[6,28,6,128]{3,2,0,1:T(8,128)(2,1)S(1)}, bf16[6,28,6,128]{3,2,0,1:T(8,128)(2,1)S(1)}, u32[]{:S(2)}, u32[]{:S(2)}) collective-permute-start(bf16[6,28,6,128]{3,2,0,1:T(8,128)(2,1)S(1)} %get-tuple-element.14), channel_id=1, source_target_pairs={{0,1},{1,2},{2,3},{4,5},{5,6},{6,7},{8,9},{9,10},{10,11},{12,13},{... | collective-permute-start | bytes 774152 | tf_op jit(solution)/shard_map/ppermute | solution.py:43
  24.5 9.2 %copy-start.7 = (bf16[2,3,3,128,128]{4,3,2,1,0:T(8,128)(2,1)}, bf16[2,3,3,128,128]{4,3,2,1,0:T(8,128)(2,1)S(1)}, u32[]{:S(2)}) copy-start(bf16[2,3,3,128,128]{4,3,2,1,0:T(8,128)(2,1)S(1)} %get-tuple-element.17) | copy-start | bytes 1769476
  28.6 2.8 %copy-start.10 = (bf16[6,28,6,128]{3,2,0,1:T(8,128)(2,1)}, bf16[6,28,6,128]{3,2,0,1:T(8,128)(2,1)S(1)}, u32[]{:S(2)}) copy-start(bf16[6,28,6,128]{3,2,0,1:T(8,128)(2,1)S(1)} %collective-permute-done.4) | copy-start | bytes 774148
  29.8 1.7 %copy-start.12 = (bf16[6,28,6,128]{3,2,0,1:T(8,128)(2,1)}, bf16[6,28,6,128]{3,2,0,1:T(8,128)(2,1)S(1)}, u32[]{:S(2)}) copy-start(bf16[6,28,6,128]{3,2,0,1:T(8,128)(2,1)S(1)} %collective-permute-done.3) | copy-start | bytes 774148
  32.4 1.4 %copy-start.23 = (pred[16,6]{0,1:T(8,128)(4,1)S(1)}, pred[16,6]{0,1:T(8,128)(4,1)}, u32[]{:S(2)}) copy-start(pred[16,6]{0,1:T(8,128)(4,1)} %constant.165) | copy-start | bytes 292
  35.9 3.5 %copy-start.9 = (bf16[2,28,44,128]{3,2,0,1:T(8,128)(2,1)S(1)}, bf16[2,28,44,128]{3,2,0,1:T(8,128)(2,1)}, u32[]{:S(2)}) copy-start(bf16[2,28,44,128]{3,2,0,1:T(8,128)(2,1)} %get-tuple-element.12) | copy-start | bytes 1892356
  50.9 1.2 %copy-start.13 = (bf16[6,28,6,128]{3,2,0,1:T(8,128)(2,1)S(1)}, bf16[6,28,6,128]{3,2,0,1:T(8,128)(2,1)}, u32[]{:S(2)}) copy-start(bf16[6,28,6,128]{3,2,0,1:T(8,128)(2,1)} %copy-done.12) | copy-start | bytes 774148
  74.0 6.1 %collective-permute-start.6 = (bf16[2,16,32,128]{3,2,0,1:T(8,128)(2,1)S(1)}, bf16[2,16,32,128]{3,2,0,1:T(8,128)(2,1)S(1)}, u32[]{:S(2)}, u32[]{:S(2)}) collective-permute-start(bf16[2,16,32,128]{3,2,0,1:T(8,128)(2,1)S(1)} %get-tuple-element.21), channel_id=1, source_target_pairs={{0,16},{16,0},{1,17},{17,1},{2,18},{18,2},{3,19},{19,3},{4,20},{20... | collective-permute-start | bytes 786440 | tf_op jit(solution)/shard_map/ppermute | solution.py:246
  77.7 3.3 %collective-permute-start.14 = (bf16[3,3,128,128]{3,2,1,0:T(8,128)(2,1)S(1)}, bf16[3,3,128,128]{3,2,1,0:T(8,128)(2,1)S(1)}, u32[]{:S(2)}, u32[]{:S(2)}) collective-permute-start(bf16[3,3,128,128]{3,2,1,0:T(8,128)(2,1)S(1)} %get-tuple-element.26), channel_id=1, source_target_pairs={{0,16},{16,0},{1,17},{17,1},{2,18},{18,2},{3,19},{19,3},{4,20},{20... | collective-permute-start | bytes 884744 | tf_op jit(solution)/shard_map/ppermute | solution.py:246
  80.0 6.2 %collective-permute-start.7 = (bf16[3,3,128,128]{3,2,1,0:T(8,128)(2,1)S(1)}, bf16[3,3,128,128]{3,2,1,0:T(8,128)(2,1)S(1)}, u32[]{:S(2)}, u32[]{:S(2)}) collective-permute-start(bf16[3,3,128,128]{3,2,1,0:T(8,128)(2,1)S(1)} %get-tuple-element.28), channel_id=1, source_target_pairs={{0,16},{16,0},{1,17},{17,1},{2,18},{18,2},{3,19},{19,3},{4,20},{20... | collective-permute-start | bytes 884744 | tf_op jit(solution)/shard_map/ppermute | solution.py:246
  81.2 9.7 %collective-permute-start.15 = (bf16[73728]{0:T(1024)(128)(2,1)S(1)}, bf16[73728]{0:T(1024)(128)(2,1)S(1)}, u32[]{:S(2)}, u32[]{:S(2)}) collective-permute-start(bf16[73728]{0:T(1024)(128)(2,1)S(1)} %select_convert_fusion), channel_id=1, source_target_pairs={{0,4},{4,0},{8,12},{12,8},{1,5},{5,1},{9,13},{13,9},{2,6},{6,2},{1... | collective-permute-start | bytes 442376 | tf_op jit(solution)/shard_map/ppermute | solution.py:100
  86.3 7.5 %collective-permute-start.8 = (bf16[73728]{0:T(1024)(128)(2,1)S(1)}, bf16[73728]{0:T(1024)(128)(2,1)S(1)}, u32[]{:S(2)}, u32[]{:S(2)}) collective-permute-start(bf16[73728]{0:T(1024)(128)(2,1)S(1)} %select_convert_fusion.2), channel_id=1, source_target_pairs={{0,4},{4,0},{8,12},{12,8},{1,5},{5,1},{9,13},{13,9},{2,6},{6,2},{1... | collective-permute-start | bytes 442376 | tf_op jit(solution)/shard_map/ppermute | solution.py:100
  91.0 5.5 %collective-permute-start.16 = (bf16[36864]{0:T(1024)(128)(2,1)S(1)}, bf16[36864]{0:T(1024)(128)(2,1)S(1)}, u32[]{:S(2)}, u32[]{:S(2)}) collective-permute-start(bf16[36864]{0:T(1024)(128)(2,1)S(1)} %select_convert_fusion.4), channel_id=1, source_target_pairs={{0,1},{1,0},{2,3},{3,2},{4,5},{5,4},{6,7},{7,6},{8,9},{9,8},{10,11... | collective-permute-start | bytes 221192 | tf_op jit(solution)/shard_map/ppermute | solution.py:100
  93.9 6.3 %collective-permute-start.9 = (bf16[36864]{0:T(1024)(128)(2,1)S(1)}, bf16[36864]{0:T(1024)(128)(2,1)S(1)}, u32[]{:S(2)}, u32[]{:S(2)}) collective-permute-start(bf16[36864]{0:T(1024)(128)(2,1)S(1)} %select_convert_fusion.6), channel_id=1, source_target_pairs={{0,1},{1,0},{2,3},{3,2},{4,5},{5,4},{6,7},{7,6},{8,9},{9,8},{10,11... | collective-permute-start | bytes 221192 | tf_op jit(solution)/shard_map/ppermute | solution.py:100
  96.5 6.4 %collective-permute-start.17 = (bf16[36864]{0:T(1024)(128)(2,1)S(1)}, bf16[36864]{0:T(1024)(128)(2,1)S(1)}, u32[]{:S(2)}, u32[]{:S(2)}) collective-permute-start(bf16[36864]{0:T(1024)(128)(2,1)S(1)} %add_convert_fusion.2), channel_id=1, source_target_pairs={{0,8},{4,12},{8,0},{12,4},{1,9},{5,13},{9,1},{13,5},{2,10},{6,14},... | collective-permute-start | bytes 221192 | tf_op jit(solution)/shard_map/ppermute | solution.py:100
  100.3 5.4 %collective-permute-start.10 = (bf16[36864]{0:T(1024)(128)(2,1)S(1)}, bf16[36864]{0:T(1024)(128)(2,1)S(1)}, u32[]{:S(2)}, u32[]{:S(2)}) collective-permute-start(bf16[36864]{0:T(1024)(128)(2,1)S(1)} %add_convert_fusion.5), channel_id=1, source_target_pairs={{0,8},{4,12},{8,0},{12,4},{1,9},{5,13},{9,1},{13,5},{2,10},{6,14},... | collective-permute-start | bytes 221192 | tf_op jit(solution)/shard_map/ppermute | solution.py:100
  103.0 7.3 %collective-permute-start.18 = (bf16[36864]{0:T(1024)(128)(2,1)S(1)}, bf16[36864]{0:T(1024)(128)(2,1)S(1)}, u32[]{:S(2)}, u32[]{:S(2)}) collective-permute-start(bf16[36864]{0:T(1024)(128)(2,1)S(1)} %add_convert_fusion.1), channel_id=1, source_target_pairs={{0,2},{1,3},{2,0},{3,1},{4,6},{5,7},{6,4},{7,5},{8,10},{9,11},{10,... | collective-permute-start | bytes 221192 | tf_op jit(solution)/shard_map/ppermute | solution.py:100
  105.7 5.4 %collective-permute-start.11 = (bf16[36864]{0:T(1024)(128)(2,1)S(1)}, bf16[36864]{0:T(1024)(128)(2,1)S(1)}, u32[]{:S(2)}, u32[]{:S(2)}) collective-permute-start(bf16[36864]{0:T(1024)(128)(2,1)S(1)} %add_convert_fusion.4), channel_id=1, source_target_pairs={{0,2},{1,3},{2,0},{3,1},{4,6},{5,7},{6,4},{7,5},{8,10},{9,11},{10,... | collective-permute-start | bytes 221192 | tf_op jit(solution)/shard_map/ppermute | solution.py:100
  110.3 4.4 %collective-permute-start.19 = (bf16[36864]{0:T(1024)(128)(2,1)S(1)}, bf16[36864]{0:T(1024)(128)(2,1)S(1)}, u32[]{:S(2)}, u32[]{:S(2)}) collective-permute-start(bf16[36864]{0:T(1024)(128)(2,1)S(1)} %add_convert_fusion), channel_id=1, source_target_pairs={{0,1},{1,0},{2,3},{3,2},{4,5},{5,4},{6,7},{7,6},{8,9},{9,8},{10,11... | collective-permute-start | bytes 221192 | tf_op jit(solution)/shard_map/ppermute | solution.py:100
  111.1 5.2 %collective-permute-start.12 = (bf16[36864]{0:T(1024)(128)(2,1)S(1)}, bf16[36864]{0:T(1024)(128)(2,1)S(1)}, u32[]{:S(2)}, u32[]{:S(2)}) collective-permute-start(bf16[36864]{0:T(1024)(128)(2,1)S(1)} %add_convert_fusion.3), channel_id=1, source_target_pairs={{0,1},{1,0},{2,3},{3,2},{4,5},{5,4},{6,7},{7,6},{8,9},{9,8},{10,11... | collective-permute-start | bytes 221192 | tf_op jit(solution)/shard_map/ppermute | solution.py:100
  114.8 5.2 %collective-permute-start.20 = (bf16[73728]{0:T(1024)(128)(2,1)S(1)}, bf16[73728]{0:T(1024)(128)(2,1)S(1)}, u32[]{:S(2)}, u32[]{:S(2)}) collective-permute-start(bf16[73728]{0:T(1024)(128)(2,1)S(1)} %maximum_select_fusion.4), channel_id=1, source_target_pairs={{0,4},{4,0},{8,12},{12,8},{1,5},{5,1},{9,13},{13,9},{2,6},{6,2},{1... | collective-permute-start | bytes 442376 | tf_op jit(solution)/shard_map/ppermute | solution.py:100
  116.4 5.2 %collective-permute-start.13 = (bf16[73728]{0:T(1024)(128)(2,1)S(1)}, bf16[73728]{0:T(1024)(128)(2,1)S(1)}, u32[]{:S(2)}, u32[]{:S(2)}) collective-permute-start(bf16[73728]{0:T(1024)(128)(2,1)S(1)} %maximum_select_fusion.3), channel_id=1, source_target_pairs={{0,4},{4,0},{8,12},{12,8},{1,5},{5,1},{9,13},{13,9},{2,6},{6,2},{1... | collective-permute-start | bytes 442376 | tf_op jit(solution)/shard_map/ppermute | solution.py:100
  (13 other events, 13.2 us)
